TPU v7x, 256 devices: a whole 4x4x8 slice. The times are simulated.
256 devices in a mesh: region: 256 (over z, x, y, core).
Axes of the slice: x: 4, y: 4, z: 8, core: 2. Of those that a mesh axis runs over, the one named last changes fastest.
Arguments:
- features: bfloat16 [8, 131072, 256], P(None, 'region'), may hold values from -6 to 6
- line_mask: int32 [131072, 512], P('region'), may hold values 0 or 1
- send_rows: int32 [1024, 128], P('region'), may hold values from 0 to 511
- attach_rows: int32 [1024, 128], P('region'), may hold values from 0 to 511
- tile_count: int32 [1024], P('region'), may hold values from 32 to 128, as said below
- self_weight: bfloat16 [2, 256, 256], replicated, may hold values from -0.375 to 0.375
- neigh_weight: bfloat16 [2, 256, 256], replicated, may hold values from -0.375 to 0.375
- layer_bias: float32 [2, 256], replicated, may hold values from -3 to 3
- readout: bfloat16 [2, 256], replicated, may hold values from -0.375 to 0.375
- load_table: float32 [16, 2, 131072], P(None, None, 'region')
- scenario_profile: int32 [8], replicated, may hold values from 0 to 15
- diag_admit: float32 [131072], P('region'), may hold values from 6 to 10
- conductance: float32 [131072], P('region'), may hold values from 0.5 to 1.5
- susceptance: float32 [131072], P('region'), may hold values from -3 to -1
- load_coeff: float32 [131072], P('region'), may hold values from 0.5 to 2.5
- region_inverse: bfloat16 [262144, 1024], P('region')
Outputs:
- voltage: float32 [8, 2, 131072], P(None, None, 'region')
Inputs may be any that keep to these rules, and one draw needn't show every extreme that they name: `tile_count`: rows of a tile at or beyond its count are padding and carry nothing; counts are uneven across tiles.
All inputs are finite; a program needn't handle non-finite values. No bound on the sum of `line_mask` on one device may be relied on, other than what follows from the above.
Results may differ from a plain program's by a relative error of at most 0.023.
Values may be sent and summed in bfloat16 or wider, within the bound.
No kernel may reach another device: no remote copies, remote signals or barrier semaphores. Data moves between devices by JAX's collectives and lax.ppermute only.
A program may use at most 128 MiB of HBM per device.

v0:
```python
import jax
import jax.numpy as jnp
from jax import lax
from jax.sharding import PartitionSpec as P

RW = 16
NEWTON = 2
SWEEPS = 3


trust_radius = 8.0
highest = lax.Precision.HIGHEST


def from_behind(value, axis, steps):
    count = lax.axis_size(axis)
    first, last = (max(0, -steps), min(count, count - steps))
    return lax.ppermute(value, axis, [(source, source + steps) for source in range(first, last)])


def rotate(conduct, suscept, beside, axis):
    real_part = jnp.take(beside, 0, axis=axis)
    imag_part = jnp.take(beside, 1, axis=axis)
    return jnp.stack(
        [conduct * real_part - suscept * imag_part, suscept * real_part + conduct * imag_part],
        axis=axis,
    )


def local(
    features,
    line_mask,
    send_rows,
    attach_rows,
    tile_count,
    self_weight,
    neigh_weight,
    layer_bias,
    readout,
    load_table,
    scenario_profile,
    diag_admit,
    conductance,
    susceptance,
    load_coeff,
    region_inverse,
):
    scenarios, buses, width = features.shape
    neighbours, tile_size = send_rows.shape
    offsets = (1, -1, RW, -RW)
    senders = send_rows.reshape(-1)
    live_rows = (
        lax.broadcasted_iota(jnp.int32, (neighbours, tile_size), 1) < tile_count[:, None]
    ).reshape(-1)
    matches = attach_rows.reshape(-1)[:, None] == lax.broadcasted_iota(
        jnp.int32, (neighbours * tile_size, buses), 1
    )
    scatter_half = matches.astype(jnp.bfloat16)
    scatter_full = matches.astype(jnp.float32)
    mask_half = line_mask.astype(jnp.bfloat16)
    mask_full = line_mask.astype(jnp.float32)
    hidden = features
    for number in range(self_weight.shape[0]):
        tile_rows = jnp.take(hidden, senders, axis=1)
        tile_rows = jnp.where(live_rows[None, :, None], tile_rows, jnp.zeros((), jnp.bfloat16))
        tile_rows = tile_rows.reshape(scenarios, neighbours, tile_size, width)
        arrived = []
        for neighbour in range(neighbours):
            outgoing = tile_rows[:, neighbour]
            arrived.append(from_behind(outgoing, "region", offsets[neighbour]))
        incoming = jnp.concatenate(arrived, axis=1)
        inside = jnp.einsum("ij,sjh->sih", mask_half, hidden, preferred_element_type=jnp.float32)
        border = jnp.einsum(
            "jb,sjh->sbh", scatter_half, incoming, preferred_element_type=jnp.float32
        )
        gathered = (0.25 * (inside + border)).astype(jnp.bfloat16)
        summed = jnp.einsum(
            "sbh,hk->sbk", hidden, self_weight[number], preferred_element_type=jnp.float32
        )
        summed = (
            summed
            + jnp.einsum(
                "sbh,hk->sbk", gathered, neigh_weight[number], preferred_element_type=jnp.float32
            )
            + layer_bias[number]
        )
        hidden = (hidden.astype(jnp.float32) + jax.nn.silu(summed)).astype(jnp.bfloat16)
    flat_start = jnp.array([1.0, 0.0], dtype=jnp.float32)[None, :, None]
    voltage = (
        jnp.einsum("sbh,ch->scb", hidden, readout, preferred_element_type=jnp.float32) + flat_start
    )
    choose = (
        scenario_profile[:, None]
        == lax.broadcasted_iota(jnp.int32, (scenarios, load_table.shape[0]), 1)
    ).astype(jnp.float32)
    injection = jnp.einsum("sp,pcb->scb", choose, load_table, precision=highest)
    bus_total = buses * lax.axis_size("region")

    def boundary(values):
        tile_rows = jnp.take(values, senders, axis=2)
        tile_rows = jnp.where(live_rows[None, None, :], tile_rows, jnp.zeros((), jnp.float32))
        tile_rows = tile_rows.reshape(scenarios, 2, neighbours, tile_size)
        arrived = [
            from_behind(tile_rows[:, :, neighbour], "region", offsets[neighbour])
            for neighbour in range(neighbours)
        ]
        incoming = jnp.concatenate(arrived, axis=2)
        return jnp.einsum("scj,jb->scb", incoming, scatter_full, precision=highest)

    for newton in range(NEWTON):
        beside = jnp.einsum("ij,scj->sci", mask_full, voltage, precision=highest) + boundary(
            voltage
        )
        magnitude = voltage[:, 0:1] ** 2 + voltage[:, 1:2] ** 2
        residual = (
            diag_admit * voltage
            - rotate(conductance, susceptance, beside, 1)
            + load_coeff * magnitude * voltage
            - injection
        )
        squares = lax.psum(jnp.sum(residual * residual, axis=(1, 2)), "region")
        damping = jnp.minimum(1.0, trust_radius / jnp.sqrt(squares / (2 * bus_total) + 1e-06))
        update = jnp.zeros_like(voltage)
        for sweep_number in range(SWEEPS):
            forcing = -residual
            if sweep_number > 0:
                forcing = forcing + rotate(conductance, susceptance, boundary(update), 1)
            forcing = forcing.reshape(scenarios, 2 * buses).astype(jnp.bfloat16)
            update = jnp.dot(forcing, region_inverse, preferred_element_type=jnp.float32).reshape(
                scenarios, 2, buses
            )
        voltage = voltage + damping[:, None, None] * update
    return voltage


def solution(mesh):
    in_specs = (
        P(None, "region", None),
        P("region", None),
        P("region", None),
        P("region", None),
        P("region"),
        P(),
        P(),
        P(),
        P(),
        P(None, None, "region"),
        P(),
        P("region"),
        P("region"),
        P("region"),
        P("region"),
        P("region", None),
    )
    out_specs = P(None, None, "region")
    return jax.shard_map(local, mesh=mesh, in_specs=in_specs, out_specs=out_specs, check_vma=False)
```

profile of v0, /device:TPU:4, one launch (start us, length us, event | category | flops | bytes accessed | tf_op | source)
XLA Modules:
  0.0 465.9 jit_solution(2789442088396616224)
XLA Ops:
  2.1 7.8 %gather_fusion = bf16[512,8,256]{2,0,1:T(8,128)(2,1)S(1)} fusion(bf16[8,512,256]{2,1,0:T(8,128)(2,1)} %param.25, s32[1024]{0:T(1024)S(1)} %pad_clamp_fusion), kind=kCustom, calls=%fused_computation.clone | custom fusion | bytes 4196352 | tf_op jit(solution)/shard_map/jit(_take)/gather | solution.py:64
  17.6 5.7 %collective-permute-start.1 = (bf16[8,128,256]{1,2,0:T(8,128)(2,1)}, bf16[8,128,256]{1,2,0:T(8,128)(2,1)}, u32[]{:S(2)}, u32[]{:S(2)}) collective-permute-start(bf16[8,128,256]{1,2,0:T(8,128)(2,1)} %bitcast.283), channel_id=1, source_target_pairs={{1,0},{2,1},{3,2},{4,3},{5,4},{6,5},{7,6},{8,7},{9,8},{10,9},{11,1... | collective-permute-start | bytes 1572872 | tf_op jit(solution)/shard_map/ppermute | solution.py:18
  24.3 5.9 %collective-permute-start.2 = (bf16[8,128,256]{1,2,0:T(8,128)(2,1)}, bf16[8,128,256]{1,2,0:T(8,128)(2,1)}, u32[]{:S(2)}, u32[]{:S(2)}) collective-permute-start(bf16[8,128,256]{1,2,0:T(8,128)(2,1)} %bitcast.284), channel_id=1, source_target_pairs={{0,16},{1,17},{2,18},{3,19},{4,20},{5,21},{6,22},{7,23},{8,24},{9,... | collective-permute-start | bytes 1572872 | tf_op jit(solution)/shard_map/ppermute | solution.py:18
  31.3 2.6 collective-permute-start.3
  33.9 2.7 fusion.68
  36.6 4.0 copy.319
  40.6 3.3 fusion.50
  43.9 7.0 %collective-permute-done.2 = bf16[8,128,256]{1,2,0:T(8,128)(2,1)} collective-permute-done((bf16[8,128,256]{1,2,0:T(8,128)(2,1)}, bf16[8,128,256]{1,2,0:T(8,128)(2,1)}, u32[]{:S(2)}, u32[]{:S(2)}) %collective-permute-start.2) | collective-permute-done | bytes 524320 | tf_op jit(solution)/shard_map/ppermute | solution.py:18
  51.0 8.3 %add_convert_fusion.1 = bf16[8,512,256]{2,1,0:T(8,128)(2,1)} fusion(f32[8,512,256]{2,1,0:T(8,128)} %fusion.68, bf16[8,512,256]{2,1,0:T(8,128)(2,1)S(1)} %copy-done.1, f32[256]{0:T(256)S(1)} %bitcast.320, f32[8,256,512]{2,1,0:T(8,128)} %fusion.50, bf16[8,128,256]{1,2,0:T(8,128)(2,1)} %collective-permute-done.3, ...), kind=kOutput, calls=%fused_computation.10 | convolution fusion | flops 1631846400 | bytes 14814208 | tf_op jit(solution)/shard_map/sbh,hk->sbk/dot_general | solution.py:82
  59.2 2.8 copy.233
  62.0 2.7 gather_fusion.1
  68.3 2.2 copy.324
  74.5 5.7 %collective-permute-start.5 = (bf16[8,128,256]{1,2,0:T(8,128)(2,1)}, bf16[8,128,256]{1,2,0:T(8,128)(2,1)}, u32[]{:S(2)}, u32[]{:S(2)}) collective-permute-start(bf16[8,128,256]{1,2,0:T(8,128)(2,1)} %bitcast.286), channel_id=1, source_target_pairs={{1,0},{2,1},{3,2},{4,3},{5,4},{6,5},{7,6},{8,7},{9,8},{10,9},{11,1... | collective-permute-start | bytes 1572872 | tf_op jit(solution)/shard_map/ppermute | solution.py:18
  82.3 6.8 %collective-permute-start.6 = (bf16[8,128,256]{1,2,0:T(8,128)(2,1)}, bf16[8,128,256]{1,2,0:T(8,128)(2,1)}, u32[]{:S(2)}, u32[]{:S(2)}) collective-permute-start(bf16[8,128,256]{1,2,0:T(8,128)(2,1)} %bitcast.287), channel_id=1, source_target_pairs={{0,16},{1,17},{2,18},{3,19},{4,20},{5,21},{6,22},{7,23},{8,24},{9,... | collective-permute-start | bytes 1572872 | tf_op jit(solution)/shard_map/ppermute | solution.py:18
  91.1 2.4 collective-permute-start.7
  93.6 2.7 fusion.65
  97.6 11.3 %collective-permute-done.6 = bf16[8,128,256]{1,2,0:T(8,128)(2,1)} collective-permute-done((bf16[8,128,256]{1,2,0:T(8,128)(2,1)}, bf16[8,128,256]{1,2,0:T(8,128)(2,1)}, u32[]{:S(2)}, u32[]{:S(2)}) %collective-permute-start.6) | collective-permute-done | bytes 524320 | tf_op jit(solution)/shard_map/ppermute | solution.py:18
  108.9 4.1 multiply_convert_fusion
  113.0 5.1 %fusion.17 = f32[8,512,2]{1,2,0:T(2,128)S(1)} fusion(f32[8,512,256]{2,1,0:T(8,128)} %fusion.65, bf16[8,512,256]{2,1,0:T(8,128)(2,1)S(1)} %copy-done.3, bf16[8,256,512]{2,1,0:T(8,128)(2,1)} %multiply_convert_fusion, f32[256]{0:T(256)S(1)} %bitcast.319, bf16[2,256,256]{2,1,0:T(8,128)(2,1)} %param.31, bf16[2,256]{1,0:T(2,128)(2,1)S(1)} %copy-done.17), kind=kOutput, calls=%fused_computation.31 | convolution fusion | flops 550502400 | bytes 8554496 | tf_op jit(solution)/shard_map/sbh,ch->scb/dot_general | solution.py:90
  120.8 3.3 gather_fusion.2
  124.1 3.5 bitcast_select_fusion.7
  129.9 5.4 %collective-permute-start.10 = (f32[8,2,128]{2,0,1:T(8,128)}, f32[8,2,128]{2,0,1:T(8,128)}, u32[]{:S(2)}, u32[]{:S(2)}) collective-permute-start(f32[8,2,128]{2,0,1:T(8,128)} %bitcast.296), channel_id=1, source_target_pairs={{0,16},{1,17},{2,18},{3,19},{4,20},{5,21},{6,22},{7,23},{8,24},{9,... | collective-permute-start | bytes 24584 | tf_op jit(solution)/shard_map/ppermute | solution.py:18
  136.9 2.5 collective-permute-start.11
  142.0 5.8 %collective-permute-start.9 = (f32[8,2,128]{2,0,1:T(8,128)S(1)}, f32[8,2,128]{2,0,1:T(8,128)S(1)}, u32[]{:S(2)}, u32[]{:S(2)}) collective-permute-start(f32[8,2,128]{2,0,1:T(8,128)S(1)} %bitcast.314), channel_id=1, source_target_pairs={{1,0},{2,1},{3,2},{4,3},{5,4},{6,5},{7,6},{8,7},{9,8},{10,9},{11,1... | collective-permute-start | bytes 24584 | tf_op jit(solution)/shard_map/ppermute | solution.py:18
  154.4 3.3 gather_fusion.3
  157.7 4.1 bitcast_select_fusion.6
  167.6 5.7 %collective-permute-start.13 = (f32[8,2,128]{2,0,1:T(8,128)}, f32[8,2,128]{2,0,1:T(8,128)}, u32[]{:S(2)}, u32[]{:S(2)}) collective-permute-start(f32[8,2,128]{2,0,1:T(8,128)} %bitcast.303), channel_id=1, source_target_pairs={{1,0},{2,1},{3,2},{4,3},{5,4},{6,5},{7,6},{8,7},{9,8},{10,9},{11,1... | collective-permute-start | bytes 24584 | tf_op jit(solution)/shard_map/ppermute | solution.py:18
  174.0 10.0 %collective-permute-start.14 = (f32[8,2,128]{2,0,1:T(8,128)}, f32[8,2,128]{2,0,1:T(8,128)S(1)}, u32[]{:S(2)}, u32[]{:S(2)}) collective-permute-start(f32[8,2,128]{2,0,1:T(8,128)} %bitcast.309), channel_id=1, source_target_pairs={{0,16},{1,17},{2,18},{3,19},{4,20},{5,21},{6,22},{7,23},{8,24},{9,... | collective-permute-start | bytes 24584 | tf_op jit(solution)/shard_map/ppermute | solution.py:18
  186.0 81.7 %psum.14 = f32[8]{0:T(128)} all-reduce(f32[8]{0:T(128)} %get-tuple-element.33), channel_id=1, replica_groups=mesh['region'=256] {'region'}, use_global_device_ids=true, to_apply=%region_1.0 | all-reduce | flops 8 | bytes 64 | tf_op jit(solution)/shard_map/psum | solution.py:121
  270.6 3.3 gather_fusion.4
  273.9 4.1 bitcast_select_fusion.5
  283.9 5.7 %collective-permute-start.17 = (f32[8,2,128]{2,0,1:T(8,128)}, f32[8,2,128]{2,0,1:T(8,128)}, u32[]{:S(2)}, u32[]{:S(2)}) collective-permute-start(f32[8,2,128]{2,0,1:T(8,128)} %bitcast.304), channel_id=1, source_target_pairs={{1,0},{2,1},{3,2},{4,3},{5,4},{6,5},{7,6},{8,7},{9,8},{10,9},{11,1... | collective-permute-start | bytes 24584 | tf_op jit(solution)/shard_map/ppermute | solution.py:18
  290.2 7.8 %collective-permute-start.18 = (f32[8,2,128]{2,0,1:T(8,128)}, f32[8,2,128]{2,0,1:T(8,128)S(1)}, u32[]{:S(2)}, u32[]{:S(2)}) collective-permute-start(f32[8,2,128]{2,0,1:T(8,128)} %bitcast.310), channel_id=1, source_target_pairs={{0,16},{1,17},{2,18},{3,19},{4,20},{5,21},{6,22},{7,23},{8,24},{9,... | collective-permute-start | bytes 24584 | tf_op jit(solution)/shard_map/ppermute | solution.py:18
  300.7 5.4 %collective-permute-done.19 = f32[8,2,128]{2,0,1:T(8,128)S(1)} collective-permute-done((f32[8,2,128]{2,0,1:T(8,128)S(1)}, f32[8,2,128]{2,0,1:T(8,128)S(1)}, u32[]{:S(2)}, u32[]{:S(2)}) %collective-permute-start.19) | collective-permute-done | bytes 8224 | tf_op jit(solution)/shard_map/ppermute | solution.py:18
  310.5 2.5 gather_fusion.5
  313.1 2.4 bitcast_select_fusion.4
  317.6 5.8 %collective-permute-start.21 = (f32[8,2,128]{2,0,1:T(8,128)S(1)}, f32[8,2,128]{2,0,1:T(8,128)S(1)}, u32[]{:S(2)}, u32[]{:S(2)}) collective-permute-start(f32[8,2,128]{2,0,1:T(8,128)S(1)} %bitcast.306), channel_id=1, source_target_pairs={{1,0},{2,1},{3,2},{4,3},{5,4},{6,5},{7,6},{8,7},{9,8},{10,9},{11,1... | collective-permute-start | bytes 24584 | tf_op jit(solution)/shard_map/ppermute | solution.py:18
  323.4 3.8 collective-permute-start.22
  327.2 3.6 collective-permute-start.23
  330.9 4.3 collective-permute-done.23
  338.8 2.4 bitcast_select_fusion.3
  343.4 5.8 %collective-permute-start.25 = (f32[8,2,128]{2,0,1:T(8,128)S(1)}, f32[8,2,128]{2,0,1:T(8,128)S(1)}, u32[]{:S(2)}, u32[]{:S(2)}) collective-permute-start(f32[8,2,128]{2,0,1:T(8,128)S(1)} %bitcast.301), channel_id=1, source_target_pairs={{1,0},{2,1},{3,2},{4,3},{5,4},{6,5},{7,6},{8,7},{9,8},{10,9},{11,1... | collective-permute-start | bytes 24584 | tf_op jit(solution)/shard_map/ppermute | solution.py:18
  349.2 5.2 %collective-permute-start.26 = (f32[8,2,128]{2,0,1:T(8,128)S(1)}, f32[8,2,128]{2,0,1:T(8,128)S(1)}, u32[]{:S(2)}, u32[]{:S(2)}) collective-permute-start(f32[8,2,128]{2,0,1:T(8,128)S(1)} %bitcast.307), channel_id=1, source_target_pairs={{0,16},{1,17},{2,18},{3,19},{4,20},{5,21},{6,22},{7,23},{8,24},{9,... | collective-permute-start | bytes 24584 | tf_op jit(solution)/shard_map/ppermute | solution.py:18
  356.6 77.5 %psum.15 = f32[8]{0:T(128)S(1)} all-reduce(f32[8]{0:T(128)S(1)} %get-tuple-element.31), channel_id=1, replica_groups=mesh['region'=256] {'region'}, use_global_device_ids=true, to_apply=%region_3.8 | all-reduce | flops 8 | bytes 64 | tf_op jit(solution)/shard_map/psum | solution.py:121
  437.7 2.4 bitcast_select_fusion.2
  442.3 5.6 %collective-permute-start.29 = (f32[8,2,128]{2,0,1:T(8,128)S(1)}, f32[8,2,128]{2,0,1:T(8,128)S(1)}, u32[]{:S(2)}, u32[]{:S(2)}) collective-permute-start(f32[8,2,128]{2,0,1:T(8,128)S(1)} %bitcast.305), channel_id=1, source_target_pairs={{1,0},{2,1},{3,2},{4,3},{5,4},{6,5},{7,6},{8,7},{9,8},{10,9},{11,1... | collective-permute-start | bytes 24584 | tf_op jit(solution)/shard_map/ppermute | solution.py:18
  448.0 7.9 %collective-permute-start.30 = (f32[8,2,128]{2,0,1:T(8,128)S(1)}, f32[8,2,128]{2,0,1:T(8,128)S(1)}, u32[]{:S(2)}, u32[]{:S(2)}) collective-permute-start(f32[8,2,128]{2,0,1:T(8,128)S(1)} %bitcast.311), channel_id=1, source_target_pairs={{0,16},{1,17},{2,18},{3,19},{4,20},{5,21},{6,22},{7,23},{8,24},{9,... | collective-permute-start | bytes 24584 | tf_op jit(solution)/shard_map/ppermute | solution.py:18
  457.9 6.0 %collective-permute-done.31 = f32[8,2,128]{2,0,1:T(8,128)S(1)} collective-permute-done((f32[8,2,128]{2,0,1:T(8,128)S(1)}, f32[8,2,128]{2,0,1:T(8,128)S(1)}, u32[]{:S(2)}, u32[]{:S(2)}) %collective-permute-start.31) | collective-permute-done | bytes 8224 | tf_op jit(solution)/shard_map/ppermute | solution.py:18
  (164 shorter events, 85.2 us)
Async XLA Ops:
  0.0 150.5 %copy-start = (f32[16,2,512]{2,1,0:T(2,128)S(1)}, f32[16,2,512]{2,1,0:T(2,128)}, u32[]{:S(2)}) copy-start(f32[16,2,512]{2,1,0:T(2,128)} %param.34) | copy-start | bytes 196612
  2.1 121.9 %copy-start.9 = (pred[512]{0:T(512)(128)(4,1)}, pred[512]{0:T(512)(128)(4,1)S(1)}, u32[]{:S(2)}) copy-start(pred[512]{0:T(512)(128)(4,1)S(1)} %fusion.137) | copy-start | bytes 1540
  11.4 22.4 %copy-start.1 = (bf16[8,512,256]{2,1,0:T(8,128)(2,1)S(1)}, bf16[8,512,256]{2,1,0:T(8,128)(2,1)}, u32[]{:S(2)}) copy-start(bf16[8,512,256]{2,1,0:T(8,128)(2,1)} %param.25) | copy-start | bytes 6291460
  11.4 22.4 %copy-start.5 = (bf16[2,256,256]{2,1,0:T(8,128)(2,1)S(1)}, bf16[2,256,256]{2,1,0:T(8,128)(2,1)}, u32[]{:S(2)}) copy-start(bf16[2,256,256]{2,1,0:T(8,128)(2,1)} %param.30) | copy-start | bytes 786436
  13.6 30.3 %collective-permute-start = (bf16[8,128,256]{1,2,0:T(8,128)(2,1)}, bf16[8,128,256]{1,2,0:T(8,128)(2,1)}, u32[]{:S(2)}, u32[]{:S(2)}) collective-permute-start(bf16[8,128,256]{1,2,0:T(8,128)(2,1)} %bitcast.282), channel_id=1, source_target_pairs={{0,1},{1,2},{2,3},{3,4},{4,5},{5,6},{6,7},{7,8},{8,9},{9,10},{10,1... | collective-permute-start | bytes 1572872 | tf_op jit(solution)/shard_map/ppermute | solution.py:18
  17.6 26.4 %collective-permute-start.1 = (bf16[8,128,256]{1,2,0:T(8,128)(2,1)}, bf16[8,128,256]{1,2,0:T(8,128)(2,1)}, u32[]{:S(2)}, u32[]{:S(2)}) collective-permute-start(bf16[8,128,256]{1,2,0:T(8,128)(2,1)} %bitcast.283), channel_id=1, source_target_pairs={{1,0},{2,1},{3,2},{4,3},{5,4},{6,5},{7,6},{8,7},{9,8},{10,9},{11,1... | collective-permute-start | bytes 1572872 | tf_op jit(solution)/shard_map/ppermute | solution.py:18
  24.3 26.6 %collective-permute-start.2 = (bf16[8,128,256]{1,2,0:T(8,128)(2,1)}, bf16[8,128,256]{1,2,0:T(8,128)(2,1)}, u32[]{:S(2)}, u32[]{:S(2)}) collective-permute-start(bf16[8,128,256]{1,2,0:T(8,128)(2,1)} %bitcast.284), channel_id=1, source_target_pairs={{0,16},{1,17},{2,18},{3,19},{4,20},{5,21},{6,22},{7,23},{8,24},{9,... | collective-permute-start | bytes 1572872 | tf_op jit(solution)/shard_map/ppermute | solution.py:18
  31.3 19.7 %collective-permute-start.3 = (bf16[8,128,256]{1,2,0:T(8,128)(2,1)}, bf16[8,128,256]{1,2,0:T(8,128)(2,1)}, u32[]{:S(2)}, u32[]{:S(2)}) collective-permute-start(bf16[8,128,256]{1,2,0:T(8,128)(2,1)} %bitcast.10), channel_id=1, source_target_pairs={{16,0},{17,1},{18,2},{19,3},{20,4},{21,5},{22,6},{23,7},{24,8},{25... | collective-permute-start | bytes 1572872 | tf_op jit(solution)/shard_map/ppermute | solution.py:18
  40.6 10.4 %copy-start.15 = (s32[4,128]{1,0:T(4,128)S(1)}, s32[4,128]{1,0:T(4,128)}, u32[]{:S(2)}) copy-start(s32[4,128]{1,0:T(4,128)} %param.28) | copy-start | bytes 6148
  68.3 25.3 %copy-start.3 = (bf16[8,512,256]{2,1,0:T(8,128)(2,1)S(1)}, bf16[8,512,256]{2,1,0:T(8,128)(2,1)}, u32[]{:S(2)}) copy-start(bf16[8,512,256]{2,1,0:T(8,128)(2,1)} %add_convert_fusion.1) | copy-start | bytes 6291460
  70.6 27.0 %collective-permute-start.4 = (bf16[8,128,256]{1,2,0:T(8,128)(2,1)}, bf16[8,128,256]{1,2,0:T(8,128)(2,1)}, u32[]{:S(2)}, u32[]{:S(2)}) collective-permute-start(bf16[8,128,256]{1,2,0:T(8,128)(2,1)} %bitcast.285), channel_id=1, source_target_pairs={{0,1},{1,2},{2,3},{3,4},{4,5},{5,6},{6,7},{7,8},{8,9},{9,10},{10,1... | collective-permute-start | bytes 1572872 | tf_op jit(solution)/shard_map/ppermute | solution.py:18
  74.5 23.1 %collective-permute-start.5 = (bf16[8,128,256]{1,2,0:T(8,128)(2,1)}, bf16[8,128,256]{1,2,0:T(8,128)(2,1)}, u32[]{:S(2)}, u32[]{:S(2)}) collective-permute-start(bf16[8,128,256]{1,2,0:T(8,128)(2,1)} %bitcast.286), channel_id=1, source_target_pairs={{1,0},{2,1},{3,2},{4,3},{5,4},{6,5},{7,6},{8,7},{9,8},{10,9},{11,1... | collective-permute-start | bytes 1572872 | tf_op jit(solution)/shard_map/ppermute | solution.py:18
  82.3 26.6 %collective-permute-start.6 = (bf16[8,128,256]{1,2,0:T(8,128)(2,1)}, bf16[8,128,256]{1,2,0:T(8,128)(2,1)}, u32[]{:S(2)}, u32[]{:S(2)}) collective-permute-start(bf16[8,128,256]{1,2,0:T(8,128)(2,1)} %bitcast.287), channel_id=1, source_target_pairs={{0,16},{1,17},{2,18},{3,19},{4,20},{5,21},{6,22},{7,23},{8,24},{9,... | collective-permute-start | bytes 1572872 | tf_op jit(solution)/shard_map/ppermute | solution.py:18
  91.1 17.8 %collective-permute-start.7 = (bf16[8,128,256]{1,2,0:T(8,128)(2,1)}, bf16[8,128,256]{1,2,0:T(8,128)(2,1)S(1)}, u32[]{:S(2)}, u32[]{:S(2)}) collective-permute-start(bf16[8,128,256]{1,2,0:T(8,128)(2,1)} %bitcast.288), channel_id=1, source_target_pairs={{16,0},{17,1},{18,2},{19,3},{20,4},{21,5},{22,6},{23,7},{24,8},{25... | collective-permute-start | bytes 1572872 | tf_op jit(solution)/shard_map/ppermute | solution.py:18
  97.6 15.4 %copy-start.17 = (bf16[2,256]{1,0:T(2,128)(2,1)S(1)}, bf16[2,256]{1,0:T(2,128)(2,1)}, u32[]{:S(2)}) copy-start(bf16[2,256]{1,0:T(2,128)(2,1)} %param.33) | copy-start | bytes 3076
  113.0 5.1 %copy-start.13 = (f32[2]{0:T(128)S(1)}, f32[2]{0:T(128)}, u32[]{:S(2)}) copy-start(f32[2]{0:T(128)} %constant.74.clone) | copy-start | bytes 28
  119.8 30.7 %copy-start.7 = (f32[512]{0:T(512)S(1)}, f32[512]{0:T(512)}, u32[]{:S(2)}) copy-start(f32[512]{0:T(512)} %param.38) | copy-start | bytes 6148
  119.8 30.7 %copy-start.8 = (f32[512]{0:T(512)S(1)}, f32[512]{0:T(512)}, u32[]{:S(2)}) copy-start(f32[512]{0:T(512)} %param.37) | copy-start | bytes 6148
  119.8 33.0 %copy-start.2 = (bf16[1024,1024]{1,0:T(8,128)(2,1)S(1)}, bf16[1024,1024]{1,0:T(8,128)(2,1)}, u32[]{:S(2)}) copy-start(bf16[1024,1024]{1,0:T(8,128)(2,1)} %copy.319) | copy-start | bytes 6291460
  129.9 18.6 %collective-permute-start.10 = (f32[8,2,128]{2,0,1:T(8,128)}, f32[8,2,128]{2,0,1:T(8,128)}, u32[]{:S(2)}, u32[]{:S(2)}) collective-permute-start(f32[8,2,128]{2,0,1:T(8,128)} %bitcast.296), channel_id=1, source_target_pairs={{0,16},{1,17},{2,18},{3,19},{4,20},{5,21},{6,22},{7,23},{8,24},{9,... | collective-permute-start | bytes 24584 | tf_op jit(solution)/shard_map/ppermute | solution.py:18
  136.9 11.6 %collective-permute-start.11 = (f32[8,2,128]{2,0,1:T(8,128)}, f32[8,2,128]{2,0,1:T(8,128)}, u32[]{:S(2)}, u32[]{:S(2)}) collective-permute-start(f32[8,2,128]{2,0,1:T(8,128)} %bitcast.302), channel_id=1, source_target_pairs={{16,0},{17,1},{18,2},{19,3},{20,4},{21,5},{22,6},{23,7},{24,8},{25... | collective-permute-start | bytes 24584 | tf_op jit(solution)/shard_map/ppermute | solution.py:18
  140.1 8.5 %collective-permute-start.8 = (f32[8,2,128]{2,0,1:T(8,128)}, f32[8,2,128]{2,0,1:T(8,128)S(1)}, u32[]{:S(2)}, u32[]{:S(2)}) collective-permute-start(f32[8,2,128]{2,0,1:T(8,128)} %bitcast.308), channel_id=1, source_target_pairs={{0,1},{1,2},{2,3},{3,4},{4,5},{5,6},{6,7},{7,8},{8,9},{9,10},{10,1... | collective-permute-start | bytes 24584 | tf_op jit(solution)/shard_map/ppermute | solution.py:18
  142.0 7.1 %collective-permute-start.9 = (f32[8,2,128]{2,0,1:T(8,128)S(1)}, f32[8,2,128]{2,0,1:T(8,128)S(1)}, u32[]{:S(2)}, u32[]{:S(2)}) collective-permute-start(f32[8,2,128]{2,0,1:T(8,128)S(1)} %bitcast.314), channel_id=1, source_target_pairs={{1,0},{2,1},{3,2},{4,3},{5,4},{6,5},{7,6},{8,7},{9,8},{10,9},{11,1... | collective-permute-start | bytes 24584 | tf_op jit(solution)/shard_map/ppermute | solution.py:18
  164.1 103.6 %collective-permute-start.12 = (f32[8,2,128]{2,0,1:T(8,128)}, f32[8,2,128]{2,0,1:T(8,128)}, u32[]{:S(2)}, u32[]{:S(2)}) collective-permute-start(f32[8,2,128]{2,0,1:T(8,128)} %bitcast.297), channel_id=1, source_target_pairs={{0,1},{1,2},{2,3},{3,4},{4,5},{5,6},{6,7},{7,8},{8,9},{9,10},{10,1... | collective-permute-start | bytes 24584 | tf_op jit(solution)/shard_map/ppermute | solution.py:18
  167.6 100.1 %collective-permute-start.13 = (f32[8,2,128]{2,0,1:T(8,128)}, f32[8,2,128]{2,0,1:T(8,128)}, u32[]{:S(2)}, u32[]{:S(2)}) collective-permute-start(f32[8,2,128]{2,0,1:T(8,128)} %bitcast.303), channel_id=1, source_target_pairs={{1,0},{2,1},{3,2},{4,3},{5,4},{6,5},{7,6},{8,7},{9,8},{10,9},{11,1... | collective-permute-start | bytes 24584 | tf_op jit(solution)/shard_map/ppermute | solution.py:18
  174.0 93.7 %collective-permute-start.14 = (f32[8,2,128]{2,0,1:T(8,128)}, f32[8,2,128]{2,0,1:T(8,128)S(1)}, u32[]{:S(2)}, u32[]{:S(2)}) collective-permute-start(f32[8,2,128]{2,0,1:T(8,128)} %bitcast.309), channel_id=1, source_target_pairs={{0,16},{1,17},{2,18},{3,19},{4,20},{5,21},{6,22},{7,23},{8,24},{9,... | collective-permute-start | bytes 24584 | tf_op jit(solution)/shard_map/ppermute | solution.py:18
  184.0 83.6 %collective-permute-start.15 = (f32[8,2,128]{2,0,1:T(8,128)S(1)}, f32[8,2,128]{2,0,1:T(8,128)S(1)}, u32[]{:S(2)}, u32[]{:S(2)}) collective-permute-start(f32[8,2,128]{2,0,1:T(8,128)S(1)} %bitcast.315), channel_id=1, source_target_pairs={{16,0},{17,1},{18,2},{19,3},{20,4},{21,5},{22,6},{23,7},{24,8},{25... | collective-permute-start | bytes 24584 | tf_op jit(solution)/shard_map/ppermute | solution.py:18
  280.3 20.3 %collective-permute-start.16 = (f32[8,2,128]{2,0,1:T(8,128)}, f32[8,2,128]{2,0,1:T(8,128)}, u32[]{:S(2)}, u32[]{:S(2)}) collective-permute-start(f32[8,2,128]{2,0,1:T(8,128)} %bitcast.298), channel_id=1, source_target_pairs={{0,1},{1,2},{2,3},{3,4},{4,5},{5,6},{6,7},{7,8},{8,9},{9,10},{10,1... | collective-permute-start | bytes 24584 | tf_op jit(solution)/shard_map/ppermute | solution.py:18
  283.9 16.8 %collective-permute-start.17 = (f32[8,2,128]{2,0,1:T(8,128)}, f32[8,2,128]{2,0,1:T(8,128)}, u32[]{:S(2)}, u32[]{:S(2)}) collective-permute-start(f32[8,2,128]{2,0,1:T(8,128)} %bitcast.304), channel_id=1, source_target_pairs={{1,0},{2,1},{3,2},{4,3},{5,4},{6,5},{7,6},{8,7},{9,8},{10,9},{11,1... | collective-permute-start | bytes 24584 | tf_op jit(solution)/shard_map/ppermute | solution.py:18
  290.2 10.4 %collective-permute-start.18 = (f32[8,2,128]{2,0,1:T(8,128)}, f32[8,2,128]{2,0,1:T(8,128)S(1)}, u32[]{:S(2)}, u32[]{:S(2)}) collective-permute-start(f32[8,2,128]{2,0,1:T(8,128)} %bitcast.310), channel_id=1, source_target_pairs={{0,16},{1,17},{2,18},{3,19},{4,20},{5,21},{6,22},{7,23},{8,24},{9,... | collective-permute-start | bytes 24584 | tf_op jit(solution)/shard_map/ppermute | solution.py:18
  298.1 8.0 %collective-permute-start.19 = (f32[8,2,128]{2,0,1:T(8,128)S(1)}, f32[8,2,128]{2,0,1:T(8,128)S(1)}, u32[]{:S(2)}, u32[]{:S(2)}) collective-permute-start(f32[8,2,128]{2,0,1:T(8,128)S(1)} %bitcast.316), channel_id=1, source_target_pairs={{16,0},{17,1},{18,2},{19,3},{20,4},{21,5},{22,6},{23,7},{24,8},{25... | collective-permute-start | bytes 24584 | tf_op jit(solution)/shard_map/ppermute | solution.py:18
  307.2 5.8 %copy-start.10 = (pred[512]{0:T(512)(128)(4,1)S(1)}, pred[512]{0:T(512)(128)(4,1)}, u32[]{:S(2)}) copy-start(pred[512]{0:T(512)(128)(4,1)} %copy-done.9) | copy-start | bytes 1540
  308.6 22.3 %copy-start.12 = (f32[512]{0:T(512)S(1)}, f32[512]{0:T(512)}, u32[]{:S(2)}) copy-start(f32[512]{0:T(512)} %param.39) | copy-start | bytes 6148
  308.6 26.6 %copy-start.16 = (s32[4,128]{1,0:T(4,128)S(1)}, s32[4,128]{1,0:T(4,128)}, u32[]{:S(2)}) copy-start(s32[4,128]{1,0:T(4,128)} %param.28) | copy-start | bytes 6148
  309.6 26.1 %copy-start.6 = (f32[8,2,512]{2,0,1:T(8,128)S(1)}, f32[8,2,512]{2,0,1:T(8,128)}, u32[]{:S(2)}) copy-start(f32[8,2,512]{2,0,1:T(8,128)} %get-tuple-element.81) | copy-start | bytes 98308
  309.6 26.1 %copy-start.11 = (f32[512]{0:T(512)S(1)}, f32[512]{0:T(512)}, u32[]{:S(2)}) copy-start(f32[512]{0:T(512)} %param.36) | copy-start | bytes 6148
  315.6 15.3 %collective-permute-start.20 = (f32[8,2,128]{2,0,1:T(8,128)S(1)}, f32[8,2,128]{2,0,1:T(8,128)S(1)}, u32[]{:S(2)}, u32[]{:S(2)}) collective-permute-start(f32[8,2,128]{2,0,1:T(8,128)S(1)} %bitcast.300), channel_id=1, source_target_pairs={{0,1},{1,2},{2,3},{3,4},{4,5},{5,6},{6,7},{7,8},{8,9},{9,10},{10,1... | collective-permute-start | bytes 24584 | tf_op jit(solution)/shard_map/ppermute | solution.py:18
  317.6 13.3 %collective-permute-start.21 = (f32[8,2,128]{2,0,1:T(8,128)S(1)}, f32[8,2,128]{2,0,1:T(8,128)S(1)}, u32[]{:S(2)}, u32[]{:S(2)}) collective-permute-start(f32[8,2,128]{2,0,1:T(8,128)S(1)} %bitcast.306), channel_id=1, source_target_pairs={{1,0},{2,1},{3,2},{4,3},{5,4},{6,5},{7,6},{8,7},{9,8},{10,9},{11,1... | collective-permute-start | bytes 24584 | tf_op jit(solution)/shard_map/ppermute | solution.py:18
  323.4 7.5 %collective-permute-start.22 = (f32[8,2,128]{2,0,1:T(8,128)S(1)}, f32[8,2,128]{2,0,1:T(8,128)S(1)}, u32[]{:S(2)}, u32[]{:S(2)}) collective-permute-start(f32[8,2,128]{2,0,1:T(8,128)S(1)} %bitcast.312), channel_id=1, source_target_pairs={{0,16},{1,17},{2,18},{3,19},{4,20},{5,21},{6,22},{7,23},{8,24},{9,... | collective-permute-start | bytes 24584 | tf_op jit(solution)/shard_map/ppermute | solution.py:18
  327.2 8.0 %collective-permute-start.23 = (f32[8,2,128]{2,0,1:T(8,128)S(1)}, f32[8,2,128]{2,0,1:T(8,128)S(1)}, u32[]{:S(2)}, u32[]{:S(2)}) collective-permute-start(f32[8,2,128]{2,0,1:T(8,128)S(1)} %bitcast.318), channel_id=1, source_target_pairs={{16,0},{17,1},{18,2},{19,3},{20,4},{21,5},{22,6},{23,7},{24,8},{25... | collective-permute-start | bytes 24584 | tf_op jit(solution)/shard_map/ppermute | solution.py:18
  341.4 92.8 %collective-permute-start.24 = (f32[8,2,128]{2,0,1:T(8,128)S(1)}, f32[8,2,128]{2,0,1:T(8,128)S(1)}, u32[]{:S(2)}, u32[]{:S(2)}) collective-permute-start(f32[8,2,128]{2,0,1:T(8,128)S(1)} %bitcast.295), channel_id=1, source_target_pairs={{0,1},{1,2},{2,3},{3,4},{4,5},{5,6},{6,7},{7,8},{8,9},{9,10},{10,1... | collective-permute-start | bytes 24584 | tf_op jit(solution)/shard_map/ppermute | solution.py:18
  343.4 90.8 %collective-permute-start.25 = (f32[8,2,128]{2,0,1:T(8,128)S(1)}, f32[8,2,128]{2,0,1:T(8,128)S(1)}, u32[]{:S(2)}, u32[]{:S(2)}) collective-permute-start(f32[8,2,128]{2,0,1:T(8,128)S(1)} %bitcast.301), channel_id=1, source_target_pairs={{1,0},{2,1},{3,2},{4,3},{5,4},{6,5},{7,6},{8,7},{9,8},{10,9},{11,1... | collective-permute-start | bytes 24584 | tf_op jit(solution)/shard_map/ppermute | solution.py:18
  349.2 85.0 %collective-permute-start.26 = (f32[8,2,128]{2,0,1:T(8,128)S(1)}, f32[8,2,128]{2,0,1:T(8,128)S(1)}, u32[]{:S(2)}, u32[]{:S(2)}) collective-permute-start(f32[8,2,128]{2,0,1:T(8,128)S(1)} %bitcast.307), channel_id=1, source_target_pairs={{0,16},{1,17},{2,18},{3,19},{4,20},{5,21},{6,22},{7,23},{8,24},{9,... | collective-permute-start | bytes 24584 | tf_op jit(solution)/shard_map/ppermute | solution.py:18
  354.4 79.7 %collective-permute-start.27 = (f32[8,2,128]{2,0,1:T(8,128)S(1)}, f32[8,2,128]{2,0,1:T(8,128)S(1)}, u32[]{:S(2)}, u32[]{:S(2)}) collective-permute-start(f32[8,2,128]{2,0,1:T(8,128)S(1)} %bitcast.313), channel_id=1, source_target_pairs={{16,0},{17,1},{18,2},{19,3},{20,4},{21,5},{22,6},{23,7},{24,8},{25... | collective-permute-start | bytes 24584 | tf_op jit(solution)/shard_map/ppermute | solution.py:18
  440.2 17.7 %collective-permute-start.28 = (f32[8,2,128]{2,0,1:T(8,128)S(1)}, f32[8,2,128]{2,0,1:T(8,128)S(1)}, u32[]{:S(2)}, u32[]{:S(2)}) collective-permute-start(f32[8,2,128]{2,0,1:T(8,128)S(1)} %bitcast.299), channel_id=1, source_target_pairs={{0,1},{1,2},{2,3},{3,4},{4,5},{5,6},{6,7},{7,8},{8,9},{9,10},{10,1... | collective-permute-start | bytes 24584 | tf_op jit(solution)/shard_map/ppermute | solution.py:18
  442.3 15.6 %collective-permute-start.29 = (f32[8,2,128]{2,0,1:T(8,128)S(1)}, f32[8,2,128]{2,0,1:T(8,128)S(1)}, u32[]{:S(2)}, u32[]{:S(2)}) collective-permute-start(f32[8,2,128]{2,0,1:T(8,128)S(1)} %bitcast.305), channel_id=1, source_target_pairs={{1,0},{2,1},{3,2},{4,3},{5,4},{6,5},{7,6},{8,7},{9,8},{10,9},{11,1... | collective-permute-start | bytes 24584 | tf_op jit(solution)/shard_map/ppermute | solution.py:18
  448.0 9.9 %collective-permute-start.30 = (f32[8,2,128]{2,0,1:T(8,128)S(1)}, f32[8,2,128]{2,0,1:T(8,128)S(1)}, u32[]{:S(2)}, u32[]{:S(2)}) collective-permute-start(f32[8,2,128]{2,0,1:T(8,128)S(1)} %bitcast.311), channel_id=1, source_target_pairs={{0,16},{1,17},{2,18},{3,19},{4,20},{5,21},{6,22},{7,23},{8,24},{9,... | collective-permute-start | bytes 24584 | tf_op jit(solution)/shard_map/ppermute | solution.py:18
  455.9 8.0 %collective-permute-start.31 = (f32[8,2,128]{2,0,1:T(8,128)S(1)}, f32[8,2,128]{2,0,1:T(8,128)S(1)}, u32[]{:S(2)}, u32[]{:S(2)}) collective-permute-start(f32[8,2,128]{2,0,1:T(8,128)S(1)} %bitcast.317), channel_id=1, source_target_pairs={{16,0},{17,1},{18,2},{19,3},{20,4},{21,5},{22,6},{23,7},{24,8},{25... | collective-permute-start | bytes 24584 | tf_op jit(solution)/shard_map/ppermute | solution.py:18
  (2 other events, 8.1 us)
where the time goes:
time: 473 us; the launch traced here: 466 us
  blocking collectives  159 us (34%)
  starting transfers between devices  133 us (28%)
  local copies, waits for them, and re-layouts  71 us (15%)
  matrix products  41.8 us (9%)
  waiting for transfers between devices  34.7 us (7%)
  other arithmetic  25.3 us (5%)
    psum x2, blocking collectives, local(): squares = lax.psum(jnp.sum(residual * residual, axis=(1, 2)), 'region')  159 us
    ppermute x32, starting transfers between devices, from_behind(): lax.ppermute(value, axis, [(source, source + steps) for source in range(f...  133 us
    ppermute x32, waiting for transfers between devices, from_behind(): lax.ppermute(value, axis, [(source, source + steps) for source in range(f...  34.7 us
    unnamed x68, local copies, waits for them, and re-layouts  27 us
    select_n x6, other arithmetic, boundary(): jnp.where(live_rows[None, None, :], tile_rows, jnp.zeros((), jnp.float32))  19 us
    gather x6, local copies, waits for them, and re-layouts, boundary(): tile_rows = jnp.take(values, senders, axis=2)  16.5 us
    gather x2, local copies, waits for them, and re-layouts, local(): tile_rows = jnp.take(hidden, senders, axis=1)  10.5 us
  transfers between devices with their start and end apart: 32, of which 6 were waited for; matrix products, arithmetic and copies ran while one was open for 7% of the time, Pallas kernels for 0%

commit v1 on v0

v1 whole, which is shorter than its diff:
```python
import jax
import jax.numpy as jnp
from jax import lax
from jax.sharding import PartitionSpec as P

RW = 16
NEWTON = 2
SWEEPS = 3


trust_radius = 8.0
highest = lax.Precision.HIGHEST


def from_behind(value, axis, steps):
    count = lax.axis_size(axis)
    first, last = (max(0, -steps), min(count, count - steps))
    return lax.ppermute(value, axis, [(source, source + steps) for source in range(first, last)])


def all_sum(value, axis):
    count = lax.axis_size(axis)
    if count & (count - 1):
        return lax.psum(value, axis)
    bit = 1
    while bit < count:
        value = value + lax.ppermute(value, axis, [(i, i ^ bit) for i in range(count)])
        bit *= 2
    return value


def rotate(conduct, suscept, beside, axis):
    real_part = jnp.take(beside, 0, axis=axis)
    imag_part = jnp.take(beside, 1, axis=axis)
    return jnp.stack(
        [conduct * real_part - suscept * imag_part, suscept * real_part + conduct * imag_part],
        axis=axis,
    )


def local(
    features,
    line_mask,
    send_rows,
    attach_rows,
    tile_count,
    self_weight,
    neigh_weight,
    layer_bias,
    readout,
    load_table,
    scenario_profile,
    diag_admit,
    conductance,
    susceptance,
    load_coeff,
    region_inverse,
):
    scenarios, buses, width = features.shape
    neighbours, tile_size = send_rows.shape
    offsets = (1, -1, RW, -RW)
    bus_iota = lax.broadcasted_iota(jnp.int32, (neighbours, tile_size, buses), 2)
    live = lax.broadcasted_iota(jnp.int32, (neighbours, tile_size), 1) < tile_count[:, None]
    pick = (send_rows[:, :, None] == bus_iota) & live[:, :, None]
    place = attach_rows[:, :, None] == bus_iota
    pick_half, pick_full = pick.astype(jnp.bfloat16), pick.astype(jnp.float32)
    place_half, place_full = place.astype(jnp.bfloat16), place.astype(jnp.float32)
    mask_half = line_mask.astype(jnp.bfloat16)
    mask_full = line_mask.astype(jnp.float32)

    def exchange(tiles):
        return jnp.stack(
            [from_behind(tiles[k], "region", offsets[k]) for k in range(neighbours)]
        )

    hidden = features
    for number in range(self_weight.shape[0]):
        tiles = jnp.einsum(
            "ktb,sbh->ksth", pick_half, hidden, preferred_element_type=jnp.float32
        ).astype(jnp.bfloat16)
        incoming = exchange(tiles)
        inside = jnp.einsum("ij,sjh->sih", mask_half, hidden, preferred_element_type=jnp.float32)
        own = jnp.einsum(
            "sbh,hk->sbk", hidden, self_weight[number], preferred_element_type=jnp.float32
        )
        border = jnp.einsum(
            "ktb,ksth->sbh", place_half, incoming, preferred_element_type=jnp.float32
        )
        gathered = (0.25 * (inside + border)).astype(jnp.bfloat16)
        summed = (
            own
            + jnp.einsum(
                "sbh,hk->sbk", gathered, neigh_weight[number], preferred_element_type=jnp.float32
            )
            + layer_bias[number]
        )
        hidden = (hidden.astype(jnp.float32) + jax.nn.silu(summed)).astype(jnp.bfloat16)
    flat_start = jnp.array([1.0, 0.0], dtype=jnp.float32)[None, :, None]
    voltage = (
        jnp.einsum("sbh,ch->scb", hidden, readout, preferred_element_type=jnp.float32) + flat_start
    )
    choose = (
        scenario_profile[:, None]
        == lax.broadcasted_iota(jnp.int32, (scenarios, load_table.shape[0]), 1)
    ).astype(jnp.float32)
    injection = jnp.einsum("sp,pcb->scb", choose, load_table, precision=highest)
    bus_total = buses * lax.axis_size("region")

    def halo(values):
        tiles = jnp.einsum("ktb,scb->ksct", pick_full, values, precision=highest)
        incoming = exchange(tiles)
        return jnp.einsum("ksct,ktb->scb", incoming, place_full, precision=highest)

    def inside_sum(values):
        return jnp.einsum("ij,scj->sci", mask_full, values, precision=highest)

    beside = inside_sum(voltage) + halo(voltage)
    for newton in range(NEWTON):
        magnitude = voltage[:, 0:1] ** 2 + voltage[:, 1:2] ** 2
        residual = (
            diag_admit * voltage
            - rotate(conductance, susceptance, beside, 1)
            + load_coeff * magnitude * voltage
            - injection
        )
        squares = all_sum(jnp.sum(residual * residual, axis=(1, 2)), "region")
        damping = jnp.minimum(1.0, trust_radius / jnp.sqrt(squares / (2 * bus_total) + 1e-06))
        update = jnp.zeros_like(voltage)
        for sweep_number in range(SWEEPS):
            forcing = -residual
            if sweep_number > 0:
                forcing = forcing + rotate(conductance, susceptance, halo(update), 1)
            forcing = forcing.reshape(scenarios, 2 * buses).astype(jnp.bfloat16)
            update = jnp.dot(forcing, region_inverse, preferred_element_type=jnp.float32).reshape(
                scenarios, 2, buses
            )
        step = damping[:, None, None]
        voltage = voltage + step * update
        if newton + 1 < NEWTON:
            beside = beside + step * (inside_sum(update) + halo(update))
    return voltage


def solution(mesh):
    in_specs = (
        P(None, "region", None),
        P("region", None),
        P("region", None),
        P("region", None),
        P("region"),
        P(),
        P(),
        P(),
        P(),
        P(None, None, "region"),
        P(),
        P("region"),
        P("region"),
        P("region"),
        P("region"),
        P("region", None),
    )
    out_specs = P(None, None, "region")
    return jax.shard_map(local, mesh=mesh, in_specs=in_specs, out_specs=out_specs, check_vma=False)
```

time: 473 us -> 300 us (0.63); the launches traced: 466 us -> 299 us
  blocking collectives: 159 us -> 0 us
  local copies, waits for them, and re-layouts: 71 us -> 4.52 us
  waiting for transfers between devices: 34.7 us -> 91.9 us
  other arithmetic: 25.3 us -> 1.23 us
  starting transfers between devices: 133 us -> 157 us
    psum x2 -> x0, blocking collectives: 159 us -> none  [local(): squares = lax.psum(jnp.sum(residual * residual, axis=(1, 2)), 'region')]
    ppermute x0 -> x16, waiting for transfers between devices: none -> 38.4 us  [all_sum(): lax.ppermute(value, axis, [(i, i ^ bit) for i in range(count)])]
    ppermute x0 -> x16, starting transfers between devices: none -> 36.4 us  [all_sum(): lax.ppermute(value, axis, [(i, i ^ bit) for i in range(count)])]
    gather x8 -> x0, local copies, waits for them, and re-layouts: 27 us -> none  [the longest x6 16.5 us: boundary(): tile_rows = jnp.take(values, senders, axis=2)]
    unnamed x68 -> x42, local copies, waits for them, and re-layouts: 27 us -> 0.9 us
    select_n x9 -> x0, other arithmetic: 22.2 us -> none  [the longest x6 19 us: boundary(): jnp.where(live_rows[None, None, :], tile_rows, jnp.zeros((), jnp.float32))]
    ppermute x32, waiting for transfers between devices: 34.7 us -> 53.6 us  [from_behind(): lax.ppermute(value, axis, [(source, source + steps) for source in range(f...]
    ppermute x32, starting transfers between devices: 133 us -> 121 us  [from_behind(): lax.ppermute(value, axis, [(source, source + steps) for source in range(f...]
  transfers between devices with their start and end apart: 32 -> 48, of which waited for: 6 -> 21; matrix products, arithmetic and copies ran while one was open for 7% -> 5% of each run, Pallas kernels for 0% -> 0%
where the time goes in v1:
time: 300 us; the launch traced here: 299 us
  starting transfers between devices  157 us (52%)
  waiting for transfers between devices  91.9 us (31%)
  matrix products  43.4 us (14%)
  local copies, waits for them, and re-layouts  4.52 us (2%)
    ppermute x32, starting transfers between devices, from_behind(): lax.ppermute(value, axis, [(source, source + steps) for source in range(f...  121 us
    ppermute x32, waiting for transfers between devices, from_behind(): lax.ppermute(value, axis, [(source, source + steps) for source in range(f...  53.6 us
    ppermute x16, waiting for transfers between devices, all_sum(): lax.ppermute(value, axis, [(i, i ^ bit) for i in range(count)])  38.4 us
    ppermute x16, starting transfers between devices, all_sum(): lax.ppermute(value, axis, [(i, i ^ bit) for i in range(count)])  36.4 us
    dot_general x1, matrix products, local(): jnp.einsum('sbh,hk->sbk', gathered, neigh_weight[number], preferred_eleme...  8.26 us
  transfers between devices with their start and end apart: 48, of which 21 were waited for; matrix products, arithmetic and copies ran while one was open for 5% of the time, Pallas kernels for 0%

profile of v1, /device:TPU:4, one launch (start us, length us, event | category | flops | bytes accessed | tf_op | source)
XLA Modules:
  0.0 299.3 jit_solution(13574415382540388946)
XLA Ops:
  0.8 2.9 convert_bitcast_fusion.1
  3.9 4.5 %collective-permute-start.1 = (bf16[8,128,256]{2,1,0:T(8,128)(2,1)S(1)}, bf16[8,128,256]{2,1,0:T(8,128)(2,1)S(1)}, u32[]{:S(2)}, u32[]{:S(2)}) collective-permute-start(bf16[8,128,256]{2,1,0:T(8,128)(2,1)S(1)} %get-tuple-element.40), channel_id=1, source_target_pairs={{1,0},{2,1},{3,2},{4,3},{5,4},{6,5},{7,6},{8,7},{9,8},{10,9},{11,1... | collective-permute-start | bytes 1572872 | tf_op jit(solution)/shard_map/ppermute | solution.py:18
  8.4 5.5 %collective-permute-start.2 = (bf16[8,128,256]{2,1,0:T(8,128)(2,1)S(1)}, bf16[8,128,256]{2,1,0:T(8,128)(2,1)S(1)}, u32[]{:S(2)}, u32[]{:S(2)}) collective-permute-start(bf16[8,128,256]{2,1,0:T(8,128)(2,1)S(1)} %get-tuple-element.39), channel_id=1, source_target_pairs={{0,16},{1,17},{2,18},{3,19},{4,20},{5,21},{6,22},{7,23},{8,24},{9,... | collective-permute-start | bytes 1572872 | tf_op jit(solution)/shard_map/ppermute | solution.py:18
  17.9 2.7 fusion.109
  20.6 3.3 %fusion.87 = f32[8,256,512]{1,2,0:T(8,128)} fusion(bf16[8,512,256]{2,1,0:T(8,128)(2,1)S(1)} %copy-done.4, s32[512,512]{1,0:T(8,128)S(1)} %copy-done.3), kind=kOutput, calls=%fused_computation.85 | convolution fusion | flops 1074003968 | bytes 7340032 | tf_op jit(solution)/shard_map/ij,sjh->sih/dot_general | solution.py:82
  23.9 11.0 %collective-permute-done.2 = bf16[8,128,256]{2,1,0:T(8,128)(2,1)S(1)} collective-permute-done((bf16[8,128,256]{2,1,0:T(8,128)(2,1)S(1)}, bf16[8,128,256]{2,1,0:T(8,128)(2,1)S(1)}, u32[]{:S(2)}, u32[]{:S(2)}) %collective-permute-start.2) | collective-permute-done | bytes 524320 | tf_op jit(solution)/shard_map/ppermute | solution.py:18
  34.9 8.1 %collective-permute-done = bf16[8,128,256]{2,1,0:T(8,128)(2,1)S(1)} collective-permute-done((bf16[8,128,256]{2,1,0:T(8,128)(2,1)S(1)}, bf16[8,128,256]{2,1,0:T(8,128)(2,1)S(1)}, u32[]{:S(2)}, u32[]{:S(2)}) %collective-permute-start) | collective-permute-done | bytes 524320 | tf_op jit(solution)/shard_map/ppermute | solution.py:18
  43.8 8.3 %add_convert_fusion.1 = bf16[8,512,256]{2,1,0:T(8,128)(2,1)} fusion(f32[8,512,256]{2,1,0:T(8,128)} %fusion.109, bf16[8,512,256]{2,1,0:T(8,128)(2,1)S(1)} %copy-done.4, f32[256]{0:T(256)S(1)} %bitcast.481, f32[8,256,512]{1,2,0:T(8,128)} %fusion.87, bf16[1,8,128,256]{3,2,1,0:T(8,128)(2,1)} %bitcast.485, bf16[1,8,128,256]{3,2,1,0:T(8,128)(2,1)} %bitcast.483, ...), kind=kOutput, calls=%fused_computation.7 | convolution fusion | flops 1626603520 | bytes 14814208 | tf_op jit(solution)/shard_map/sbh,hk->sbk/dot_general | solution.py:92
  52.0 3.1 %convert_bitcast_fusion = bf16[4,8,128,256]{2,3,0,1:T(8,128)(2,1)S(1)} fusion(bf16[8,512,256]{2,1,0:T(8,128)(2,1)} %add_convert_fusion.1, s32[4,128]{1,0:T(4,128)S(1)} %copy-done.18, pred[4,128]{1,0:T(4,128)(4,1)S(1)} %iota_compare_fusion.3), kind=kOutput, calls=%fused_computation.36 | convolution fusion | flops 1075314688 | bytes 4196864 | tf_op jit(solution)/shard_map/ktb,sbh->ksth/dot_general | solution.py:78
  57.4 5.8 %collective-permute-start.5 = (bf16[8,128,256]{1,2,0:T(8,128)(2,1)S(1)}, bf16[8,128,256]{1,2,0:T(8,128)(2,1)S(1)}, u32[]{:S(2)}, u32[]{:S(2)}) collective-permute-start(bf16[8,128,256]{1,2,0:T(8,128)(2,1)S(1)} %get-tuple-element.34), channel_id=1, source_target_pairs={{1,0},{2,1},{3,2},{4,3},{5,4},{6,5},{7,6},{8,7},{9,8},{10,9},{11,1... | collective-permute-start | bytes 1572872 | tf_op jit(solution)/shard_map/ppermute | solution.py:18
  65.0 5.6 %collective-permute-start.7 = (bf16[8,128,256]{1,2,0:T(8,128)(2,1)S(1)}, bf16[8,128,256]{1,2,0:T(8,128)(2,1)S(1)}, u32[]{:S(2)}, u32[]{:S(2)}) collective-permute-start(bf16[8,128,256]{1,2,0:T(8,128)(2,1)S(1)} %get-tuple-element.35), channel_id=1, source_target_pairs={{16,0},{17,1},{18,2},{19,3},{20,4},{21,5},{22,6},{23,7},{24,8},{25... | collective-permute-start | bytes 1572872 | tf_op jit(solution)/shard_map/ppermute | solution.py:18
  70.7 2.7 fusion.106
  74.7 13.6 %collective-permute-done.6 = bf16[8,128,256]{1,2,0:T(8,128)(2,1)S(1)} collective-permute-done((bf16[8,128,256]{1,2,0:T(8,128)(2,1)S(1)}, bf16[8,128,256]{1,2,0:T(8,128)(2,1)S(1)}, u32[]{:S(2)}, u32[]{:S(2)}) %collective-permute-start.6) | collective-permute-done | bytes 524320 | tf_op jit(solution)/shard_map/ppermute | solution.py:18
  88.2 2.7 fusion.1
  90.9 4.5 %fusion.37 = f32[8,512,2]{1,2,0:T(2,128)S(1)} fusion(f32[8,512,256]{2,1,0:T(8,128)} %fusion.106, bf16[8,512,256]{2,1,0:T(8,128)(2,1)S(1)} %copy-done.5, bf16[8,256,512]{1,2,0:T(8,128)(2,1)} %fusion.1, f32[256]{0:T(256)S(1)} %bitcast.480, bf16[2,256,256]{2,1,0:T(8,128)(2,1)} %param.27, bf16[2,256]{1,0:T(2,128)(2,1)S(1)} %copy-done.20), kind=kOutput, calls=%fused_computation.38 | convolution fusion | flops 550502400 | bytes 8554496 | tf_op jit(solution)/shard_map/sbh,ch->scb/dot_general | solution.py:100
  99.1 5.8 %collective-permute-start.9 = (f32[8,2,128]{2,0,1:T(8,128)S(1)}, f32[8,2,128]{2,0,1:T(8,128)S(1)}, u32[]{:S(2)}, u32[]{:S(2)}) collective-permute-start(f32[8,2,128]{2,0,1:T(8,128)S(1)} %get-tuple-element.74), channel_id=1, source_target_pairs={{1,0},{2,1},{3,2},{4,3},{5,4},{6,5},{7,6},{8,7},{9,8},{10,9},{11,1... | collective-permute-start | bytes 24584 | tf_op jit(solution)/shard_map/ppermute | solution.py:18
  104.8 5.2 %collective-permute-start.10 = (f32[8,2,128]{2,0,1:T(8,128)S(1)}, f32[8,2,128]{2,0,1:T(8,128)S(1)}, u32[]{:S(2)}, u32[]{:S(2)}) collective-permute-start(f32[8,2,128]{2,0,1:T(8,128)S(1)} %get-tuple-element.76), channel_id=1, source_target_pairs={{0,16},{1,17},{2,18},{3,19},{4,20},{5,21},{6,22},{7,23},{8,24},{9,... | collective-permute-start | bytes 24584 | tf_op jit(solution)/shard_map/ppermute | solution.py:18
  112.3 5.7 %collective-permute-done.11 = f32[8,2,128]{2,0,1:T(8,128)S(1)} collective-permute-done((f32[8,2,128]{2,0,1:T(8,128)S(1)}, f32[8,2,128]{2,0,1:T(8,128)S(1)}, u32[]{:S(2)}, u32[]{:S(2)}) %collective-permute-start.11) | collective-permute-done | bytes 8224 | tf_op jit(solution)/shard_map/ppermute | solution.py:18
  121.9 5.8 %collective-permute-start.21 = (f32[8,2,128]{2,0,1:T(8,128)S(1)}, f32[8,2,128]{2,0,1:T(8,128)S(1)}, u32[]{:S(2)}, u32[]{:S(2)}) collective-permute-start(f32[8,2,128]{2,0,1:T(8,128)S(1)} %get-tuple-element.70), channel_id=1, source_target_pairs={{1,0},{2,1},{3,2},{4,3},{5,4},{6,5},{7,6},{8,7},{9,8},{10,9},{11,1... | collective-permute-start | bytes 24584 | tf_op jit(solution)/shard_map/ppermute | solution.py:18
  127.7 4.7 %collective-permute-start.22 = (f32[8,2,128]{2,0,1:T(8,128)S(1)}, f32[8,2,128]{2,0,1:T(8,128)S(1)}, u32[]{:S(2)}, u32[]{:S(2)}) collective-permute-start(f32[8,2,128]{2,0,1:T(8,128)S(1)} %get-tuple-element.72), channel_id=1, source_target_pairs={{0,16},{1,17},{2,18},{3,19},{4,20},{5,21},{6,22},{7,23},{8,24},{9,... | collective-permute-start | bytes 24584 | tf_op jit(solution)/shard_map/ppermute | solution.py:18
  138.8 3.5 %collective-permute-done.13 = f32[8]{0:T(128)S(1)} collective-permute-done((f32[8]{0:T(128)S(1)}, f32[8]{0:T(128)S(1)}, u32[]{:S(2)}, u32[]{:S(2)}) %collective-permute-start.13) | collective-permute-done | bytes 64 | tf_op jit(solution)/shard_map/ppermute | solution.py:27
  142.3 4.8 %collective-permute-start.14 = (f32[8]{0:T(128)S(1)}, f32[8]{0:T(128)S(1)}, u32[]{:S(2)}, u32[]{:S(2)}) collective-permute-start(f32[8]{0:T(128)S(1)} %add.193), channel_id=1, source_target_pairs={{0,4},{1,5},{2,6},{3,7},{4,0},{5,1},{6,2},{7,3},{8,12},{9,13},{10,... | collective-permute-start | bytes 104 | tf_op jit(solution)/shard_map/ppermute | solution.py:27
  148.7 6.0 %collective-permute-start.15 = (f32[8]{0:T(128)S(1)}, f32[8]{0:T(128)S(1)}, u32[]{:S(2)}, u32[]{:S(2)}) collective-permute-start(f32[8]{0:T(128)S(1)} %add.194), channel_id=1, source_target_pairs={{0,8},{1,9},{2,10},{3,11},{4,12},{5,13},{6,14},{7,15},{8,0},{9,1},... | collective-permute-start | bytes 104 | tf_op jit(solution)/shard_map/ppermute | solution.py:27
  156.2 5.0 %collective-permute-done.16 = f32[8]{0:T(128)S(1)} collective-permute-done((f32[8]{0:T(128)S(1)}, f32[8]{0:T(128)S(1)}, u32[]{:S(2)}, u32[]{:S(2)}) %collective-permute-start.16) | collective-permute-done | bytes 64 | tf_op jit(solution)/shard_map/ppermute | solution.py:27
  161.2 3.6 %collective-permute-start.17 = (f32[8]{0:T(128)S(1)}, f32[8]{0:T(128)S(1)}, u32[]{:S(2)}, u32[]{:S(2)}) collective-permute-start(f32[8]{0:T(128)S(1)} %add.196), channel_id=1, source_target_pairs={{0,32},{1,33},{2,34},{3,35},{4,36},{5,37},{6,38},{7,39},{8,40},{9,... | collective-permute-start | bytes 104 | tf_op jit(solution)/shard_map/ppermute | solution.py:27
  166.4 5.7 %collective-permute-start.18 = (f32[8]{0:T(128)S(1)}, f32[8]{0:T(128)S(1)}, u32[]{:S(2)}, u32[]{:S(2)}) collective-permute-start(f32[8]{0:T(128)S(1)} %add.197), channel_id=1, source_target_pairs={{0,64},{1,65},{2,66},{3,67},{4,68},{5,69},{6,70},{7,71},{8,72},{9,... | collective-permute-start | bytes 104 | tf_op jit(solution)/shard_map/ppermute | solution.py:27
  173.6 5.7 %collective-permute-start.19 = (f32[8]{0:T(128)S(1)}, f32[8]{0:T(128)S(1)}, u32[]{:S(2)}, u32[]{:S(2)}) collective-permute-start(f32[8]{0:T(128)S(1)} %add.198), channel_id=1, source_target_pairs={{0,128},{1,129},{2,130},{3,131},{4,132},{5,133},{6,134},{7,135},{8... | collective-permute-start | bytes 104 | tf_op jit(solution)/shard_map/ppermute | solution.py:27
  182.9 5.8 %collective-permute-start.25 = (f32[8,2,128]{2,0,1:T(8,128)S(1)}, f32[8,2,128]{2,0,1:T(8,128)S(1)}, u32[]{:S(2)}, u32[]{:S(2)}) collective-permute-start(f32[8,2,128]{2,0,1:T(8,128)S(1)} %get-tuple-element.66), channel_id=1, source_target_pairs={{1,0},{2,1},{3,2},{4,3},{5,4},{6,5},{7,6},{8,7},{9,8},{10,9},{11,1... | collective-permute-start | bytes 24584 | tf_op jit(solution)/shard_map/ppermute | solution.py:18
  188.7 4.3 %collective-permute-start.26 = (f32[8,2,128]{2,0,1:T(8,128)S(1)}, f32[8,2,128]{2,0,1:T(8,128)S(1)}, u32[]{:S(2)}, u32[]{:S(2)}) collective-permute-start(f32[8,2,128]{2,0,1:T(8,128)S(1)} %get-tuple-element.68), channel_id=1, source_target_pairs={{0,16},{1,17},{2,18},{3,19},{4,20},{5,21},{6,22},{7,23},{8,24},{9,... | collective-permute-start | bytes 24584 | tf_op jit(solution)/shard_map/ppermute | solution.py:18
  193.0 3.0 %collective-permute-start.27 = (f32[8,2,128]{2,0,1:T(8,128)S(1)}, f32[8,2,128]{2,0,1:T(8,128)S(1)}, u32[]{:S(2)}, u32[]{:S(2)}) collective-permute-start(f32[8,2,128]{2,0,1:T(8,128)S(1)} %get-tuple-element.67), channel_id=1, source_target_pairs={{16,0},{17,1},{18,2},{19,3},{20,4},{21,5},{22,6},{23,7},{24,8},{25... | collective-permute-start | bytes 24584 | tf_op jit(solution)/shard_map/ppermute | solution.py:18
  196.1 4.9 %collective-permute-done.27 = f32[8,2,128]{2,0,1:T(8,128)S(1)} collective-permute-done((f32[8,2,128]{2,0,1:T(8,128)S(1)}, f32[8,2,128]{2,0,1:T(8,128)S(1)}, u32[]{:S(2)}, u32[]{:S(2)}) %collective-permute-start.27) | collective-permute-done | bytes 8224 | tf_op jit(solution)/shard_map/ppermute | solution.py:18
  205.7 5.8 %collective-permute-start.29 = (f32[8,2,128]{2,0,1:T(8,128)S(1)}, f32[8,2,128]{2,0,1:T(8,128)S(1)}, u32[]{:S(2)}, u32[]{:S(2)}) collective-permute-start(f32[8,2,128]{2,0,1:T(8,128)S(1)} %get-tuple-element.62), channel_id=1, source_target_pairs={{1,0},{2,1},{3,2},{4,3},{5,4},{6,5},{7,6},{8,7},{9,8},{10,9},{11,1... | collective-permute-start | bytes 24584 | tf_op jit(solution)/shard_map/ppermute | solution.py:18
  211.5 3.8 %collective-permute-start.30 = (f32[8,2,128]{2,0,1:T(8,128)S(1)}, f32[8,2,128]{2,0,1:T(8,128)S(1)}, u32[]{:S(2)}, u32[]{:S(2)}) collective-permute-start(f32[8,2,128]{2,0,1:T(8,128)S(1)} %get-tuple-element.64), channel_id=1, source_target_pairs={{0,16},{1,17},{2,18},{3,19},{4,20},{5,21},{6,22},{7,23},{8,24},{9,... | collective-permute-start | bytes 24584 | tf_op jit(solution)/shard_map/ppermute | solution.py:18
  215.2 3.6 %collective-permute-start.31 = (f32[8,2,128]{2,0,1:T(8,128)S(1)}, f32[8,2,128]{2,0,1:T(8,128)S(1)}, u32[]{:S(2)}, u32[]{:S(2)}) collective-permute-start(f32[8,2,128]{2,0,1:T(8,128)S(1)} %get-tuple-element.63), channel_id=1, source_target_pairs={{16,0},{17,1},{18,2},{19,3},{20,4},{21,5},{22,6},{23,7},{24,8},{25... | collective-permute-start | bytes 24584 | tf_op jit(solution)/shard_map/ppermute | solution.py:18
  218.9 4.3 %collective-permute-done.31 = f32[8,2,128]{2,0,1:T(8,128)S(1)} collective-permute-done((f32[8,2,128]{2,0,1:T(8,128)S(1)}, f32[8,2,128]{2,0,1:T(8,128)S(1)}, u32[]{:S(2)}, u32[]{:S(2)}) %collective-permute-start.31) | collective-permute-done | bytes 8224 | tf_op jit(solution)/shard_map/ppermute | solution.py:18
  226.8 5.8 %collective-permute-start.41 = (f32[8,2,128]{2,0,1:T(8,128)S(1)}, f32[8,2,128]{2,0,1:T(8,128)S(1)}, u32[]{:S(2)}, u32[]{:S(2)}) collective-permute-start(f32[8,2,128]{2,0,1:T(8,128)S(1)} %get-tuple-element.58), channel_id=1, source_target_pairs={{1,0},{2,1},{3,2},{4,3},{5,4},{6,5},{7,6},{8,7},{9,8},{10,9},{11,1... | collective-permute-start | bytes 24584 | tf_op jit(solution)/shard_map/ppermute | solution.py:18
  232.6 4.5 %collective-permute-start.42 = (f32[8,2,128]{2,0,1:T(8,128)S(1)}, f32[8,2,128]{2,0,1:T(8,128)S(1)}, u32[]{:S(2)}, u32[]{:S(2)}) collective-permute-start(f32[8,2,128]{2,0,1:T(8,128)S(1)} %get-tuple-element.60), channel_id=1, source_target_pairs={{0,16},{1,17},{2,18},{3,19},{4,20},{5,21},{6,22},{7,23},{8,24},{9,... | collective-permute-start | bytes 24584 | tf_op jit(solution)/shard_map/ppermute | solution.py:18
  237.2 2.8 collective-permute-start.43
  241.2 3.5 %collective-permute-done.33 = f32[8]{0:T(128)S(1)} collective-permute-done((f32[8]{0:T(128)S(1)}, f32[8]{0:T(128)S(1)}, u32[]{:S(2)}, u32[]{:S(2)}) %collective-permute-start.33) | collective-permute-done | bytes 64 | tf_op jit(solution)/shard_map/ppermute | solution.py:27
  244.7 5.0 %collective-permute-done.34 = f32[8]{0:T(128)S(1)} collective-permute-done((f32[8]{0:T(128)S(1)}, f32[8]{0:T(128)S(1)}, u32[]{:S(2)}, u32[]{:S(2)}) %collective-permute-start.34) | collective-permute-done | bytes 64 | tf_op jit(solution)/shard_map/ppermute | solution.py:27
  249.8 3.5 %collective-permute-done.35 = f32[8]{0:T(128)S(1)} collective-permute-done((f32[8]{0:T(128)S(1)}, f32[8]{0:T(128)S(1)}, u32[]{:S(2)}, u32[]{:S(2)}) %collective-permute-start.35) | collective-permute-done | bytes 64 | tf_op jit(solution)/shard_map/ppermute | solution.py:27
  253.3 5.0 %collective-permute-done.36 = f32[8]{0:T(128)S(1)} collective-permute-done((f32[8]{0:T(128)S(1)}, f32[8]{0:T(128)S(1)}, u32[]{:S(2)}, u32[]{:S(2)}) %collective-permute-start.36) | collective-permute-done | bytes 64 | tf_op jit(solution)/shard_map/ppermute | solution.py:27
  259.1 2.8 collective-permute-done.37
  261.9 3.7 %collective-permute-start.38 = (f32[8]{0:T(128)S(1)}, f32[8]{0:T(128)S(1)}, u32[]{:S(2)}, u32[]{:S(2)}) collective-permute-start(f32[8]{0:T(128)S(1)} %add.216), channel_id=1, source_target_pairs={{0,64},{1,65},{2,66},{3,67},{4,68},{5,69},{6,70},{7,71},{8,72},{9,... | collective-permute-start | bytes 104 | tf_op jit(solution)/shard_map/ppermute | solution.py:27
  267.2 6.0 %collective-permute-start.39 = (f32[8]{0:T(128)S(1)}, f32[8]{0:T(128)S(1)}, u32[]{:S(2)}, u32[]{:S(2)}) collective-permute-start(f32[8]{0:T(128)S(1)} %add.217), channel_id=1, source_target_pairs={{0,128},{1,129},{2,130},{3,131},{4,132},{5,133},{6,134},{7,135},{8... | collective-permute-start | bytes 104 | tf_op jit(solution)/shard_map/ppermute | solution.py:27
  276.7 5.8 %collective-permute-start.45 = (f32[8,2,128]{2,0,1:T(8,128)S(1)}, f32[8,2,128]{2,0,1:T(8,128)S(1)}, u32[]{:S(2)}, u32[]{:S(2)}) collective-permute-start(f32[8,2,128]{2,0,1:T(8,128)S(1)} %get-tuple-element.54), channel_id=1, source_target_pairs={{1,0},{2,1},{3,2},{4,3},{5,4},{6,5},{7,6},{8,7},{9,8},{10,9},{11,1... | collective-permute-start | bytes 24584 | tf_op jit(solution)/shard_map/ppermute | solution.py:18
  282.5 7.0 %collective-permute-start.46 = (f32[8,2,128]{2,0,1:T(8,128)S(1)}, f32[8,2,128]{2,0,1:T(8,128)S(1)}, u32[]{:S(2)}, u32[]{:S(2)}) collective-permute-start(f32[8,2,128]{2,0,1:T(8,128)S(1)} %get-tuple-element.56), channel_id=1, source_target_pairs={{0,16},{1,17},{2,18},{3,19},{4,20},{5,21},{6,22},{7,23},{8,24},{9,... | collective-permute-start | bytes 24584 | tf_op jit(solution)/shard_map/ppermute | solution.py:18
  291.5 6.0 %collective-permute-done.47 = f32[8,2,128]{2,0,1:T(8,128)S(1)} collective-permute-done((f32[8,2,128]{2,0,1:T(8,128)S(1)}, f32[8,2,128]{2,0,1:T(8,128)S(1)}, u32[]{:S(2)}, u32[]{:S(2)}) %collective-permute-start.47) | collective-permute-done | bytes 8224 | tf_op jit(solution)/shard_map/ppermute | solution.py:18
  (164 shorter events, 56.0 us)
Async XLA Ops:
  3.9 20.0 %collective-permute-start.1 = (bf16[8,128,256]{2,1,0:T(8,128)(2,1)S(1)}, bf16[8,128,256]{2,1,0:T(8,128)(2,1)S(1)}, u32[]{:S(2)}, u32[]{:S(2)}) collective-permute-start(bf16[8,128,256]{2,1,0:T(8,128)(2,1)S(1)} %get-tuple-element.40), channel_id=1, source_target_pairs={{1,0},{2,1},{3,2},{4,3},{5,4},{6,5},{7,6},{8,7},{9,8},{10,9},{11,1... | collective-permute-start | bytes 1572872 | tf_op jit(solution)/shard_map/ppermute | solution.py:18
  8.4 26.5 %collective-permute-start.2 = (bf16[8,128,256]{2,1,0:T(8,128)(2,1)S(1)}, bf16[8,128,256]{2,1,0:T(8,128)(2,1)S(1)}, u32[]{:S(2)}, u32[]{:S(2)}) collective-permute-start(bf16[8,128,256]{2,1,0:T(8,128)(2,1)S(1)} %get-tuple-element.39), channel_id=1, source_target_pairs={{0,16},{1,17},{2,18},{3,19},{4,20},{5,21},{6,22},{7,23},{8,24},{9,... | collective-permute-start | bytes 1572872 | tf_op jit(solution)/shard_map/ppermute | solution.py:18
  13.9 21.0 %collective-permute-start.3 = (bf16[8,128,256]{2,1,0:T(8,128)(2,1)S(1)}, bf16[8,128,256]{2,1,0:T(8,128)(2,1)S(1)}, u32[]{:S(2)}, u32[]{:S(2)}) collective-permute-start(bf16[8,128,256]{2,1,0:T(8,128)(2,1)S(1)} %get-tuple-element.38), channel_id=1, source_target_pairs={{16,0},{17,1},{18,2},{19,3},{20,4},{21,5},{22,6},{23,7},{24,8},{25... | collective-permute-start | bytes 1572872 | tf_op jit(solution)/shard_map/ppermute | solution.py:18
  15.8 27.1 %collective-permute-start = (bf16[8,128,256]{2,1,0:T(8,128)(2,1)S(1)}, bf16[8,128,256]{2,1,0:T(8,128)(2,1)S(1)}, u32[]{:S(2)}, u32[]{:S(2)}) collective-permute-start(bf16[8,128,256]{2,1,0:T(8,128)(2,1)S(1)} %get-tuple-element.37), channel_id=1, source_target_pairs={{0,1},{1,2},{2,3},{3,4},{4,5},{5,6},{6,7},{7,8},{8,9},{9,10},{10,1... | collective-permute-start | bytes 1572872 | tf_op jit(solution)/shard_map/ppermute | solution.py:18
  55.3 19.4 %collective-permute-start.4 = (bf16[8,128,256]{1,2,0:T(8,128)(2,1)S(1)}, bf16[8,128,256]{1,2,0:T(8,128)(2,1)S(1)}, u32[]{:S(2)}, u32[]{:S(2)}) collective-permute-start(bf16[8,128,256]{1,2,0:T(8,128)(2,1)S(1)} %get-tuple-element.33), channel_id=1, source_target_pairs={{0,1},{1,2},{2,3},{3,4},{4,5},{5,6},{6,7},{7,8},{8,9},{9,10},{10,1... | collective-permute-start | bytes 1572872 | tf_op jit(solution)/shard_map/ppermute | solution.py:18
  57.4 17.3 %collective-permute-start.5 = (bf16[8,128,256]{1,2,0:T(8,128)(2,1)S(1)}, bf16[8,128,256]{1,2,0:T(8,128)(2,1)S(1)}, u32[]{:S(2)}, u32[]{:S(2)}) collective-permute-start(bf16[8,128,256]{1,2,0:T(8,128)(2,1)S(1)} %get-tuple-element.34), channel_id=1, source_target_pairs={{1,0},{2,1},{3,2},{4,3},{5,4},{6,5},{7,6},{8,7},{9,8},{10,9},{11,1... | collective-permute-start | bytes 1572872 | tf_op jit(solution)/shard_map/ppermute | solution.py:18
  63.1 25.1 %collective-permute-start.6 = (bf16[8,128,256]{1,2,0:T(8,128)(2,1)S(1)}, bf16[8,128,256]{1,2,0:T(8,128)(2,1)S(1)}, u32[]{:S(2)}, u32[]{:S(2)}) collective-permute-start(bf16[8,128,256]{1,2,0:T(8,128)(2,1)S(1)} %get-tuple-element.36), channel_id=1, source_target_pairs={{0,16},{1,17},{2,18},{3,19},{4,20},{5,21},{6,22},{7,23},{8,24},{9,... | collective-permute-start | bytes 1572872 | tf_op jit(solution)/shard_map/ppermute | solution.py:18
  65.0 23.2 %collective-permute-start.7 = (bf16[8,128,256]{1,2,0:T(8,128)(2,1)S(1)}, bf16[8,128,256]{1,2,0:T(8,128)(2,1)S(1)}, u32[]{:S(2)}, u32[]{:S(2)}) collective-permute-start(bf16[8,128,256]{1,2,0:T(8,128)(2,1)S(1)} %get-tuple-element.35), channel_id=1, source_target_pairs={{16,0},{17,1},{18,2},{19,3},{20,4},{21,5},{22,6},{23,7},{24,8},{25... | collective-permute-start | bytes 1572872 | tf_op jit(solution)/shard_map/ppermute | solution.py:18
  97.2 15.1 %collective-permute-start.8 = (f32[8,2,128]{2,0,1:T(8,128)S(1)}, f32[8,2,128]{2,0,1:T(8,128)S(1)}, u32[]{:S(2)}, u32[]{:S(2)}) collective-permute-start(f32[8,2,128]{2,0,1:T(8,128)S(1)} %get-tuple-element.73), channel_id=1, source_target_pairs={{0,1},{1,2},{2,3},{3,4},{4,5},{5,6},{6,7},{7,8},{8,9},{9,10},{10,1... | collective-permute-start | bytes 24584 | tf_op jit(solution)/shard_map/ppermute | solution.py:18
  99.1 13.2 %collective-permute-start.9 = (f32[8,2,128]{2,0,1:T(8,128)S(1)}, f32[8,2,128]{2,0,1:T(8,128)S(1)}, u32[]{:S(2)}, u32[]{:S(2)}) collective-permute-start(f32[8,2,128]{2,0,1:T(8,128)S(1)} %get-tuple-element.74), channel_id=1, source_target_pairs={{1,0},{2,1},{3,2},{4,3},{5,4},{6,5},{7,6},{8,7},{9,8},{10,9},{11,1... | collective-permute-start | bytes 24584 | tf_op jit(solution)/shard_map/ppermute | solution.py:18
  104.8 7.4 %collective-permute-start.10 = (f32[8,2,128]{2,0,1:T(8,128)S(1)}, f32[8,2,128]{2,0,1:T(8,128)S(1)}, u32[]{:S(2)}, u32[]{:S(2)}) collective-permute-start(f32[8,2,128]{2,0,1:T(8,128)S(1)} %get-tuple-element.76), channel_id=1, source_target_pairs={{0,16},{1,17},{2,18},{3,19},{4,20},{5,21},{6,22},{7,23},{8,24},{9,... | collective-permute-start | bytes 24584 | tf_op jit(solution)/shard_map/ppermute | solution.py:18
  110.1 7.9 %collective-permute-start.11 = (f32[8,2,128]{2,0,1:T(8,128)S(1)}, f32[8,2,128]{2,0,1:T(8,128)S(1)}, u32[]{:S(2)}, u32[]{:S(2)}) collective-permute-start(f32[8,2,128]{2,0,1:T(8,128)S(1)} %get-tuple-element.75), channel_id=1, source_target_pairs={{16,0},{17,1},{18,2},{19,3},{20,4},{21,5},{22,6},{23,7},{24,8},{25... | collective-permute-start | bytes 24584 | tf_op jit(solution)/shard_map/ppermute | solution.py:18
  120.0 59.3 %collective-permute-start.20 = (f32[8,2,128]{2,0,1:T(8,128)S(1)}, f32[8,2,128]{2,0,1:T(8,128)S(1)}, u32[]{:S(2)}, u32[]{:S(2)}) collective-permute-start(f32[8,2,128]{2,0,1:T(8,128)S(1)} %get-tuple-element.69), channel_id=1, source_target_pairs={{0,1},{1,2},{2,3},{3,4},{4,5},{5,6},{6,7},{7,8},{8,9},{9,10},{10,1... | collective-permute-start | bytes 24584 | tf_op jit(solution)/shard_map/ppermute | solution.py:18
  121.9 57.4 %collective-permute-start.21 = (f32[8,2,128]{2,0,1:T(8,128)S(1)}, f32[8,2,128]{2,0,1:T(8,128)S(1)}, u32[]{:S(2)}, u32[]{:S(2)}) collective-permute-start(f32[8,2,128]{2,0,1:T(8,128)S(1)} %get-tuple-element.70), channel_id=1, source_target_pairs={{1,0},{2,1},{3,2},{4,3},{5,4},{6,5},{7,6},{8,7},{9,8},{10,9},{11,1... | collective-permute-start | bytes 24584 | tf_op jit(solution)/shard_map/ppermute | solution.py:18
  127.7 51.6 %collective-permute-start.22 = (f32[8,2,128]{2,0,1:T(8,128)S(1)}, f32[8,2,128]{2,0,1:T(8,128)S(1)}, u32[]{:S(2)}, u32[]{:S(2)}) collective-permute-start(f32[8,2,128]{2,0,1:T(8,128)S(1)} %get-tuple-element.72), channel_id=1, source_target_pairs={{0,16},{1,17},{2,18},{3,19},{4,20},{5,21},{6,22},{7,23},{8,24},{9,... | collective-permute-start | bytes 24584 | tf_op jit(solution)/shard_map/ppermute | solution.py:18
  132.4 46.9 %collective-permute-start.23 = (f32[8,2,128]{2,0,1:T(8,128)S(1)}, f32[8,2,128]{2,0,1:T(8,128)S(1)}, u32[]{:S(2)}, u32[]{:S(2)}) collective-permute-start(f32[8,2,128]{2,0,1:T(8,128)S(1)} %get-tuple-element.71), channel_id=1, source_target_pairs={{16,0},{17,1},{18,2},{19,3},{20,4},{21,5},{22,6},{23,7},{24,8},{25... | collective-permute-start | bytes 24584 | tf_op jit(solution)/shard_map/ppermute | solution.py:18
  137.7 1.1 collective-permute-start.12
  138.8 3.5 %collective-permute-start.13 = (f32[8]{0:T(128)S(1)}, f32[8]{0:T(128)S(1)}, u32[]{:S(2)}, u32[]{:S(2)}) collective-permute-start(f32[8]{0:T(128)S(1)} %add.192), channel_id=1, source_target_pairs={{0,2},{1,3},{2,0},{3,1},{4,6},{5,7},{6,4},{7,5},{8,10},{9,11},{10,... | collective-permute-start | bytes 104 | tf_op jit(solution)/shard_map/ppermute | solution.py:27
  142.3 6.3 %collective-permute-start.14 = (f32[8]{0:T(128)S(1)}, f32[8]{0:T(128)S(1)}, u32[]{:S(2)}, u32[]{:S(2)}) collective-permute-start(f32[8]{0:T(128)S(1)} %add.193), channel_id=1, source_target_pairs={{0,4},{1,5},{2,6},{3,7},{4,0},{5,1},{6,2},{7,3},{8,12},{9,13},{10,... | collective-permute-start | bytes 104 | tf_op jit(solution)/shard_map/ppermute | solution.py:27
  148.7 7.5 %collective-permute-start.15 = (f32[8]{0:T(128)S(1)}, f32[8]{0:T(128)S(1)}, u32[]{:S(2)}, u32[]{:S(2)}) collective-permute-start(f32[8]{0:T(128)S(1)} %add.194), channel_id=1, source_target_pairs={{0,8},{1,9},{2,10},{3,11},{4,12},{5,13},{6,14},{7,15},{8,0},{9,1},... | collective-permute-start | bytes 104 | tf_op jit(solution)/shard_map/ppermute | solution.py:27
  156.2 5.0 %collective-permute-start.16 = (f32[8]{0:T(128)S(1)}, f32[8]{0:T(128)S(1)}, u32[]{:S(2)}, u32[]{:S(2)}) collective-permute-start(f32[8]{0:T(128)S(1)} %add.195), channel_id=1, source_target_pairs={{0,16},{1,17},{2,18},{3,19},{4,20},{5,21},{6,22},{7,23},{8,24},{9,... | collective-permute-start | bytes 104 | tf_op jit(solution)/shard_map/ppermute | solution.py:27
  161.2 5.2 %collective-permute-start.17 = (f32[8]{0:T(128)S(1)}, f32[8]{0:T(128)S(1)}, u32[]{:S(2)}, u32[]{:S(2)}) collective-permute-start(f32[8]{0:T(128)S(1)} %add.196), channel_id=1, source_target_pairs={{0,32},{1,33},{2,34},{3,35},{4,36},{5,37},{6,38},{7,39},{8,40},{9,... | collective-permute-start | bytes 104 | tf_op jit(solution)/shard_map/ppermute | solution.py:27
  166.4 7.2 %collective-permute-start.18 = (f32[8]{0:T(128)S(1)}, f32[8]{0:T(128)S(1)}, u32[]{:S(2)}, u32[]{:S(2)}) collective-permute-start(f32[8]{0:T(128)S(1)} %add.197), channel_id=1, source_target_pairs={{0,64},{1,65},{2,66},{3,67},{4,68},{5,69},{6,70},{7,71},{8,72},{9,... | collective-permute-start | bytes 104 | tf_op jit(solution)/shard_map/ppermute | solution.py:27
  173.6 22.4 %collective-permute-start.19 = (f32[8]{0:T(128)S(1)}, f32[8]{0:T(128)S(1)}, u32[]{:S(2)}, u32[]{:S(2)}) collective-permute-start(f32[8]{0:T(128)S(1)} %add.198), channel_id=1, source_target_pairs={{0,128},{1,129},{2,130},{3,131},{4,132},{5,133},{6,134},{7,135},{8... | collective-permute-start | bytes 104 | tf_op jit(solution)/shard_map/ppermute | solution.py:27
  181.0 15.1 %collective-permute-start.24 = (f32[8,2,128]{2,0,1:T(8,128)S(1)}, f32[8,2,128]{2,0,1:T(8,128)S(1)}, u32[]{:S(2)}, u32[]{:S(2)}) collective-permute-start(f32[8,2,128]{2,0,1:T(8,128)S(1)} %get-tuple-element.65), channel_id=1, source_target_pairs={{0,1},{1,2},{2,3},{3,4},{4,5},{5,6},{6,7},{7,8},{8,9},{9,10},{10,1... | collective-permute-start | bytes 24584 | tf_op jit(solution)/shard_map/ppermute | solution.py:18
  182.9 13.2 %collective-permute-start.25 = (f32[8,2,128]{2,0,1:T(8,128)S(1)}, f32[8,2,128]{2,0,1:T(8,128)S(1)}, u32[]{:S(2)}, u32[]{:S(2)}) collective-permute-start(f32[8,2,128]{2,0,1:T(8,128)S(1)} %get-tuple-element.66), channel_id=1, source_target_pairs={{1,0},{2,1},{3,2},{4,3},{5,4},{6,5},{7,6},{8,7},{9,8},{10,9},{11,1... | collective-permute-start | bytes 24584 | tf_op jit(solution)/shard_map/ppermute | solution.py:18
  188.7 7.4 %collective-permute-start.26 = (f32[8,2,128]{2,0,1:T(8,128)S(1)}, f32[8,2,128]{2,0,1:T(8,128)S(1)}, u32[]{:S(2)}, u32[]{:S(2)}) collective-permute-start(f32[8,2,128]{2,0,1:T(8,128)S(1)} %get-tuple-element.68), channel_id=1, source_target_pairs={{0,16},{1,17},{2,18},{3,19},{4,20},{5,21},{6,22},{7,23},{8,24},{9,... | collective-permute-start | bytes 24584 | tf_op jit(solution)/shard_map/ppermute | solution.py:18
  193.0 7.9 %collective-permute-start.27 = (f32[8,2,128]{2,0,1:T(8,128)S(1)}, f32[8,2,128]{2,0,1:T(8,128)S(1)}, u32[]{:S(2)}, u32[]{:S(2)}) collective-permute-start(f32[8,2,128]{2,0,1:T(8,128)S(1)} %get-tuple-element.67), channel_id=1, source_target_pairs={{16,0},{17,1},{18,2},{19,3},{20,4},{21,5},{22,6},{23,7},{24,8},{25... | collective-permute-start | bytes 24584 | tf_op jit(solution)/shard_map/ppermute | solution.py:18
  203.8 15.1 %collective-permute-start.28 = (f32[8,2,128]{2,0,1:T(8,128)S(1)}, f32[8,2,128]{2,0,1:T(8,128)S(1)}, u32[]{:S(2)}, u32[]{:S(2)}) collective-permute-start(f32[8,2,128]{2,0,1:T(8,128)S(1)} %get-tuple-element.61), channel_id=1, source_target_pairs={{0,1},{1,2},{2,3},{3,4},{4,5},{5,6},{6,7},{7,8},{8,9},{9,10},{10,1... | collective-permute-start | bytes 24584 | tf_op jit(solution)/shard_map/ppermute | solution.py:18
  205.7 13.1 %collective-permute-start.29 = (f32[8,2,128]{2,0,1:T(8,128)S(1)}, f32[8,2,128]{2,0,1:T(8,128)S(1)}, u32[]{:S(2)}, u32[]{:S(2)}) collective-permute-start(f32[8,2,128]{2,0,1:T(8,128)S(1)} %get-tuple-element.62), channel_id=1, source_target_pairs={{1,0},{2,1},{3,2},{4,3},{5,4},{6,5},{7,6},{8,7},{9,8},{10,9},{11,1... | collective-permute-start | bytes 24584 | tf_op jit(solution)/shard_map/ppermute | solution.py:18
  211.5 7.4 %collective-permute-start.30 = (f32[8,2,128]{2,0,1:T(8,128)S(1)}, f32[8,2,128]{2,0,1:T(8,128)S(1)}, u32[]{:S(2)}, u32[]{:S(2)}) collective-permute-start(f32[8,2,128]{2,0,1:T(8,128)S(1)} %get-tuple-element.64), channel_id=1, source_target_pairs={{0,16},{1,17},{2,18},{3,19},{4,20},{5,21},{6,22},{7,23},{8,24},{9,... | collective-permute-start | bytes 24584 | tf_op jit(solution)/shard_map/ppermute | solution.py:18
  215.2 7.9 %collective-permute-start.31 = (f32[8,2,128]{2,0,1:T(8,128)S(1)}, f32[8,2,128]{2,0,1:T(8,128)S(1)}, u32[]{:S(2)}, u32[]{:S(2)}) collective-permute-start(f32[8,2,128]{2,0,1:T(8,128)S(1)} %get-tuple-element.63), channel_id=1, source_target_pairs={{16,0},{17,1},{18,2},{19,3},{20,4},{21,5},{22,6},{23,7},{24,8},{25... | collective-permute-start | bytes 24584 | tf_op jit(solution)/shard_map/ppermute | solution.py:18
  224.9 48.3 %collective-permute-start.40 = (f32[8,2,128]{2,0,1:T(8,128)S(1)}, f32[8,2,128]{2,0,1:T(8,128)S(1)}, u32[]{:S(2)}, u32[]{:S(2)}) collective-permute-start(f32[8,2,128]{2,0,1:T(8,128)S(1)} %get-tuple-element.57), channel_id=1, source_target_pairs={{0,1},{1,2},{2,3},{3,4},{4,5},{5,6},{6,7},{7,8},{8,9},{9,10},{10,1... | collective-permute-start | bytes 24584 | tf_op jit(solution)/shard_map/ppermute | solution.py:18
  226.8 46.3 %collective-permute-start.41 = (f32[8,2,128]{2,0,1:T(8,128)S(1)}, f32[8,2,128]{2,0,1:T(8,128)S(1)}, u32[]{:S(2)}, u32[]{:S(2)}) collective-permute-start(f32[8,2,128]{2,0,1:T(8,128)S(1)} %get-tuple-element.58), channel_id=1, source_target_pairs={{1,0},{2,1},{3,2},{4,3},{5,4},{6,5},{7,6},{8,7},{9,8},{10,9},{11,1... | collective-permute-start | bytes 24584 | tf_op jit(solution)/shard_map/ppermute | solution.py:18
  232.6 40.6 %collective-permute-start.42 = (f32[8,2,128]{2,0,1:T(8,128)S(1)}, f32[8,2,128]{2,0,1:T(8,128)S(1)}, u32[]{:S(2)}, u32[]{:S(2)}) collective-permute-start(f32[8,2,128]{2,0,1:T(8,128)S(1)} %get-tuple-element.60), channel_id=1, source_target_pairs={{0,16},{1,17},{2,18},{3,19},{4,20},{5,21},{6,22},{7,23},{8,24},{9,... | collective-permute-start | bytes 24584 | tf_op jit(solution)/shard_map/ppermute | solution.py:18
  237.2 36.0 %collective-permute-start.43 = (f32[8,2,128]{2,0,1:T(8,128)S(1)}, f32[8,2,128]{2,0,1:T(8,128)S(1)}, u32[]{:S(2)}, u32[]{:S(2)}) collective-permute-start(f32[8,2,128]{2,0,1:T(8,128)S(1)} %get-tuple-element.59), channel_id=1, source_target_pairs={{16,0},{17,1},{18,2},{19,3},{20,4},{21,5},{22,6},{23,7},{24,8},{25... | collective-permute-start | bytes 24584 | tf_op jit(solution)/shard_map/ppermute | solution.py:18
  240.0 1.2 collective-permute-start.32
  241.2 3.5 %collective-permute-start.33 = (f32[8]{0:T(128)S(1)}, f32[8]{0:T(128)S(1)}, u32[]{:S(2)}, u32[]{:S(2)}) collective-permute-start(f32[8]{0:T(128)S(1)} %add.211), channel_id=1, source_target_pairs={{0,2},{1,3},{2,0},{3,1},{4,6},{5,7},{6,4},{7,5},{8,10},{9,11},{10,... | collective-permute-start | bytes 104 | tf_op jit(solution)/shard_map/ppermute | solution.py:27
  244.7 5.0 %collective-permute-start.34 = (f32[8]{0:T(128)S(1)}, f32[8]{0:T(128)S(1)}, u32[]{:S(2)}, u32[]{:S(2)}) collective-permute-start(f32[8]{0:T(128)S(1)} %add.212), channel_id=1, source_target_pairs={{0,4},{1,5},{2,6},{3,7},{4,0},{5,1},{6,2},{7,3},{8,12},{9,13},{10,... | collective-permute-start | bytes 104 | tf_op jit(solution)/shard_map/ppermute | solution.py:27
  249.8 3.5 %collective-permute-start.35 = (f32[8]{0:T(128)S(1)}, f32[8]{0:T(128)S(1)}, u32[]{:S(2)}, u32[]{:S(2)}) collective-permute-start(f32[8]{0:T(128)S(1)} %add.213), channel_id=1, source_target_pairs={{0,8},{1,9},{2,10},{3,11},{4,12},{5,13},{6,14},{7,15},{8,0},{9,1},... | collective-permute-start | bytes 104 | tf_op jit(solution)/shard_map/ppermute | solution.py:27
  253.3 5.0 %collective-permute-start.36 = (f32[8]{0:T(128)S(1)}, f32[8]{0:T(128)S(1)}, u32[]{:S(2)}, u32[]{:S(2)}) collective-permute-start(f32[8]{0:T(128)S(1)} %add.214), channel_id=1, source_target_pairs={{0,16},{1,17},{2,18},{3,19},{4,20},{5,21},{6,22},{7,23},{8,24},{9,... | collective-permute-start | bytes 104 | tf_op jit(solution)/shard_map/ppermute | solution.py:27
  258.4 3.5 %collective-permute-start.37 = (f32[8]{0:T(128)S(1)}, f32[8]{0:T(128)S(1)}, u32[]{:S(2)}, u32[]{:S(2)}) collective-permute-start(f32[8]{0:T(128)S(1)} %add.215), channel_id=1, source_target_pairs={{0,32},{1,33},{2,34},{3,35},{4,36},{5,37},{6,38},{7,39},{8,40},{9,... | collective-permute-start | bytes 104 | tf_op jit(solution)/shard_map/ppermute | solution.py:27
  261.9 5.2 %collective-permute-start.38 = (f32[8]{0:T(128)S(1)}, f32[8]{0:T(128)S(1)}, u32[]{:S(2)}, u32[]{:S(2)}) collective-permute-start(f32[8]{0:T(128)S(1)} %add.216), channel_id=1, source_target_pairs={{0,64},{1,65},{2,66},{3,67},{4,68},{5,69},{6,70},{7,71},{8,72},{9,... | collective-permute-start | bytes 104 | tf_op jit(solution)/shard_map/ppermute | solution.py:27
  267.2 24.3 %collective-permute-start.39 = (f32[8]{0:T(128)S(1)}, f32[8]{0:T(128)S(1)}, u32[]{:S(2)}, u32[]{:S(2)}) collective-permute-start(f32[8]{0:T(128)S(1)} %add.217), channel_id=1, source_target_pairs={{0,128},{1,129},{2,130},{3,131},{4,132},{5,133},{6,134},{7,135},{8... | collective-permute-start | bytes 104 | tf_op jit(solution)/shard_map/ppermute | solution.py:27
  274.8 16.6 %collective-permute-start.44 = (f32[8,2,128]{2,0,1:T(8,128)S(1)}, f32[8,2,128]{2,0,1:T(8,128)S(1)}, u32[]{:S(2)}, u32[]{:S(2)}) collective-permute-start(f32[8,2,128]{2,0,1:T(8,128)S(1)} %get-tuple-element.53), channel_id=1, source_target_pairs={{0,1},{1,2},{2,3},{3,4},{4,5},{5,6},{6,7},{7,8},{8,9},{9,10},{10,1... | collective-permute-start | bytes 24584 | tf_op jit(solution)/shard_map/ppermute | solution.py:18
  276.7 14.7 %collective-permute-start.45 = (f32[8,2,128]{2,0,1:T(8,128)S(1)}, f32[8,2,128]{2,0,1:T(8,128)S(1)}, u32[]{:S(2)}, u32[]{:S(2)}) collective-permute-start(f32[8,2,128]{2,0,1:T(8,128)S(1)} %get-tuple-element.54), channel_id=1, source_target_pairs={{1,0},{2,1},{3,2},{4,3},{5,4},{6,5},{7,6},{8,7},{9,8},{10,9},{11,1... | collective-permute-start | bytes 24584 | tf_op jit(solution)/shard_map/ppermute | solution.py:18
  282.5 9.0 %collective-permute-start.46 = (f32[8,2,128]{2,0,1:T(8,128)S(1)}, f32[8,2,128]{2,0,1:T(8,128)S(1)}, u32[]{:S(2)}, u32[]{:S(2)}) collective-permute-start(f32[8,2,128]{2,0,1:T(8,128)S(1)} %get-tuple-element.56), channel_id=1, source_target_pairs={{0,16},{1,17},{2,18},{3,19},{4,20},{5,21},{6,22},{7,23},{8,24},{9,... | collective-permute-start | bytes 24584 | tf_op jit(solution)/shard_map/ppermute | solution.py:18
  289.5 7.9 %collective-permute-start.47 = (f32[8,2,128]{2,0,1:T(8,128)S(1)}, f32[8,2,128]{2,0,1:T(8,128)S(1)}, u32[]{:S(2)}, u32[]{:S(2)}) collective-permute-start(f32[8,2,128]{2,0,1:T(8,128)S(1)} %get-tuple-element.55), channel_id=1, source_target_pairs={{16,0},{17,1},{18,2},{19,3},{20,4},{21,5},{22,6},{23,7},{24,8},{25... | collective-permute-start | bytes 24584 | tf_op jit(solution)/shard_map/ppermute | solution.py:18
  (21 other events, 447.8 us)

commit v2 on v1

--- a/solution.py
+++ b/solution.py
@@ -18,15 +18,23 @@
     return lax.ppermute(value, axis, [(source, source + steps) for source in range(first, last)])
 
 
-def all_sum(value, axis):
+def sum_bits(axis):
     count = lax.axis_size(axis)
     if count & (count - 1):
-        return lax.psum(value, axis)
-    bit = 1
-    while bit < count:
+        return None
+    return [1 << b for b in range(count.bit_length() - 1)]
+
+
+def sum_rounds(value, axis, bits):
+    count = lax.axis_size(axis)
+    for bit in bits:
         value = value + lax.ppermute(value, axis, [(i, i ^ bit) for i in range(count)])
-        bit *= 2
     return value
+
+
+def split_even(items, parts):
+    cuts = [len(items) * p // parts for p in range(parts + 1)]
+    return [items[cuts[p] : cuts[p + 1]] for p in range(parts)]
 
 
 def rotate(conduct, suscept, beside, axis):
@@ -115,7 +123,9 @@
         return jnp.einsum("ij,scj->sci", mask_full, values, precision=highest)
 
     beside = inside_sum(voltage) + halo(voltage)
+    bits = sum_bits("region")
     for newton in range(NEWTON):
+        last = newton + 1 == NEWTON
         magnitude = voltage[:, 0:1] ** 2 + voltage[:, 1:2] ** 2
         residual = (
             diag_admit * voltage
@@ -123,21 +133,34 @@
             + load_coeff * magnitude * voltage
             - injection
         )
-        squares = all_sum(jnp.sum(residual * residual, axis=(1, 2)), "region")
-        damping = jnp.minimum(1.0, trust_radius / jnp.sqrt(squares / (2 * bus_total) + 1e-06))
+        partial = jnp.sum(residual * residual, axis=(1, 2))
+        if bits is None:
+            partial = lax.psum(partial, "region")
+            chunks = [[]] * SWEEPS
+        else:
+            chunks = split_even(bits, SWEEPS - 1 if last else SWEEPS)
         update = jnp.zeros_like(voltage)
         for sweep_number in range(SWEEPS):
             forcing = -residual
             if sweep_number > 0:
-                forcing = forcing + rotate(conductance, susceptance, halo(update), 1)
+                partial = sum_rounds(partial, "region", chunks[sweep_number - 1])
+                arrived = halo(update)
+                partial, arrived = lax.optimization_barrier((partial, arrived))
+                forcing = forcing + rotate(conductance, susceptance, arrived, 1)
             forcing = forcing.reshape(scenarios, 2 * buses).astype(jnp.bfloat16)
             update = jnp.dot(forcing, region_inverse, preferred_element_type=jnp.float32).reshape(
                 scenarios, 2, buses
             )
+        if not last:
+            partial = sum_rounds(partial, "region", chunks[SWEEPS - 1])
+            extra = inside_sum(update) + halo(update)
+            partial, extra = lax.optimization_barrier((partial, extra))
+        squares = partial
+        damping = jnp.minimum(1.0, trust_radius / jnp.sqrt(squares / (2 * bus_total) + 1e-06))
         step = damping[:, None, None]
         voltage = voltage + step * update
-        if newton + 1 < NEWTON:
-            beside = beside + step * (inside_sum(update) + halo(update))
+        if not last:
+            beside = beside + step * extra
     return voltage
 
 

time: 300 us -> 306 us (1.020)
  starting transfers between devices: 157 us -> 167 us
  waiting for transfers between devices: 91.9 us -> 84.3 us
    ppermute x32, waiting for transfers between devices: 53.6 us -> 38.9 us  [from_behind(): lax.ppermute(value, axis, [(source, source + steps) for source in range(f...]
    ppermute x32, starting transfers between devices: 121 us -> 129 us  [from_behind(): lax.ppermute(value, axis, [(source, source + steps) for source in range(f...]
    ppermute x16, waiting for transfers between devices: 38.4 us -> 45.4 us  [sum_rounds(): lax.ppermute(value, axis, [(i, i ^ bit) for i in range(count)])]
where the time goes in v2:
time: 306 us; the launch traced here: 303 us
  starting transfers between devices  167 us (55%)
  waiting for transfers between devices  84.3 us (28%)
  matrix products  44.9 us (15%)
  local copies, waits for them, and re-layouts  4.53 us (1%)
    ppermute x32, starting transfers between devices, from_behind(): lax.ppermute(value, axis, [(source, source + steps) for source in range(f...  129 us
    ppermute x16, waiting for transfers between devices, sum_rounds(): lax.ppermute(value, axis, [(i, i ^ bit) for i in range(count)])  45.4 us
    ppermute x32, waiting for transfers between devices, from_behind(): lax.ppermute(value, axis, [(source, source + steps) for source in range(f...  38.9 us
    ppermute x16, starting transfers between devices, sum_rounds(): lax.ppermute(value, axis, [(i, i ^ bit) for i in range(count)])  38.3 us
    dot_general x1, matrix products, local(): jnp.einsum('sbh,hk->sbk', gathered, neigh_weight[number], preferred_eleme...  8.26 us
  transfers between devices with their start and end apart: 48, of which 21 were waited for; matrix products, arithmetic and copies ran while one was open for 5% of the time, Pallas kernels for 0%

profile of v2, /device:TPU:4, one launch (start us, length us, event | category | flops | bytes accessed | tf_op | source)
XLA Modules:
  0.0 302.8 jit_solution(16626144659854370415)
XLA Ops:
  0.8 2.9 convert_bitcast_fusion.1
  3.9 4.5 %collective-permute-start.1 = (bf16[8,128,256]{2,1,0:T(8,128)(2,1)S(1)}, bf16[8,128,256]{2,1,0:T(8,128)(2,1)S(1)}, u32[]{:S(2)}, u32[]{:S(2)}) collective-permute-start(bf16[8,128,256]{2,1,0:T(8,128)(2,1)S(1)} %get-tuple-element.60), channel_id=1, source_target_pairs={{1,0},{2,1},{3,2},{4,3},{5,4},{6,5},{7,6},{8,7},{9,8},{10,9},{11,1... | collective-permute-start | bytes 1572872 | tf_op jit(solution)/shard_map/ppermute | solution.py:18
  8.4 5.5 %collective-permute-start.2 = (bf16[8,128,256]{2,1,0:T(8,128)(2,1)S(1)}, bf16[8,128,256]{2,1,0:T(8,128)(2,1)S(1)}, u32[]{:S(2)}, u32[]{:S(2)}) collective-permute-start(bf16[8,128,256]{2,1,0:T(8,128)(2,1)S(1)} %get-tuple-element.59), channel_id=1, source_target_pairs={{0,16},{1,17},{2,18},{3,19},{4,20},{5,21},{6,22},{7,23},{8,24},{9,... | collective-permute-start | bytes 1572872 | tf_op jit(solution)/shard_map/ppermute | solution.py:18
  15.8 2.1 collective-permute-start
  17.9 2.7 fusion.107
  20.6 3.3 %fusion.85 = f32[8,256,512]{1,2,0:T(8,128)} fusion(bf16[8,512,256]{2,1,0:T(8,128)(2,1)S(1)} %copy-done.4, s32[512,512]{1,0:T(8,128)S(1)} %copy-done.3), kind=kOutput, calls=%fused_computation.83 | convolution fusion | flops 1074003968 | bytes 7340032 | tf_op jit(solution)/shard_map/ij,sjh->sih/dot_general | solution.py:90
  23.9 11.0 %collective-permute-done.2 = bf16[8,128,256]{2,1,0:T(8,128)(2,1)S(1)} collective-permute-done((bf16[8,128,256]{2,1,0:T(8,128)(2,1)S(1)}, bf16[8,128,256]{2,1,0:T(8,128)(2,1)S(1)}, u32[]{:S(2)}, u32[]{:S(2)}) %collective-permute-start.2) | collective-permute-done | bytes 524320 | tf_op jit(solution)/shard_map/ppermute | solution.py:18
  34.9 8.1 %collective-permute-done = bf16[8,128,256]{2,1,0:T(8,128)(2,1)S(1)} collective-permute-done((bf16[8,128,256]{2,1,0:T(8,128)(2,1)S(1)}, bf16[8,128,256]{2,1,0:T(8,128)(2,1)S(1)}, u32[]{:S(2)}, u32[]{:S(2)}) %collective-permute-start) | collective-permute-done | bytes 524320 | tf_op jit(solution)/shard_map/ppermute | solution.py:18
  43.8 8.3 %add_convert_fusion.1 = bf16[8,512,256]{2,1,0:T(8,128)(2,1)} fusion(f32[8,512,256]{2,1,0:T(8,128)} %fusion.107, bf16[8,512,256]{2,1,0:T(8,128)(2,1)S(1)} %copy-done.4, f32[256]{0:T(256)S(1)} %bitcast.501, f32[8,256,512]{1,2,0:T(8,128)} %fusion.85, bf16[1,8,128,256]{3,2,1,0:T(8,128)(2,1)} %bitcast.505, bf16[1,8,128,256]{3,2,1,0:T(8,128)(2,1)} %bitcast.503, ...), kind=kOutput, calls=%fused_computation.7 | convolution fusion | flops 1626603520 | bytes 14814208 | tf_op jit(solution)/shard_map/sbh,hk->sbk/dot_general | solution.py:100
  52.0 3.1 %convert_bitcast_fusion = bf16[4,8,128,256]{2,3,0,1:T(8,128)(2,1)S(1)} fusion(bf16[8,512,256]{2,1,0:T(8,128)(2,1)} %add_convert_fusion.1, s32[4,128]{1,0:T(4,128)S(1)} %copy-done.18, pred[4,128]{1,0:T(4,128)(4,1)S(1)} %iota_compare_fusion.3), kind=kOutput, calls=%fused_computation.36 | convolution fusion | flops 1075314688 | bytes 4196864 | tf_op jit(solution)/shard_map/ktb,sbh->ksth/dot_general | solution.py:86
  55.3 2.1 collective-permute-start.4
  57.4 5.8 %collective-permute-start.5 = (bf16[8,128,256]{1,2,0:T(8,128)(2,1)S(1)}, bf16[8,128,256]{1,2,0:T(8,128)(2,1)S(1)}, u32[]{:S(2)}, u32[]{:S(2)}) collective-permute-start(bf16[8,128,256]{1,2,0:T(8,128)(2,1)S(1)} %get-tuple-element.54), channel_id=1, source_target_pairs={{1,0},{2,1},{3,2},{4,3},{5,4},{6,5},{7,6},{8,7},{9,8},{10,9},{11,1... | collective-permute-start | bytes 1572872 | tf_op jit(solution)/shard_map/ppermute | solution.py:18
  65.0 5.6 %collective-permute-start.7 = (bf16[8,128,256]{1,2,0:T(8,128)(2,1)S(1)}, bf16[8,128,256]{1,2,0:T(8,128)(2,1)S(1)}, u32[]{:S(2)}, u32[]{:S(2)}) collective-permute-start(bf16[8,128,256]{1,2,0:T(8,128)(2,1)S(1)} %get-tuple-element.55), channel_id=1, source_target_pairs={{16,0},{17,1},{18,2},{19,3},{20,4},{21,5},{22,6},{23,7},{24,8},{25... | collective-permute-start | bytes 1572872 | tf_op jit(solution)/shard_map/ppermute | solution.py:18
  70.7 2.7 fusion.104
  74.7 13.6 %collective-permute-done.6 = bf16[8,128,256]{1,2,0:T(8,128)(2,1)S(1)} collective-permute-done((bf16[8,128,256]{1,2,0:T(8,128)(2,1)S(1)}, bf16[8,128,256]{1,2,0:T(8,128)(2,1)S(1)}, u32[]{:S(2)}, u32[]{:S(2)}) %collective-permute-start.6) | collective-permute-done | bytes 524320 | tf_op jit(solution)/shard_map/ppermute | solution.py:18
  88.2 2.7 fusion.1
  90.9 4.5 %fusion.37 = f32[8,512,2]{1,2,0:T(2,128)S(1)} fusion(f32[8,512,256]{2,1,0:T(8,128)} %fusion.104, bf16[8,512,256]{2,1,0:T(8,128)(2,1)S(1)} %copy-done.5, bf16[8,256,512]{1,2,0:T(8,128)(2,1)} %fusion.1, f32[256]{0:T(256)S(1)} %bitcast.500, bf16[2,256,256]{2,1,0:T(8,128)(2,1)} %param.27, bf16[2,256]{1,0:T(2,128)(2,1)S(1)} %copy-done.20), kind=kOutput, calls=%fused_computation.38 | convolution fusion | flops 550502400 | bytes 8554496 | tf_op jit(solution)/shard_map/sbh,ch->scb/dot_general | solution.py:108
  99.1 5.8 %collective-permute-start.9 = (f32[8,2,128]{2,0,1:T(8,128)S(1)}, f32[8,2,128]{2,0,1:T(8,128)S(1)}, u32[]{:S(2)}, u32[]{:S(2)}) collective-permute-start(f32[8,2,128]{2,0,1:T(8,128)S(1)} %get-tuple-element.94), channel_id=1, source_target_pairs={{1,0},{2,1},{3,2},{4,3},{5,4},{6,5},{7,6},{8,7},{9,8},{10,9},{11,1... | collective-permute-start | bytes 24584 | tf_op jit(solution)/shard_map/ppermute | solution.py:18
  104.8 5.2 %collective-permute-start.10 = (f32[8,2,128]{2,0,1:T(8,128)S(1)}, f32[8,2,128]{2,0,1:T(8,128)S(1)}, u32[]{:S(2)}, u32[]{:S(2)}) collective-permute-start(f32[8,2,128]{2,0,1:T(8,128)S(1)} %get-tuple-element.96), channel_id=1, source_target_pairs={{0,16},{1,17},{2,18},{3,19},{4,20},{5,21},{6,22},{7,23},{8,24},{9,... | collective-permute-start | bytes 24584 | tf_op jit(solution)/shard_map/ppermute | solution.py:18
  110.1 2.1 collective-permute-start.11
  112.3 5.7 %collective-permute-done.11 = f32[8,2,128]{2,0,1:T(8,128)S(1)} collective-permute-done((f32[8,2,128]{2,0,1:T(8,128)S(1)}, f32[8,2,128]{2,0,1:T(8,128)S(1)}, u32[]{:S(2)}, u32[]{:S(2)}) %collective-permute-start.11) | collective-permute-done | bytes 8224 | tf_op jit(solution)/shard_map/ppermute | solution.py:18
  121.8 5.8 %collective-permute-start.15 = (f32[8,2,128]{2,0,1:T(8,128)S(1)}, f32[8,2,128]{2,0,1:T(8,128)S(1)}, u32[]{:S(2)}, u32[]{:S(2)}) collective-permute-start(f32[8,2,128]{2,0,1:T(8,128)S(1)} %get-tuple-element.90), channel_id=1, source_target_pairs={{1,0},{2,1},{3,2},{4,3},{5,4},{6,5},{7,6},{8,7},{9,8},{10,9},{11,1... | collective-permute-start | bytes 24584 | tf_op jit(solution)/shard_map/ppermute | solution.py:18
  127.6 4.7 %collective-permute-start.16 = (f32[8,2,128]{2,0,1:T(8,128)S(1)}, f32[8,2,128]{2,0,1:T(8,128)S(1)}, u32[]{:S(2)}, u32[]{:S(2)}) collective-permute-start(f32[8,2,128]{2,0,1:T(8,128)S(1)} %get-tuple-element.92), channel_id=1, source_target_pairs={{0,16},{1,17},{2,18},{3,19},{4,20},{5,21},{6,22},{7,23},{8,24},{9,... | collective-permute-start | bytes 24584 | tf_op jit(solution)/shard_map/ppermute | solution.py:18
  132.3 2.6 collective-permute-start.17
  136.2 3.5 %collective-permute-done.13 = f32[8]{0:T(128)S(1)} collective-permute-done((f32[8]{0:T(128)S(1)}, f32[8]{0:T(128)S(1)}, u32[]{:S(2)}, u32[]{:S(2)}) %collective-permute-start.13) | collective-permute-done | bytes 64 | tf_op jit(solution)/shard_map/ppermute | solution.py:31
  143.8 5.8 %collective-permute-start.22 = (f32[8,2,128]{2,0,1:T(8,128)S(1)}, f32[8,2,128]{2,0,1:T(8,128)S(1)}, u32[]{:S(2)}, u32[]{:S(2)}) collective-permute-start(f32[8,2,128]{2,0,1:T(8,128)S(1)} %get-tuple-element.86), channel_id=1, source_target_pairs={{1,0},{2,1},{3,2},{4,3},{5,4},{6,5},{7,6},{8,7},{9,8},{10,9},{11,1... | collective-permute-start | bytes 24584 | tf_op jit(solution)/shard_map/ppermute | solution.py:18
  149.5 7.3 %collective-permute-start.23 = (f32[8,2,128]{2,0,1:T(8,128)S(1)}, f32[8,2,128]{2,0,1:T(8,128)S(1)}, u32[]{:S(2)}, u32[]{:S(2)}) collective-permute-start(f32[8,2,128]{2,0,1:T(8,128)S(1)} %get-tuple-element.88), channel_id=1, source_target_pairs={{0,16},{1,17},{2,18},{3,19},{4,20},{5,21},{6,22},{7,23},{8,24},{9,... | collective-permute-start | bytes 24584 | tf_op jit(solution)/shard_map/ppermute | solution.py:18
  158.8 2.6 copy.170
  161.8 4.6 %collective-permute-done.18 = f32[8]{0:T(128)S(1)} collective-permute-done((f32[8]{0:T(128)S(1)}, f32[8]{0:T(128)S(1)}, u32[]{:S(2)}, u32[]{:S(2)}) %collective-permute-start.18) | collective-permute-done | bytes 64 | tf_op jit(solution)/shard_map/ppermute | solution.py:31
  166.5 5.0 %collective-permute-start.19 = (f32[8]{0:T(128)S(1)}, f32[8]{0:T(128)S(1)}, u32[]{:S(2)}, u32[]{:S(2)}) collective-permute-start(f32[8]{0:T(128)S(1)} %add.194), channel_id=1, source_target_pairs={{0,8},{1,9},{2,10},{3,11},{4,12},{5,13},{6,14},{7,15},{8,0},{9,1},... | collective-permute-start | bytes 104 | tf_op jit(solution)/shard_map/ppermute | solution.py:31
  173.0 5.0 %collective-permute-done.20 = f32[8]{0:T(128)S(1)} collective-permute-done((f32[8]{0:T(128)S(1)}, f32[8]{0:T(128)S(1)}, u32[]{:S(2)}, u32[]{:S(2)}) %collective-permute-start.20) | collective-permute-done | bytes 64 | tf_op jit(solution)/shard_map/ppermute | solution.py:31
  178.6 2.2 fusion.218
  183.5 5.8 %collective-permute-start.29 = (f32[8,2,128]{2,0,1:T(8,128)S(1)}, f32[8,2,128]{2,0,1:T(8,128)S(1)}, u32[]{:S(2)}, u32[]{:S(2)}) collective-permute-start(f32[8,2,128]{2,0,1:T(8,128)S(1)} %get-tuple-element.82), channel_id=1, source_target_pairs={{1,0},{2,1},{3,2},{4,3},{5,4},{6,5},{7,6},{8,7},{9,8},{10,9},{11,1... | collective-permute-start | bytes 24584 | tf_op jit(solution)/shard_map/ppermute | solution.py:18
  189.2 7.6 %collective-permute-start.30 = (f32[8,2,128]{2,0,1:T(8,128)S(1)}, f32[8,2,128]{2,0,1:T(8,128)S(1)}, u32[]{:S(2)}, u32[]{:S(2)}) collective-permute-start(f32[8,2,128]{2,0,1:T(8,128)S(1)} %get-tuple-element.84), channel_id=1, source_target_pairs={{0,16},{1,17},{2,18},{3,19},{4,20},{5,21},{6,22},{7,23},{8,24},{9,... | collective-permute-start | bytes 24584 | tf_op jit(solution)/shard_map/ppermute | solution.py:18
  203.3 9.7 %collective-permute-start.26 = (f32[8]{0:T(128)S(1)}, f32[8]{0:T(128)S(1)}, u32[]{:S(2)}, u32[]{:S(2)}) collective-permute-start(f32[8]{0:T(128)S(1)} %add.199), channel_id=1, source_target_pairs={{0,64},{1,65},{2,66},{3,67},{4,68},{5,69},{6,70},{7,71},{8,72},{9,... | collective-permute-start | bytes 104 | tf_op jit(solution)/shard_map/ppermute | solution.py:31
  214.5 4.4 %collective-permute-start.27 = (f32[8]{0:T(128)S(1)}, f32[8]{0:T(128)S(1)}, u32[]{:S(2)}, u32[]{:S(2)}) collective-permute-start(f32[8]{0:T(128)S(1)} %add.200), channel_id=1, source_target_pairs={{0,128},{1,129},{2,130},{3,131},{4,132},{5,133},{6,134},{7,135},{8... | collective-permute-start | bytes 104 | tf_op jit(solution)/shard_map/ppermute | solution.py:31
  218.9 3.1 %collective-permute-done.27 = f32[8]{0:T(128)S(1)} collective-permute-done((f32[8]{0:T(128)S(1)}, f32[8]{0:T(128)S(1)}, u32[]{:S(2)}, u32[]{:S(2)}) %collective-permute-start.27) | collective-permute-done | bytes 64 | tf_op jit(solution)/shard_map/ppermute | solution.py:31
  225.7 5.8 %collective-permute-start.37 = (f32[8,2,128]{2,0,1:T(8,128)S(1)}, f32[8,2,128]{2,0,1:T(8,128)S(1)}, u32[]{:S(2)}, u32[]{:S(2)}) collective-permute-start(f32[8,2,128]{2,0,1:T(8,128)S(1)} %get-tuple-element.78), channel_id=1, source_target_pairs={{1,0},{2,1},{3,2},{4,3},{5,4},{6,5},{7,6},{8,7},{9,8},{10,9},{11,1... | collective-permute-start | bytes 24584 | tf_op jit(solution)/shard_map/ppermute | solution.py:18
  231.4 7.5 %collective-permute-start.38 = (f32[8,2,128]{2,0,1:T(8,128)S(1)}, f32[8,2,128]{2,0,1:T(8,128)S(1)}, u32[]{:S(2)}, u32[]{:S(2)}) collective-permute-start(f32[8,2,128]{2,0,1:T(8,128)S(1)} %get-tuple-element.80), channel_id=1, source_target_pairs={{0,16},{1,17},{2,18},{3,19},{4,20},{5,21},{6,22},{7,23},{8,24},{9,... | collective-permute-start | bytes 24584 | tf_op jit(solution)/shard_map/ppermute | solution.py:18
  242.2 3.5 %collective-permute-done.33 = f32[8]{0:T(128)S(1)} collective-permute-done((f32[8]{0:T(128)S(1)}, f32[8]{0:T(128)S(1)}, u32[]{:S(2)}, u32[]{:S(2)}) %collective-permute-start.33) | collective-permute-done | bytes 64 | tf_op jit(solution)/shard_map/ppermute | solution.py:31
  245.8 5.0 %collective-permute-done.34 = f32[8]{0:T(128)S(1)} collective-permute-done((f32[8]{0:T(128)S(1)}, f32[8]{0:T(128)S(1)}, u32[]{:S(2)}, u32[]{:S(2)}) %collective-permute-start.34) | collective-permute-done | bytes 64 | tf_op jit(solution)/shard_map/ppermute | solution.py:31
  250.8 3.5 %collective-permute-done.35 = f32[8]{0:T(128)S(1)} collective-permute-done((f32[8]{0:T(128)S(1)}, f32[8]{0:T(128)S(1)}, u32[]{:S(2)}, u32[]{:S(2)}) %collective-permute-start.35) | collective-permute-done | bytes 64 | tf_op jit(solution)/shard_map/ppermute | solution.py:31
  257.9 5.8 %collective-permute-start.45 = (f32[8,2,128]{2,0,1:T(8,128)S(1)}, f32[8,2,128]{2,0,1:T(8,128)S(1)}, u32[]{:S(2)}, u32[]{:S(2)}) collective-permute-start(f32[8,2,128]{2,0,1:T(8,128)S(1)} %get-tuple-element.74), channel_id=1, source_target_pairs={{1,0},{2,1},{3,2},{4,3},{5,4},{6,5},{7,6},{8,7},{9,8},{10,9},{11,1... | collective-permute-start | bytes 24584 | tf_op jit(solution)/shard_map/ppermute | solution.py:18
  263.7 8.4 %collective-permute-start.46 = (f32[8,2,128]{2,0,1:T(8,128)S(1)}, f32[8,2,128]{2,0,1:T(8,128)S(1)}, u32[]{:S(2)}, u32[]{:S(2)}) collective-permute-start(f32[8,2,128]{2,0,1:T(8,128)S(1)} %get-tuple-element.76), channel_id=1, source_target_pairs={{0,16},{1,17},{2,18},{3,19},{4,20},{5,21},{6,22},{7,23},{8,24},{9,... | collective-permute-start | bytes 24584 | tf_op jit(solution)/shard_map/ppermute | solution.py:18
  274.2 5.0 %collective-permute-done.40 = f32[8]{0:T(128)S(1)} collective-permute-done((f32[8]{0:T(128)S(1)}, f32[8]{0:T(128)S(1)}, u32[]{:S(2)}, u32[]{:S(2)}) %collective-permute-start.40) | collective-permute-done | bytes 64 | tf_op jit(solution)/shard_map/ppermute | solution.py:31
  280.7 2.1 collective-permute-done.41
  282.8 8.7 %collective-permute-start.42 = (f32[8]{0:T(128)S(1)}, f32[8]{0:T(128)S(1)}, u32[]{:S(2)}, u32[]{:S(2)}) collective-permute-start(f32[8]{0:T(128)S(1)} %add.216), channel_id=1, source_target_pairs={{0,64},{1,65},{2,66},{3,67},{4,68},{5,69},{6,70},{7,71},{8,72},{9,... | collective-permute-start | bytes 104 | tf_op jit(solution)/shard_map/ppermute | solution.py:31
  292.9 6.5 %collective-permute-start.43 = (f32[8]{0:T(128)S(1)}, f32[8]{0:T(128)S(1)}, u32[]{:S(2)}, u32[]{:S(2)}) collective-permute-start(f32[8]{0:T(128)S(1)} %add.217), channel_id=1, source_target_pairs={{0,128},{1,129},{2,130},{3,131},{4,132},{5,133},{6,134},{7,135},{8... | collective-permute-start | bytes 104 | tf_op jit(solution)/shard_map/ppermute | solution.py:31
  (167 shorter events, 53.4 us)
Async XLA Ops:
  3.9 20.0 %collective-permute-start.1 = (bf16[8,128,256]{2,1,0:T(8,128)(2,1)S(1)}, bf16[8,128,256]{2,1,0:T(8,128)(2,1)S(1)}, u32[]{:S(2)}, u32[]{:S(2)}) collective-permute-start(bf16[8,128,256]{2,1,0:T(8,128)(2,1)S(1)} %get-tuple-element.60), channel_id=1, source_target_pairs={{1,0},{2,1},{3,2},{4,3},{5,4},{6,5},{7,6},{8,7},{9,8},{10,9},{11,1... | collective-permute-start | bytes 1572872 | tf_op jit(solution)/shard_map/ppermute | solution.py:18
  8.4 26.5 %collective-permute-start.2 = (bf16[8,128,256]{2,1,0:T(8,128)(2,1)S(1)}, bf16[8,128,256]{2,1,0:T(8,128)(2,1)S(1)}, u32[]{:S(2)}, u32[]{:S(2)}) collective-permute-start(bf16[8,128,256]{2,1,0:T(8,128)(2,1)S(1)} %get-tuple-element.59), channel_id=1, source_target_pairs={{0,16},{1,17},{2,18},{3,19},{4,20},{5,21},{6,22},{7,23},{8,24},{9,... | collective-permute-start | bytes 1572872 | tf_op jit(solution)/shard_map/ppermute | solution.py:18
  13.9 21.0 %collective-permute-start.3 = (bf16[8,128,256]{2,1,0:T(8,128)(2,1)S(1)}, bf16[8,128,256]{2,1,0:T(8,128)(2,1)S(1)}, u32[]{:S(2)}, u32[]{:S(2)}) collective-permute-start(bf16[8,128,256]{2,1,0:T(8,128)(2,1)S(1)} %get-tuple-element.58), channel_id=1, source_target_pairs={{16,0},{17,1},{18,2},{19,3},{20,4},{21,5},{22,6},{23,7},{24,8},{25... | collective-permute-start | bytes 1572872 | tf_op jit(solution)/shard_map/ppermute | solution.py:18
  15.8 27.1 %collective-permute-start = (bf16[8,128,256]{2,1,0:T(8,128)(2,1)S(1)}, bf16[8,128,256]{2,1,0:T(8,128)(2,1)S(1)}, u32[]{:S(2)}, u32[]{:S(2)}) collective-permute-start(bf16[8,128,256]{2,1,0:T(8,128)(2,1)S(1)} %get-tuple-element.57), channel_id=1, source_target_pairs={{0,1},{1,2},{2,3},{3,4},{4,5},{5,6},{6,7},{7,8},{8,9},{9,10},{10,1... | collective-permute-start | bytes 1572872 | tf_op jit(solution)/shard_map/ppermute | solution.py:18
  55.3 19.4 %collective-permute-start.4 = (bf16[8,128,256]{1,2,0:T(8,128)(2,1)S(1)}, bf16[8,128,256]{1,2,0:T(8,128)(2,1)S(1)}, u32[]{:S(2)}, u32[]{:S(2)}) collective-permute-start(bf16[8,128,256]{1,2,0:T(8,128)(2,1)S(1)} %get-tuple-element.53), channel_id=1, source_target_pairs={{0,1},{1,2},{2,3},{3,4},{4,5},{5,6},{6,7},{7,8},{8,9},{9,10},{10,1... | collective-permute-start | bytes 1572872 | tf_op jit(solution)/shard_map/ppermute | solution.py:18
  57.4 17.3 %collective-permute-start.5 = (bf16[8,128,256]{1,2,0:T(8,128)(2,1)S(1)}, bf16[8,128,256]{1,2,0:T(8,128)(2,1)S(1)}, u32[]{:S(2)}, u32[]{:S(2)}) collective-permute-start(bf16[8,128,256]{1,2,0:T(8,128)(2,1)S(1)} %get-tuple-element.54), channel_id=1, source_target_pairs={{1,0},{2,1},{3,2},{4,3},{5,4},{6,5},{7,6},{8,7},{9,8},{10,9},{11,1... | collective-permute-start | bytes 1572872 | tf_op jit(solution)/shard_map/ppermute | solution.py:18
  63.1 25.1 %collective-permute-start.6 = (bf16[8,128,256]{1,2,0:T(8,128)(2,1)S(1)}, bf16[8,128,256]{1,2,0:T(8,128)(2,1)S(1)}, u32[]{:S(2)}, u32[]{:S(2)}) collective-permute-start(bf16[8,128,256]{1,2,0:T(8,128)(2,1)S(1)} %get-tuple-element.56), channel_id=1, source_target_pairs={{0,16},{1,17},{2,18},{3,19},{4,20},{5,21},{6,22},{7,23},{8,24},{9,... | collective-permute-start | bytes 1572872 | tf_op jit(solution)/shard_map/ppermute | solution.py:18
  65.0 23.2 %collective-permute-start.7 = (bf16[8,128,256]{1,2,0:T(8,128)(2,1)S(1)}, bf16[8,128,256]{1,2,0:T(8,128)(2,1)S(1)}, u32[]{:S(2)}, u32[]{:S(2)}) collective-permute-start(bf16[8,128,256]{1,2,0:T(8,128)(2,1)S(1)} %get-tuple-element.55), channel_id=1, source_target_pairs={{16,0},{17,1},{18,2},{19,3},{20,4},{21,5},{22,6},{23,7},{24,8},{25... | collective-permute-start | bytes 1572872 | tf_op jit(solution)/shard_map/ppermute | solution.py:18
  97.2 15.1 %collective-permute-start.8 = (f32[8,2,128]{2,0,1:T(8,128)S(1)}, f32[8,2,128]{2,0,1:T(8,128)S(1)}, u32[]{:S(2)}, u32[]{:S(2)}) collective-permute-start(f32[8,2,128]{2,0,1:T(8,128)S(1)} %get-tuple-element.93), channel_id=1, source_target_pairs={{0,1},{1,2},{2,3},{3,4},{4,5},{5,6},{6,7},{7,8},{8,9},{9,10},{10,1... | collective-permute-start | bytes 24584 | tf_op jit(solution)/shard_map/ppermute | solution.py:18
  99.1 13.2 %collective-permute-start.9 = (f32[8,2,128]{2,0,1:T(8,128)S(1)}, f32[8,2,128]{2,0,1:T(8,128)S(1)}, u32[]{:S(2)}, u32[]{:S(2)}) collective-permute-start(f32[8,2,128]{2,0,1:T(8,128)S(1)} %get-tuple-element.94), channel_id=1, source_target_pairs={{1,0},{2,1},{3,2},{4,3},{5,4},{6,5},{7,6},{8,7},{9,8},{10,9},{11,1... | collective-permute-start | bytes 24584 | tf_op jit(solution)/shard_map/ppermute | solution.py:18
  104.8 7.4 %collective-permute-start.10 = (f32[8,2,128]{2,0,1:T(8,128)S(1)}, f32[8,2,128]{2,0,1:T(8,128)S(1)}, u32[]{:S(2)}, u32[]{:S(2)}) collective-permute-start(f32[8,2,128]{2,0,1:T(8,128)S(1)} %get-tuple-element.96), channel_id=1, source_target_pairs={{0,16},{1,17},{2,18},{3,19},{4,20},{5,21},{6,22},{7,23},{8,24},{9,... | collective-permute-start | bytes 24584 | tf_op jit(solution)/shard_map/ppermute | solution.py:18
  110.1 7.9 %collective-permute-start.11 = (f32[8,2,128]{2,0,1:T(8,128)S(1)}, f32[8,2,128]{2,0,1:T(8,128)S(1)}, u32[]{:S(2)}, u32[]{:S(2)}) collective-permute-start(f32[8,2,128]{2,0,1:T(8,128)S(1)} %get-tuple-element.95), channel_id=1, source_target_pairs={{16,0},{17,1},{18,2},{19,3},{20,4},{21,5},{22,6},{23,7},{24,8},{25... | collective-permute-start | bytes 24584 | tf_op jit(solution)/shard_map/ppermute | solution.py:18
  119.9 19.9 %collective-permute-start.14 = (f32[8,2,128]{2,0,1:T(8,128)S(1)}, f32[8,2,128]{2,0,1:T(8,128)S(1)}, u32[]{:S(2)}, u32[]{:S(2)}) collective-permute-start(f32[8,2,128]{2,0,1:T(8,128)S(1)} %get-tuple-element.89), channel_id=1, source_target_pairs={{0,1},{1,2},{2,3},{3,4},{4,5},{5,6},{6,7},{7,8},{8,9},{9,10},{10,1... | collective-permute-start | bytes 24584 | tf_op jit(solution)/shard_map/ppermute | solution.py:18
  121.8 18.0 %collective-permute-start.15 = (f32[8,2,128]{2,0,1:T(8,128)S(1)}, f32[8,2,128]{2,0,1:T(8,128)S(1)}, u32[]{:S(2)}, u32[]{:S(2)}) collective-permute-start(f32[8,2,128]{2,0,1:T(8,128)S(1)} %get-tuple-element.90), channel_id=1, source_target_pairs={{1,0},{2,1},{3,2},{4,3},{5,4},{6,5},{7,6},{8,7},{9,8},{10,9},{11,1... | collective-permute-start | bytes 24584 | tf_op jit(solution)/shard_map/ppermute | solution.py:18
  127.6 12.2 %collective-permute-start.16 = (f32[8,2,128]{2,0,1:T(8,128)S(1)}, f32[8,2,128]{2,0,1:T(8,128)S(1)}, u32[]{:S(2)}, u32[]{:S(2)}) collective-permute-start(f32[8,2,128]{2,0,1:T(8,128)S(1)} %get-tuple-element.92), channel_id=1, source_target_pairs={{0,16},{1,17},{2,18},{3,19},{4,20},{5,21},{6,22},{7,23},{8,24},{9,... | collective-permute-start | bytes 24584 | tf_op jit(solution)/shard_map/ppermute | solution.py:18
  132.3 7.9 %collective-permute-start.17 = (f32[8,2,128]{2,0,1:T(8,128)S(1)}, f32[8,2,128]{2,0,1:T(8,128)S(1)}, u32[]{:S(2)}, u32[]{:S(2)}) collective-permute-start(f32[8,2,128]{2,0,1:T(8,128)S(1)} %get-tuple-element.91), channel_id=1, source_target_pairs={{16,0},{17,1},{18,2},{19,3},{20,4},{21,5},{22,6},{23,7},{24,8},{25... | collective-permute-start | bytes 24584 | tf_op jit(solution)/shard_map/ppermute | solution.py:18
  135.0 1.2 collective-permute-start.12
  136.2 3.5 %collective-permute-start.13 = (f32[8]{0:T(128)S(1)}, f32[8]{0:T(128)S(1)}, u32[]{:S(2)}, u32[]{:S(2)}) collective-permute-start(f32[8]{0:T(128)S(1)} %add.192), channel_id=1, source_target_pairs={{0,2},{1,3},{2,0},{3,1},{4,6},{5,7},{6,4},{7,5},{8,10},{9,11},{10,... | collective-permute-start | bytes 104 | tf_op jit(solution)/shard_map/ppermute | solution.py:31
  141.8 36.2 %collective-permute-start.21 = (f32[8,2,128]{2,0,1:T(8,128)S(1)}, f32[8,2,128]{2,0,1:T(8,128)S(1)}, u32[]{:S(2)}, u32[]{:S(2)}) collective-permute-start(f32[8,2,128]{2,0,1:T(8,128)S(1)} %get-tuple-element.85), channel_id=1, source_target_pairs={{0,1},{1,2},{2,3},{3,4},{4,5},{5,6},{6,7},{7,8},{8,9},{9,10},{10,1... | collective-permute-start | bytes 24584 | tf_op jit(solution)/shard_map/ppermute | solution.py:18
  143.8 34.3 %collective-permute-start.22 = (f32[8,2,128]{2,0,1:T(8,128)S(1)}, f32[8,2,128]{2,0,1:T(8,128)S(1)}, u32[]{:S(2)}, u32[]{:S(2)}) collective-permute-start(f32[8,2,128]{2,0,1:T(8,128)S(1)} %get-tuple-element.86), channel_id=1, source_target_pairs={{1,0},{2,1},{3,2},{4,3},{5,4},{6,5},{7,6},{8,7},{9,8},{10,9},{11,1... | collective-permute-start | bytes 24584 | tf_op jit(solution)/shard_map/ppermute | solution.py:18
  149.5 28.5 %collective-permute-start.23 = (f32[8,2,128]{2,0,1:T(8,128)S(1)}, f32[8,2,128]{2,0,1:T(8,128)S(1)}, u32[]{:S(2)}, u32[]{:S(2)}) collective-permute-start(f32[8,2,128]{2,0,1:T(8,128)S(1)} %get-tuple-element.88), channel_id=1, source_target_pairs={{0,16},{1,17},{2,18},{3,19},{4,20},{5,21},{6,22},{7,23},{8,24},{9,... | collective-permute-start | bytes 24584 | tf_op jit(solution)/shard_map/ppermute | solution.py:18
  156.9 21.2 %collective-permute-start.24 = (f32[8,2,128]{2,0,1:T(8,128)S(1)}, f32[8,2,128]{2,0,1:T(8,128)S(1)}, u32[]{:S(2)}, u32[]{:S(2)}) collective-permute-start(f32[8,2,128]{2,0,1:T(8,128)S(1)} %get-tuple-element.87), channel_id=1, source_target_pairs={{16,0},{17,1},{18,2},{19,3},{20,4},{21,5},{22,6},{23,7},{24,8},{25... | collective-permute-start | bytes 24584 | tf_op jit(solution)/shard_map/ppermute | solution.py:18
  161.4 5.0 %collective-permute-start.18 = (f32[8]{0:T(128)S(1)}, f32[8]{0:T(128)S(1)}, u32[]{:S(2)}, u32[]{:S(2)}) collective-permute-start(f32[8]{0:T(128)S(1)} %add.193), channel_id=1, source_target_pairs={{0,4},{1,5},{2,6},{3,7},{4,0},{5,1},{6,2},{7,3},{8,12},{9,13},{10,... | collective-permute-start | bytes 104 | tf_op jit(solution)/shard_map/ppermute | solution.py:31
  166.5 6.5 %collective-permute-start.19 = (f32[8]{0:T(128)S(1)}, f32[8]{0:T(128)S(1)}, u32[]{:S(2)}, u32[]{:S(2)}) collective-permute-start(f32[8]{0:T(128)S(1)} %add.194), channel_id=1, source_target_pairs={{0,8},{1,9},{2,10},{3,11},{4,12},{5,13},{6,14},{7,15},{8,0},{9,1},... | collective-permute-start | bytes 104 | tf_op jit(solution)/shard_map/ppermute | solution.py:31
  173.0 5.0 %collective-permute-start.20 = (f32[8]{0:T(128)S(1)}, f32[8]{0:T(128)S(1)}, u32[]{:S(2)}, u32[]{:S(2)}) collective-permute-start(f32[8]{0:T(128)S(1)} %add.195), channel_id=1, source_target_pairs={{0,16},{1,17},{2,18},{3,19},{4,20},{5,21},{6,22},{7,23},{8,24},{9,... | collective-permute-start | bytes 104 | tf_op jit(solution)/shard_map/ppermute | solution.py:31
  181.5 40.5 %collective-permute-start.28 = (f32[8,2,128]{2,0,1:T(8,128)S(1)}, f32[8,2,128]{2,0,1:T(8,128)S(1)}, u32[]{:S(2)}, u32[]{:S(2)}) collective-permute-start(f32[8,2,128]{2,0,1:T(8,128)S(1)} %get-tuple-element.81), channel_id=1, source_target_pairs={{0,1},{1,2},{2,3},{3,4},{4,5},{5,6},{6,7},{7,8},{8,9},{9,10},{10,1... | collective-permute-start | bytes 24584 | tf_op jit(solution)/shard_map/ppermute | solution.py:18
  183.5 38.5 %collective-permute-start.29 = (f32[8,2,128]{2,0,1:T(8,128)S(1)}, f32[8,2,128]{2,0,1:T(8,128)S(1)}, u32[]{:S(2)}, u32[]{:S(2)}) collective-permute-start(f32[8,2,128]{2,0,1:T(8,128)S(1)} %get-tuple-element.82), channel_id=1, source_target_pairs={{1,0},{2,1},{3,2},{4,3},{5,4},{6,5},{7,6},{8,7},{9,8},{10,9},{11,1... | collective-permute-start | bytes 24584 | tf_op jit(solution)/shard_map/ppermute | solution.py:18
  189.2 32.8 %collective-permute-start.30 = (f32[8,2,128]{2,0,1:T(8,128)S(1)}, f32[8,2,128]{2,0,1:T(8,128)S(1)}, u32[]{:S(2)}, u32[]{:S(2)}) collective-permute-start(f32[8,2,128]{2,0,1:T(8,128)S(1)} %get-tuple-element.84), channel_id=1, source_target_pairs={{0,16},{1,17},{2,18},{3,19},{4,20},{5,21},{6,22},{7,23},{8,24},{9,... | collective-permute-start | bytes 24584 | tf_op jit(solution)/shard_map/ppermute | solution.py:18
  196.9 25.1 %collective-permute-start.31 = (f32[8,2,128]{2,0,1:T(8,128)S(1)}, f32[8,2,128]{2,0,1:T(8,128)S(1)}, u32[]{:S(2)}, u32[]{:S(2)}) collective-permute-start(f32[8,2,128]{2,0,1:T(8,128)S(1)} %get-tuple-element.83), channel_id=1, source_target_pairs={{16,0},{17,1},{18,2},{19,3},{20,4},{21,5},{22,6},{23,7},{24,8},{25... | collective-permute-start | bytes 24584 | tf_op jit(solution)/shard_map/ppermute | solution.py:18
  199.7 3.6 %collective-permute-start.25 = (f32[8]{0:T(128)S(1)}, f32[8]{0:T(128)S(1)}, u32[]{:S(2)}, u32[]{:S(2)}) collective-permute-start(f32[8]{0:T(128)S(1)} %add.196), channel_id=1, source_target_pairs={{0,32},{1,33},{2,34},{3,35},{4,36},{5,37},{6,38},{7,39},{8,40},{9,... | collective-permute-start | bytes 104 | tf_op jit(solution)/shard_map/ppermute | solution.py:31
  203.3 11.3 %collective-permute-start.26 = (f32[8]{0:T(128)S(1)}, f32[8]{0:T(128)S(1)}, u32[]{:S(2)}, u32[]{:S(2)}) collective-permute-start(f32[8]{0:T(128)S(1)} %add.199), channel_id=1, source_target_pairs={{0,64},{1,65},{2,66},{3,67},{4,68},{5,69},{6,70},{7,71},{8,72},{9,... | collective-permute-start | bytes 104 | tf_op jit(solution)/shard_map/ppermute | solution.py:31
  214.5 7.4 %collective-permute-start.27 = (f32[8]{0:T(128)S(1)}, f32[8]{0:T(128)S(1)}, u32[]{:S(2)}, u32[]{:S(2)}) collective-permute-start(f32[8]{0:T(128)S(1)} %add.200), channel_id=1, source_target_pairs={{0,128},{1,129},{2,130},{3,131},{4,132},{5,133},{6,134},{7,135},{8... | collective-permute-start | bytes 104 | tf_op jit(solution)/shard_map/ppermute | solution.py:31
  223.7 30.6 %collective-permute-start.36 = (f32[8,2,128]{2,0,1:T(8,128)S(1)}, f32[8,2,128]{2,0,1:T(8,128)S(1)}, u32[]{:S(2)}, u32[]{:S(2)}) collective-permute-start(f32[8,2,128]{2,0,1:T(8,128)S(1)} %get-tuple-element.77), channel_id=1, source_target_pairs={{0,1},{1,2},{2,3},{3,4},{4,5},{5,6},{6,7},{7,8},{8,9},{9,10},{10,1... | collective-permute-start | bytes 24584 | tf_op jit(solution)/shard_map/ppermute | solution.py:18
  225.7 28.7 %collective-permute-start.37 = (f32[8,2,128]{2,0,1:T(8,128)S(1)}, f32[8,2,128]{2,0,1:T(8,128)S(1)}, u32[]{:S(2)}, u32[]{:S(2)}) collective-permute-start(f32[8,2,128]{2,0,1:T(8,128)S(1)} %get-tuple-element.78), channel_id=1, source_target_pairs={{1,0},{2,1},{3,2},{4,3},{5,4},{6,5},{7,6},{8,7},{9,8},{10,9},{11,1... | collective-permute-start | bytes 24584 | tf_op jit(solution)/shard_map/ppermute | solution.py:18
  231.4 22.9 %collective-permute-start.38 = (f32[8,2,128]{2,0,1:T(8,128)S(1)}, f32[8,2,128]{2,0,1:T(8,128)S(1)}, u32[]{:S(2)}, u32[]{:S(2)}) collective-permute-start(f32[8,2,128]{2,0,1:T(8,128)S(1)} %get-tuple-element.80), channel_id=1, source_target_pairs={{0,16},{1,17},{2,18},{3,19},{4,20},{5,21},{6,22},{7,23},{8,24},{9,... | collective-permute-start | bytes 24584 | tf_op jit(solution)/shard_map/ppermute | solution.py:18
  239.0 15.4 %collective-permute-start.39 = (f32[8,2,128]{2,0,1:T(8,128)S(1)}, f32[8,2,128]{2,0,1:T(8,128)S(1)}, u32[]{:S(2)}, u32[]{:S(2)}) collective-permute-start(f32[8,2,128]{2,0,1:T(8,128)S(1)} %get-tuple-element.79), channel_id=1, source_target_pairs={{16,0},{17,1},{18,2},{19,3},{20,4},{21,5},{22,6},{23,7},{24,8},{25... | collective-permute-start | bytes 24584 | tf_op jit(solution)/shard_map/ppermute | solution.py:18
  241.0 1.2 collective-permute-start.32
  242.2 3.5 %collective-permute-start.33 = (f32[8]{0:T(128)S(1)}, f32[8]{0:T(128)S(1)}, u32[]{:S(2)}, u32[]{:S(2)}) collective-permute-start(f32[8]{0:T(128)S(1)} %add.211), channel_id=1, source_target_pairs={{0,2},{1,3},{2,0},{3,1},{4,6},{5,7},{6,4},{7,5},{8,10},{9,11},{10,... | collective-permute-start | bytes 104 | tf_op jit(solution)/shard_map/ppermute | solution.py:31
  245.8 5.0 %collective-permute-start.34 = (f32[8]{0:T(128)S(1)}, f32[8]{0:T(128)S(1)}, u32[]{:S(2)}, u32[]{:S(2)}) collective-permute-start(f32[8]{0:T(128)S(1)} %add.212), channel_id=1, source_target_pairs={{0,4},{1,5},{2,6},{3,7},{4,0},{5,1},{6,2},{7,3},{8,12},{9,13},{10,... | collective-permute-start | bytes 104 | tf_op jit(solution)/shard_map/ppermute | solution.py:31
  250.8 3.5 %collective-permute-start.35 = (f32[8]{0:T(128)S(1)}, f32[8]{0:T(128)S(1)}, u32[]{:S(2)}, u32[]{:S(2)}) collective-permute-start(f32[8]{0:T(128)S(1)} %add.213), channel_id=1, source_target_pairs={{0,8},{1,9},{2,10},{3,11},{4,12},{5,13},{6,14},{7,15},{8,0},{9,1},... | collective-permute-start | bytes 104 | tf_op jit(solution)/shard_map/ppermute | solution.py:31
  256.0 44.9 %collective-permute-start.44 = (f32[8,2,128]{2,0,1:T(8,128)S(1)}, f32[8,2,128]{2,0,1:T(8,128)S(1)}, u32[]{:S(2)}, u32[]{:S(2)}) collective-permute-start(f32[8,2,128]{2,0,1:T(8,128)S(1)} %get-tuple-element.73), channel_id=1, source_target_pairs={{0,1},{1,2},{2,3},{3,4},{4,5},{5,6},{6,7},{7,8},{8,9},{9,10},{10,1... | collective-permute-start | bytes 24584 | tf_op jit(solution)/shard_map/ppermute | solution.py:18
  257.9 43.0 %collective-permute-start.45 = (f32[8,2,128]{2,0,1:T(8,128)S(1)}, f32[8,2,128]{2,0,1:T(8,128)S(1)}, u32[]{:S(2)}, u32[]{:S(2)}) collective-permute-start(f32[8,2,128]{2,0,1:T(8,128)S(1)} %get-tuple-element.74), channel_id=1, source_target_pairs={{1,0},{2,1},{3,2},{4,3},{5,4},{6,5},{7,6},{8,7},{9,8},{10,9},{11,1... | collective-permute-start | bytes 24584 | tf_op jit(solution)/shard_map/ppermute | solution.py:18
  263.7 37.3 %collective-permute-start.46 = (f32[8,2,128]{2,0,1:T(8,128)S(1)}, f32[8,2,128]{2,0,1:T(8,128)S(1)}, u32[]{:S(2)}, u32[]{:S(2)}) collective-permute-start(f32[8,2,128]{2,0,1:T(8,128)S(1)} %get-tuple-element.76), channel_id=1, source_target_pairs={{0,16},{1,17},{2,18},{3,19},{4,20},{5,21},{6,22},{7,23},{8,24},{9,... | collective-permute-start | bytes 24584 | tf_op jit(solution)/shard_map/ppermute | solution.py:18
  272.1 28.8 %collective-permute-start.47 = (f32[8,2,128]{2,0,1:T(8,128)S(1)}, f32[8,2,128]{2,0,1:T(8,128)S(1)}, u32[]{:S(2)}, u32[]{:S(2)}) collective-permute-start(f32[8,2,128]{2,0,1:T(8,128)S(1)} %get-tuple-element.75), channel_id=1, source_target_pairs={{16,0},{17,1},{18,2},{19,3},{20,4},{21,5},{22,6},{23,7},{24,8},{25... | collective-permute-start | bytes 24584 | tf_op jit(solution)/shard_map/ppermute | solution.py:18
  274.1 5.1 %collective-permute-start.40 = (f32[8]{0:T(128)S(1)}, f32[8]{0:T(128)S(1)}, u32[]{:S(2)}, u32[]{:S(2)}) collective-permute-start(f32[8]{0:T(128)S(1)} %add.214), channel_id=1, source_target_pairs={{0,16},{1,17},{2,18},{3,19},{4,20},{5,21},{6,22},{7,23},{8,24},{9,... | collective-permute-start | bytes 104 | tf_op jit(solution)/shard_map/ppermute | solution.py:31
  279.2 3.5 %collective-permute-start.41 = (f32[8]{0:T(128)S(1)}, f32[8]{0:T(128)S(1)}, u32[]{:S(2)}, u32[]{:S(2)}) collective-permute-start(f32[8]{0:T(128)S(1)} %add.215), channel_id=1, source_target_pairs={{0,32},{1,33},{2,34},{3,35},{4,36},{5,37},{6,38},{7,39},{8,40},{9,... | collective-permute-start | bytes 104 | tf_op jit(solution)/shard_map/ppermute | solution.py:31
  282.8 10.2 %collective-permute-start.42 = (f32[8]{0:T(128)S(1)}, f32[8]{0:T(128)S(1)}, u32[]{:S(2)}, u32[]{:S(2)}) collective-permute-start(f32[8]{0:T(128)S(1)} %add.216), channel_id=1, source_target_pairs={{0,64},{1,65},{2,66},{3,67},{4,68},{5,69},{6,70},{7,71},{8,72},{9,... | collective-permute-start | bytes 104 | tf_op jit(solution)/shard_map/ppermute | solution.py:31
  292.9 8.0 %collective-permute-start.43 = (f32[8]{0:T(128)S(1)}, f32[8]{0:T(128)S(1)}, u32[]{:S(2)}, u32[]{:S(2)}) collective-permute-start(f32[8]{0:T(128)S(1)} %add.217), channel_id=1, source_target_pairs={{0,128},{1,129},{2,130},{3,131},{4,132},{5,133},{6,134},{7,135},{8... | collective-permute-start | bytes 104 | tf_op jit(solution)/shard_map/ppermute | solution.py:31
  (21 other events, 462.4 us)

commit v3 on v1

--- a/solution.py
+++ b/solution.py
@@ -18,15 +18,23 @@
     return lax.ppermute(value, axis, [(source, source + steps) for source in range(first, last)])
 
 
-def all_sum(value, axis):
+def sum_bits(axis):
     count = lax.axis_size(axis)
     if count & (count - 1):
-        return lax.psum(value, axis)
-    bit = 1
-    while bit < count:
+        return None
+    return [1 << b for b in range(count.bit_length() - 1)]
+
+
+def sum_rounds(value, axis, bits):
+    count = lax.axis_size(axis)
+    for bit in bits:
         value = value + lax.ppermute(value, axis, [(i, i ^ bit) for i in range(count)])
-        bit *= 2
     return value
+
+
+def split_even(items, parts):
+    cuts = [len(items) * p // parts for p in range(parts + 1)]
+    return [items[cuts[p] : cuts[p + 1]] for p in range(parts)]
 
 
 def rotate(conduct, suscept, beside, axis):
@@ -107,37 +115,82 @@
     bus_total = buses * lax.axis_size("region")
 
     def halo(values):
-        tiles = jnp.einsum("ktb,scb->ksct", pick_full, values, precision=highest)
+        shape = values.shape
+        flat = values.reshape((-1,) + shape[-2:])
+        tiles = jnp.einsum("ktb,ncb->knct", pick_full, flat, precision=highest)
         incoming = exchange(tiles)
-        return jnp.einsum("ksct,ktb->scb", incoming, place_full, precision=highest)
+        spread = jnp.einsum("knct,ktb->ncb", incoming, place_full, precision=highest)
+        return spread.reshape(shape)
 
     def inside_sum(values):
-        return jnp.einsum("ij,scj->sci", mask_full, values, precision=highest)
-
+        return jnp.einsum("ij,...cj->...ci", mask_full, values, precision=highest)
+
+    def damp(squares):
+        return jnp.minimum(1.0, trust_radius / jnp.sqrt(squares / (2 * bus_total) + 1e-06))
+
+    def sweeps(residuals, partial, chunks):
+        count = residuals.shape[0]
+        update = None
+        for sweep_number in range(SWEEPS):
+            forcing = -residuals
+            if sweep_number > 0:
+                arrived = halo(update)
+                if chunks:
+                    partial = sum_rounds(partial, "region", chunks[sweep_number - 1])
+                    partial, arrived = lax.optimization_barrier((partial, arrived))
+                forcing = forcing + rotate(conductance, susceptance, arrived, -2)
+            forcing = forcing.reshape(count * scenarios, 2 * buses).astype(jnp.bfloat16)
+            update = jnp.dot(forcing, region_inverse, preferred_element_type=jnp.float32)
+            update = update.reshape(count, scenarios, 2, buses)
+        return update, partial
+
+    assert NEWTON == 2
+    bits = sum_bits("region")
     beside = inside_sum(voltage) + halo(voltage)
-    for newton in range(NEWTON):
-        magnitude = voltage[:, 0:1] ** 2 + voltage[:, 1:2] ** 2
-        residual = (
-            diag_admit * voltage
-            - rotate(conductance, susceptance, beside, 1)
-            + load_coeff * magnitude * voltage
-            - injection
-        )
-        squares = all_sum(jnp.sum(residual * residual, axis=(1, 2)), "region")
-        damping = jnp.minimum(1.0, trust_radius / jnp.sqrt(squares / (2 * bus_total) + 1e-06))
-        update = jnp.zeros_like(voltage)
-        for sweep_number in range(SWEEPS):
-            forcing = -residual
-            if sweep_number > 0:
-                forcing = forcing + rotate(conductance, susceptance, halo(update), 1)
-            forcing = forcing.reshape(scenarios, 2 * buses).astype(jnp.bfloat16)
-            update = jnp.dot(forcing, region_inverse, preferred_element_type=jnp.float32).reshape(
-                scenarios, 2, buses
-            )
-        step = damping[:, None, None]
-        voltage = voltage + step * update
-        if newton + 1 < NEWTON:
-            beside = beside + step * (inside_sum(update) + halo(update))
+    magnitude = voltage[:, 0:1] ** 2 + voltage[:, 1:2] ** 2
+    residual = (
+        diag_admit * voltage
+        - rotate(conductance, susceptance, beside, 1)
+        + load_coeff * magnitude * voltage
+        - injection
+    )
+    partial = jnp.sum(residual * residual, axis=(1, 2))[None]
+    update, partial = sweeps(residual[None], partial, None)
+    update = update[0]
+    extra = inside_sum(update) + halo(update)
+    cross = 2.0 * (voltage[:, 0:1] * update[:, 0:1] + voltage[:, 1:2] * update[:, 1:2])
+    square = update[:, 0:1] ** 2 + update[:, 1:2] ** 2
+    coeffs = jnp.stack(
+        [
+            residual,
+            diag_admit * update
+            - rotate(conductance, susceptance, extra, 1)
+            + load_coeff * (magnitude * update + cross * voltage),
+            load_coeff * (cross * update + square * voltage),
+            load_coeff * square * update,
+        ]
+    )
+    terms = coeffs.shape[0]
+    powers = [0.0] * (2 * terms - 1)
+    for i in range(terms):
+        for j in range(i, terms):
+            product = jnp.sum(coeffs[i] * coeffs[j], axis=(1, 2))
+            powers[i + j] = powers[i + j] + (product if i == j else 2.0 * product)
+    partial = jnp.concatenate([partial, jnp.stack(powers)])
+    chunks = None if bits is None else split_even(bits, SWEEPS - 1)
+    second, partial = sweeps(coeffs, partial, chunks)
+    if bits is None:
+        partial = lax.psum(partial, "region")
+    first_damping = damp(partial[0])
+    poly = partial[-1]
+    for k in range(len(powers) - 2, -1, -1):
+        poly = poly * first_damping + partial[1 + k]
+    second_damping = damp(jnp.maximum(poly, 0.0))
+    voltage = voltage + first_damping[:, None, None] * update
+    step_update = second[-1]
+    for k in range(terms - 2, -1, -1):
+        step_update = step_update * first_damping[:, None, None] + second[k]
+    voltage = voltage + second_damping[:, None, None] * step_update
     return voltage
 
 

time: 300 us -> 272 us (0.907)
  waiting for transfers between devices: 91.9 us -> 75.4 us
  starting transfers between devices: 157 us -> 145 us
    ppermute x16 -> x8, waiting for transfers between devices: 38.4 us -> 21.3 us  [sum_rounds(): lax.ppermute(value, axis, [(i, i ^ bit) for i in range(count)])]
    ppermute x16 -> x8, starting transfers between devices: 36.4 us -> 21.2 us  [sum_rounds(): lax.ppermute(value, axis, [(i, i ^ bit) for i in range(count)])]
    ppermute x32, starting transfers between devices: 121 us -> 124 us  [from_behind(): lax.ppermute(value, axis, [(source, source + steps) for source in range(f...]
  transfers between devices with their start and end apart: 48 -> 40, of which waited for: 21 -> 15; matrix products, arithmetic and copies ran while one was open for 5% -> 4% of each run, Pallas kernels for 0% -> 0%
where the time goes in v3:
time: 272 us; the launch traced here: 270 us
  starting transfers between devices  145 us (53%)
  waiting for transfers between devices  75.4 us (28%)
  matrix products  43.3 us (16%)
    ppermute x32, starting transfers between devices, from_behind(): lax.ppermute(value, axis, [(source, source + steps) for source in range(f...  124 us
    ppermute x32, waiting for transfers between devices, from_behind(): lax.ppermute(value, axis, [(source, source + steps) for source in range(f...  54.1 us
    ppermute x8, waiting for transfers between devices, sum_rounds(): lax.ppermute(value, axis, [(i, i ^ bit) for i in range(count)])  21.3 us
    ppermute x8, starting transfers between devices, sum_rounds(): lax.ppermute(value, axis, [(i, i ^ bit) for i in range(count)])  21.2 us
    dot_general x1, matrix products, local(): jnp.einsum('sbh,hk->sbk', gathered, neigh_weight[number], preferred_eleme...  8.26 us
    dot_general x2, matrix products, local(): jnp.einsum('ktb,sbh->ksth', pick_half, hidden, preferred_element_type=jnp...  5.98 us
  transfers between devices with their start and end apart: 40, of which 15 were waited for; matrix products, arithmetic and copies ran while one was open for 4% of the time, Pallas kernels for 0%

profile of v3, /device:TPU:4, one launch (start us, length us, event | category | flops | bytes accessed | tf_op | source)
XLA Modules:
  0.0 269.6 jit_solution(13059745826296337145)
XLA Ops:
  0.8 2.9 %convert_bitcast_fusion.1 = bf16[4,8,128,256]{3,2,1,0:T(8,128)(2,1)S(1)} fusion(bf16[8,512,256]{2,1,0:T(8,128)(2,1)} %param.29, s32[4,128]{1,0:T(4,128)} %param.31, pred[4,128]{1,0:T(4,128)(4,1)S(1)} %iota_compare_fusion.3), kind=kOutput, calls=%fused_computation.39 | convolution fusion | flops 1075314688 | bytes 4196864 | tf_op jit(solution)/shard_map/ktb,sbh->ksth/dot_general | solution.py:86
  3.9 4.5 %collective-permute-start.1 = (bf16[8,128,256]{2,1,0:T(8,128)(2,1)S(1)}, bf16[8,128,256]{2,1,0:T(8,128)(2,1)S(1)}, u32[]{:S(2)}, u32[]{:S(2)}) collective-permute-start(bf16[8,128,256]{2,1,0:T(8,128)(2,1)S(1)} %get-tuple-element.112), channel_id=1, source_target_pairs={{1,0},{2,1},{3,2},{4,3},{5,4},{6,5},{7,6},{8,7},{9,8},{10,9},{11,1... | collective-permute-start | bytes 1572872 | tf_op jit(solution)/shard_map/ppermute | solution.py:18
  8.4 5.5 %collective-permute-start.2 = (bf16[8,128,256]{2,1,0:T(8,128)(2,1)S(1)}, bf16[8,128,256]{2,1,0:T(8,128)(2,1)S(1)}, u32[]{:S(2)}, u32[]{:S(2)}) collective-permute-start(bf16[8,128,256]{2,1,0:T(8,128)(2,1)S(1)} %get-tuple-element.111), channel_id=1, source_target_pairs={{0,16},{1,17},{2,18},{3,19},{4,20},{5,21},{6,22},{7,23},{8,24},{9,... | collective-permute-start | bytes 1572872 | tf_op jit(solution)/shard_map/ppermute | solution.py:18
  13.9 1.9 collective-permute-start.3
  15.9 2.1 collective-permute-start
  17.9 2.7 %fusion.128 = f32[8,512,256]{2,1,0:T(8,128)} fusion(bf16[8,512,256]{2,1,0:T(8,128)(2,1)S(1)} %copy-done.3, bf16[2,256,256]{2,1,0:T(8,128)(2,1)S(1)} %copy-done.5), kind=kOutput, calls=%fused_computation.124 | convolution fusion | flops 536870912 | bytes 6422528 | tf_op jit(solution)/shard_map/sbh,hk->sbk/dot_general | solution.py:91
  20.9 3.3 %fusion.90 = f32[8,256,512]{1,2,0:T(8,128)} fusion(bf16[8,512,256]{2,1,0:T(8,128)(2,1)S(1)} %copy-done.3, s32[512,512]{1,0:T(8,128)S(1)} %copy-done.2), kind=kOutput, calls=%fused_computation.85 | convolution fusion | flops 1074003968 | bytes 7340032 | tf_op jit(solution)/shard_map/ij,sjh->sih/dot_general | solution.py:90
  24.2 10.7 %collective-permute-done.2 = bf16[8,128,256]{2,1,0:T(8,128)(2,1)S(1)} collective-permute-done((bf16[8,128,256]{2,1,0:T(8,128)(2,1)S(1)}, bf16[8,128,256]{2,1,0:T(8,128)(2,1)S(1)}, u32[]{:S(2)}, u32[]{:S(2)}) %collective-permute-start.2) | collective-permute-done | bytes 524320 | tf_op jit(solution)/shard_map/ppermute | solution.py:18
  34.9 8.1 %collective-permute-done = bf16[8,128,256]{2,1,0:T(8,128)(2,1)S(1)} collective-permute-done((bf16[8,128,256]{2,1,0:T(8,128)(2,1)S(1)}, bf16[8,128,256]{2,1,0:T(8,128)(2,1)S(1)}, u32[]{:S(2)}, u32[]{:S(2)}) %collective-permute-start) | collective-permute-done | bytes 524320 | tf_op jit(solution)/shard_map/ppermute | solution.py:18
  43.8 8.3 %add_convert_fusion.1 = bf16[8,512,256]{2,1,0:T(8,128)(2,1)} fusion(f32[8,512,256]{2,1,0:T(8,128)} %fusion.128, bf16[8,512,256]{2,1,0:T(8,128)(2,1)S(1)} %copy-done.3, f32[256]{0:T(256)S(1)} %bitcast.563, f32[8,256,512]{1,2,0:T(8,128)} %fusion.90, bf16[1,8,128,256]{3,2,1,0:T(8,128)(2,1)} %bitcast.567, bf16[1,8,128,256]{3,2,1,0:T(8,128)(2,1)} %bitcast.565, ...), kind=kOutput, calls=%fused_computation.7 | convolution fusion | flops 1626603520 | bytes 14814208 | tf_op jit(solution)/shard_map/sbh,hk->sbk/dot_general | solution.py:100
  52.1 3.1 %convert_bitcast_fusion = bf16[4,8,128,256]{2,3,0,1:T(8,128)(2,1)S(1)} fusion(bf16[8,512,256]{2,1,0:T(8,128)(2,1)} %add_convert_fusion.1, s32[4,128]{1,0:T(4,128)S(1)} %copy-done.16, pred[4,128]{1,0:T(4,128)(4,1)S(1)} %iota_compare_fusion.3), kind=kOutput, calls=%fused_computation.38 | convolution fusion | flops 1075314688 | bytes 4196864 | tf_op jit(solution)/shard_map/ktb,sbh->ksth/dot_general | solution.py:86
  55.3 2.1 collective-permute-start.4
  57.4 5.8 %collective-permute-start.5 = (bf16[8,128,256]{1,2,0:T(8,128)(2,1)S(1)}, bf16[8,128,256]{1,2,0:T(8,128)(2,1)S(1)}, u32[]{:S(2)}, u32[]{:S(2)}) collective-permute-start(bf16[8,128,256]{1,2,0:T(8,128)(2,1)S(1)} %get-tuple-element.106), channel_id=1, source_target_pairs={{1,0},{2,1},{3,2},{4,3},{5,4},{6,5},{7,6},{8,7},{9,8},{10,9},{11,1... | collective-permute-start | bytes 1572872 | tf_op jit(solution)/shard_map/ppermute | solution.py:18
  65.1 5.6 %collective-permute-start.7 = (bf16[8,128,256]{1,2,0:T(8,128)(2,1)S(1)}, bf16[8,128,256]{1,2,0:T(8,128)(2,1)S(1)}, u32[]{:S(2)}, u32[]{:S(2)}) collective-permute-start(bf16[8,128,256]{1,2,0:T(8,128)(2,1)S(1)} %get-tuple-element.107), channel_id=1, source_target_pairs={{16,0},{17,1},{18,2},{19,3},{20,4},{21,5},{22,6},{23,7},{24,8},{25... | collective-permute-start | bytes 1572872 | tf_op jit(solution)/shard_map/ppermute | solution.py:18
  70.7 2.7 %fusion.125 = f32[8,512,256]{2,1,0:T(8,128)} fusion(bf16[8,512,256]{2,1,0:T(8,128)(2,1)S(1)} %copy-done.4, bf16[2,256,256]{2,1,0:T(8,128)(2,1)S(1)} %copy-done.5), kind=kOutput, calls=%fused_computation.121 | convolution fusion | flops 536870912 | bytes 6422528 | tf_op jit(solution)/shard_map/sbh,hk->sbk/dot_general | solution.py:91
  74.7 13.6 %collective-permute-done.6 = bf16[8,128,256]{1,2,0:T(8,128)(2,1)S(1)} collective-permute-done((bf16[8,128,256]{1,2,0:T(8,128)(2,1)S(1)}, bf16[8,128,256]{1,2,0:T(8,128)(2,1)S(1)}, u32[]{:S(2)}, u32[]{:S(2)}) %collective-permute-start.6) | collective-permute-done | bytes 524320 | tf_op jit(solution)/shard_map/ppermute | solution.py:18
  88.3 2.7 fusion.1
  91.0 4.5 %fusion.55 = f32[8,512,2]{1,2,0:T(2,128)S(1)} fusion(f32[8,512,256]{2,1,0:T(8,128)} %fusion.125, bf16[8,512,256]{2,1,0:T(8,128)(2,1)S(1)} %copy-done.4, bf16[8,256,512]{1,2,0:T(8,128)(2,1)} %fusion.1, f32[256]{0:T(256)S(1)} %bitcast.562, bf16[2,256,256]{2,1,0:T(8,128)(2,1)} %param.35, f32[2]{0:T(128)S(1)} %copy-done.19, bf16[2,256]{1,0:T(2,128)(2,1)S(1)} %copy-done.18), kind=kOutput, calls=%fused_computation.59 | convolution fusion | flops 550510592 | bytes 8554504 | tf_op jit(solution)/shard_map/sbh,ch->scb/dot_general | solution.py:108
  96.2 1.9 collective-permute-start.8
  98.1 5.8 %collective-permute-start.9 = (f32[8,2,128]{2,0,1:T(8,128)S(1)}, f32[8,2,128]{2,0,1:T(8,128)S(1)}, u32[]{:S(2)}, u32[]{:S(2)}) collective-permute-start(f32[8,2,128]{2,0,1:T(8,128)S(1)} %get-tuple-element.156), channel_id=1, source_target_pairs={{1,0},{2,1},{3,2},{4,3},{5,4},{6,5},{7,6},{8,7},{9,8},{10,9},{11,1... | collective-permute-start | bytes 24584 | tf_op jit(solution)/shard_map/ppermute | solution.py:18
  103.9 5.2 %collective-permute-start.10 = (f32[8,2,128]{2,0,1:T(8,128)S(1)}, f32[8,2,128]{2,0,1:T(8,128)S(1)}, u32[]{:S(2)}, u32[]{:S(2)}) collective-permute-start(f32[8,2,128]{2,0,1:T(8,128)S(1)} %get-tuple-element.158), channel_id=1, source_target_pairs={{0,16},{1,17},{2,18},{3,19},{4,20},{5,21},{6,22},{7,23},{8,24},{9,... | collective-permute-start | bytes 24584 | tf_op jit(solution)/shard_map/ppermute | solution.py:18
  109.1 2.2 collective-permute-start.11
  112.3 4.7 %collective-permute-done.11 = f32[8,2,128]{2,0,1:T(8,128)S(1)} collective-permute-done((f32[8,2,128]{2,0,1:T(8,128)S(1)}, f32[8,2,128]{2,0,1:T(8,128)S(1)}, u32[]{:S(2)}, u32[]{:S(2)}) %collective-permute-start.11) | collective-permute-done | bytes 8224 | tf_op jit(solution)/shard_map/ppermute | solution.py:18
  118.8 1.9 collective-permute-start.12
  120.8 5.8 %collective-permute-start.13 = (f32[8,2,128]{2,0,1:T(8,128)S(1)}, f32[8,2,128]{2,0,1:T(8,128)S(1)}, u32[]{:S(2)}, u32[]{:S(2)}) collective-permute-start(f32[8,2,128]{2,0,1:T(8,128)S(1)} %get-tuple-element.152), channel_id=1, source_target_pairs={{1,0},{2,1},{3,2},{4,3},{5,4},{6,5},{7,6},{8,7},{9,8},{10,9},{11,1... | collective-permute-start | bytes 24584 | tf_op jit(solution)/shard_map/ppermute | solution.py:18
  126.5 4.7 %collective-permute-start.14 = (f32[8,2,128]{2,0,1:T(8,128)S(1)}, f32[8,2,128]{2,0,1:T(8,128)S(1)}, u32[]{:S(2)}, u32[]{:S(2)}) collective-permute-start(f32[8,2,128]{2,0,1:T(8,128)S(1)} %get-tuple-element.154), channel_id=1, source_target_pairs={{0,16},{1,17},{2,18},{3,19},{4,20},{5,21},{6,22},{7,23},{8,24},{9,... | collective-permute-start | bytes 24584 | tf_op jit(solution)/shard_map/ppermute | solution.py:18
  131.2 2.6 collective-permute-start.15
  133.9 5.3 %collective-permute-done.15 = f32[8,2,128]{2,0,1:T(8,128)S(1)} collective-permute-done((f32[8,2,128]{2,0,1:T(8,128)S(1)}, f32[8,2,128]{2,0,1:T(8,128)S(1)}, u32[]{:S(2)}, u32[]{:S(2)}) %collective-permute-start.15) | collective-permute-done | bytes 8224 | tf_op jit(solution)/shard_map/ppermute | solution.py:18
  140.9 1.9 collective-permute-start.16
  142.8 5.8 %collective-permute-start.17 = (f32[8,2,128]{2,0,1:T(8,128)S(1)}, f32[8,2,128]{2,0,1:T(8,128)S(1)}, u32[]{:S(2)}, u32[]{:S(2)}) collective-permute-start(f32[8,2,128]{2,0,1:T(8,128)S(1)} %get-tuple-element.146), channel_id=1, source_target_pairs={{1,0},{2,1},{3,2},{4,3},{5,4},{6,5},{7,6},{8,7},{9,8},{10,9},{11,1... | collective-permute-start | bytes 24584 | tf_op jit(solution)/shard_map/ppermute | solution.py:18
  148.6 5.2 %collective-permute-start.18 = (f32[8,2,128]{2,0,1:T(8,128)S(1)}, f32[8,2,128]{2,0,1:T(8,128)S(1)}, u32[]{:S(2)}, u32[]{:S(2)}) collective-permute-start(f32[8,2,128]{2,0,1:T(8,128)S(1)} %get-tuple-element.148), channel_id=1, source_target_pairs={{0,16},{1,17},{2,18},{3,19},{4,20},{5,21},{6,22},{7,23},{8,24},{9,... | collective-permute-start | bytes 24584 | tf_op jit(solution)/shard_map/ppermute | solution.py:18
  153.8 2.2 collective-permute-start.19
  156.0 5.8 %collective-permute-done.19 = f32[8,2,128]{2,0,1:T(8,128)S(1)} collective-permute-done((f32[8,2,128]{2,0,1:T(8,128)S(1)}, f32[8,2,128]{2,0,1:T(8,128)S(1)}, u32[]{:S(2)}, u32[]{:S(2)}) %collective-permute-start.19) | collective-permute-done | bytes 8224 | tf_op jit(solution)/shard_map/ppermute | solution.py:18
  166.4 5.8 %collective-permute-start.21 = (f32[8,2,128]{2,0,1:T(8,128)S(1)}, f32[8,2,128]{2,0,1:T(8,128)S(1)}, u32[]{:S(2)}, u32[]{:S(2)}) collective-permute-start(f32[8,2,128]{2,0,1:T(8,128)S(1)} %get-tuple-element.139), channel_id=1, source_target_pairs={{1,0},{2,1},{3,2},{4,3},{5,4},{6,5},{7,6},{8,7},{9,8},{10,9},{11,1... | collective-permute-start | bytes 24584 | tf_op jit(solution)/shard_map/ppermute | solution.py:18
  172.1 6.0 %collective-permute-start.22 = (f32[8,2,128]{2,0,1:T(8,128)S(1)}, f32[8,2,128]{2,0,1:T(8,128)S(1)}, u32[]{:S(2)}, u32[]{:S(2)}) collective-permute-start(f32[8,2,128]{2,0,1:T(8,128)S(1)} %get-tuple-element.141), channel_id=1, source_target_pairs={{0,16},{1,17},{2,18},{3,19},{4,20},{5,21},{6,22},{7,23},{8,24},{9,... | collective-permute-start | bytes 24584 | tf_op jit(solution)/shard_map/ppermute | solution.py:18
  178.1 1.9 collective-permute-start.23
  180.1 5.9 %collective-permute-done.23 = f32[8,2,128]{2,0,1:T(8,128)S(1)} collective-permute-done((f32[8,2,128]{2,0,1:T(8,128)S(1)}, f32[8,2,128]{2,0,1:T(8,128)S(1)}, u32[]{:S(2)}, u32[]{:S(2)}) %collective-permute-start.23) | collective-permute-done | bytes 8224 | tf_op jit(solution)/shard_map/ppermute | solution.py:18
  190.3 5.8 %collective-permute-start.29 = (f32[32,2,128]{2,0,1:T(8,128)S(1)}, f32[32,2,128]{2,0,1:T(8,128)S(1)}, u32[]{:S(2)}, u32[]{:S(2)}) collective-permute-start(f32[32,2,128]{2,0,1:T(8,128)S(1)} %get-tuple-element.126), channel_id=1, source_target_pairs={{1,0},{2,1},{3,2},{4,3},{5,4},{6,5},{7,6},{8,7},{9,8},{10,9},{11,1... | collective-permute-start | bytes 98312 | tf_op jit(solution)/shard_map/ppermute | solution.py:18
  196.0 6.6 %collective-permute-start.30 = (f32[32,2,128]{2,0,1:T(8,128)S(1)}, f32[32,2,128]{2,0,1:T(8,128)S(1)}, u32[]{:S(2)}, u32[]{:S(2)}) collective-permute-start(f32[32,2,128]{2,0,1:T(8,128)S(1)} %get-tuple-element.128), channel_id=1, source_target_pairs={{0,16},{1,17},{2,18},{3,19},{4,20},{5,21},{6,22},{7,23},{8,24},{9,... | collective-permute-start | bytes 98312 | tf_op jit(solution)/shard_map/ppermute | solution.py:18
  206.2 3.6 %collective-permute-done.25 = f32[8,8]{1,0:T(8,128)S(1)} collective-permute-done((f32[8,8]{1,0:T(8,128)S(1)}, f32[8,8]{1,0:T(8,128)S(1)}, u32[]{:S(2)}, u32[]{:S(2)}) %collective-permute-start.25) | collective-permute-done | bytes 288 | tf_op jit(solution)/shard_map/ppermute | solution.py:31
  209.8 5.1 %collective-permute-done.26 = f32[8,8]{1,0:T(8,128)S(1)} collective-permute-done((f32[8,8]{1,0:T(8,128)S(1)}, f32[8,8]{1,0:T(8,128)S(1)}, u32[]{:S(2)}, u32[]{:S(2)}) %collective-permute-start.26) | collective-permute-done | bytes 288 | tf_op jit(solution)/shard_map/ppermute | solution.py:31
  214.9 2.1 collective-permute-start.27
  222.6 5.8 %collective-permute-start.37 = (f32[32,2,128]{2,0,1:T(8,128)S(1)}, f32[32,2,128]{2,0,1:T(8,128)S(1)}, u32[]{:S(2)}, u32[]{:S(2)}) collective-permute-start(f32[32,2,128]{2,0,1:T(8,128)S(1)} %get-tuple-element.122), channel_id=1, source_target_pairs={{1,0},{2,1},{3,2},{4,3},{5,4},{6,5},{7,6},{8,7},{9,8},{10,9},{11,1... | collective-permute-start | bytes 98312 | tf_op jit(solution)/shard_map/ppermute | solution.py:18
  228.3 8.3 %collective-permute-start.38 = (f32[32,2,128]{2,0,1:T(8,128)S(1)}, f32[32,2,128]{2,0,1:T(8,128)S(1)}, u32[]{:S(2)}, u32[]{:S(2)}) collective-permute-start(f32[32,2,128]{2,0,1:T(8,128)S(1)} %get-tuple-element.124), channel_id=1, source_target_pairs={{0,16},{1,17},{2,18},{3,19},{4,20},{5,21},{6,22},{7,23},{8,24},{9,... | collective-permute-start | bytes 98312 | tf_op jit(solution)/shard_map/ppermute | solution.py:18
  238.7 5.1 %collective-permute-done.32 = f32[8,8]{1,0:T(8,128)S(1)} collective-permute-done((f32[8,8]{1,0:T(8,128)S(1)}, f32[8,8]{1,0:T(8,128)S(1)}, u32[]{:S(2)}, u32[]{:S(2)}) %collective-permute-start.32) | collective-permute-done | bytes 288 | tf_op jit(solution)/shard_map/ppermute | solution.py:31
  243.8 3.8 %collective-permute-start.33 = (f32[8,8]{1,0:T(8,128)S(1)}, f32[8,8]{1,0:T(8,128)S(1)}, u32[]{:S(2)}, u32[]{:S(2)}) collective-permute-start(f32[8,8]{1,0:T(8,128)S(1)} %add.314), channel_id=1, source_target_pairs={{0,32},{1,33},{2,34},{3,35},{4,36},{5,37},{6,38},{7,39},{8,40},{9,... | collective-permute-start | bytes 776 | tf_op jit(solution)/shard_map/ppermute | solution.py:31
  249.2 8.4 %collective-permute-start.34 = (f32[8,8]{1,0:T(8,128)S(1)}, f32[8,8]{1,0:T(8,128)S(1)}, u32[]{:S(2)}, u32[]{:S(2)}) collective-permute-start(f32[8,8]{1,0:T(8,128)S(1)} %add.315), channel_id=1, source_target_pairs={{0,64},{1,65},{2,66},{3,67},{4,68},{5,69},{6,70},{7,71},{8,72},{9,... | collective-permute-start | bytes 776 | tf_op jit(solution)/shard_map/ppermute | solution.py:31
  259.2 6.5 %collective-permute-start.35 = (f32[8,8]{1,0:T(8,128)S(1)}, f32[8,8]{1,0:T(8,128)S(1)}, u32[]{:S(2)}, u32[]{:S(2)}) collective-permute-start(f32[8,8]{1,0:T(8,128)S(1)} %add.316), channel_id=1, source_target_pairs={{0,128},{1,129},{2,130},{3,131},{4,132},{5,133},{6,134},{7,135},{8... | collective-permute-start | bytes 776 | tf_op jit(solution)/shard_map/ppermute | solution.py:31
  (169 shorter events, 37.3 us)
Async XLA Ops:
  0.0 20.6 %copy-start = (f32[16,2,512]{2,1,0:T(2,128)S(1)}, f32[16,2,512]{2,1,0:T(2,128)}, u32[]{:S(2)}) copy-start(f32[16,2,512]{2,1,0:T(2,128)} %param.38) | copy-start | bytes 196612
  3.9 20.3 %collective-permute-start.1 = (bf16[8,128,256]{2,1,0:T(8,128)(2,1)S(1)}, bf16[8,128,256]{2,1,0:T(8,128)(2,1)S(1)}, u32[]{:S(2)}, u32[]{:S(2)}) collective-permute-start(bf16[8,128,256]{2,1,0:T(8,128)(2,1)S(1)} %get-tuple-element.112), channel_id=1, source_target_pairs={{1,0},{2,1},{3,2},{4,3},{5,4},{6,5},{7,6},{8,7},{9,8},{10,9},{11,1... | collective-permute-start | bytes 1572872 | tf_op jit(solution)/shard_map/ppermute | solution.py:18
  8.4 26.5 %collective-permute-start.2 = (bf16[8,128,256]{2,1,0:T(8,128)(2,1)S(1)}, bf16[8,128,256]{2,1,0:T(8,128)(2,1)S(1)}, u32[]{:S(2)}, u32[]{:S(2)}) collective-permute-start(bf16[8,128,256]{2,1,0:T(8,128)(2,1)S(1)} %get-tuple-element.111), channel_id=1, source_target_pairs={{0,16},{1,17},{2,18},{3,19},{4,20},{5,21},{6,22},{7,23},{8,24},{9,... | collective-permute-start | bytes 1572872 | tf_op jit(solution)/shard_map/ppermute | solution.py:18
  13.9 21.0 %collective-permute-start.3 = (bf16[8,128,256]{2,1,0:T(8,128)(2,1)S(1)}, bf16[8,128,256]{2,1,0:T(8,128)(2,1)S(1)}, u32[]{:S(2)}, u32[]{:S(2)}) collective-permute-start(bf16[8,128,256]{2,1,0:T(8,128)(2,1)S(1)} %get-tuple-element.110), channel_id=1, source_target_pairs={{16,0},{17,1},{18,2},{19,3},{20,4},{21,5},{22,6},{23,7},{24,8},{25... | collective-permute-start | bytes 1572872 | tf_op jit(solution)/shard_map/ppermute | solution.py:18
  15.9 27.1 %collective-permute-start = (bf16[8,128,256]{2,1,0:T(8,128)(2,1)S(1)}, bf16[8,128,256]{2,1,0:T(8,128)(2,1)S(1)}, u32[]{:S(2)}, u32[]{:S(2)}) collective-permute-start(bf16[8,128,256]{2,1,0:T(8,128)(2,1)S(1)} %get-tuple-element.109), channel_id=1, source_target_pairs={{0,1},{1,2},{2,3},{3,4},{4,5},{5,6},{6,7},{7,8},{8,9},{9,10},{10,1... | collective-permute-start | bytes 1572872 | tf_op jit(solution)/shard_map/ppermute | solution.py:18
  20.9 23.0 %copy-start.17 = (s32[4,128]{1,0:T(4,128)S(1)}, s32[4,128]{1,0:T(4,128)}, u32[]{:S(2)}) copy-start(s32[4,128]{1,0:T(4,128)} %param.32) | copy-start | bytes 6148
  24.2 18.8 %copy-start.12 = (bf16[8,128,256]{2,1,0:T(8,128)(2,1)}, bf16[8,128,256]{2,1,0:T(8,128)(2,1)S(1)}, u32[]{:S(2)}) copy-start(bf16[8,128,256]{2,1,0:T(8,128)(2,1)S(1)} %collective-permute-done.1) | copy-start | bytes 1572868
  55.3 19.4 %collective-permute-start.4 = (bf16[8,128,256]{1,2,0:T(8,128)(2,1)S(1)}, bf16[8,128,256]{1,2,0:T(8,128)(2,1)S(1)}, u32[]{:S(2)}, u32[]{:S(2)}) collective-permute-start(bf16[8,128,256]{1,2,0:T(8,128)(2,1)S(1)} %get-tuple-element.105), channel_id=1, source_target_pairs={{0,1},{1,2},{2,3},{3,4},{4,5},{5,6},{6,7},{7,8},{8,9},{9,10},{10,1... | collective-permute-start | bytes 1572872 | tf_op jit(solution)/shard_map/ppermute | solution.py:18
  57.4 17.3 %collective-permute-start.5 = (bf16[8,128,256]{1,2,0:T(8,128)(2,1)S(1)}, bf16[8,128,256]{1,2,0:T(8,128)(2,1)S(1)}, u32[]{:S(2)}, u32[]{:S(2)}) collective-permute-start(bf16[8,128,256]{1,2,0:T(8,128)(2,1)S(1)} %get-tuple-element.106), channel_id=1, source_target_pairs={{1,0},{2,1},{3,2},{4,3},{5,4},{6,5},{7,6},{8,7},{9,8},{10,9},{11,1... | collective-permute-start | bytes 1572872 | tf_op jit(solution)/shard_map/ppermute | solution.py:18
  63.2 25.1 %collective-permute-start.6 = (bf16[8,128,256]{1,2,0:T(8,128)(2,1)S(1)}, bf16[8,128,256]{1,2,0:T(8,128)(2,1)S(1)}, u32[]{:S(2)}, u32[]{:S(2)}) collective-permute-start(bf16[8,128,256]{1,2,0:T(8,128)(2,1)S(1)} %get-tuple-element.108), channel_id=1, source_target_pairs={{0,16},{1,17},{2,18},{3,19},{4,20},{5,21},{6,22},{7,23},{8,24},{9,... | collective-permute-start | bytes 1572872 | tf_op jit(solution)/shard_map/ppermute | solution.py:18
  65.1 23.2 %collective-permute-start.7 = (bf16[8,128,256]{1,2,0:T(8,128)(2,1)S(1)}, bf16[8,128,256]{1,2,0:T(8,128)(2,1)S(1)}, u32[]{:S(2)}, u32[]{:S(2)}) collective-permute-start(bf16[8,128,256]{1,2,0:T(8,128)(2,1)S(1)} %get-tuple-element.107), channel_id=1, source_target_pairs={{16,0},{17,1},{18,2},{19,3},{20,4},{21,5},{22,6},{23,7},{24,8},{25... | collective-permute-start | bytes 1572872 | tf_op jit(solution)/shard_map/ppermute | solution.py:18
  91.0 21.2 %copy-start.8 = (f32[512]{0:T(512)S(1)}, f32[512]{0:T(512)}, u32[]{:S(2)}) copy-start(f32[512]{0:T(512)} %param.43) | copy-start | bytes 6148
  91.0 21.2 %copy-start.9 = (f32[512]{0:T(512)S(1)}, f32[512]{0:T(512)}, u32[]{:S(2)}) copy-start(f32[512]{0:T(512)} %param.40) | copy-start | bytes 6148
  95.5 22.0 %copy-start.6 = (f32[512]{0:T(512)S(1)}, f32[512]{0:T(512)}, u32[]{:S(2)}) copy-start(f32[512]{0:T(512)} %param.42) | copy-start | bytes 6148
  95.5 22.1 %copy-start.7 = (f32[512]{0:T(512)S(1)}, f32[512]{0:T(512)}, u32[]{:S(2)}) copy-start(f32[512]{0:T(512)} %param.41) | copy-start | bytes 6148
  95.5 22.3 %copy-start.1 = (bf16[1024,1024]{1,0:T(8,128)(2,1)S(1)}, bf16[1024,1024]{1,0:T(8,128)(2,1)}, u32[]{:S(2)}) copy-start(bf16[1024,1024]{1,0:T(8,128)(2,1)} %param.44) | copy-start | bytes 6291460
  96.2 16.1 %collective-permute-start.8 = (f32[8,2,128]{2,0,1:T(8,128)S(1)}, f32[8,2,128]{2,0,1:T(8,128)S(1)}, u32[]{:S(2)}, u32[]{:S(2)}) collective-permute-start(f32[8,2,128]{2,0,1:T(8,128)S(1)} %get-tuple-element.155), channel_id=1, source_target_pairs={{0,1},{1,2},{2,3},{3,4},{4,5},{5,6},{6,7},{7,8},{8,9},{9,10},{10,1... | collective-permute-start | bytes 24584 | tf_op jit(solution)/shard_map/ppermute | solution.py:18
  98.1 14.1 %collective-permute-start.9 = (f32[8,2,128]{2,0,1:T(8,128)S(1)}, f32[8,2,128]{2,0,1:T(8,128)S(1)}, u32[]{:S(2)}, u32[]{:S(2)}) collective-permute-start(f32[8,2,128]{2,0,1:T(8,128)S(1)} %get-tuple-element.156), channel_id=1, source_target_pairs={{1,0},{2,1},{3,2},{4,3},{5,4},{6,5},{7,6},{8,7},{9,8},{10,9},{11,1... | collective-permute-start | bytes 24584 | tf_op jit(solution)/shard_map/ppermute | solution.py:18
  103.9 8.4 %collective-permute-start.10 = (f32[8,2,128]{2,0,1:T(8,128)S(1)}, f32[8,2,128]{2,0,1:T(8,128)S(1)}, u32[]{:S(2)}, u32[]{:S(2)}) collective-permute-start(f32[8,2,128]{2,0,1:T(8,128)S(1)} %get-tuple-element.158), channel_id=1, source_target_pairs={{0,16},{1,17},{2,18},{3,19},{4,20},{5,21},{6,22},{7,23},{8,24},{9,... | collective-permute-start | bytes 24584 | tf_op jit(solution)/shard_map/ppermute | solution.py:18
  109.1 7.9 %collective-permute-start.11 = (f32[8,2,128]{2,0,1:T(8,128)S(1)}, f32[8,2,128]{2,0,1:T(8,128)S(1)}, u32[]{:S(2)}, u32[]{:S(2)}) collective-permute-start(f32[8,2,128]{2,0,1:T(8,128)S(1)} %get-tuple-element.157), channel_id=1, source_target_pairs={{16,0},{17,1},{18,2},{19,3},{20,4},{21,5},{22,6},{23,7},{24,8},{25... | collective-permute-start | bytes 24584 | tf_op jit(solution)/shard_map/ppermute | solution.py:18
  118.8 15.1 %collective-permute-start.12 = (f32[8,2,128]{2,0,1:T(8,128)S(1)}, f32[8,2,128]{2,0,1:T(8,128)S(1)}, u32[]{:S(2)}, u32[]{:S(2)}) collective-permute-start(f32[8,2,128]{2,0,1:T(8,128)S(1)} %get-tuple-element.151), channel_id=1, source_target_pairs={{0,1},{1,2},{2,3},{3,4},{4,5},{5,6},{6,7},{7,8},{8,9},{9,10},{10,1... | collective-permute-start | bytes 24584 | tf_op jit(solution)/shard_map/ppermute | solution.py:18
  120.8 13.1 %collective-permute-start.13 = (f32[8,2,128]{2,0,1:T(8,128)S(1)}, f32[8,2,128]{2,0,1:T(8,128)S(1)}, u32[]{:S(2)}, u32[]{:S(2)}) collective-permute-start(f32[8,2,128]{2,0,1:T(8,128)S(1)} %get-tuple-element.152), channel_id=1, source_target_pairs={{1,0},{2,1},{3,2},{4,3},{5,4},{6,5},{7,6},{8,7},{9,8},{10,9},{11,1... | collective-permute-start | bytes 24584 | tf_op jit(solution)/shard_map/ppermute | solution.py:18
  126.5 7.4 %collective-permute-start.14 = (f32[8,2,128]{2,0,1:T(8,128)S(1)}, f32[8,2,128]{2,0,1:T(8,128)S(1)}, u32[]{:S(2)}, u32[]{:S(2)}) collective-permute-start(f32[8,2,128]{2,0,1:T(8,128)S(1)} %get-tuple-element.154), channel_id=1, source_target_pairs={{0,16},{1,17},{2,18},{3,19},{4,20},{5,21},{6,22},{7,23},{8,24},{9,... | collective-permute-start | bytes 24584 | tf_op jit(solution)/shard_map/ppermute | solution.py:18
  131.2 7.9 %collective-permute-start.15 = (f32[8,2,128]{2,0,1:T(8,128)S(1)}, f32[8,2,128]{2,0,1:T(8,128)S(1)}, u32[]{:S(2)}, u32[]{:S(2)}) collective-permute-start(f32[8,2,128]{2,0,1:T(8,128)S(1)} %get-tuple-element.153), channel_id=1, source_target_pairs={{16,0},{17,1},{18,2},{19,3},{20,4},{21,5},{22,6},{23,7},{24,8},{25... | collective-permute-start | bytes 24584 | tf_op jit(solution)/shard_map/ppermute | solution.py:18
  140.9 15.1 %collective-permute-start.16 = (f32[8,2,128]{2,0,1:T(8,128)S(1)}, f32[8,2,128]{2,0,1:T(8,128)S(1)}, u32[]{:S(2)}, u32[]{:S(2)}) collective-permute-start(f32[8,2,128]{2,0,1:T(8,128)S(1)} %get-tuple-element.145), channel_id=1, source_target_pairs={{0,1},{1,2},{2,3},{3,4},{4,5},{5,6},{6,7},{7,8},{8,9},{9,10},{10,1... | collective-permute-start | bytes 24584 | tf_op jit(solution)/shard_map/ppermute | solution.py:18
  142.8 13.1 %collective-permute-start.17 = (f32[8,2,128]{2,0,1:T(8,128)S(1)}, f32[8,2,128]{2,0,1:T(8,128)S(1)}, u32[]{:S(2)}, u32[]{:S(2)}) collective-permute-start(f32[8,2,128]{2,0,1:T(8,128)S(1)} %get-tuple-element.146), channel_id=1, source_target_pairs={{1,0},{2,1},{3,2},{4,3},{5,4},{6,5},{7,6},{8,7},{9,8},{10,9},{11,1... | collective-permute-start | bytes 24584 | tf_op jit(solution)/shard_map/ppermute | solution.py:18
  148.6 7.4 %collective-permute-start.18 = (f32[8,2,128]{2,0,1:T(8,128)S(1)}, f32[8,2,128]{2,0,1:T(8,128)S(1)}, u32[]{:S(2)}, u32[]{:S(2)}) collective-permute-start(f32[8,2,128]{2,0,1:T(8,128)S(1)} %get-tuple-element.148), channel_id=1, source_target_pairs={{0,16},{1,17},{2,18},{3,19},{4,20},{5,21},{6,22},{7,23},{8,24},{9,... | collective-permute-start | bytes 24584 | tf_op jit(solution)/shard_map/ppermute | solution.py:18
  153.8 7.9 %collective-permute-start.19 = (f32[8,2,128]{2,0,1:T(8,128)S(1)}, f32[8,2,128]{2,0,1:T(8,128)S(1)}, u32[]{:S(2)}, u32[]{:S(2)}) collective-permute-start(f32[8,2,128]{2,0,1:T(8,128)S(1)} %get-tuple-element.147), channel_id=1, source_target_pairs={{16,0},{17,1},{18,2},{19,3},{20,4},{21,5},{22,6},{23,7},{24,8},{25... | collective-permute-start | bytes 24584 | tf_op jit(solution)/shard_map/ppermute | solution.py:18
  164.4 15.7 %collective-permute-start.20 = (f32[8,2,128]{2,0,1:T(8,128)S(1)}, f32[8,2,128]{2,0,1:T(8,128)S(1)}, u32[]{:S(2)}, u32[]{:S(2)}) collective-permute-start(f32[8,2,128]{2,0,1:T(8,128)S(1)} %get-tuple-element.138), channel_id=1, source_target_pairs={{0,1},{1,2},{2,3},{3,4},{4,5},{5,6},{6,7},{7,8},{8,9},{9,10},{10,1... | collective-permute-start | bytes 24584 | tf_op jit(solution)/shard_map/ppermute | solution.py:18
  166.4 13.8 %collective-permute-start.21 = (f32[8,2,128]{2,0,1:T(8,128)S(1)}, f32[8,2,128]{2,0,1:T(8,128)S(1)}, u32[]{:S(2)}, u32[]{:S(2)}) collective-permute-start(f32[8,2,128]{2,0,1:T(8,128)S(1)} %get-tuple-element.139), channel_id=1, source_target_pairs={{1,0},{2,1},{3,2},{4,3},{5,4},{6,5},{7,6},{8,7},{9,8},{10,9},{11,1... | collective-permute-start | bytes 24584 | tf_op jit(solution)/shard_map/ppermute | solution.py:18
  172.1 8.0 %collective-permute-start.22 = (f32[8,2,128]{2,0,1:T(8,128)S(1)}, f32[8,2,128]{2,0,1:T(8,128)S(1)}, u32[]{:S(2)}, u32[]{:S(2)}) collective-permute-start(f32[8,2,128]{2,0,1:T(8,128)S(1)} %get-tuple-element.141), channel_id=1, source_target_pairs={{0,16},{1,17},{2,18},{3,19},{4,20},{5,21},{6,22},{7,23},{8,24},{9,... | collective-permute-start | bytes 24584 | tf_op jit(solution)/shard_map/ppermute | solution.py:18
  178.1 7.9 %collective-permute-start.23 = (f32[8,2,128]{2,0,1:T(8,128)S(1)}, f32[8,2,128]{2,0,1:T(8,128)S(1)}, u32[]{:S(2)}, u32[]{:S(2)}) collective-permute-start(f32[8,2,128]{2,0,1:T(8,128)S(1)} %get-tuple-element.140), channel_id=1, source_target_pairs={{16,0},{17,1},{18,2},{19,3},{20,4},{21,5},{22,6},{23,7},{24,8},{25... | collective-permute-start | bytes 24584 | tf_op jit(solution)/shard_map/ppermute | solution.py:18
  188.3 30.3 %collective-permute-start.28 = (f32[32,2,128]{2,0,1:T(8,128)S(1)}, f32[32,2,128]{2,0,1:T(8,128)S(1)}, u32[]{:S(2)}, u32[]{:S(2)}) collective-permute-start(f32[32,2,128]{2,0,1:T(8,128)S(1)} %get-tuple-element.125), channel_id=1, source_target_pairs={{0,1},{1,2},{2,3},{3,4},{4,5},{5,6},{6,7},{7,8},{8,9},{9,10},{10,1... | collective-permute-start | bytes 98312 | tf_op jit(solution)/shard_map/ppermute | solution.py:18
  190.3 28.3 %collective-permute-start.29 = (f32[32,2,128]{2,0,1:T(8,128)S(1)}, f32[32,2,128]{2,0,1:T(8,128)S(1)}, u32[]{:S(2)}, u32[]{:S(2)}) collective-permute-start(f32[32,2,128]{2,0,1:T(8,128)S(1)} %get-tuple-element.126), channel_id=1, source_target_pairs={{1,0},{2,1},{3,2},{4,3},{5,4},{6,5},{7,6},{8,7},{9,8},{10,9},{11,1... | collective-permute-start | bytes 98312 | tf_op jit(solution)/shard_map/ppermute | solution.py:18
  196.0 22.6 %collective-permute-start.30 = (f32[32,2,128]{2,0,1:T(8,128)S(1)}, f32[32,2,128]{2,0,1:T(8,128)S(1)}, u32[]{:S(2)}, u32[]{:S(2)}) collective-permute-start(f32[32,2,128]{2,0,1:T(8,128)S(1)} %get-tuple-element.128), channel_id=1, source_target_pairs={{0,16},{1,17},{2,18},{3,19},{4,20},{5,21},{6,22},{7,23},{8,24},{9,... | collective-permute-start | bytes 98312 | tf_op jit(solution)/shard_map/ppermute | solution.py:18
  202.7 15.9 %collective-permute-start.31 = (f32[32,2,128]{2,0,1:T(8,128)S(1)}, f32[32,2,128]{2,0,1:T(8,128)S(1)}, u32[]{:S(2)}, u32[]{:S(2)}) collective-permute-start(f32[32,2,128]{2,0,1:T(8,128)S(1)} %get-tuple-element.127), channel_id=1, source_target_pairs={{16,0},{17,1},{18,2},{19,3},{20,4},{21,5},{22,6},{23,7},{24,8},{25... | collective-permute-start | bytes 98312 | tf_op jit(solution)/shard_map/ppermute | solution.py:18
  204.7 1.5 collective-permute-start.24
  206.2 3.6 %collective-permute-start.25 = (f32[8,8]{1,0:T(8,128)S(1)}, f32[8,8]{1,0:T(8,128)S(1)}, u32[]{:S(2)}, u32[]{:S(2)}) collective-permute-start(f32[8,8]{1,0:T(8,128)S(1)} %add.310), channel_id=1, source_target_pairs={{0,2},{1,3},{2,0},{3,1},{4,6},{5,7},{6,4},{7,5},{8,10},{9,11},{10,... | collective-permute-start | bytes 776 | tf_op jit(solution)/shard_map/ppermute | solution.py:31
  209.8 5.1 %collective-permute-start.26 = (f32[8,8]{1,0:T(8,128)S(1)}, f32[8,8]{1,0:T(8,128)S(1)}, u32[]{:S(2)}, u32[]{:S(2)}) collective-permute-start(f32[8,8]{1,0:T(8,128)S(1)} %add.311), channel_id=1, source_target_pairs={{0,4},{1,5},{2,6},{3,7},{4,0},{5,1},{6,2},{7,3},{8,12},{9,13},{10,... | collective-permute-start | bytes 776 | tf_op jit(solution)/shard_map/ppermute | solution.py:31
  214.9 3.7 %collective-permute-start.27 = (f32[8,8]{1,0:T(8,128)S(1)}, f32[8,8]{1,0:T(8,128)S(1)}, u32[]{:S(2)}, u32[]{:S(2)}) collective-permute-start(f32[8,8]{1,0:T(8,128)S(1)} %add.312), channel_id=1, source_target_pairs={{0,8},{1,9},{2,10},{3,11},{4,12},{5,13},{6,14},{7,15},{8,0},{9,1},... | collective-permute-start | bytes 776 | tf_op jit(solution)/shard_map/ppermute | solution.py:31
  220.6 46.7 %collective-permute-start.36 = (f32[32,2,128]{2,0,1:T(8,128)S(1)}, f32[32,2,128]{2,0,1:T(8,128)S(1)}, u32[]{:S(2)}, u32[]{:S(2)}) collective-permute-start(f32[32,2,128]{2,0,1:T(8,128)S(1)} %get-tuple-element.121), channel_id=1, source_target_pairs={{0,1},{1,2},{2,3},{3,4},{4,5},{5,6},{6,7},{7,8},{8,9},{9,10},{10,1... | collective-permute-start | bytes 98312 | tf_op jit(solution)/shard_map/ppermute | solution.py:18
  222.6 44.7 %collective-permute-start.37 = (f32[32,2,128]{2,0,1:T(8,128)S(1)}, f32[32,2,128]{2,0,1:T(8,128)S(1)}, u32[]{:S(2)}, u32[]{:S(2)}) collective-permute-start(f32[32,2,128]{2,0,1:T(8,128)S(1)} %get-tuple-element.122), channel_id=1, source_target_pairs={{1,0},{2,1},{3,2},{4,3},{5,4},{6,5},{7,6},{8,7},{9,8},{10,9},{11,1... | collective-permute-start | bytes 98312 | tf_op jit(solution)/shard_map/ppermute | solution.py:18
  228.3 39.0 %collective-permute-start.38 = (f32[32,2,128]{2,0,1:T(8,128)S(1)}, f32[32,2,128]{2,0,1:T(8,128)S(1)}, u32[]{:S(2)}, u32[]{:S(2)}) collective-permute-start(f32[32,2,128]{2,0,1:T(8,128)S(1)} %get-tuple-element.124), channel_id=1, source_target_pairs={{0,16},{1,17},{2,18},{3,19},{4,20},{5,21},{6,22},{7,23},{8,24},{9,... | collective-permute-start | bytes 98312 | tf_op jit(solution)/shard_map/ppermute | solution.py:18
  236.7 30.6 %collective-permute-start.39 = (f32[32,2,128]{2,0,1:T(8,128)S(1)}, f32[32,2,128]{2,0,1:T(8,128)S(1)}, u32[]{:S(2)}, u32[]{:S(2)}) collective-permute-start(f32[32,2,128]{2,0,1:T(8,128)S(1)} %get-tuple-element.123), channel_id=1, source_target_pairs={{16,0},{17,1},{18,2},{19,3},{20,4},{21,5},{22,6},{23,7},{24,8},{25... | collective-permute-start | bytes 98312 | tf_op jit(solution)/shard_map/ppermute | solution.py:18
  238.6 5.2 %collective-permute-start.32 = (f32[8,8]{1,0:T(8,128)S(1)}, f32[8,8]{1,0:T(8,128)S(1)}, u32[]{:S(2)}, u32[]{:S(2)}) collective-permute-start(f32[8,8]{1,0:T(8,128)S(1)} %add.313), channel_id=1, source_target_pairs={{0,16},{1,17},{2,18},{3,19},{4,20},{5,21},{6,22},{7,23},{8,24},{9,... | collective-permute-start | bytes 776 | tf_op jit(solution)/shard_map/ppermute | solution.py:31
  243.8 5.4 %collective-permute-start.33 = (f32[8,8]{1,0:T(8,128)S(1)}, f32[8,8]{1,0:T(8,128)S(1)}, u32[]{:S(2)}, u32[]{:S(2)}) collective-permute-start(f32[8,8]{1,0:T(8,128)S(1)} %add.314), channel_id=1, source_target_pairs={{0,32},{1,33},{2,34},{3,35},{4,36},{5,37},{6,38},{7,39},{8,40},{9,... | collective-permute-start | bytes 776 | tf_op jit(solution)/shard_map/ppermute | solution.py:31
  249.2 10.0 %collective-permute-start.34 = (f32[8,8]{1,0:T(8,128)S(1)}, f32[8,8]{1,0:T(8,128)S(1)}, u32[]{:S(2)}, u32[]{:S(2)}) collective-permute-start(f32[8,8]{1,0:T(8,128)S(1)} %add.315), channel_id=1, source_target_pairs={{0,64},{1,65},{2,66},{3,67},{4,68},{5,69},{6,70},{7,71},{8,72},{9,... | collective-permute-start | bytes 776 | tf_op jit(solution)/shard_map/ppermute | solution.py:31
  259.2 8.1 %collective-permute-start.35 = (f32[8,8]{1,0:T(8,128)S(1)}, f32[8,8]{1,0:T(8,128)S(1)}, u32[]{:S(2)}, u32[]{:S(2)}) collective-permute-start(f32[8,8]{1,0:T(8,128)S(1)} %add.316), channel_id=1, source_target_pairs={{0,128},{1,129},{2,130},{3,131},{4,132},{5,133},{6,134},{7,135},{8... | collective-permute-start | bytes 776 | tf_op jit(solution)/shard_map/ppermute | solution.py:31
  (12 other events, 89.5 us)

commit v4 on v3

--- a/solution.py
+++ b/solution.py
@@ -12,10 +12,12 @@
 highest = lax.Precision.HIGHEST
 
 
-def from_behind(value, axis, steps):
-    count = lax.axis_size(axis)
-    first, last = (max(0, -steps), min(count, count - steps))
-    return lax.ppermute(value, axis, [(source, source + steps) for source in range(first, last)])
+def swap_pairs(count, offset, phase):
+    pairs = []
+    for low in range(count - offset):
+        if (low // offset) % 2 == phase:
+            pairs += [(low, low + offset), (low + offset, low)]
+    return pairs
 
 
 def sum_bits(axis):
@@ -67,10 +69,25 @@
     scenarios, buses, width = features.shape
     neighbours, tile_size = send_rows.shape
     offsets = (1, -1, RW, -RW)
+    count = lax.axis_size("region")
+    me = lax.axis_index("region")
+    routes, send_slots, recv_slots = [], [], []
+    for offset, up, down in ((offsets[0], 0, 1), (offsets[2], 2, 3)):
+        lower = (me // offset) % 2 == 0
+        for phase in (0, 1):
+            first = lower if phase == 0 else jnp.logical_not(lower)
+            routes.append(swap_pairs(count, offset, phase))
+            send_slots.append(jnp.where(first, up, down))
+            recv_slots.append(jnp.where(first, down, up))
+    send_slots = jnp.stack(send_slots)
+    recv_slots = jnp.stack(recv_slots)
     bus_iota = lax.broadcasted_iota(jnp.int32, (neighbours, tile_size, buses), 2)
     live = lax.broadcasted_iota(jnp.int32, (neighbours, tile_size), 1) < tile_count[:, None]
-    pick = (send_rows[:, :, None] == bus_iota) & live[:, :, None]
-    place = attach_rows[:, :, None] == bus_iota
+    send_route = jnp.take(send_rows, send_slots, axis=0)
+    live_route = jnp.take(live, send_slots, axis=0)
+    attach_route = jnp.take(attach_rows, recv_slots, axis=0)
+    pick = (send_route[:, :, None] == bus_iota) & live_route[:, :, None]
+    place = attach_route[:, :, None] == bus_iota
     pick_half, pick_full = pick.astype(jnp.bfloat16), pick.astype(jnp.float32)
     place_half, place_full = place.astype(jnp.bfloat16), place.astype(jnp.float32)
     mask_half = line_mask.astype(jnp.bfloat16)
@@ -78,7 +95,7 @@
 
     def exchange(tiles):
         return jnp.stack(
-            [from_behind(tiles[k], "region", offsets[k]) for k in range(neighbours)]
+            [lax.ppermute(tiles[j], "region", routes[j]) for j in range(len(routes))]
         )
 
     hidden = features

time: 272 us -> 228 us (0.84)
  starting transfers between devices: 145 us -> 117 us
  waiting for transfers between devices: 75.4 us -> 58 us
  local copies, waits for them, and re-layouts: 1.88 us -> 4.62 us
    ppermute x32, starting transfers between devices: 124 us -> 98 us  [exchange(): lax.ppermute(tiles[j], 'region', routes[j])]
    ppermute x32, waiting for transfers between devices: 54.1 us -> 38.1 us  [exchange(): lax.ppermute(tiles[j], 'region', routes[j])]
  transfers between devices with their start and end apart: 40 -> 40, of which waited for: 15 -> 14; matrix products, arithmetic and copies ran while one was open for 4% -> 5% of each run, Pallas kernels for 0% -> 0%
where the time goes in v4:
time: 228 us; the launch traced here: 227 us
  starting transfers between devices  117 us (51%)
  waiting for transfers between devices  58 us (25%)
  matrix products  43.2 us (19%)
  local copies, waits for them, and re-layouts  4.62 us (2%)
  other arithmetic  3.05 us (1%)
    ppermute x32, starting transfers between devices, exchange(): lax.ppermute(tiles[j], 'region', routes[j])  98 us
    ppermute x32, waiting for transfers between devices, exchange(): lax.ppermute(tiles[j], 'region', routes[j])  38.1 us
    ppermute x8, waiting for transfers between devices, sum_rounds(): lax.ppermute(value, axis, [(i, i ^ bit) for i in range(count)])  20 us
    ppermute x8, starting transfers between devices, sum_rounds(): lax.ppermute(value, axis, [(i, i ^ bit) for i in range(count)])  19 us
    dot_general x1, matrix products, local(): jnp.einsum('sbh,hk->sbk', gathered, neigh_weight[number], preferred_eleme...  8.25 us
    dot_general x2, matrix products, local(): jnp.einsum('ktb,sbh->ksth', pick_half, hidden, preferred_element_type=jnp...  5.96 us
    dot_general x2, matrix products, local(): jnp.einsum('sbh,hk->sbk', hidden, self_weight[number], preferred_element_...  5.33 us
  transfers between devices with their start and end apart: 40, of which 14 were waited for; matrix products, arithmetic and copies ran while one was open for 5% of the time, Pallas kernels for 0%

profile of v4, /device:TPU:4, one launch (start us, length us, event | category | flops | bytes accessed | tf_op | source)
XLA Modules:
  0.0 226.8 jit_solution(17596400292893620523)
XLA Ops:
  1.6 1.2 gather_fusion.1
  2.9 2.9 %convert_bitcast_fusion.1 = bf16[4,8,128,256]{3,2,1,0:T(8,128)(2,1)S(1)} fusion(bf16[8,512,256]{2,1,0:T(8,128)(2,1)} %param.31, s32[4,128]{1,0:T(4,128)S(1)} %broadcast_select_fusion.1, pred[4,128]{1,0:T(4,128)(4,1)S(1)} %broadcast_select_fusion.2), kind=kOutput, calls=%fused_computation.42 | convolution fusion | flops 1075314688 | bytes 4196864 | tf_op jit(solution)/shard_map/ktb,sbh->ksth/dot_general | solution.py:103
  5.8 1.4 slice_bitcast_fusion.7
  7.2 5.0 %collective-permute-start.1 = (bf16[8,128,256]{2,1,0:T(8,128)(2,1)}, bf16[8,128,256]{2,1,0:T(8,128)(2,1)}, u32[]{:S(2)}, u32[]{:S(2)}) collective-permute-start(bf16[8,128,256]{2,1,0:T(8,128)(2,1)} %get-tuple-element.117), channel_id=1, source_target_pairs={{1,2},{2,1},{3,4},{4,3},{5,6},{6,5},{7,8},{8,7},{9,10},{10,9},{11,... | collective-permute-start | bytes 1572872 | tf_op jit(solution)/shard_map/ppermute | solution.py:98
  12.3 6.8 %collective-permute-start.3 = (bf16[8,128,256]{2,1,0:T(8,128)(2,1)}, bf16[8,128,256]{2,1,0:T(8,128)(2,1)}, u32[]{:S(2)}, u32[]{:S(2)}) collective-permute-start(bf16[8,128,256]{2,1,0:T(8,128)(2,1)} %get-tuple-element.115), channel_id=1, source_target_pairs={{16,32},{32,16},{17,33},{33,17},{18,34},{34,18},{19,35},{35,19},{2... | collective-permute-start | bytes 1572872 | tf_op jit(solution)/shard_map/ppermute | solution.py:98
  19.2 2.7 %fusion.128 = f32[8,512,256]{2,1,0:T(8,128)} fusion(bf16[8,512,256]{2,1,0:T(8,128)(2,1)S(1)} %copy-done.3, bf16[2,256,256]{2,1,0:T(8,128)(2,1)S(1)} %copy-done.5), kind=kOutput, calls=%fused_computation.127 | convolution fusion | flops 536870912 | bytes 6422528 | tf_op jit(solution)/shard_map/sbh,hk->sbk/dot_general | solution.py:108
  22.7 3.3 %fusion.90 = f32[8,256,512]{1,2,0:T(8,128)} fusion(bf16[8,512,256]{2,1,0:T(8,128)(2,1)S(1)} %copy-done.3, s32[512,512]{1,0:T(8,128)S(1)} %copy-done.2), kind=kOutput, calls=%fused_computation.88 | convolution fusion | flops 1074003968 | bytes 7340032 | tf_op jit(solution)/shard_map/ij,sjh->sih/dot_general | solution.py:107
  26.0 16.7 %collective-permute-done.1 = bf16[8,128,256]{2,1,0:T(8,128)(2,1)} collective-permute-done((bf16[8,128,256]{2,1,0:T(8,128)(2,1)}, bf16[8,128,256]{2,1,0:T(8,128)(2,1)}, u32[]{:S(2)}, u32[]{:S(2)}) %collective-permute-start.1) | collective-permute-done | bytes 524320 | tf_op jit(solution)/shard_map/ppermute | solution.py:98
  42.7 8.2 %add_convert_fusion.1 = bf16[8,512,256]{2,1,0:T(8,128)(2,1)} fusion(f32[8,512,256]{2,1,0:T(8,128)} %fusion.128, bf16[8,512,256]{2,1,0:T(8,128)(2,1)S(1)} %copy-done.3, f32[256]{0:T(256)S(1)} %bitcast.577, f32[8,256,512]{1,2,0:T(8,128)} %fusion.90, bf16[1,8,128,256]{3,2,1,0:T(8,128)(2,1)} %bitcast.23, bf16[1,8,128,256]{3,2,1,0:T(8,128)(2,1)} %bitcast.21, ...), kind=kOutput, calls=%fused_computation.10 | convolution fusion | flops 1626603520 | bytes 14814208 | tf_op jit(solution)/shard_map/sbh,hk->sbk/dot_general | solution.py:117
  51.0 3.1 %convert_bitcast_fusion = bf16[4,8,128,256]{2,3,0,1:T(8,128)(2,1)S(1)} fusion(bf16[8,512,256]{2,1,0:T(8,128)(2,1)} %add_convert_fusion.1, s32[4,128]{1,0:T(4,128)S(1)} %broadcast_select_fusion.1, pred[4,128]{1,0:T(4,128)(4,1)S(1)} %broadcast_select_fusion.2), kind=kOutput, calls=%fused_computation.41 | convolution fusion | flops 1075314688 | bytes 4196864 | tf_op jit(solution)/shard_map/ktb,sbh->ksth/dot_general | solution.py:103
  54.3 2.1 collective-permute-start.5
  56.5 6.9 %collective-permute-start.7 = (bf16[8,128,256]{1,2,0:T(8,128)(2,1)S(1)}, bf16[8,128,256]{1,2,0:T(8,128)(2,1)S(1)}, u32[]{:S(2)}, u32[]{:S(2)}) collective-permute-start(bf16[8,128,256]{1,2,0:T(8,128)(2,1)S(1)} %get-tuple-element.112), channel_id=1, source_target_pairs={{16,32},{32,16},{17,33},{33,17},{18,34},{34,18},{19,35},{35,19},{2... | collective-permute-start | bytes 1572872 | tf_op jit(solution)/shard_map/ppermute | solution.py:98
  63.4 2.7 %fusion.125 = f32[8,512,256]{2,1,0:T(8,128)} fusion(bf16[8,512,256]{2,1,0:T(8,128)(2,1)S(1)} %copy-done.4, bf16[2,256,256]{2,1,0:T(8,128)(2,1)S(1)} %copy-done.5), kind=kOutput, calls=%fused_computation.124 | convolution fusion | flops 536870912 | bytes 6422528 | tf_op jit(solution)/shard_map/sbh,hk->sbk/dot_general | solution.py:108
  66.1 1.3 fusion.92
  67.4 16.3 %collective-permute-done.5 = bf16[8,128,256]{1,2,0:T(8,128)(2,1)S(1)} collective-permute-done((bf16[8,128,256]{1,2,0:T(8,128)(2,1)S(1)}, bf16[8,128,256]{1,2,0:T(8,128)(2,1)S(1)}, u32[]{:S(2)}, u32[]{:S(2)}) %collective-permute-start.5) | collective-permute-done | bytes 524320 | tf_op jit(solution)/shard_map/ppermute | solution.py:98
  83.7 2.7 %fusion.1 = bf16[8,256,512]{1,2,0:T(8,128)(2,1)} fusion(f32[8,256,512]{1,2,0:T(8,128)S(1)} %fusion.92, bf16[1,8,128,256]{2,3,1,0:T(8,128)(2,1)S(1)} %bitcast.581, bf16[1,8,128,256]{2,3,1,0:T(8,128)(2,1)S(1)} %bitcast.580, bf16[1,8,128,256]{2,3,1,0:T(8,128)(2,1)S(1)} %bitcast.579, bf16[1,8,128,256]{2,3,1,0:T(8,128)(2,1)S(1)} %bitcast.578, ...), kind=kOutput, calls=%fused_computation.5 | convolution fusion | flops 1080295424 | bytes 8390656 | tf_op jit(solution)/shard_map/ktb,ksth->sbh/dot_general | solution.py:111
  86.3 4.5 %fusion.55 = f32[8,512,2]{1,2,0:T(2,128)S(1)} fusion(f32[8,512,256]{2,1,0:T(8,128)} %fusion.125, bf16[8,512,256]{2,1,0:T(8,128)(2,1)S(1)} %copy-done.4, bf16[8,256,512]{1,2,0:T(8,128)(2,1)} %fusion.1, f32[256]{0:T(256)S(1)} %bitcast.576, bf16[2,256,256]{2,1,0:T(8,128)(2,1)} %param.37, f32[2]{0:T(128)S(1)} %copy-done.14, bf16[2,256]{1,0:T(2,128)(2,1)S(1)} %copy-done.13), kind=kOutput, calls=%fused_computation.62 | convolution fusion | flops 550510592 | bytes 8554504 | tf_op jit(solution)/shard_map/sbh,ch->scb/dot_general | solution.py:125
  91.6 1.9 collective-permute-start.9
  93.6 7.0 %collective-permute-start.11 = (f32[8,2,128]{2,0,1:T(8,128)S(1)}, f32[8,2,128]{2,0,1:T(8,128)S(1)}, u32[]{:S(2)}, u32[]{:S(2)}) collective-permute-start(f32[8,2,128]{2,0,1:T(8,128)S(1)} %get-tuple-element.162), channel_id=1, source_target_pairs={{16,32},{32,16},{17,33},{33,17},{18,34},{34,18},{19,35},{35,19},{2... | collective-permute-start | bytes 24584 | tf_op jit(solution)/shard_map/ppermute | solution.py:98
  100.7 0.9 fusion.65
  104.2 1.9 collective-permute-start.13
  106.2 10.4 %collective-permute-start.15 = (f32[8,2,128]{2,0,1:T(8,128)S(1)}, f32[8,2,128]{2,0,1:T(8,128)S(1)}, u32[]{:S(2)}, u32[]{:S(2)}) collective-permute-start(f32[8,2,128]{2,0,1:T(8,128)S(1)} %get-tuple-element.158), channel_id=1, source_target_pairs={{16,32},{32,16},{17,33},{33,17},{18,34},{34,18},{19,35},{35,19},{2... | collective-permute-start | bytes 24584 | tf_op jit(solution)/shard_map/ppermute | solution.py:98
  116.7 1.6 collective-permute-done.15
  120.0 1.9 collective-permute-start.17
  122.1 10.3 %collective-permute-start.19 = (f32[8,2,128]{2,0,1:T(8,128)S(1)}, f32[8,2,128]{2,0,1:T(8,128)S(1)}, u32[]{:S(2)}, u32[]{:S(2)}) collective-permute-start(f32[8,2,128]{2,0,1:T(8,128)S(1)} %get-tuple-element.152), channel_id=1, source_target_pairs={{16,32},{32,16},{17,33},{33,17},{18,34},{34,18},{19,35},{35,19},{2... | collective-permute-start | bytes 24584 | tf_op jit(solution)/shard_map/ppermute | solution.py:98
  132.4 1.4 collective-permute-done.19
  135.5 0.9 fusion.63
  136.5 1.0 collective-permute-start.20
  137.4 4.7 %collective-permute-start.21 = (f32[8,2,128]{2,0,1:T(8,128)S(1)}, f32[8,2,128]{2,0,1:T(8,128)S(1)}, u32[]{:S(2)}, u32[]{:S(2)}) collective-permute-start(f32[8,2,128]{2,0,1:T(8,128)S(1)} %get-tuple-element.144), channel_id=1, source_target_pairs={{1,2},{2,1},{3,4},{4,3},{5,6},{6,5},{7,8},{8,7},{9,10},{10,9},{11,... | collective-permute-start | bytes 24584 | tf_op jit(solution)/shard_map/ppermute | solution.py:98
  142.3 13.1 %collective-permute-start.23 = (f32[8,2,128]{2,0,1:T(8,128)S(1)}, f32[8,2,128]{2,0,1:T(8,128)S(1)}, u32[]{:S(2)}, u32[]{:S(2)}) collective-permute-start(f32[8,2,128]{2,0,1:T(8,128)S(1)} %get-tuple-element.145), channel_id=1, source_target_pairs={{16,32},{32,16},{17,33},{33,17},{18,34},{34,18},{19,35},{35,19},{2... | collective-permute-start | bytes 24584 | tf_op jit(solution)/shard_map/ppermute | solution.py:98
  155.5 1.5 collective-permute-done.23
  159.4 1.9 collective-permute-start.29
  161.4 9.4 %collective-permute-start.31 = (f32[32,2,128]{2,0,1:T(8,128)S(1)}, f32[32,2,128]{2,0,1:T(8,128)S(1)}, u32[]{:S(2)}, u32[]{:S(2)}) collective-permute-start(f32[32,2,128]{2,0,1:T(8,128)S(1)} %get-tuple-element.132), channel_id=1, source_target_pairs={{16,32},{32,16},{17,33},{33,17},{18,34},{34,18},{19,35},{35,19},{2... | collective-permute-start | bytes 98312 | tf_op jit(solution)/shard_map/ppermute | solution.py:98
  171.0 1.2 collective-permute-done.24
  172.8 2.9 %collective-permute-done.25 = f32[8,8]{1,0:T(8,128)S(1)} collective-permute-done((f32[8,8]{1,0:T(8,128)S(1)}, f32[8,8]{1,0:T(8,128)S(1)}, u32[]{:S(2)}, u32[]{:S(2)}) %collective-permute-start.25) | collective-permute-done | bytes 288 | tf_op jit(solution)/shard_map/ppermute | solution.py:33
  175.8 1.7 collective-permute-start.26
  177.5 3.4 %collective-permute-done.26 = f32[8,8]{1,0:T(8,128)S(1)} collective-permute-done((f32[8,8]{1,0:T(8,128)S(1)}, f32[8,8]{1,0:T(8,128)S(1)}, u32[]{:S(2)}, u32[]{:S(2)}) %collective-permute-start.26) | collective-permute-done | bytes 288 | tf_op jit(solution)/shard_map/ppermute | solution.py:33
  180.9 1.9 collective-permute-start.27
  182.8 1.7 collective-permute-done.27
  186.7 1.9 collective-permute-start.37
  188.7 10.4 %collective-permute-start.39 = (f32[32,2,128]{2,0,1:T(8,128)S(1)}, f32[32,2,128]{2,0,1:T(8,128)S(1)}, u32[]{:S(2)}, u32[]{:S(2)}) collective-permute-start(f32[32,2,128]{2,0,1:T(8,128)S(1)} %get-tuple-element.128), channel_id=1, source_target_pairs={{16,32},{32,16},{17,33},{33,17},{18,34},{34,18},{19,35},{35,19},{2... | collective-permute-start | bytes 98312 | tf_op jit(solution)/shard_map/ppermute | solution.py:98
  199.2 5.1 %collective-permute-done.32 = f32[8,8]{1,0:T(8,128)S(1)} collective-permute-done((f32[8,8]{1,0:T(8,128)S(1)}, f32[8,8]{1,0:T(8,128)S(1)}, u32[]{:S(2)}, u32[]{:S(2)}) %collective-permute-start.32) | collective-permute-done | bytes 288 | tf_op jit(solution)/shard_map/ppermute | solution.py:33
  204.3 2.7 %collective-permute-start.33 = (f32[8,8]{1,0:T(8,128)S(1)}, f32[8,8]{1,0:T(8,128)S(1)}, u32[]{:S(2)}, u32[]{:S(2)}) collective-permute-start(f32[8,8]{1,0:T(8,128)S(1)} %add.345), channel_id=1, source_target_pairs={{0,32},{1,33},{2,34},{3,35},{4,36},{5,37},{6,38},{7,39},{8,40},{9,... | collective-permute-start | bytes 776 | tf_op jit(solution)/shard_map/ppermute | solution.py:33
  207.0 1.6 collective-permute-done.33
  208.6 6.8 %collective-permute-start.34 = (f32[8,8]{1,0:T(8,128)S(1)}, f32[8,8]{1,0:T(8,128)S(1)}, u32[]{:S(2)}, u32[]{:S(2)}) collective-permute-start(f32[8,8]{1,0:T(8,128)S(1)} %add.346), channel_id=1, source_target_pairs={{0,64},{1,65},{2,66},{3,67},{4,68},{5,69},{6,70},{7,71},{8,72},{9,... | collective-permute-start | bytes 776 | tf_op jit(solution)/shard_map/ppermute | solution.py:33
  215.4 1.6 collective-permute-done.34
  217.0 5.0 %collective-permute-start.35 = (f32[8,8]{1,0:T(8,128)S(1)}, f32[8,8]{1,0:T(8,128)S(1)}, u32[]{:S(2)}, u32[]{:S(2)}) collective-permute-start(f32[8,8]{1,0:T(8,128)S(1)} %add.347), channel_id=1, source_target_pairs={{0,128},{1,129},{2,130},{3,131},{4,132},{5,133},{6,134},{7,135},{8... | collective-permute-start | bytes 776 | tf_op jit(solution)/shard_map/ppermute | solution.py:33
  222.0 2.5 %collective-permute-done.35 = f32[8,8]{1,0:T(8,128)S(1)} collective-permute-done((f32[8,8]{1,0:T(8,128)S(1)}, f32[8,8]{1,0:T(8,128)S(1)}, u32[]{:S(2)}, u32[]{:S(2)}) %collective-permute-start.35) | collective-permute-done | bytes 288 | tf_op jit(solution)/shard_map/ppermute | solution.py:33
  (171 shorter events, 18.0 us)
Async XLA Ops:
  0.0 22.5 %copy-start = (f32[16,2,512]{2,1,0:T(2,128)S(1)}, f32[16,2,512]{2,1,0:T(2,128)}, u32[]{:S(2)}) copy-start(f32[16,2,512]{2,1,0:T(2,128)} %param.40) | copy-start | bytes 196612
  5.8 13.3 %copy-start.3 = (bf16[8,512,256]{2,1,0:T(8,128)(2,1)S(1)}, bf16[8,512,256]{2,1,0:T(8,128)(2,1)}, u32[]{:S(2)}) copy-start(bf16[8,512,256]{2,1,0:T(8,128)(2,1)} %param.31) | copy-start | bytes 6291460
  5.8 13.3 %copy-start.5 = (bf16[2,256,256]{2,1,0:T(8,128)(2,1)S(1)}, bf16[2,256,256]{2,1,0:T(8,128)(2,1)}, u32[]{:S(2)}) copy-start(bf16[2,256,256]{2,1,0:T(8,128)(2,1)} %param.36) | copy-start | bytes 786436
  7.2 18.8 %collective-permute-start = (bf16[8,128,256]{2,1,0:T(8,128)(2,1)}, bf16[8,128,256]{2,1,0:T(8,128)(2,1)}, u32[]{:S(2)}, u32[]{:S(2)}) collective-permute-start(bf16[8,128,256]{2,1,0:T(8,128)(2,1)} %get-tuple-element.114), channel_id=1, source_target_pairs={{0,1},{1,0},{2,3},{3,2},{4,5},{5,4},{6,7},{7,6},{8,9},{9,8},{10,11... | collective-permute-start | bytes 1572872 | tf_op jit(solution)/shard_map/ppermute | solution.py:98
  7.2 35.5 %collective-permute-start.1 = (bf16[8,128,256]{2,1,0:T(8,128)(2,1)}, bf16[8,128,256]{2,1,0:T(8,128)(2,1)}, u32[]{:S(2)}, u32[]{:S(2)}) collective-permute-start(bf16[8,128,256]{2,1,0:T(8,128)(2,1)} %get-tuple-element.117), channel_id=1, source_target_pairs={{1,2},{2,1},{3,4},{4,3},{5,6},{6,5},{7,8},{8,7},{9,10},{10,9},{11,... | collective-permute-start | bytes 1572872 | tf_op jit(solution)/shard_map/ppermute | solution.py:98
  12.2 30.5 %collective-permute-start.2 = (bf16[8,128,256]{2,1,0:T(8,128)(2,1)}, bf16[8,128,256]{2,1,0:T(8,128)(2,1)}, u32[]{:S(2)}, u32[]{:S(2)}) collective-permute-start(bf16[8,128,256]{2,1,0:T(8,128)(2,1)} %get-tuple-element.116), channel_id=1, source_target_pairs={{0,16},{16,0},{1,17},{17,1},{2,18},{18,2},{3,19},{19,3},{4,20},{20... | collective-permute-start | bytes 1572872 | tf_op jit(solution)/shard_map/ppermute | solution.py:98
  12.3 30.4 %collective-permute-start.3 = (bf16[8,128,256]{2,1,0:T(8,128)(2,1)}, bf16[8,128,256]{2,1,0:T(8,128)(2,1)}, u32[]{:S(2)}, u32[]{:S(2)}) collective-permute-start(bf16[8,128,256]{2,1,0:T(8,128)(2,1)} %get-tuple-element.115), channel_id=1, source_target_pairs={{16,32},{32,16},{17,33},{33,17},{18,34},{34,18},{19,35},{35,19},{2... | collective-permute-start | bytes 1572872 | tf_op jit(solution)/shard_map/ppermute | solution.py:98
  54.2 13.2 %collective-permute-start.4 = (bf16[8,128,256]{1,2,0:T(8,128)(2,1)S(1)}, bf16[8,128,256]{1,2,0:T(8,128)(2,1)S(1)}, u32[]{:S(2)}, u32[]{:S(2)}) collective-permute-start(bf16[8,128,256]{1,2,0:T(8,128)(2,1)S(1)} %get-tuple-element.110), channel_id=1, source_target_pairs={{0,1},{1,0},{2,3},{3,2},{4,5},{5,4},{6,7},{7,6},{8,9},{9,8},{10,11... | collective-permute-start | bytes 1572872 | tf_op jit(solution)/shard_map/ppermute | solution.py:98
  54.3 29.3 %collective-permute-start.5 = (bf16[8,128,256]{1,2,0:T(8,128)(2,1)S(1)}, bf16[8,128,256]{1,2,0:T(8,128)(2,1)S(1)}, u32[]{:S(2)}, u32[]{:S(2)}) collective-permute-start(bf16[8,128,256]{1,2,0:T(8,128)(2,1)S(1)} %get-tuple-element.111), channel_id=1, source_target_pairs={{1,2},{2,1},{3,4},{4,3},{5,6},{6,5},{7,8},{8,7},{9,10},{10,9},{11,... | collective-permute-start | bytes 1572872 | tf_op jit(solution)/shard_map/ppermute | solution.py:98
  56.4 27.3 %collective-permute-start.6 = (bf16[8,128,256]{1,2,0:T(8,128)(2,1)S(1)}, bf16[8,128,256]{1,2,0:T(8,128)(2,1)S(1)}, u32[]{:S(2)}, u32[]{:S(2)}) collective-permute-start(bf16[8,128,256]{1,2,0:T(8,128)(2,1)S(1)} %get-tuple-element.113), channel_id=1, source_target_pairs={{0,16},{16,0},{1,17},{17,1},{2,18},{18,2},{3,19},{19,3},{4,20},{20... | collective-permute-start | bytes 1572872 | tf_op jit(solution)/shard_map/ppermute | solution.py:98
  56.5 27.2 %collective-permute-start.7 = (bf16[8,128,256]{1,2,0:T(8,128)(2,1)S(1)}, bf16[8,128,256]{1,2,0:T(8,128)(2,1)S(1)}, u32[]{:S(2)}, u32[]{:S(2)}) collective-permute-start(bf16[8,128,256]{1,2,0:T(8,128)(2,1)S(1)} %get-tuple-element.112), channel_id=1, source_target_pairs={{16,32},{32,16},{17,33},{33,17},{18,34},{34,18},{19,35},{35,19},{2... | collective-permute-start | bytes 1572872 | tf_op jit(solution)/shard_map/ppermute | solution.py:98
  86.3 15.3 %copy-start.9 = (f32[512]{0:T(512)S(1)}, f32[512]{0:T(512)}, u32[]{:S(2)}) copy-start(f32[512]{0:T(512)} %param.45) | copy-start | bytes 6148
  86.3 15.4 %copy-start.10 = (f32[512]{0:T(512)S(1)}, f32[512]{0:T(512)}, u32[]{:S(2)}) copy-start(f32[512]{0:T(512)} %param.42) | copy-start | bytes 6148
  90.8 12.0 %copy-start.7 = (f32[512]{0:T(512)S(1)}, f32[512]{0:T(512)}, u32[]{:S(2)}) copy-start(f32[512]{0:T(512)} %param.44) | copy-start | bytes 6148
  90.8 12.0 %copy-start.8 = (f32[512]{0:T(512)S(1)}, f32[512]{0:T(512)}, u32[]{:S(2)}) copy-start(f32[512]{0:T(512)} %param.43) | copy-start | bytes 6148
  90.8 12.2 %copy-start.1 = (bf16[1024,1024]{1,0:T(8,128)(2,1)S(1)}, bf16[1024,1024]{1,0:T(8,128)(2,1)}, u32[]{:S(2)}) copy-start(bf16[1024,1024]{1,0:T(8,128)(2,1)} %param.46) | copy-start | bytes 6291460
  91.5 10.2 %collective-permute-start.8 = (f32[8,2,128]{2,0,1:T(8,128)S(1)}, f32[8,2,128]{2,0,1:T(8,128)S(1)}, u32[]{:S(2)}, u32[]{:S(2)}) collective-permute-start(f32[8,2,128]{2,0,1:T(8,128)S(1)} %get-tuple-element.160), channel_id=1, source_target_pairs={{0,1},{1,0},{2,3},{3,2},{4,5},{5,4},{6,7},{7,6},{8,9},{9,8},{10,11... | collective-permute-start | bytes 24584 | tf_op jit(solution)/shard_map/ppermute | solution.py:98
  91.6 10.1 %collective-permute-start.9 = (f32[8,2,128]{2,0,1:T(8,128)S(1)}, f32[8,2,128]{2,0,1:T(8,128)S(1)}, u32[]{:S(2)}, u32[]{:S(2)}) collective-permute-start(f32[8,2,128]{2,0,1:T(8,128)S(1)} %get-tuple-element.161), channel_id=1, source_target_pairs={{1,2},{2,1},{3,4},{4,3},{5,6},{6,5},{7,8},{8,7},{9,10},{10,9},{11,... | collective-permute-start | bytes 24584 | tf_op jit(solution)/shard_map/ppermute | solution.py:98
  93.5 8.2 %collective-permute-start.10 = (f32[8,2,128]{2,0,1:T(8,128)S(1)}, f32[8,2,128]{2,0,1:T(8,128)S(1)}, u32[]{:S(2)}, u32[]{:S(2)}) collective-permute-start(f32[8,2,128]{2,0,1:T(8,128)S(1)} %get-tuple-element.163), channel_id=1, source_target_pairs={{0,16},{16,0},{1,17},{17,1},{2,18},{18,2},{3,19},{19,3},{4,20},{20... | collective-permute-start | bytes 24584 | tf_op jit(solution)/shard_map/ppermute | solution.py:98
  93.6 8.7 %collective-permute-start.11 = (f32[8,2,128]{2,0,1:T(8,128)S(1)}, f32[8,2,128]{2,0,1:T(8,128)S(1)}, u32[]{:S(2)}, u32[]{:S(2)}) collective-permute-start(f32[8,2,128]{2,0,1:T(8,128)S(1)} %get-tuple-element.162), channel_id=1, source_target_pairs={{16,32},{32,16},{17,33},{33,17},{18,34},{34,18},{19,35},{35,19},{2... | collective-permute-start | bytes 24584 | tf_op jit(solution)/shard_map/ppermute | solution.py:98
  104.1 12.5 %collective-permute-start.12 = (f32[8,2,128]{2,0,1:T(8,128)S(1)}, f32[8,2,128]{2,0,1:T(8,128)S(1)}, u32[]{:S(2)}, u32[]{:S(2)}) collective-permute-start(f32[8,2,128]{2,0,1:T(8,128)S(1)} %get-tuple-element.156), channel_id=1, source_target_pairs={{0,1},{1,0},{2,3},{3,2},{4,5},{5,4},{6,7},{7,6},{8,9},{9,8},{10,11... | collective-permute-start | bytes 24584 | tf_op jit(solution)/shard_map/ppermute | solution.py:98
  104.2 12.5 %collective-permute-start.13 = (f32[8,2,128]{2,0,1:T(8,128)S(1)}, f32[8,2,128]{2,0,1:T(8,128)S(1)}, u32[]{:S(2)}, u32[]{:S(2)}) collective-permute-start(f32[8,2,128]{2,0,1:T(8,128)S(1)} %get-tuple-element.157), channel_id=1, source_target_pairs={{1,2},{2,1},{3,4},{4,3},{5,6},{6,5},{7,8},{8,7},{9,10},{10,9},{11,... | collective-permute-start | bytes 24584 | tf_op jit(solution)/shard_map/ppermute | solution.py:98
  106.1 10.5 %collective-permute-start.14 = (f32[8,2,128]{2,0,1:T(8,128)S(1)}, f32[8,2,128]{2,0,1:T(8,128)S(1)}, u32[]{:S(2)}, u32[]{:S(2)}) collective-permute-start(f32[8,2,128]{2,0,1:T(8,128)S(1)} %get-tuple-element.159), channel_id=1, source_target_pairs={{0,16},{16,0},{1,17},{17,1},{2,18},{18,2},{3,19},{19,3},{4,20},{20... | collective-permute-start | bytes 24584 | tf_op jit(solution)/shard_map/ppermute | solution.py:98
  106.2 12.0 %collective-permute-start.15 = (f32[8,2,128]{2,0,1:T(8,128)S(1)}, f32[8,2,128]{2,0,1:T(8,128)S(1)}, u32[]{:S(2)}, u32[]{:S(2)}) collective-permute-start(f32[8,2,128]{2,0,1:T(8,128)S(1)} %get-tuple-element.158), channel_id=1, source_target_pairs={{16,32},{32,16},{17,33},{33,17},{18,34},{34,18},{19,35},{35,19},{2... | collective-permute-start | bytes 24584 | tf_op jit(solution)/shard_map/ppermute | solution.py:98
  119.9 12.4 %collective-permute-start.16 = (f32[8,2,128]{2,0,1:T(8,128)S(1)}, f32[8,2,128]{2,0,1:T(8,128)S(1)}, u32[]{:S(2)}, u32[]{:S(2)}) collective-permute-start(f32[8,2,128]{2,0,1:T(8,128)S(1)} %get-tuple-element.150), channel_id=1, source_target_pairs={{0,1},{1,0},{2,3},{3,2},{4,5},{5,4},{6,7},{7,6},{8,9},{9,8},{10,11... | collective-permute-start | bytes 24584 | tf_op jit(solution)/shard_map/ppermute | solution.py:98
  120.0 12.4 %collective-permute-start.17 = (f32[8,2,128]{2,0,1:T(8,128)S(1)}, f32[8,2,128]{2,0,1:T(8,128)S(1)}, u32[]{:S(2)}, u32[]{:S(2)}) collective-permute-start(f32[8,2,128]{2,0,1:T(8,128)S(1)} %get-tuple-element.151), channel_id=1, source_target_pairs={{1,2},{2,1},{3,4},{4,3},{5,6},{6,5},{7,8},{8,7},{9,10},{10,9},{11,... | collective-permute-start | bytes 24584 | tf_op jit(solution)/shard_map/ppermute | solution.py:98
  122.0 10.5 %collective-permute-start.18 = (f32[8,2,128]{2,0,1:T(8,128)S(1)}, f32[8,2,128]{2,0,1:T(8,128)S(1)}, u32[]{:S(2)}, u32[]{:S(2)}) collective-permute-start(f32[8,2,128]{2,0,1:T(8,128)S(1)} %get-tuple-element.153), channel_id=1, source_target_pairs={{0,16},{16,0},{1,17},{17,1},{2,18},{18,2},{3,19},{19,3},{4,20},{20... | collective-permute-start | bytes 24584 | tf_op jit(solution)/shard_map/ppermute | solution.py:98
  122.1 11.7 %collective-permute-start.19 = (f32[8,2,128]{2,0,1:T(8,128)S(1)}, f32[8,2,128]{2,0,1:T(8,128)S(1)}, u32[]{:S(2)}, u32[]{:S(2)}) collective-permute-start(f32[8,2,128]{2,0,1:T(8,128)S(1)} %get-tuple-element.152), channel_id=1, source_target_pairs={{16,32},{32,16},{17,33},{33,17},{18,34},{34,18},{19,35},{35,19},{2... | collective-permute-start | bytes 24584 | tf_op jit(solution)/shard_map/ppermute | solution.py:98
  136.5 19.0 %collective-permute-start.20 = (f32[8,2,128]{2,0,1:T(8,128)S(1)}, f32[8,2,128]{2,0,1:T(8,128)S(1)}, u32[]{:S(2)}, u32[]{:S(2)}) collective-permute-start(f32[8,2,128]{2,0,1:T(8,128)S(1)} %get-tuple-element.143), channel_id=1, source_target_pairs={{0,1},{1,0},{2,3},{3,2},{4,5},{5,4},{6,7},{7,6},{8,9},{9,8},{10,11... | collective-permute-start | bytes 24584 | tf_op jit(solution)/shard_map/ppermute | solution.py:98
  137.4 18.0 %collective-permute-start.21 = (f32[8,2,128]{2,0,1:T(8,128)S(1)}, f32[8,2,128]{2,0,1:T(8,128)S(1)}, u32[]{:S(2)}, u32[]{:S(2)}) collective-permute-start(f32[8,2,128]{2,0,1:T(8,128)S(1)} %get-tuple-element.144), channel_id=1, source_target_pairs={{1,2},{2,1},{3,4},{4,3},{5,6},{6,5},{7,8},{8,7},{9,10},{10,9},{11,... | collective-permute-start | bytes 24584 | tf_op jit(solution)/shard_map/ppermute | solution.py:98
  142.2 13.3 %collective-permute-start.22 = (f32[8,2,128]{2,0,1:T(8,128)S(1)}, f32[8,2,128]{2,0,1:T(8,128)S(1)}, u32[]{:S(2)}, u32[]{:S(2)}) collective-permute-start(f32[8,2,128]{2,0,1:T(8,128)S(1)} %get-tuple-element.146), channel_id=1, source_target_pairs={{0,16},{16,0},{1,17},{17,1},{2,18},{18,2},{3,19},{19,3},{4,20},{20... | collective-permute-start | bytes 24584 | tf_op jit(solution)/shard_map/ppermute | solution.py:98
  142.3 14.7 %collective-permute-start.23 = (f32[8,2,128]{2,0,1:T(8,128)S(1)}, f32[8,2,128]{2,0,1:T(8,128)S(1)}, u32[]{:S(2)}, u32[]{:S(2)}) collective-permute-start(f32[8,2,128]{2,0,1:T(8,128)S(1)} %get-tuple-element.145), channel_id=1, source_target_pairs={{16,32},{32,16},{17,33},{33,17},{18,34},{34,18},{19,35},{35,19},{2... | collective-permute-start | bytes 24584 | tf_op jit(solution)/shard_map/ppermute | solution.py:98
  159.3 25.2 %collective-permute-start.28 = (f32[32,2,128]{2,0,1:T(8,128)S(1)}, f32[32,2,128]{2,0,1:T(8,128)S(1)}, u32[]{:S(2)}, u32[]{:S(2)}) collective-permute-start(f32[32,2,128]{2,0,1:T(8,128)S(1)} %get-tuple-element.130), channel_id=1, source_target_pairs={{0,1},{1,0},{2,3},{3,2},{4,5},{5,4},{6,7},{7,6},{8,9},{9,8},{10,11... | collective-permute-start | bytes 98312 | tf_op jit(solution)/shard_map/ppermute | solution.py:98
  159.4 25.1 %collective-permute-start.29 = (f32[32,2,128]{2,0,1:T(8,128)S(1)}, f32[32,2,128]{2,0,1:T(8,128)S(1)}, u32[]{:S(2)}, u32[]{:S(2)}) collective-permute-start(f32[32,2,128]{2,0,1:T(8,128)S(1)} %get-tuple-element.131), channel_id=1, source_target_pairs={{1,2},{2,1},{3,4},{4,3},{5,6},{6,5},{7,8},{8,7},{9,10},{10,9},{11,... | collective-permute-start | bytes 98312 | tf_op jit(solution)/shard_map/ppermute | solution.py:98
  161.3 23.2 %collective-permute-start.30 = (f32[32,2,128]{2,0,1:T(8,128)S(1)}, f32[32,2,128]{2,0,1:T(8,128)S(1)}, u32[]{:S(2)}, u32[]{:S(2)}) collective-permute-start(f32[32,2,128]{2,0,1:T(8,128)S(1)} %get-tuple-element.133), channel_id=1, source_target_pairs={{0,16},{16,0},{1,17},{17,1},{2,18},{18,2},{3,19},{19,3},{4,20},{20... | collective-permute-start | bytes 98312 | tf_op jit(solution)/shard_map/ppermute | solution.py:98
  161.4 23.1 %collective-permute-start.31 = (f32[32,2,128]{2,0,1:T(8,128)S(1)}, f32[32,2,128]{2,0,1:T(8,128)S(1)}, u32[]{:S(2)}, u32[]{:S(2)}) collective-permute-start(f32[32,2,128]{2,0,1:T(8,128)S(1)} %get-tuple-element.132), channel_id=1, source_target_pairs={{16,32},{32,16},{17,33},{33,17},{18,34},{34,18},{19,35},{35,19},{2... | collective-permute-start | bytes 98312 | tf_op jit(solution)/shard_map/ppermute | solution.py:98
  170.9 1.3 collective-permute-start.24
  172.2 3.6 %collective-permute-start.25 = (f32[8,8]{1,0:T(8,128)S(1)}, f32[8,8]{1,0:T(8,128)S(1)}, u32[]{:S(2)}, u32[]{:S(2)}) collective-permute-start(f32[8,8]{1,0:T(8,128)S(1)} %add.341), channel_id=1, source_target_pairs={{0,2},{1,3},{2,0},{3,1},{4,6},{5,7},{6,4},{7,5},{8,10},{9,11},{10,... | collective-permute-start | bytes 776 | tf_op jit(solution)/shard_map/ppermute | solution.py:33
  175.8 5.1 %collective-permute-start.26 = (f32[8,8]{1,0:T(8,128)S(1)}, f32[8,8]{1,0:T(8,128)S(1)}, u32[]{:S(2)}, u32[]{:S(2)}) collective-permute-start(f32[8,8]{1,0:T(8,128)S(1)} %add.342), channel_id=1, source_target_pairs={{0,4},{1,5},{2,6},{3,7},{4,0},{5,1},{6,2},{7,3},{8,12},{9,13},{10,... | collective-permute-start | bytes 776 | tf_op jit(solution)/shard_map/ppermute | solution.py:33
  180.9 3.6 %collective-permute-start.27 = (f32[8,8]{1,0:T(8,128)S(1)}, f32[8,8]{1,0:T(8,128)S(1)}, u32[]{:S(2)}, u32[]{:S(2)}) collective-permute-start(f32[8,8]{1,0:T(8,128)S(1)} %add.343), channel_id=1, source_target_pairs={{0,8},{1,9},{2,10},{3,11},{4,12},{5,13},{6,14},{7,15},{8,0},{9,1},... | collective-permute-start | bytes 776 | tf_op jit(solution)/shard_map/ppermute | solution.py:33
  186.6 37.9 %collective-permute-start.36 = (f32[32,2,128]{2,0,1:T(8,128)S(1)}, f32[32,2,128]{2,0,1:T(8,128)S(1)}, u32[]{:S(2)}, u32[]{:S(2)}) collective-permute-start(f32[32,2,128]{2,0,1:T(8,128)S(1)} %get-tuple-element.126), channel_id=1, source_target_pairs={{0,1},{1,0},{2,3},{3,2},{4,5},{5,4},{6,7},{7,6},{8,9},{9,8},{10,11... | collective-permute-start | bytes 98312 | tf_op jit(solution)/shard_map/ppermute | solution.py:98
  186.7 37.8 %collective-permute-start.37 = (f32[32,2,128]{2,0,1:T(8,128)S(1)}, f32[32,2,128]{2,0,1:T(8,128)S(1)}, u32[]{:S(2)}, u32[]{:S(2)}) collective-permute-start(f32[32,2,128]{2,0,1:T(8,128)S(1)} %get-tuple-element.127), channel_id=1, source_target_pairs={{1,2},{2,1},{3,4},{4,3},{5,6},{6,5},{7,8},{8,7},{9,10},{10,9},{11,... | collective-permute-start | bytes 98312 | tf_op jit(solution)/shard_map/ppermute | solution.py:98
  188.6 35.9 %collective-permute-start.38 = (f32[32,2,128]{2,0,1:T(8,128)S(1)}, f32[32,2,128]{2,0,1:T(8,128)S(1)}, u32[]{:S(2)}, u32[]{:S(2)}) collective-permute-start(f32[32,2,128]{2,0,1:T(8,128)S(1)} %get-tuple-element.129), channel_id=1, source_target_pairs={{0,16},{16,0},{1,17},{17,1},{2,18},{18,2},{3,19},{19,3},{4,20},{20... | collective-permute-start | bytes 98312 | tf_op jit(solution)/shard_map/ppermute | solution.py:98
  188.7 35.8 %collective-permute-start.39 = (f32[32,2,128]{2,0,1:T(8,128)S(1)}, f32[32,2,128]{2,0,1:T(8,128)S(1)}, u32[]{:S(2)}, u32[]{:S(2)}) collective-permute-start(f32[32,2,128]{2,0,1:T(8,128)S(1)} %get-tuple-element.128), channel_id=1, source_target_pairs={{16,32},{32,16},{17,33},{33,17},{18,34},{34,18},{19,35},{35,19},{2... | collective-permute-start | bytes 98312 | tf_op jit(solution)/shard_map/ppermute | solution.py:98
  199.1 5.2 %collective-permute-start.32 = (f32[8,8]{1,0:T(8,128)S(1)}, f32[8,8]{1,0:T(8,128)S(1)}, u32[]{:S(2)}, u32[]{:S(2)}) collective-permute-start(f32[8,8]{1,0:T(8,128)S(1)} %add.344), channel_id=1, source_target_pairs={{0,16},{1,17},{2,18},{3,19},{4,20},{5,21},{6,22},{7,23},{8,24},{9,... | collective-permute-start | bytes 776 | tf_op jit(solution)/shard_map/ppermute | solution.py:33
  204.3 4.3 %collective-permute-start.33 = (f32[8,8]{1,0:T(8,128)S(1)}, f32[8,8]{1,0:T(8,128)S(1)}, u32[]{:S(2)}, u32[]{:S(2)}) collective-permute-start(f32[8,8]{1,0:T(8,128)S(1)} %add.345), channel_id=1, source_target_pairs={{0,32},{1,33},{2,34},{3,35},{4,36},{5,37},{6,38},{7,39},{8,40},{9,... | collective-permute-start | bytes 776 | tf_op jit(solution)/shard_map/ppermute | solution.py:33
  208.6 8.4 %collective-permute-start.34 = (f32[8,8]{1,0:T(8,128)S(1)}, f32[8,8]{1,0:T(8,128)S(1)}, u32[]{:S(2)}, u32[]{:S(2)}) collective-permute-start(f32[8,8]{1,0:T(8,128)S(1)} %add.346), channel_id=1, source_target_pairs={{0,64},{1,65},{2,66},{3,67},{4,68},{5,69},{6,70},{7,71},{8,72},{9,... | collective-permute-start | bytes 776 | tf_op jit(solution)/shard_map/ppermute | solution.py:33
  217.0 7.5 %collective-permute-start.35 = (f32[8,8]{1,0:T(8,128)S(1)}, f32[8,8]{1,0:T(8,128)S(1)}, u32[]{:S(2)}, u32[]{:S(2)}) collective-permute-start(f32[8,8]{1,0:T(8,128)S(1)} %add.347), channel_id=1, source_target_pairs={{0,128},{1,129},{2,130},{3,131},{4,132},{5,133},{6,134},{7,135},{8... | collective-permute-start | bytes 776 | tf_op jit(solution)/shard_map/ppermute | solution.py:33
  (7 other events, 27.9 us)

commit v5 on v4

--- a/solution.py
+++ b/solution.py
@@ -121,9 +121,10 @@
         )
         hidden = (hidden.astype(jnp.float32) + jax.nn.silu(summed)).astype(jnp.bfloat16)
     flat_start = jnp.array([1.0, 0.0], dtype=jnp.float32)[None, :, None]
-    voltage = (
-        jnp.einsum("sbh,ch->scb", hidden, readout, preferred_element_type=jnp.float32) + flat_start
-    )
+    readout_pad = jnp.pad(readout.T, ((0, 0), (0, 128 - readout.shape[0])))
+    projected = jnp.dot(hidden.reshape(-1, width), readout_pad, preferred_element_type=jnp.float32)
+    projected = projected[:, : readout.shape[0]].reshape(scenarios, buses, -1)
+    voltage = jnp.transpose(projected, (0, 2, 1)) + flat_start
     choose = (
         scenario_profile[:, None]
         == lax.broadcasted_iota(jnp.int32, (scenarios, load_table.shape[0]), 1)

time: 228 us -> 235 us (1.031)
  starting transfers between devices: 117 us -> 94 us
  waiting for transfers between devices: 58 us -> 80.6 us
  matrix products: 43.2 us -> 48.7 us
    ppermute x32, starting transfers between devices: 98 us -> 72.7 us  [exchange(): lax.ppermute(tiles[j], 'region', routes[j])]
    ppermute x32, waiting for transfers between devices: 38.1 us -> 61.7 us  [exchange(): lax.ppermute(tiles[j], 'region', routes[j])]
    dot_general x1 -> x2, matrix products: 8.25 us -> 16.4 us  [local(): jnp.einsum('sbh,hk->sbk', gathered, neigh_weight[number], preferred_eleme...]
    dot_general x2 -> x1, matrix products: 7.14 us -> 2.38 us  [local(): jnp.dot(hidden.reshape(-1, width), readout_pad, preferred_element_type=jn...]
  transfers between devices with their start and end apart: 40 -> 40, of which waited for: 14 -> 22; matrix products, arithmetic and copies ran while one was open for 5% -> 5% of each run, Pallas kernels for 0% -> 0%
where the time goes in v5:
time: 235 us; the launch traced here: 232 us
  starting transfers between devices  94 us (40%)
  waiting for transfers between devices  80.6 us (34%)
  matrix products  48.7 us (21%)
  local copies, waits for them, and re-layouts  5.62 us (2%)
    ppermute x32, starting transfers between devices, exchange(): lax.ppermute(tiles[j], 'region', routes[j])  72.7 us
    ppermute x32, waiting for transfers between devices, exchange(): lax.ppermute(tiles[j], 'region', routes[j])  61.7 us
    ppermute x8, starting transfers between devices, sum_rounds(): lax.ppermute(value, axis, [(i, i ^ bit) for i in range(count)])  21.3 us
    ppermute x8, waiting for transfers between devices, sum_rounds(): lax.ppermute(value, axis, [(i, i ^ bit) for i in range(count)])  18.9 us
    dot_general x2, matrix products, local(): jnp.einsum('sbh,hk->sbk', gathered, neigh_weight[number], preferred_eleme...  16.4 us
    dot_general x2, matrix products, local(): jnp.einsum('ij,sjh->sih', mask_half, hidden, preferred_element_type=jnp.f...  6.56 us
    dot_general x2, matrix products, local(): jnp.einsum('ktb,sbh->ksth', pick_half, hidden, preferred_element_type=jnp...  5.96 us
    dot_general x2, matrix products, local(): jnp.einsum('sbh,hk->sbk', hidden, self_weight[number], preferred_element_...  5.34 us
  transfers between devices with their start and end apart: 40, of which 22 were waited for; matrix products, arithmetic and copies ran while one was open for 5% of the time, Pallas kernels for 0%

profile of v5, /device:TPU:4, one launch (start us, length us, event | category | flops | bytes accessed | tf_op | source)
XLA Modules:
  0.0 231.7 jit_solution(1859923940322429767)
XLA Ops:
  2.9 2.9 %convert_bitcast_fusion.1 = bf16[4,8,128,256]{3,2,1,0:T(8,128)(2,1)S(1)} fusion(bf16[8,512,256]{2,1,0:T(8,128)(2,1)} %param.31, s32[4,128]{1,0:T(4,128)S(1)} %broadcast_select_fusion.1, pred[4,128]{1,0:T(4,128)(4,1)S(1)} %broadcast_select_fusion.2), kind=kOutput, calls=%fused_computation.42 | convolution fusion | flops 1075314688 | bytes 4196864 | tf_op jit(solution)/shard_map/ktb,sbh->ksth/dot_general | solution.py:103
  7.2 3.9 %collective-permute-start.3 = (bf16[8,128,256]{2,1,0:T(8,128)(2,1)}, bf16[8,128,256]{2,1,0:T(8,128)(2,1)}, u32[]{:S(2)}, u32[]{:S(2)}) collective-permute-start(bf16[8,128,256]{2,1,0:T(8,128)(2,1)} %get-tuple-element.107), channel_id=1, source_target_pairs={{16,32},{32,16},{17,33},{33,17},{18,34},{34,18},{19,35},{35,19},{2... | collective-permute-start | bytes 1572872 | tf_op jit(solution)/shard_map/ppermute | solution.py:98
  11.2 7.3 %collective-permute-start.1 = (bf16[8,128,256]{2,1,0:T(8,128)(2,1)}, bf16[8,128,256]{2,1,0:T(8,128)(2,1)}, u32[]{:S(2)}, u32[]{:S(2)}) collective-permute-start(bf16[8,128,256]{2,1,0:T(8,128)(2,1)} %get-tuple-element.109), channel_id=1, source_target_pairs={{1,2},{2,1},{3,4},{4,3},{5,6},{6,5},{7,8},{8,7},{9,10},{10,9},{11,... | collective-permute-start | bytes 1572872 | tf_op jit(solution)/shard_map/ppermute | solution.py:98
  18.6 2.7 %fusion.130 = f32[8,512,256]{2,1,0:T(8,128)} fusion(bf16[8,512,256]{2,1,0:T(8,128)(2,1)S(1)} %copy-done.3, bf16[2,256,256]{2,1,0:T(8,128)(2,1)S(1)} %copy-done.5), kind=kOutput, calls=%fused_computation.126 | convolution fusion | flops 536870912 | bytes 6422528 | tf_op jit(solution)/shard_map/sbh,hk->sbk/dot_general | solution.py:108
  21.9 3.3 %fusion.92 = f32[8,256,512]{1,2,0:T(8,128)} fusion(bf16[8,512,256]{2,1,0:T(8,128)(2,1)S(1)} %copy-done.3, s32[512,512]{1,0:T(8,128)S(1)} %copy-done.2), kind=kOutput, calls=%fused_computation.87 | convolution fusion | flops 1074003968 | bytes 7340032 | tf_op jit(solution)/shard_map/ij,sjh->sih/dot_general | solution.py:107
  26.3 11.1 %collective-permute-done.2 = bf16[8,128,256]{2,1,0:T(8,128)(2,1)} collective-permute-done((bf16[8,128,256]{2,1,0:T(8,128)(2,1)}, bf16[8,128,256]{2,1,0:T(8,128)(2,1)}, u32[]{:S(2)}, u32[]{:S(2)}) %collective-permute-start.2) | collective-permute-done | bytes 524320 | tf_op jit(solution)/shard_map/ppermute | solution.py:98
  37.4 8.1 %collective-permute-done.1 = bf16[8,128,256]{2,1,0:T(8,128)(2,1)} collective-permute-done((bf16[8,128,256]{2,1,0:T(8,128)(2,1)}, bf16[8,128,256]{2,1,0:T(8,128)(2,1)}, u32[]{:S(2)}, u32[]{:S(2)}) %collective-permute-start.1) | collective-permute-done | bytes 524320 | tf_op jit(solution)/shard_map/ppermute | solution.py:98
  45.5 8.2 %add_convert_fusion.1 = bf16[8,512,256]{2,1,0:T(8,128)(2,1)} fusion(f32[8,512,256]{2,1,0:T(8,128)} %fusion.130, bf16[8,512,256]{2,1,0:T(8,128)(2,1)S(1)} %copy-done.3, f32[256]{0:T(256)S(1)} %bitcast.636, f32[8,256,512]{1,2,0:T(8,128)} %fusion.92, bf16[1,8,128,256]{3,2,1,0:T(8,128)(2,1)} %bitcast.23, bf16[1,8,128,256]{3,2,1,0:T(8,128)(2,1)} %bitcast.21, ...), kind=kOutput, calls=%fused_computation.10 | convolution fusion | flops 1626603520 | bytes 14814208 | tf_op jit(solution)/shard_map/sbh,hk->sbk/dot_general | solution.py:117
  53.7 3.1 %convert_bitcast_fusion = bf16[4,8,128,256]{2,3,0,1:T(8,128)(2,1)S(1)} fusion(bf16[8,512,256]{2,1,0:T(8,128)(2,1)} %add_convert_fusion.1, s32[4,128]{1,0:T(4,128)S(1)} %broadcast_select_fusion.1, pred[4,128]{1,0:T(4,128)(4,1)S(1)} %broadcast_select_fusion.2), kind=kOutput, calls=%fused_computation.41 | convolution fusion | flops 1075314688 | bytes 4196864 | tf_op jit(solution)/shard_map/ktb,sbh->ksth/dot_general | solution.py:103
  57.0 2.1 collective-permute-start.5
  59.1 1.9 collective-permute-start.7
  61.3 2.7 %fusion.127 = f32[8,512,256]{2,1,0:T(8,128)} fusion(bf16[8,512,256]{2,1,0:T(8,128)(2,1)S(1)} %copy-done.4, bf16[2,256,256]{2,1,0:T(8,128)(2,1)S(1)} %copy-done.5), kind=kOutput, calls=%fused_computation.123 | convolution fusion | flops 536870912 | bytes 6422528 | tf_op jit(solution)/shard_map/sbh,hk->sbk/dot_general | solution.py:108
  64.0 3.3 %fusion.94 = f32[8,256,512]{1,2,0:T(8,128)} fusion(bf16[8,512,256]{2,1,0:T(8,128)(2,1)S(1)} %copy-done.4, s32[512,512]{1,0:T(8,128)S(1)} %copy-done.2), kind=kOutput, calls=%fused_computation.89 | convolution fusion | flops 1074003968 | bytes 7340032 | tf_op jit(solution)/shard_map/ij,sjh->sih/dot_general | solution.py:107
  67.3 14.5 %collective-permute-done.5 = bf16[8,128,256]{1,2,0:T(8,128)(2,1)S(1)} collective-permute-done((bf16[8,128,256]{1,2,0:T(8,128)(2,1)S(1)}, bf16[8,128,256]{1,2,0:T(8,128)(2,1)S(1)}, u32[]{:S(2)}, u32[]{:S(2)}) %collective-permute-start.5) | collective-permute-done | bytes 524320 | tf_op jit(solution)/shard_map/ppermute | solution.py:98
  81.8 6.4 %collective-permute-done.6 = bf16[8,128,256]{1,2,0:T(8,128)(2,1)S(1)} collective-permute-done((bf16[8,128,256]{1,2,0:T(8,128)(2,1)S(1)}, bf16[8,128,256]{1,2,0:T(8,128)(2,1)S(1)}, u32[]{:S(2)}, u32[]{:S(2)}) %collective-permute-start.6) | collective-permute-done | bytes 524320 | tf_op jit(solution)/shard_map/ppermute | solution.py:98
  89.0 8.2 %add_convert_fusion = bf16[8,512,256]{2,1,0:T(8,128)(2,1)} fusion(f32[8,512,256]{2,1,0:T(8,128)} %fusion.127, bf16[8,512,256]{2,1,0:T(8,128)(2,1)S(1)} %copy-done.4, f32[256]{0:T(256)S(1)} %bitcast.635, f32[8,256,512]{1,2,0:T(8,128)} %fusion.94, bf16[1,8,128,256]{2,3,1,0:T(8,128)(2,1)} %bitcast.639, bf16[1,8,128,256]{2,3,1,0:T(8,128)(2,1)} %bitcast.640, ...), kind=kOutput, calls=%fused_computation.9 | convolution fusion | flops 1626603520 | bytes 14814208 | tf_op jit(solution)/shard_map/sbh,hk->sbk/dot_general | solution.py:117
  97.2 2.4 %fusion.186 = f32[4096,2]{0,1:T(2,128)S(1)} fusion(bf16[4096,256]{1,0:T(8,128)(2,1)} %bitcast.610, bf16[2,256]{1,0:T(2,128)(2,1)S(1)} %copy-done.13), kind=kOutput, calls=%fused_computation.263 | convolution fusion | flops 4194304 | bytes 2130944 | tf_op jit(solution)/shard_map/dot_general | solution.py:125
  101.4 1.9 collective-permute-start.9
  103.4 4.9 %collective-permute-start.11 = (f32[8,2,128]{2,0,1:T(8,128)S(1)}, f32[8,2,128]{2,0,1:T(8,128)S(1)}, u32[]{:S(2)}, u32[]{:S(2)}) collective-permute-start(f32[8,2,128]{2,0,1:T(8,128)S(1)} %get-tuple-element.156), channel_id=1, source_target_pairs={{16,32},{32,16},{17,33},{33,17},{18,34},{34,18},{19,35},{35,19},{2... | collective-permute-start | bytes 24584 | tf_op jit(solution)/shard_map/ppermute | solution.py:98
  108.5 2.8 %collective-permute-done.11 = f32[8,2,128]{2,0,1:T(8,128)S(1)} collective-permute-done((f32[8,2,128]{2,0,1:T(8,128)S(1)}, f32[8,2,128]{2,0,1:T(8,128)S(1)}, u32[]{:S(2)}, u32[]{:S(2)}) %collective-permute-start.11) | collective-permute-done | bytes 8224 | tf_op jit(solution)/shard_map/ppermute | solution.py:98
  111.3 2.2 collective-permute-done.10
  115.5 2.9 %collective-permute-start.13 = (f32[8,2,128]{2,0,1:T(8,128)S(1)}, f32[8,2,128]{2,0,1:T(8,128)S(1)}, u32[]{:S(2)}, u32[]{:S(2)}) collective-permute-start(f32[8,2,128]{2,0,1:T(8,128)S(1)} %get-tuple-element.151), channel_id=1, source_target_pairs={{1,2},{2,1},{3,4},{4,3},{5,6},{6,5},{7,8},{8,7},{9,10},{10,9},{11,... | collective-permute-start | bytes 24584 | tf_op jit(solution)/shard_map/ppermute | solution.py:98
  118.4 6.7 %collective-permute-start.15 = (f32[8,2,128]{2,0,1:T(8,128)S(1)}, f32[8,2,128]{2,0,1:T(8,128)S(1)}, u32[]{:S(2)}, u32[]{:S(2)}) collective-permute-start(f32[8,2,128]{2,0,1:T(8,128)S(1)} %get-tuple-element.152), channel_id=1, source_target_pairs={{16,32},{32,16},{17,33},{33,17},{18,34},{34,18},{19,35},{35,19},{2... | collective-permute-start | bytes 24584 | tf_op jit(solution)/shard_map/ppermute | solution.py:98
  125.2 1.5 collective-permute-done.15
  126.7 3.6 %collective-permute-done.14 = f32[8,2,128]{2,0,1:T(8,128)S(1)} collective-permute-done((f32[8,2,128]{2,0,1:T(8,128)S(1)}, f32[8,2,128]{2,0,1:T(8,128)S(1)}, u32[]{:S(2)}, u32[]{:S(2)}) %collective-permute-start.14) | collective-permute-done | bytes 8224 | tf_op jit(solution)/shard_map/ppermute | solution.py:98
  132.1 1.9 collective-permute-start.17
  134.0 4.9 %collective-permute-start.19 = (f32[8,2,128]{2,0,1:T(8,128)S(1)}, f32[8,2,128]{2,0,1:T(8,128)S(1)}, u32[]{:S(2)}, u32[]{:S(2)}) collective-permute-start(f32[8,2,128]{2,0,1:T(8,128)S(1)} %get-tuple-element.148), channel_id=1, source_target_pairs={{16,32},{32,16},{17,33},{33,17},{18,34},{34,18},{19,35},{35,19},{2... | collective-permute-start | bytes 24584 | tf_op jit(solution)/shard_map/ppermute | solution.py:98
  139.2 2.7 %collective-permute-done.19 = f32[8,2,128]{2,0,1:T(8,128)S(1)} collective-permute-done((f32[8,2,128]{2,0,1:T(8,128)S(1)}, f32[8,2,128]{2,0,1:T(8,128)S(1)}, u32[]{:S(2)}, u32[]{:S(2)}) %collective-permute-start.19) | collective-permute-done | bytes 8224 | tf_op jit(solution)/shard_map/ppermute | solution.py:98
  141.9 2.4 %collective-permute-done.18 = f32[8,2,128]{2,0,1:T(8,128)S(1)} collective-permute-done((f32[8,2,128]{2,0,1:T(8,128)S(1)}, f32[8,2,128]{2,0,1:T(8,128)S(1)}, u32[]{:S(2)}, u32[]{:S(2)}) %collective-permute-start.18) | collective-permute-done | bytes 8224 | tf_op jit(solution)/shard_map/ppermute | solution.py:98
  146.9 1.9 collective-permute-start.20
  148.8 5.0 %collective-permute-start.21 = (f32[8,2,128]{2,0,1:T(8,128)S(1)}, f32[8,2,128]{2,0,1:T(8,128)S(1)}, u32[]{:S(2)}, u32[]{:S(2)}) collective-permute-start(f32[8,2,128]{2,0,1:T(8,128)S(1)} %get-tuple-element.138), channel_id=1, source_target_pairs={{1,2},{2,1},{3,4},{4,3},{5,6},{6,5},{7,8},{8,7},{9,10},{10,9},{11,... | collective-permute-start | bytes 24584 | tf_op jit(solution)/shard_map/ppermute | solution.py:98
  153.8 6.9 %collective-permute-start.23 = (f32[8,2,128]{2,0,1:T(8,128)S(1)}, f32[8,2,128]{2,0,1:T(8,128)S(1)}, u32[]{:S(2)}, u32[]{:S(2)}) collective-permute-start(f32[8,2,128]{2,0,1:T(8,128)S(1)} %get-tuple-element.139), channel_id=1, source_target_pairs={{16,32},{32,16},{17,33},{33,17},{18,34},{34,18},{19,35},{35,19},{2... | collective-permute-start | bytes 24584 | tf_op jit(solution)/shard_map/ppermute | solution.py:98
  162.4 3.6 %collective-permute-done.22 = f32[8,2,128]{2,0,1:T(8,128)S(1)} collective-permute-done((f32[8,2,128]{2,0,1:T(8,128)S(1)}, f32[8,2,128]{2,0,1:T(8,128)S(1)}, u32[]{:S(2)}, u32[]{:S(2)}) %collective-permute-start.22) | collective-permute-done | bytes 8224 | tf_op jit(solution)/shard_map/ppermute | solution.py:98
  168.3 2.5 %collective-permute-start.29 = (f32[32,2,128]{2,0,1:T(8,128)S(1)}, f32[32,2,128]{2,0,1:T(8,128)S(1)}, u32[]{:S(2)}, u32[]{:S(2)}) collective-permute-start(f32[32,2,128]{2,0,1:T(8,128)S(1)} %get-tuple-element.125), channel_id=1, source_target_pairs={{1,2},{2,1},{3,4},{4,3},{5,6},{6,5},{7,8},{8,7},{9,10},{10,9},{11,... | collective-permute-start | bytes 98312 | tf_op jit(solution)/shard_map/ppermute | solution.py:98
  170.8 6.9 %collective-permute-start.31 = (f32[32,2,128]{2,0,1:T(8,128)S(1)}, f32[32,2,128]{2,0,1:T(8,128)S(1)}, u32[]{:S(2)}, u32[]{:S(2)}) collective-permute-start(f32[32,2,128]{2,0,1:T(8,128)S(1)} %get-tuple-element.126), channel_id=1, source_target_pairs={{16,32},{32,16},{17,33},{33,17},{18,34},{34,18},{19,35},{35,19},{2... | collective-permute-start | bytes 98312 | tf_op jit(solution)/shard_map/ppermute | solution.py:98
  179.2 3.6 %collective-permute-done.25 = f32[8,8]{1,0:T(8,128)S(1)} collective-permute-done((f32[8,8]{1,0:T(8,128)S(1)}, f32[8,8]{1,0:T(8,128)S(1)}, u32[]{:S(2)}, u32[]{:S(2)}) %collective-permute-start.25) | collective-permute-done | bytes 288 | tf_op jit(solution)/shard_map/ppermute | solution.py:33
  183.1 4.9 %collective-permute-done.26 = f32[8,8]{1,0:T(8,128)S(1)} collective-permute-done((f32[8,8]{1,0:T(8,128)S(1)}, f32[8,8]{1,0:T(8,128)S(1)}, u32[]{:S(2)}, u32[]{:S(2)}) %collective-permute-start.26) | collective-permute-done | bytes 288 | tf_op jit(solution)/shard_map/ppermute | solution.py:33
  188.9 2.6 %collective-permute-done.27 = f32[8,8]{1,0:T(8,128)S(1)} collective-permute-done((f32[8,8]{1,0:T(8,128)S(1)}, f32[8,8]{1,0:T(8,128)S(1)}, u32[]{:S(2)}, u32[]{:S(2)}) %collective-permute-start.27) | collective-permute-done | bytes 288 | tf_op jit(solution)/shard_map/ppermute | solution.py:33
  193.7 5.3 %collective-permute-start.37 = (f32[32,2,128]{2,0,1:T(8,128)S(1)}, f32[32,2,128]{2,0,1:T(8,128)S(1)}, u32[]{:S(2)}, u32[]{:S(2)}) collective-permute-start(f32[32,2,128]{2,0,1:T(8,128)S(1)} %get-tuple-element.119), channel_id=1, source_target_pairs={{1,2},{2,1},{3,4},{4,3},{5,6},{6,5},{7,8},{8,7},{9,10},{10,9},{11,... | collective-permute-start | bytes 98312 | tf_op jit(solution)/shard_map/ppermute | solution.py:98
  199.0 4.1 %collective-permute-start.39 = (f32[32,2,128]{2,0,1:T(8,128)S(1)}, f32[32,2,128]{2,0,1:T(8,128)S(1)}, u32[]{:S(2)}, u32[]{:S(2)}) collective-permute-start(f32[32,2,128]{2,0,1:T(8,128)S(1)} %get-tuple-element.120), channel_id=1, source_target_pairs={{16,32},{32,16},{17,33},{33,17},{18,34},{34,18},{19,35},{35,19},{2... | collective-permute-start | bytes 98312 | tf_op jit(solution)/shard_map/ppermute | solution.py:98
  203.1 3.5 %collective-permute-start.32 = (f32[8,8]{1,0:T(8,128)S(1)}, f32[8,8]{1,0:T(8,128)S(1)}, u32[]{:S(2)}, u32[]{:S(2)}) collective-permute-start(f32[8,8]{1,0:T(8,128)S(1)} %add.346), channel_id=1, source_target_pairs={{0,16},{1,17},{2,18},{3,19},{4,20},{5,21},{6,22},{7,23},{8,24},{9,... | collective-permute-start | bytes 776 | tf_op jit(solution)/shard_map/ppermute | solution.py:33
  206.7 1.9 collective-permute-done.32
  208.6 4.2 %collective-permute-start.33 = (f32[8,8]{1,0:T(8,128)S(1)}, f32[8,8]{1,0:T(8,128)S(1)}, u32[]{:S(2)}, u32[]{:S(2)}) collective-permute-start(f32[8,8]{1,0:T(8,128)S(1)} %add.347), channel_id=1, source_target_pairs={{0,32},{1,33},{2,34},{3,35},{4,36},{5,37},{6,38},{7,39},{8,40},{9,... | collective-permute-start | bytes 776 | tf_op jit(solution)/shard_map/ppermute | solution.py:33
  212.8 1.6 collective-permute-done.33
  214.4 5.8 %collective-permute-start.34 = (f32[8,8]{1,0:T(8,128)S(1)}, f32[8,8]{1,0:T(8,128)S(1)}, u32[]{:S(2)}, u32[]{:S(2)}) collective-permute-start(f32[8,8]{1,0:T(8,128)S(1)} %add.348), channel_id=1, source_target_pairs={{0,64},{1,65},{2,66},{3,67},{4,68},{5,69},{6,70},{7,71},{8,72},{9,... | collective-permute-start | bytes 776 | tf_op jit(solution)/shard_map/ppermute | solution.py:33
  220.2 1.6 collective-permute-done.34
  221.8 6.4 %collective-permute-start.35 = (f32[8,8]{1,0:T(8,128)S(1)}, f32[8,8]{1,0:T(8,128)S(1)}, u32[]{:S(2)}, u32[]{:S(2)}) collective-permute-start(f32[8,8]{1,0:T(8,128)S(1)} %add.349), channel_id=1, source_target_pairs={{0,128},{1,129},{2,130},{3,131},{4,132},{5,133},{6,134},{7,135},{8... | collective-permute-start | bytes 776 | tf_op jit(solution)/shard_map/ppermute | solution.py:33
  228.2 1.6 collective-permute-done.35
  (159 shorter events, 26.4 us)
Async XLA Ops:
  0.0 114.1 %copy-start = (f32[16,2,512]{2,1,0:T(2,128)S(1)}, f32[16,2,512]{2,1,0:T(2,128)}, u32[]{:S(2)}) copy-start(f32[16,2,512]{2,1,0:T(2,128)} %param.40) | copy-start | bytes 196612
  7.2 18.0 %collective-permute-start = (bf16[8,128,256]{2,1,0:T(8,128)(2,1)}, bf16[8,128,256]{2,1,0:T(8,128)(2,1)}, u32[]{:S(2)}, u32[]{:S(2)}) collective-permute-start(bf16[8,128,256]{2,1,0:T(8,128)(2,1)} %get-tuple-element.106), channel_id=1, source_target_pairs={{0,1},{1,0},{2,3},{3,2},{4,5},{5,4},{6,7},{7,6},{8,9},{9,8},{10,11... | collective-permute-start | bytes 1572872 | tf_op jit(solution)/shard_map/ppermute | solution.py:98
  7.2 19.0 %collective-permute-start.3 = (bf16[8,128,256]{2,1,0:T(8,128)(2,1)}, bf16[8,128,256]{2,1,0:T(8,128)(2,1)}, u32[]{:S(2)}, u32[]{:S(2)}) collective-permute-start(bf16[8,128,256]{2,1,0:T(8,128)(2,1)} %get-tuple-element.107), channel_id=1, source_target_pairs={{16,32},{32,16},{17,33},{33,17},{18,34},{34,18},{19,35},{35,19},{2... | collective-permute-start | bytes 1572872 | tf_op jit(solution)/shard_map/ppermute | solution.py:98
  11.1 26.3 %collective-permute-start.2 = (bf16[8,128,256]{2,1,0:T(8,128)(2,1)}, bf16[8,128,256]{2,1,0:T(8,128)(2,1)}, u32[]{:S(2)}, u32[]{:S(2)}) collective-permute-start(bf16[8,128,256]{2,1,0:T(8,128)(2,1)} %get-tuple-element.108), channel_id=1, source_target_pairs={{0,16},{16,0},{1,17},{17,1},{2,18},{18,2},{3,19},{19,3},{4,20},{20... | collective-permute-start | bytes 1572872 | tf_op jit(solution)/shard_map/ppermute | solution.py:98
  11.2 34.2 %collective-permute-start.1 = (bf16[8,128,256]{2,1,0:T(8,128)(2,1)}, bf16[8,128,256]{2,1,0:T(8,128)(2,1)}, u32[]{:S(2)}, u32[]{:S(2)}) collective-permute-start(bf16[8,128,256]{2,1,0:T(8,128)(2,1)} %get-tuple-element.109), channel_id=1, source_target_pairs={{1,2},{2,1},{3,4},{4,3},{5,6},{6,5},{7,8},{8,7},{9,10},{10,9},{11,... | collective-permute-start | bytes 1572872 | tf_op jit(solution)/shard_map/ppermute | solution.py:98
  56.9 10.3 %collective-permute-start.4 = (bf16[8,128,256]{1,2,0:T(8,128)(2,1)S(1)}, bf16[8,128,256]{1,2,0:T(8,128)(2,1)S(1)}, u32[]{:S(2)}, u32[]{:S(2)}) collective-permute-start(bf16[8,128,256]{1,2,0:T(8,128)(2,1)S(1)} %get-tuple-element.102), channel_id=1, source_target_pairs={{0,1},{1,0},{2,3},{3,2},{4,5},{5,4},{6,7},{7,6},{8,9},{9,8},{10,11... | collective-permute-start | bytes 1572872 | tf_op jit(solution)/shard_map/ppermute | solution.py:98
  57.0 24.8 %collective-permute-start.5 = (bf16[8,128,256]{1,2,0:T(8,128)(2,1)S(1)}, bf16[8,128,256]{1,2,0:T(8,128)(2,1)S(1)}, u32[]{:S(2)}, u32[]{:S(2)}) collective-permute-start(bf16[8,128,256]{1,2,0:T(8,128)(2,1)S(1)} %get-tuple-element.103), channel_id=1, source_target_pairs={{1,2},{2,1},{3,4},{4,3},{5,6},{6,5},{7,8},{8,7},{9,10},{10,9},{11,... | collective-permute-start | bytes 1572872 | tf_op jit(solution)/shard_map/ppermute | solution.py:98
  59.1 22.7 %collective-permute-start.7 = (bf16[8,128,256]{1,2,0:T(8,128)(2,1)S(1)}, bf16[8,128,256]{1,2,0:T(8,128)(2,1)S(1)}, u32[]{:S(2)}, u32[]{:S(2)}) collective-permute-start(bf16[8,128,256]{1,2,0:T(8,128)(2,1)S(1)} %get-tuple-element.104), channel_id=1, source_target_pairs={{16,32},{32,16},{17,33},{33,17},{18,34},{34,18},{19,35},{35,19},{2... | collective-permute-start | bytes 1572872 | tf_op jit(solution)/shard_map/ppermute | solution.py:98
  61.0 27.2 %collective-permute-start.6 = (bf16[8,128,256]{1,2,0:T(8,128)(2,1)S(1)}, bf16[8,128,256]{1,2,0:T(8,128)(2,1)S(1)}, u32[]{:S(2)}, u32[]{:S(2)}) collective-permute-start(bf16[8,128,256]{1,2,0:T(8,128)(2,1)S(1)} %get-tuple-element.105), channel_id=1, source_target_pairs={{0,16},{16,0},{1,17},{17,1},{2,18},{18,2},{3,19},{19,3},{4,20},{20... | collective-permute-start | bytes 1572872 | tf_op jit(solution)/shard_map/ppermute | solution.py:98
  64.0 25.0 %copy-start.19 = (bf16[2,256,256]{2,1,0:T(8,128)(2,1)S(1)}, bf16[2,256,256]{2,1,0:T(8,128)(2,1)}, u32[]{:S(2)}) copy-start(bf16[2,256,256]{2,1,0:T(8,128)(2,1)} %param.37) | copy-start | bytes 786436
  67.3 21.0 %copy-start.15 = (bf16[8,128,256]{1,2,0:T(8,128)(2,1)}, bf16[8,128,256]{1,2,0:T(8,128)(2,1)S(1)}, u32[]{:S(2)}) copy-start(bf16[8,128,256]{1,2,0:T(8,128)(2,1)S(1)} %collective-permute-done.4) | copy-start | bytes 1572868
  97.2 16.9 %copy-start.7 = (f32[512]{0:T(512)S(1)}, f32[512]{0:T(512)}, u32[]{:S(2)}) copy-start(f32[512]{0:T(512)} %param.44) | copy-start | bytes 6148
  97.2 16.9 %copy-start.8 = (f32[512]{0:T(512)S(1)}, f32[512]{0:T(512)}, u32[]{:S(2)}) copy-start(f32[512]{0:T(512)} %param.43) | copy-start | bytes 6148
  97.2 16.9 %copy-start.11 = (f32[512]{0:T(512)S(1)}, f32[512]{0:T(512)}, u32[]{:S(2)}) copy-start(f32[512]{0:T(512)} %param.42) | copy-start | bytes 6148
  97.2 16.9 %copy-start.14 = (s32[8]{0:T(128)S(1)}, s32[8]{0:T(128)}, u32[]{:S(2)}) copy-start(s32[8]{0:T(128)} %param.41) | copy-start | bytes 100
  97.2 17.1 %copy-start.1 = (bf16[1024,1024]{1,0:T(8,128)(2,1)S(1)}, bf16[1024,1024]{1,0:T(8,128)(2,1)}, u32[]{:S(2)}) copy-start(bf16[1024,1024]{1,0:T(8,128)(2,1)} %param.46) | copy-start | bytes 6291460
  101.4 7.1 %collective-permute-start.8 = (f32[8,2,128]{2,0,1:T(8,128)S(1)}, f32[8,2,128]{2,0,1:T(8,128)S(1)}, u32[]{:S(2)}, u32[]{:S(2)}) collective-permute-start(f32[8,2,128]{2,0,1:T(8,128)S(1)} %get-tuple-element.154), channel_id=1, source_target_pairs={{0,1},{1,0},{2,3},{3,2},{4,5},{5,4},{6,7},{7,6},{8,9},{9,8},{10,11... | collective-permute-start | bytes 24584 | tf_op jit(solution)/shard_map/ppermute | solution.py:98
  101.4 7.1 %collective-permute-start.9 = (f32[8,2,128]{2,0,1:T(8,128)S(1)}, f32[8,2,128]{2,0,1:T(8,128)S(1)}, u32[]{:S(2)}, u32[]{:S(2)}) collective-permute-start(f32[8,2,128]{2,0,1:T(8,128)S(1)} %get-tuple-element.155), channel_id=1, source_target_pairs={{1,2},{2,1},{3,4},{4,3},{5,6},{6,5},{7,8},{8,7},{9,10},{10,9},{11,... | collective-permute-start | bytes 24584 | tf_op jit(solution)/shard_map/ppermute | solution.py:98
  103.4 7.9 %collective-permute-start.11 = (f32[8,2,128]{2,0,1:T(8,128)S(1)}, f32[8,2,128]{2,0,1:T(8,128)S(1)}, u32[]{:S(2)}, u32[]{:S(2)}) collective-permute-start(f32[8,2,128]{2,0,1:T(8,128)S(1)} %get-tuple-element.156), channel_id=1, source_target_pairs={{16,32},{32,16},{17,33},{33,17},{18,34},{34,18},{19,35},{35,19},{2... | collective-permute-start | bytes 24584 | tf_op jit(solution)/shard_map/ppermute | solution.py:98
  108.3 5.2 %collective-permute-start.10 = (f32[8,2,128]{2,0,1:T(8,128)S(1)}, f32[8,2,128]{2,0,1:T(8,128)S(1)}, u32[]{:S(2)}, u32[]{:S(2)}) collective-permute-start(f32[8,2,128]{2,0,1:T(8,128)S(1)} %get-tuple-element.157), channel_id=1, source_target_pairs={{0,16},{16,0},{1,17},{17,1},{2,18},{18,2},{3,19},{19,3},{4,20},{20... | collective-permute-start | bytes 24584 | tf_op jit(solution)/shard_map/ppermute | solution.py:98
  115.4 9.8 %collective-permute-start.12 = (f32[8,2,128]{2,0,1:T(8,128)S(1)}, f32[8,2,128]{2,0,1:T(8,128)S(1)}, u32[]{:S(2)}, u32[]{:S(2)}) collective-permute-start(f32[8,2,128]{2,0,1:T(8,128)S(1)} %get-tuple-element.150), channel_id=1, source_target_pairs={{0,1},{1,0},{2,3},{3,2},{4,5},{5,4},{6,7},{7,6},{8,9},{9,8},{10,11... | collective-permute-start | bytes 24584 | tf_op jit(solution)/shard_map/ppermute | solution.py:98
  115.5 9.7 %collective-permute-start.13 = (f32[8,2,128]{2,0,1:T(8,128)S(1)}, f32[8,2,128]{2,0,1:T(8,128)S(1)}, u32[]{:S(2)}, u32[]{:S(2)}) collective-permute-start(f32[8,2,128]{2,0,1:T(8,128)S(1)} %get-tuple-element.151), channel_id=1, source_target_pairs={{1,2},{2,1},{3,4},{4,3},{5,6},{6,5},{7,8},{8,7},{9,10},{10,9},{11,... | collective-permute-start | bytes 24584 | tf_op jit(solution)/shard_map/ppermute | solution.py:98
  118.4 8.3 %collective-permute-start.15 = (f32[8,2,128]{2,0,1:T(8,128)S(1)}, f32[8,2,128]{2,0,1:T(8,128)S(1)}, u32[]{:S(2)}, u32[]{:S(2)}) collective-permute-start(f32[8,2,128]{2,0,1:T(8,128)S(1)} %get-tuple-element.152), channel_id=1, source_target_pairs={{16,32},{32,16},{17,33},{33,17},{18,34},{34,18},{19,35},{35,19},{2... | collective-permute-start | bytes 24584 | tf_op jit(solution)/shard_map/ppermute | solution.py:98
  125.1 5.2 %collective-permute-start.14 = (f32[8,2,128]{2,0,1:T(8,128)S(1)}, f32[8,2,128]{2,0,1:T(8,128)S(1)}, u32[]{:S(2)}, u32[]{:S(2)}) collective-permute-start(f32[8,2,128]{2,0,1:T(8,128)S(1)} %get-tuple-element.153), channel_id=1, source_target_pairs={{0,16},{16,0},{1,17},{17,1},{2,18},{18,2},{3,19},{19,3},{4,20},{20... | collective-permute-start | bytes 24584 | tf_op jit(solution)/shard_map/ppermute | solution.py:98
  132.0 7.3 %collective-permute-start.16 = (f32[8,2,128]{2,0,1:T(8,128)S(1)}, f32[8,2,128]{2,0,1:T(8,128)S(1)}, u32[]{:S(2)}, u32[]{:S(2)}) collective-permute-start(f32[8,2,128]{2,0,1:T(8,128)S(1)} %get-tuple-element.146), channel_id=1, source_target_pairs={{0,1},{1,0},{2,3},{3,2},{4,5},{5,4},{6,7},{7,6},{8,9},{9,8},{10,11... | collective-permute-start | bytes 24584 | tf_op jit(solution)/shard_map/ppermute | solution.py:98
  132.1 7.2 %collective-permute-start.17 = (f32[8,2,128]{2,0,1:T(8,128)S(1)}, f32[8,2,128]{2,0,1:T(8,128)S(1)}, u32[]{:S(2)}, u32[]{:S(2)}) collective-permute-start(f32[8,2,128]{2,0,1:T(8,128)S(1)} %get-tuple-element.147), channel_id=1, source_target_pairs={{1,2},{2,1},{3,4},{4,3},{5,6},{6,5},{7,8},{8,7},{9,10},{10,9},{11,... | collective-permute-start | bytes 24584 | tf_op jit(solution)/shard_map/ppermute | solution.py:98
  134.0 7.9 %collective-permute-start.19 = (f32[8,2,128]{2,0,1:T(8,128)S(1)}, f32[8,2,128]{2,0,1:T(8,128)S(1)}, u32[]{:S(2)}, u32[]{:S(2)}) collective-permute-start(f32[8,2,128]{2,0,1:T(8,128)S(1)} %get-tuple-element.148), channel_id=1, source_target_pairs={{16,32},{32,16},{17,33},{33,17},{18,34},{34,18},{19,35},{35,19},{2... | collective-permute-start | bytes 24584 | tf_op jit(solution)/shard_map/ppermute | solution.py:98
  138.9 5.5 %collective-permute-start.18 = (f32[8,2,128]{2,0,1:T(8,128)S(1)}, f32[8,2,128]{2,0,1:T(8,128)S(1)}, u32[]{:S(2)}, u32[]{:S(2)}) collective-permute-start(f32[8,2,128]{2,0,1:T(8,128)S(1)} %get-tuple-element.149), channel_id=1, source_target_pairs={{0,16},{16,0},{1,17},{17,1},{2,18},{18,2},{3,19},{19,3},{4,20},{20... | collective-permute-start | bytes 24584 | tf_op jit(solution)/shard_map/ppermute | solution.py:98
  146.9 14.0 %collective-permute-start.20 = (f32[8,2,128]{2,0,1:T(8,128)S(1)}, f32[8,2,128]{2,0,1:T(8,128)S(1)}, u32[]{:S(2)}, u32[]{:S(2)}) collective-permute-start(f32[8,2,128]{2,0,1:T(8,128)S(1)} %get-tuple-element.137), channel_id=1, source_target_pairs={{0,1},{1,0},{2,3},{3,2},{4,5},{5,4},{6,7},{7,6},{8,9},{9,8},{10,11... | collective-permute-start | bytes 24584 | tf_op jit(solution)/shard_map/ppermute | solution.py:98
  148.8 12.1 %collective-permute-start.21 = (f32[8,2,128]{2,0,1:T(8,128)S(1)}, f32[8,2,128]{2,0,1:T(8,128)S(1)}, u32[]{:S(2)}, u32[]{:S(2)}) collective-permute-start(f32[8,2,128]{2,0,1:T(8,128)S(1)} %get-tuple-element.138), channel_id=1, source_target_pairs={{1,2},{2,1},{3,4},{4,3},{5,6},{6,5},{7,8},{8,7},{9,10},{10,9},{11,... | collective-permute-start | bytes 24584 | tf_op jit(solution)/shard_map/ppermute | solution.py:98
  153.8 8.6 %collective-permute-start.23 = (f32[8,2,128]{2,0,1:T(8,128)S(1)}, f32[8,2,128]{2,0,1:T(8,128)S(1)}, u32[]{:S(2)}, u32[]{:S(2)}) collective-permute-start(f32[8,2,128]{2,0,1:T(8,128)S(1)} %get-tuple-element.139), channel_id=1, source_target_pairs={{16,32},{32,16},{17,33},{33,17},{18,34},{34,18},{19,35},{35,19},{2... | collective-permute-start | bytes 24584 | tf_op jit(solution)/shard_map/ppermute | solution.py:98
  160.8 5.2 %collective-permute-start.22 = (f32[8,2,128]{2,0,1:T(8,128)S(1)}, f32[8,2,128]{2,0,1:T(8,128)S(1)}, u32[]{:S(2)}, u32[]{:S(2)}) collective-permute-start(f32[8,2,128]{2,0,1:T(8,128)S(1)} %get-tuple-element.140), channel_id=1, source_target_pairs={{0,16},{16,0},{1,17},{17,1},{2,18},{18,2},{3,19},{19,3},{4,20},{20... | collective-permute-start | bytes 24584 | tf_op jit(solution)/shard_map/ppermute | solution.py:98
  168.2 23.4 %collective-permute-start.28 = (f32[32,2,128]{2,0,1:T(8,128)S(1)}, f32[32,2,128]{2,0,1:T(8,128)S(1)}, u32[]{:S(2)}, u32[]{:S(2)}) collective-permute-start(f32[32,2,128]{2,0,1:T(8,128)S(1)} %get-tuple-element.124), channel_id=1, source_target_pairs={{0,1},{1,0},{2,3},{3,2},{4,5},{5,4},{6,7},{7,6},{8,9},{9,8},{10,11... | collective-permute-start | bytes 98312 | tf_op jit(solution)/shard_map/ppermute | solution.py:98
  168.3 23.3 %collective-permute-start.29 = (f32[32,2,128]{2,0,1:T(8,128)S(1)}, f32[32,2,128]{2,0,1:T(8,128)S(1)}, u32[]{:S(2)}, u32[]{:S(2)}) collective-permute-start(f32[32,2,128]{2,0,1:T(8,128)S(1)} %get-tuple-element.125), channel_id=1, source_target_pairs={{1,2},{2,1},{3,4},{4,3},{5,6},{6,5},{7,8},{8,7},{9,10},{10,9},{11,... | collective-permute-start | bytes 98312 | tf_op jit(solution)/shard_map/ppermute | solution.py:98
  170.8 20.7 %collective-permute-start.31 = (f32[32,2,128]{2,0,1:T(8,128)S(1)}, f32[32,2,128]{2,0,1:T(8,128)S(1)}, u32[]{:S(2)}, u32[]{:S(2)}) collective-permute-start(f32[32,2,128]{2,0,1:T(8,128)S(1)} %get-tuple-element.126), channel_id=1, source_target_pairs={{16,32},{32,16},{17,33},{33,17},{18,34},{34,18},{19,35},{35,19},{2... | collective-permute-start | bytes 98312 | tf_op jit(solution)/shard_map/ppermute | solution.py:98
  177.8 13.8 %collective-permute-start.30 = (f32[32,2,128]{2,0,1:T(8,128)S(1)}, f32[32,2,128]{2,0,1:T(8,128)S(1)}, u32[]{:S(2)}, u32[]{:S(2)}) collective-permute-start(f32[32,2,128]{2,0,1:T(8,128)S(1)} %get-tuple-element.127), channel_id=1, source_target_pairs={{0,16},{16,0},{1,17},{17,1},{2,18},{18,2},{3,19},{19,3},{4,20},{20... | collective-permute-start | bytes 98312 | tf_op jit(solution)/shard_map/ppermute | solution.py:98
  178.0 1.3 collective-permute-start.24
  179.2 3.6 %collective-permute-start.25 = (f32[8,8]{1,0:T(8,128)S(1)}, f32[8,8]{1,0:T(8,128)S(1)}, u32[]{:S(2)}, u32[]{:S(2)}) collective-permute-start(f32[8,8]{1,0:T(8,128)S(1)} %add.343), channel_id=1, source_target_pairs={{0,2},{1,3},{2,0},{3,1},{4,6},{5,7},{6,4},{7,5},{8,10},{9,11},{10,... | collective-permute-start | bytes 776 | tf_op jit(solution)/shard_map/ppermute | solution.py:33
  182.8 5.1 %collective-permute-start.26 = (f32[8,8]{1,0:T(8,128)S(1)}, f32[8,8]{1,0:T(8,128)S(1)}, u32[]{:S(2)}, u32[]{:S(2)}) collective-permute-start(f32[8,8]{1,0:T(8,128)S(1)} %add.344), channel_id=1, source_target_pairs={{0,4},{1,5},{2,6},{3,7},{4,0},{5,1},{6,2},{7,3},{8,12},{9,13},{10,... | collective-permute-start | bytes 776 | tf_op jit(solution)/shard_map/ppermute | solution.py:33
  187.9 3.6 %collective-permute-start.27 = (f32[8,8]{1,0:T(8,128)S(1)}, f32[8,8]{1,0:T(8,128)S(1)}, u32[]{:S(2)}, u32[]{:S(2)}) collective-permute-start(f32[8,8]{1,0:T(8,128)S(1)} %add.345), channel_id=1, source_target_pairs={{0,8},{1,9},{2,10},{3,11},{4,12},{5,13},{6,14},{7,15},{8,0},{9,1},... | collective-permute-start | bytes 776 | tf_op jit(solution)/shard_map/ppermute | solution.py:33
  193.6 36.2 %collective-permute-start.36 = (f32[32,2,128]{2,0,1:T(8,128)S(1)}, f32[32,2,128]{2,0,1:T(8,128)S(1)}, u32[]{:S(2)}, u32[]{:S(2)}) collective-permute-start(f32[32,2,128]{2,0,1:T(8,128)S(1)} %get-tuple-element.118), channel_id=1, source_target_pairs={{0,1},{1,0},{2,3},{3,2},{4,5},{5,4},{6,7},{7,6},{8,9},{9,8},{10,11... | collective-permute-start | bytes 98312 | tf_op jit(solution)/shard_map/ppermute | solution.py:98
  193.7 36.1 %collective-permute-start.37 = (f32[32,2,128]{2,0,1:T(8,128)S(1)}, f32[32,2,128]{2,0,1:T(8,128)S(1)}, u32[]{:S(2)}, u32[]{:S(2)}) collective-permute-start(f32[32,2,128]{2,0,1:T(8,128)S(1)} %get-tuple-element.119), channel_id=1, source_target_pairs={{1,2},{2,1},{3,4},{4,3},{5,6},{6,5},{7,8},{8,7},{9,10},{10,9},{11,... | collective-permute-start | bytes 98312 | tf_op jit(solution)/shard_map/ppermute | solution.py:98
  199.0 30.8 %collective-permute-start.39 = (f32[32,2,128]{2,0,1:T(8,128)S(1)}, f32[32,2,128]{2,0,1:T(8,128)S(1)}, u32[]{:S(2)}, u32[]{:S(2)}) collective-permute-start(f32[32,2,128]{2,0,1:T(8,128)S(1)} %get-tuple-element.120), channel_id=1, source_target_pairs={{16,32},{32,16},{17,33},{33,17},{18,34},{34,18},{19,35},{35,19},{2... | collective-permute-start | bytes 98312 | tf_op jit(solution)/shard_map/ppermute | solution.py:98
  203.0 26.8 %collective-permute-start.38 = (f32[32,2,128]{2,0,1:T(8,128)S(1)}, f32[32,2,128]{2,0,1:T(8,128)S(1)}, u32[]{:S(2)}, u32[]{:S(2)}) collective-permute-start(f32[32,2,128]{2,0,1:T(8,128)S(1)} %get-tuple-element.121), channel_id=1, source_target_pairs={{0,16},{16,0},{1,17},{17,1},{2,18},{18,2},{3,19},{19,3},{4,20},{20... | collective-permute-start | bytes 98312 | tf_op jit(solution)/shard_map/ppermute | solution.py:98
  203.1 5.4 %collective-permute-start.32 = (f32[8,8]{1,0:T(8,128)S(1)}, f32[8,8]{1,0:T(8,128)S(1)}, u32[]{:S(2)}, u32[]{:S(2)}) collective-permute-start(f32[8,8]{1,0:T(8,128)S(1)} %add.346), channel_id=1, source_target_pairs={{0,16},{1,17},{2,18},{3,19},{4,20},{5,21},{6,22},{7,23},{8,24},{9,... | collective-permute-start | bytes 776 | tf_op jit(solution)/shard_map/ppermute | solution.py:33
  208.6 5.8 %collective-permute-start.33 = (f32[8,8]{1,0:T(8,128)S(1)}, f32[8,8]{1,0:T(8,128)S(1)}, u32[]{:S(2)}, u32[]{:S(2)}) collective-permute-start(f32[8,8]{1,0:T(8,128)S(1)} %add.347), channel_id=1, source_target_pairs={{0,32},{1,33},{2,34},{3,35},{4,36},{5,37},{6,38},{7,39},{8,40},{9,... | collective-permute-start | bytes 776 | tf_op jit(solution)/shard_map/ppermute | solution.py:33
  214.4 7.4 %collective-permute-start.34 = (f32[8,8]{1,0:T(8,128)S(1)}, f32[8,8]{1,0:T(8,128)S(1)}, u32[]{:S(2)}, u32[]{:S(2)}) collective-permute-start(f32[8,8]{1,0:T(8,128)S(1)} %add.348), channel_id=1, source_target_pairs={{0,64},{1,65},{2,66},{3,67},{4,68},{5,69},{6,70},{7,71},{8,72},{9,... | collective-permute-start | bytes 776 | tf_op jit(solution)/shard_map/ppermute | solution.py:33
  221.8 8.0 %collective-permute-start.35 = (f32[8,8]{1,0:T(8,128)S(1)}, f32[8,8]{1,0:T(8,128)S(1)}, u32[]{:S(2)}, u32[]{:S(2)}) collective-permute-start(f32[8,8]{1,0:T(8,128)S(1)} %add.349), channel_id=1, source_target_pairs={{0,128},{1,129},{2,130},{3,131},{4,132},{5,133},{6,134},{7,135},{8... | collective-permute-start | bytes 776 | tf_op jit(solution)/shard_map/ppermute | solution.py:33
  (12 other events, 74.9 us)

commit v6 on v4

--- a/solution.py
+++ b/solution.py
@@ -20,11 +20,25 @@
     return pairs
 
 
+RINGS = (8, 4, 4, 2)
+
+
 def sum_bits(axis):
     count = lax.axis_size(axis)
     if count & (count - 1):
         return None
-    return [1 << b for b in range(count.bit_length() - 1)]
+    sizes = RINGS
+    total = 1
+    for size in sizes:
+        total *= size
+    if total != count:
+        return [1 << b for b in range(count.bit_length() - 1)]
+    near = {2: [1], 4: [1, 3], 8: [1, 2, 7]}
+    masks, stride = [], 1
+    for size in reversed(sizes):
+        masks += [m * stride for m in near[size]]
+        stride *= size
+    return masks
 
 
 def sum_rounds(value, axis, bits):

time: 228 us -> 226 us (level); the launches traced: 227 us -> 222 us
  starting transfers between devices: 117 us -> 113 us
    ppermute x8, starting transfers between devices: 19 us -> 15.7 us  [sum_rounds(): lax.ppermute(value, axis, [(i, i ^ bit) for i in range(count)])]
where the time goes in v6:
time: 226 us; the launch traced here: 222 us
  starting transfers between devices  113 us (50%)
  waiting for transfers between devices  57.5 us (25%)
  matrix products  43.2 us (19%)
  local copies, waits for them, and re-layouts  4.62 us (2%)
  other arithmetic  3.05 us (1%)
    ppermute x32, starting transfers between devices, exchange(): lax.ppermute(tiles[j], 'region', routes[j])  97.2 us
    ppermute x32, waiting for transfers between devices, exchange(): lax.ppermute(tiles[j], 'region', routes[j])  38.1 us
    ppermute x8, waiting for transfers between devices, sum_rounds(): lax.ppermute(value, axis, [(i, i ^ bit) for i in range(count)])  19.5 us
    ppermute x8, starting transfers between devices, sum_rounds(): lax.ppermute(value, axis, [(i, i ^ bit) for i in range(count)])  15.7 us
    dot_general x1, matrix products, local(): jnp.einsum('sbh,hk->sbk', gathered, neigh_weight[number], preferred_eleme...  8.25 us
    dot_general x2, matrix products, local(): jnp.einsum('ktb,sbh->ksth', pick_half, hidden, preferred_element_type=jnp...  5.96 us
    dot_general x2, matrix products, local(): jnp.einsum('sbh,hk->sbk', hidden, self_weight[number], preferred_element_...  5.33 us
    dot_general x2, matrix products, local(): jnp.einsum('ij,sjh->sih', mask_half, hidden, preferred_element_type=jnp.f...  4.53 us
  transfers between devices with their start and end apart: 40, of which 14 were waited for; matrix products, arithmetic and copies ran while one was open for 5% of the time, Pallas kernels for 0%

profile of v6, /device:TPU:4, one launch (start us, length us, event | category | flops | bytes accessed | tf_op | source)
XLA Modules:
  0.0 222.3 jit_solution(6267801470293771989)
XLA Ops:
  1.6 1.2 gather_fusion.1
  2.9 2.9 %convert_bitcast_fusion.1 = bf16[4,8,128,256]{3,2,1,0:T(8,128)(2,1)S(1)} fusion(bf16[8,512,256]{2,1,0:T(8,128)(2,1)} %param.31, s32[4,128]{1,0:T(4,128)S(1)} %broadcast_select_fusion.1, pred[4,128]{1,0:T(4,128)(4,1)S(1)} %broadcast_select_fusion.2), kind=kOutput, calls=%fused_computation.42 | convolution fusion | flops 1075314688 | bytes 4196864 | tf_op jit(solution)/shard_map/ktb,sbh->ksth/dot_general | solution.py:117
  5.8 1.4 slice_bitcast_fusion.7
  7.2 5.0 %collective-permute-start.1 = (bf16[8,128,256]{2,1,0:T(8,128)(2,1)}, bf16[8,128,256]{2,1,0:T(8,128)(2,1)}, u32[]{:S(2)}, u32[]{:S(2)}) collective-permute-start(bf16[8,128,256]{2,1,0:T(8,128)(2,1)} %get-tuple-element.117), channel_id=1, source_target_pairs={{1,2},{2,1},{3,4},{4,3},{5,6},{6,5},{7,8},{8,7},{9,10},{10,9},{11,... | collective-permute-start | bytes 1572872 | tf_op jit(solution)/shard_map/ppermute | solution.py:112
  12.3 6.8 %collective-permute-start.3 = (bf16[8,128,256]{2,1,0:T(8,128)(2,1)}, bf16[8,128,256]{2,1,0:T(8,128)(2,1)}, u32[]{:S(2)}, u32[]{:S(2)}) collective-permute-start(bf16[8,128,256]{2,1,0:T(8,128)(2,1)} %get-tuple-element.115), channel_id=1, source_target_pairs={{16,32},{32,16},{17,33},{33,17},{18,34},{34,18},{19,35},{35,19},{2... | collective-permute-start | bytes 1572872 | tf_op jit(solution)/shard_map/ppermute | solution.py:112
  19.2 2.7 %fusion.128 = f32[8,512,256]{2,1,0:T(8,128)} fusion(bf16[8,512,256]{2,1,0:T(8,128)(2,1)S(1)} %copy-done.3, bf16[2,256,256]{2,1,0:T(8,128)(2,1)S(1)} %copy-done.5), kind=kOutput, calls=%fused_computation.127 | convolution fusion | flops 536870912 | bytes 6422528 | tf_op jit(solution)/shard_map/sbh,hk->sbk/dot_general | solution.py:122
  22.7 3.3 %fusion.90 = f32[8,256,512]{1,2,0:T(8,128)} fusion(bf16[8,512,256]{2,1,0:T(8,128)(2,1)S(1)} %copy-done.3, s32[512,512]{1,0:T(8,128)S(1)} %copy-done.2), kind=kOutput, calls=%fused_computation.88 | convolution fusion | flops 1074003968 | bytes 7340032 | tf_op jit(solution)/shard_map/ij,sjh->sih/dot_general | solution.py:121
  26.0 16.7 %collective-permute-done.1 = bf16[8,128,256]{2,1,0:T(8,128)(2,1)} collective-permute-done((bf16[8,128,256]{2,1,0:T(8,128)(2,1)}, bf16[8,128,256]{2,1,0:T(8,128)(2,1)}, u32[]{:S(2)}, u32[]{:S(2)}) %collective-permute-start.1) | collective-permute-done | bytes 524320 | tf_op jit(solution)/shard_map/ppermute | solution.py:112
  42.7 8.2 %add_convert_fusion.1 = bf16[8,512,256]{2,1,0:T(8,128)(2,1)} fusion(f32[8,512,256]{2,1,0:T(8,128)} %fusion.128, bf16[8,512,256]{2,1,0:T(8,128)(2,1)S(1)} %copy-done.3, f32[256]{0:T(256)S(1)} %bitcast.577, f32[8,256,512]{1,2,0:T(8,128)} %fusion.90, bf16[1,8,128,256]{3,2,1,0:T(8,128)(2,1)} %bitcast.23, bf16[1,8,128,256]{3,2,1,0:T(8,128)(2,1)} %bitcast.21, ...), kind=kOutput, calls=%fused_computation.10 | convolution fusion | flops 1626603520 | bytes 14814208 | tf_op jit(solution)/shard_map/sbh,hk->sbk/dot_general | solution.py:131
  51.0 3.1 %convert_bitcast_fusion = bf16[4,8,128,256]{2,3,0,1:T(8,128)(2,1)S(1)} fusion(bf16[8,512,256]{2,1,0:T(8,128)(2,1)} %add_convert_fusion.1, s32[4,128]{1,0:T(4,128)S(1)} %broadcast_select_fusion.1, pred[4,128]{1,0:T(4,128)(4,1)S(1)} %broadcast_select_fusion.2), kind=kOutput, calls=%fused_computation.41 | convolution fusion | flops 1075314688 | bytes 4196864 | tf_op jit(solution)/shard_map/ktb,sbh->ksth/dot_general | solution.py:117
  54.3 2.1 collective-permute-start.5
  56.5 6.9 %collective-permute-start.7 = (bf16[8,128,256]{1,2,0:T(8,128)(2,1)S(1)}, bf16[8,128,256]{1,2,0:T(8,128)(2,1)S(1)}, u32[]{:S(2)}, u32[]{:S(2)}) collective-permute-start(bf16[8,128,256]{1,2,0:T(8,128)(2,1)S(1)} %get-tuple-element.112), channel_id=1, source_target_pairs={{16,32},{32,16},{17,33},{33,17},{18,34},{34,18},{19,35},{35,19},{2... | collective-permute-start | bytes 1572872 | tf_op jit(solution)/shard_map/ppermute | solution.py:112
  63.4 2.7 %fusion.125 = f32[8,512,256]{2,1,0:T(8,128)} fusion(bf16[8,512,256]{2,1,0:T(8,128)(2,1)S(1)} %copy-done.4, bf16[2,256,256]{2,1,0:T(8,128)(2,1)S(1)} %copy-done.5), kind=kOutput, calls=%fused_computation.124 | convolution fusion | flops 536870912 | bytes 6422528 | tf_op jit(solution)/shard_map/sbh,hk->sbk/dot_general | solution.py:122
  66.1 1.3 fusion.92
  67.4 16.3 %collective-permute-done.5 = bf16[8,128,256]{1,2,0:T(8,128)(2,1)S(1)} collective-permute-done((bf16[8,128,256]{1,2,0:T(8,128)(2,1)S(1)}, bf16[8,128,256]{1,2,0:T(8,128)(2,1)S(1)}, u32[]{:S(2)}, u32[]{:S(2)}) %collective-permute-start.5) | collective-permute-done | bytes 524320 | tf_op jit(solution)/shard_map/ppermute | solution.py:112
  83.7 2.7 %fusion.1 = bf16[8,256,512]{1,2,0:T(8,128)(2,1)} fusion(f32[8,256,512]{1,2,0:T(8,128)S(1)} %fusion.92, bf16[1,8,128,256]{2,3,1,0:T(8,128)(2,1)S(1)} %bitcast.581, bf16[1,8,128,256]{2,3,1,0:T(8,128)(2,1)S(1)} %bitcast.580, bf16[1,8,128,256]{2,3,1,0:T(8,128)(2,1)S(1)} %bitcast.579, bf16[1,8,128,256]{2,3,1,0:T(8,128)(2,1)S(1)} %bitcast.578, ...), kind=kOutput, calls=%fused_computation.5 | convolution fusion | flops 1080295424 | bytes 8390656 | tf_op jit(solution)/shard_map/ktb,ksth->sbh/dot_general | solution.py:125
  86.3 4.5 %fusion.55 = f32[8,512,2]{1,2,0:T(2,128)S(1)} fusion(f32[8,512,256]{2,1,0:T(8,128)} %fusion.125, bf16[8,512,256]{2,1,0:T(8,128)(2,1)S(1)} %copy-done.4, bf16[8,256,512]{1,2,0:T(8,128)(2,1)} %fusion.1, f32[256]{0:T(256)S(1)} %bitcast.576, bf16[2,256,256]{2,1,0:T(8,128)(2,1)} %param.37, f32[2]{0:T(128)S(1)} %copy-done.14, bf16[2,256]{1,0:T(2,128)(2,1)S(1)} %copy-done.13), kind=kOutput, calls=%fused_computation.62 | convolution fusion | flops 550510592 | bytes 8554504 | tf_op jit(solution)/shard_map/sbh,ch->scb/dot_general | solution.py:139
  91.6 1.9 collective-permute-start.9
  93.6 7.0 %collective-permute-start.11 = (f32[8,2,128]{2,0,1:T(8,128)S(1)}, f32[8,2,128]{2,0,1:T(8,128)S(1)}, u32[]{:S(2)}, u32[]{:S(2)}) collective-permute-start(f32[8,2,128]{2,0,1:T(8,128)S(1)} %get-tuple-element.162), channel_id=1, source_target_pairs={{16,32},{32,16},{17,33},{33,17},{18,34},{34,18},{19,35},{35,19},{2... | collective-permute-start | bytes 24584 | tf_op jit(solution)/shard_map/ppermute | solution.py:112
  100.7 0.9 fusion.65
  104.2 1.9 collective-permute-start.13
  106.2 10.4 %collective-permute-start.15 = (f32[8,2,128]{2,0,1:T(8,128)S(1)}, f32[8,2,128]{2,0,1:T(8,128)S(1)}, u32[]{:S(2)}, u32[]{:S(2)}) collective-permute-start(f32[8,2,128]{2,0,1:T(8,128)S(1)} %get-tuple-element.158), channel_id=1, source_target_pairs={{16,32},{32,16},{17,33},{33,17},{18,34},{34,18},{19,35},{35,19},{2... | collective-permute-start | bytes 24584 | tf_op jit(solution)/shard_map/ppermute | solution.py:112
  116.7 1.6 collective-permute-done.15
  120.0 1.9 collective-permute-start.17
  122.1 10.3 %collective-permute-start.19 = (f32[8,2,128]{2,0,1:T(8,128)S(1)}, f32[8,2,128]{2,0,1:T(8,128)S(1)}, u32[]{:S(2)}, u32[]{:S(2)}) collective-permute-start(f32[8,2,128]{2,0,1:T(8,128)S(1)} %get-tuple-element.152), channel_id=1, source_target_pairs={{16,32},{32,16},{17,33},{33,17},{18,34},{34,18},{19,35},{35,19},{2... | collective-permute-start | bytes 24584 | tf_op jit(solution)/shard_map/ppermute | solution.py:112
  132.4 1.4 collective-permute-done.19
  135.5 0.9 fusion.63
  136.5 1.0 collective-permute-start.20
  137.4 4.7 %collective-permute-start.21 = (f32[8,2,128]{2,0,1:T(8,128)S(1)}, f32[8,2,128]{2,0,1:T(8,128)S(1)}, u32[]{:S(2)}, u32[]{:S(2)}) collective-permute-start(f32[8,2,128]{2,0,1:T(8,128)S(1)} %get-tuple-element.144), channel_id=1, source_target_pairs={{1,2},{2,1},{3,4},{4,3},{5,6},{6,5},{7,8},{8,7},{9,10},{10,9},{11,... | collective-permute-start | bytes 24584 | tf_op jit(solution)/shard_map/ppermute | solution.py:112
  142.3 13.1 %collective-permute-start.23 = (f32[8,2,128]{2,0,1:T(8,128)S(1)}, f32[8,2,128]{2,0,1:T(8,128)S(1)}, u32[]{:S(2)}, u32[]{:S(2)}) collective-permute-start(f32[8,2,128]{2,0,1:T(8,128)S(1)} %get-tuple-element.145), channel_id=1, source_target_pairs={{16,32},{32,16},{17,33},{33,17},{18,34},{34,18},{19,35},{35,19},{2... | collective-permute-start | bytes 24584 | tf_op jit(solution)/shard_map/ppermute | solution.py:112
  155.5 1.5 collective-permute-done.23
  158.5 0.8 convolution_bitcast_fusion.3
  159.4 1.9 collective-permute-start.29
  161.4 9.4 %collective-permute-start.31 = (f32[32,2,128]{2,0,1:T(8,128)S(1)}, f32[32,2,128]{2,0,1:T(8,128)S(1)}, u32[]{:S(2)}, u32[]{:S(2)}) collective-permute-start(f32[32,2,128]{2,0,1:T(8,128)S(1)} %get-tuple-element.132), channel_id=1, source_target_pairs={{16,32},{32,16},{17,33},{33,17},{18,34},{34,18},{19,35},{35,19},{2... | collective-permute-start | bytes 98312 | tf_op jit(solution)/shard_map/ppermute | solution.py:112
  171.0 1.2 collective-permute-done.24
  172.8 2.9 %collective-permute-done.25 = f32[8,8]{1,0:T(8,128)S(1)} collective-permute-done((f32[8,8]{1,0:T(8,128)S(1)}, f32[8,8]{1,0:T(8,128)S(1)}, u32[]{:S(2)}, u32[]{:S(2)}) %collective-permute-start.25) | collective-permute-done | bytes 288 | tf_op jit(solution)/shard_map/ppermute | solution.py:47
  175.8 2.3 %collective-permute-start.26 = (f32[8,8]{1,0:T(8,128)S(1)}, f32[8,8]{1,0:T(8,128)S(1)}, u32[]{:S(2)}, u32[]{:S(2)}) collective-permute-start(f32[8,8]{1,0:T(8,128)S(1)} %add.342), channel_id=1, source_target_pairs={{0,6},{1,7},{2,4},{3,5},{4,2},{5,3},{6,0},{7,1},{8,14},{9,15},{10,... | collective-permute-start | bytes 776 | tf_op jit(solution)/shard_map/ppermute | solution.py:47
  178.0 2.6 %collective-permute-done.26 = f32[8,8]{1,0:T(8,128)S(1)} collective-permute-done((f32[8,8]{1,0:T(8,128)S(1)}, f32[8,8]{1,0:T(8,128)S(1)}, u32[]{:S(2)}, u32[]{:S(2)}) %collective-permute-start.26) | collective-permute-done | bytes 288 | tf_op jit(solution)/shard_map/ppermute | solution.py:47
  180.6 2.8 %collective-permute-start.27 = (f32[8,8]{1,0:T(8,128)S(1)}, f32[8,8]{1,0:T(8,128)S(1)}, u32[]{:S(2)}, u32[]{:S(2)}) collective-permute-start(f32[8,8]{1,0:T(8,128)S(1)} %add.343), channel_id=1, source_target_pairs={{0,8},{1,9},{2,10},{3,11},{4,12},{5,13},{6,14},{7,15},{8,0},{9,1},... | collective-permute-start | bytes 776 | tf_op jit(solution)/shard_map/ppermute | solution.py:47
  183.4 1.6 collective-permute-done.27
  187.1 1.9 collective-permute-start.37
  189.2 9.6 %collective-permute-start.39 = (f32[32,2,128]{2,0,1:T(8,128)S(1)}, f32[32,2,128]{2,0,1:T(8,128)S(1)}, u32[]{:S(2)}, u32[]{:S(2)}) collective-permute-start(f32[32,2,128]{2,0,1:T(8,128)S(1)} %get-tuple-element.128), channel_id=1, source_target_pairs={{16,32},{32,16},{17,33},{33,17},{18,34},{34,18},{19,35},{35,19},{2... | collective-permute-start | bytes 98312 | tf_op jit(solution)/shard_map/ppermute | solution.py:112
  198.9 3.6 %collective-permute-done.32 = f32[8,8]{1,0:T(8,128)S(1)} collective-permute-done((f32[8,8]{1,0:T(8,128)S(1)}, f32[8,8]{1,0:T(8,128)S(1)}, u32[]{:S(2)}, u32[]{:S(2)}) %collective-permute-start.32) | collective-permute-done | bytes 288 | tf_op jit(solution)/shard_map/ppermute | solution.py:47
  202.5 3.2 %collective-permute-start.33 = (f32[8,8]{1,0:T(8,128)S(1)}, f32[8,8]{1,0:T(8,128)S(1)}, u32[]{:S(2)}, u32[]{:S(2)}) collective-permute-start(f32[8,8]{1,0:T(8,128)S(1)} %add.345), channel_id=1, source_target_pairs={{0,32},{1,33},{2,34},{3,35},{4,36},{5,37},{6,38},{7,39},{8,40},{9,... | collective-permute-start | bytes 776 | tf_op jit(solution)/shard_map/ppermute | solution.py:47
  205.7 1.6 collective-permute-done.33
  207.3 6.3 %collective-permute-start.34 = (f32[8,8]{1,0:T(8,128)S(1)}, f32[8,8]{1,0:T(8,128)S(1)}, u32[]{:S(2)}, u32[]{:S(2)}) collective-permute-start(f32[8,8]{1,0:T(8,128)S(1)} %add.346), channel_id=1, source_target_pairs={{0,64},{1,65},{2,66},{3,67},{4,68},{5,69},{6,70},{7,71},{8,72},{9,... | collective-permute-start | bytes 776 | tf_op jit(solution)/shard_map/ppermute | solution.py:47
  213.6 1.6 collective-permute-done.34
  215.5 4.5 %collective-permute-done.35 = f32[8,8]{1,0:T(8,128)S(1)} collective-permute-done((f32[8,8]{1,0:T(8,128)S(1)}, f32[8,8]{1,0:T(8,128)S(1)}, u32[]{:S(2)}, u32[]{:S(2)}) %collective-permute-start.35) | collective-permute-done | bytes 288 | tf_op jit(solution)/shard_map/ppermute | solution.py:47
  (171 shorter events, 17.5 us)
Async XLA Ops:
  0.0 22.5 %copy-start = (f32[16,2,512]{2,1,0:T(2,128)S(1)}, f32[16,2,512]{2,1,0:T(2,128)}, u32[]{:S(2)}) copy-start(f32[16,2,512]{2,1,0:T(2,128)} %param.40) | copy-start | bytes 196612
  5.8 13.3 %copy-start.3 = (bf16[8,512,256]{2,1,0:T(8,128)(2,1)S(1)}, bf16[8,512,256]{2,1,0:T(8,128)(2,1)}, u32[]{:S(2)}) copy-start(bf16[8,512,256]{2,1,0:T(8,128)(2,1)} %param.31) | copy-start | bytes 6291460
  5.8 13.3 %copy-start.5 = (bf16[2,256,256]{2,1,0:T(8,128)(2,1)S(1)}, bf16[2,256,256]{2,1,0:T(8,128)(2,1)}, u32[]{:S(2)}) copy-start(bf16[2,256,256]{2,1,0:T(8,128)(2,1)} %param.36) | copy-start | bytes 786436
  7.2 18.8 %collective-permute-start = (bf16[8,128,256]{2,1,0:T(8,128)(2,1)}, bf16[8,128,256]{2,1,0:T(8,128)(2,1)}, u32[]{:S(2)}, u32[]{:S(2)}) collective-permute-start(bf16[8,128,256]{2,1,0:T(8,128)(2,1)} %get-tuple-element.114), channel_id=1, source_target_pairs={{0,1},{1,0},{2,3},{3,2},{4,5},{5,4},{6,7},{7,6},{8,9},{9,8},{10,11... | collective-permute-start | bytes 1572872 | tf_op jit(solution)/shard_map/ppermute | solution.py:112
  7.2 35.5 %collective-permute-start.1 = (bf16[8,128,256]{2,1,0:T(8,128)(2,1)}, bf16[8,128,256]{2,1,0:T(8,128)(2,1)}, u32[]{:S(2)}, u32[]{:S(2)}) collective-permute-start(bf16[8,128,256]{2,1,0:T(8,128)(2,1)} %get-tuple-element.117), channel_id=1, source_target_pairs={{1,2},{2,1},{3,4},{4,3},{5,6},{6,5},{7,8},{8,7},{9,10},{10,9},{11,... | collective-permute-start | bytes 1572872 | tf_op jit(solution)/shard_map/ppermute | solution.py:112
  12.2 30.5 %collective-permute-start.2 = (bf16[8,128,256]{2,1,0:T(8,128)(2,1)}, bf16[8,128,256]{2,1,0:T(8,128)(2,1)}, u32[]{:S(2)}, u32[]{:S(2)}) collective-permute-start(bf16[8,128,256]{2,1,0:T(8,128)(2,1)} %get-tuple-element.116), channel_id=1, source_target_pairs={{0,16},{16,0},{1,17},{17,1},{2,18},{18,2},{3,19},{19,3},{4,20},{20... | collective-permute-start | bytes 1572872 | tf_op jit(solution)/shard_map/ppermute | solution.py:112
  12.3 30.4 %collective-permute-start.3 = (bf16[8,128,256]{2,1,0:T(8,128)(2,1)}, bf16[8,128,256]{2,1,0:T(8,128)(2,1)}, u32[]{:S(2)}, u32[]{:S(2)}) collective-permute-start(bf16[8,128,256]{2,1,0:T(8,128)(2,1)} %get-tuple-element.115), channel_id=1, source_target_pairs={{16,32},{32,16},{17,33},{33,17},{18,34},{34,18},{19,35},{35,19},{2... | collective-permute-start | bytes 1572872 | tf_op jit(solution)/shard_map/ppermute | solution.py:112
  54.2 13.2 %collective-permute-start.4 = (bf16[8,128,256]{1,2,0:T(8,128)(2,1)S(1)}, bf16[8,128,256]{1,2,0:T(8,128)(2,1)S(1)}, u32[]{:S(2)}, u32[]{:S(2)}) collective-permute-start(bf16[8,128,256]{1,2,0:T(8,128)(2,1)S(1)} %get-tuple-element.110), channel_id=1, source_target_pairs={{0,1},{1,0},{2,3},{3,2},{4,5},{5,4},{6,7},{7,6},{8,9},{9,8},{10,11... | collective-permute-start | bytes 1572872 | tf_op jit(solution)/shard_map/ppermute | solution.py:112
  54.3 29.3 %collective-permute-start.5 = (bf16[8,128,256]{1,2,0:T(8,128)(2,1)S(1)}, bf16[8,128,256]{1,2,0:T(8,128)(2,1)S(1)}, u32[]{:S(2)}, u32[]{:S(2)}) collective-permute-start(bf16[8,128,256]{1,2,0:T(8,128)(2,1)S(1)} %get-tuple-element.111), channel_id=1, source_target_pairs={{1,2},{2,1},{3,4},{4,3},{5,6},{6,5},{7,8},{8,7},{9,10},{10,9},{11,... | collective-permute-start | bytes 1572872 | tf_op jit(solution)/shard_map/ppermute | solution.py:112
  56.4 27.3 %collective-permute-start.6 = (bf16[8,128,256]{1,2,0:T(8,128)(2,1)S(1)}, bf16[8,128,256]{1,2,0:T(8,128)(2,1)S(1)}, u32[]{:S(2)}, u32[]{:S(2)}) collective-permute-start(bf16[8,128,256]{1,2,0:T(8,128)(2,1)S(1)} %get-tuple-element.113), channel_id=1, source_target_pairs={{0,16},{16,0},{1,17},{17,1},{2,18},{18,2},{3,19},{19,3},{4,20},{20... | collective-permute-start | bytes 1572872 | tf_op jit(solution)/shard_map/ppermute | solution.py:112
  56.5 27.2 %collective-permute-start.7 = (bf16[8,128,256]{1,2,0:T(8,128)(2,1)S(1)}, bf16[8,128,256]{1,2,0:T(8,128)(2,1)S(1)}, u32[]{:S(2)}, u32[]{:S(2)}) collective-permute-start(bf16[8,128,256]{1,2,0:T(8,128)(2,1)S(1)} %get-tuple-element.112), channel_id=1, source_target_pairs={{16,32},{32,16},{17,33},{33,17},{18,34},{34,18},{19,35},{35,19},{2... | collective-permute-start | bytes 1572872 | tf_op jit(solution)/shard_map/ppermute | solution.py:112
  86.3 15.3 %copy-start.9 = (f32[512]{0:T(512)S(1)}, f32[512]{0:T(512)}, u32[]{:S(2)}) copy-start(f32[512]{0:T(512)} %param.45) | copy-start | bytes 6148
  86.3 15.4 %copy-start.10 = (f32[512]{0:T(512)S(1)}, f32[512]{0:T(512)}, u32[]{:S(2)}) copy-start(f32[512]{0:T(512)} %param.42) | copy-start | bytes 6148
  90.8 12.0 %copy-start.7 = (f32[512]{0:T(512)S(1)}, f32[512]{0:T(512)}, u32[]{:S(2)}) copy-start(f32[512]{0:T(512)} %param.44) | copy-start | bytes 6148
  90.8 12.0 %copy-start.8 = (f32[512]{0:T(512)S(1)}, f32[512]{0:T(512)}, u32[]{:S(2)}) copy-start(f32[512]{0:T(512)} %param.43) | copy-start | bytes 6148
  90.8 12.2 %copy-start.1 = (bf16[1024,1024]{1,0:T(8,128)(2,1)S(1)}, bf16[1024,1024]{1,0:T(8,128)(2,1)}, u32[]{:S(2)}) copy-start(bf16[1024,1024]{1,0:T(8,128)(2,1)} %param.46) | copy-start | bytes 6291460
  91.5 10.2 %collective-permute-start.8 = (f32[8,2,128]{2,0,1:T(8,128)S(1)}, f32[8,2,128]{2,0,1:T(8,128)S(1)}, u32[]{:S(2)}, u32[]{:S(2)}) collective-permute-start(f32[8,2,128]{2,0,1:T(8,128)S(1)} %get-tuple-element.160), channel_id=1, source_target_pairs={{0,1},{1,0},{2,3},{3,2},{4,5},{5,4},{6,7},{7,6},{8,9},{9,8},{10,11... | collective-permute-start | bytes 24584 | tf_op jit(solution)/shard_map/ppermute | solution.py:112
  91.6 10.1 %collective-permute-start.9 = (f32[8,2,128]{2,0,1:T(8,128)S(1)}, f32[8,2,128]{2,0,1:T(8,128)S(1)}, u32[]{:S(2)}, u32[]{:S(2)}) collective-permute-start(f32[8,2,128]{2,0,1:T(8,128)S(1)} %get-tuple-element.161), channel_id=1, source_target_pairs={{1,2},{2,1},{3,4},{4,3},{5,6},{6,5},{7,8},{8,7},{9,10},{10,9},{11,... | collective-permute-start | bytes 24584 | tf_op jit(solution)/shard_map/ppermute | solution.py:112
  93.5 8.2 %collective-permute-start.10 = (f32[8,2,128]{2,0,1:T(8,128)S(1)}, f32[8,2,128]{2,0,1:T(8,128)S(1)}, u32[]{:S(2)}, u32[]{:S(2)}) collective-permute-start(f32[8,2,128]{2,0,1:T(8,128)S(1)} %get-tuple-element.163), channel_id=1, source_target_pairs={{0,16},{16,0},{1,17},{17,1},{2,18},{18,2},{3,19},{19,3},{4,20},{20... | collective-permute-start | bytes 24584 | tf_op jit(solution)/shard_map/ppermute | solution.py:112
  93.6 8.7 %collective-permute-start.11 = (f32[8,2,128]{2,0,1:T(8,128)S(1)}, f32[8,2,128]{2,0,1:T(8,128)S(1)}, u32[]{:S(2)}, u32[]{:S(2)}) collective-permute-start(f32[8,2,128]{2,0,1:T(8,128)S(1)} %get-tuple-element.162), channel_id=1, source_target_pairs={{16,32},{32,16},{17,33},{33,17},{18,34},{34,18},{19,35},{35,19},{2... | collective-permute-start | bytes 24584 | tf_op jit(solution)/shard_map/ppermute | solution.py:112
  104.1 12.5 %collective-permute-start.12 = (f32[8,2,128]{2,0,1:T(8,128)S(1)}, f32[8,2,128]{2,0,1:T(8,128)S(1)}, u32[]{:S(2)}, u32[]{:S(2)}) collective-permute-start(f32[8,2,128]{2,0,1:T(8,128)S(1)} %get-tuple-element.156), channel_id=1, source_target_pairs={{0,1},{1,0},{2,3},{3,2},{4,5},{5,4},{6,7},{7,6},{8,9},{9,8},{10,11... | collective-permute-start | bytes 24584 | tf_op jit(solution)/shard_map/ppermute | solution.py:112
  104.2 12.5 %collective-permute-start.13 = (f32[8,2,128]{2,0,1:T(8,128)S(1)}, f32[8,2,128]{2,0,1:T(8,128)S(1)}, u32[]{:S(2)}, u32[]{:S(2)}) collective-permute-start(f32[8,2,128]{2,0,1:T(8,128)S(1)} %get-tuple-element.157), channel_id=1, source_target_pairs={{1,2},{2,1},{3,4},{4,3},{5,6},{6,5},{7,8},{8,7},{9,10},{10,9},{11,... | collective-permute-start | bytes 24584 | tf_op jit(solution)/shard_map/ppermute | solution.py:112
  106.1 10.5 %collective-permute-start.14 = (f32[8,2,128]{2,0,1:T(8,128)S(1)}, f32[8,2,128]{2,0,1:T(8,128)S(1)}, u32[]{:S(2)}, u32[]{:S(2)}) collective-permute-start(f32[8,2,128]{2,0,1:T(8,128)S(1)} %get-tuple-element.159), channel_id=1, source_target_pairs={{0,16},{16,0},{1,17},{17,1},{2,18},{18,2},{3,19},{19,3},{4,20},{20... | collective-permute-start | bytes 24584 | tf_op jit(solution)/shard_map/ppermute | solution.py:112
  106.2 12.0 %collective-permute-start.15 = (f32[8,2,128]{2,0,1:T(8,128)S(1)}, f32[8,2,128]{2,0,1:T(8,128)S(1)}, u32[]{:S(2)}, u32[]{:S(2)}) collective-permute-start(f32[8,2,128]{2,0,1:T(8,128)S(1)} %get-tuple-element.158), channel_id=1, source_target_pairs={{16,32},{32,16},{17,33},{33,17},{18,34},{34,18},{19,35},{35,19},{2... | collective-permute-start | bytes 24584 | tf_op jit(solution)/shard_map/ppermute | solution.py:112
  119.9 12.4 %collective-permute-start.16 = (f32[8,2,128]{2,0,1:T(8,128)S(1)}, f32[8,2,128]{2,0,1:T(8,128)S(1)}, u32[]{:S(2)}, u32[]{:S(2)}) collective-permute-start(f32[8,2,128]{2,0,1:T(8,128)S(1)} %get-tuple-element.150), channel_id=1, source_target_pairs={{0,1},{1,0},{2,3},{3,2},{4,5},{5,4},{6,7},{7,6},{8,9},{9,8},{10,11... | collective-permute-start | bytes 24584 | tf_op jit(solution)/shard_map/ppermute | solution.py:112
  120.0 12.4 %collective-permute-start.17 = (f32[8,2,128]{2,0,1:T(8,128)S(1)}, f32[8,2,128]{2,0,1:T(8,128)S(1)}, u32[]{:S(2)}, u32[]{:S(2)}) collective-permute-start(f32[8,2,128]{2,0,1:T(8,128)S(1)} %get-tuple-element.151), channel_id=1, source_target_pairs={{1,2},{2,1},{3,4},{4,3},{5,6},{6,5},{7,8},{8,7},{9,10},{10,9},{11,... | collective-permute-start | bytes 24584 | tf_op jit(solution)/shard_map/ppermute | solution.py:112
  122.0 10.5 %collective-permute-start.18 = (f32[8,2,128]{2,0,1:T(8,128)S(1)}, f32[8,2,128]{2,0,1:T(8,128)S(1)}, u32[]{:S(2)}, u32[]{:S(2)}) collective-permute-start(f32[8,2,128]{2,0,1:T(8,128)S(1)} %get-tuple-element.153), channel_id=1, source_target_pairs={{0,16},{16,0},{1,17},{17,1},{2,18},{18,2},{3,19},{19,3},{4,20},{20... | collective-permute-start | bytes 24584 | tf_op jit(solution)/shard_map/ppermute | solution.py:112
  122.1 11.7 %collective-permute-start.19 = (f32[8,2,128]{2,0,1:T(8,128)S(1)}, f32[8,2,128]{2,0,1:T(8,128)S(1)}, u32[]{:S(2)}, u32[]{:S(2)}) collective-permute-start(f32[8,2,128]{2,0,1:T(8,128)S(1)} %get-tuple-element.152), channel_id=1, source_target_pairs={{16,32},{32,16},{17,33},{33,17},{18,34},{34,18},{19,35},{35,19},{2... | collective-permute-start | bytes 24584 | tf_op jit(solution)/shard_map/ppermute | solution.py:112
  136.5 19.0 %collective-permute-start.20 = (f32[8,2,128]{2,0,1:T(8,128)S(1)}, f32[8,2,128]{2,0,1:T(8,128)S(1)}, u32[]{:S(2)}, u32[]{:S(2)}) collective-permute-start(f32[8,2,128]{2,0,1:T(8,128)S(1)} %get-tuple-element.143), channel_id=1, source_target_pairs={{0,1},{1,0},{2,3},{3,2},{4,5},{5,4},{6,7},{7,6},{8,9},{9,8},{10,11... | collective-permute-start | bytes 24584 | tf_op jit(solution)/shard_map/ppermute | solution.py:112
  137.4 18.0 %collective-permute-start.21 = (f32[8,2,128]{2,0,1:T(8,128)S(1)}, f32[8,2,128]{2,0,1:T(8,128)S(1)}, u32[]{:S(2)}, u32[]{:S(2)}) collective-permute-start(f32[8,2,128]{2,0,1:T(8,128)S(1)} %get-tuple-element.144), channel_id=1, source_target_pairs={{1,2},{2,1},{3,4},{4,3},{5,6},{6,5},{7,8},{8,7},{9,10},{10,9},{11,... | collective-permute-start | bytes 24584 | tf_op jit(solution)/shard_map/ppermute | solution.py:112
  142.2 13.3 %collective-permute-start.22 = (f32[8,2,128]{2,0,1:T(8,128)S(1)}, f32[8,2,128]{2,0,1:T(8,128)S(1)}, u32[]{:S(2)}, u32[]{:S(2)}) collective-permute-start(f32[8,2,128]{2,0,1:T(8,128)S(1)} %get-tuple-element.146), channel_id=1, source_target_pairs={{0,16},{16,0},{1,17},{17,1},{2,18},{18,2},{3,19},{19,3},{4,20},{20... | collective-permute-start | bytes 24584 | tf_op jit(solution)/shard_map/ppermute | solution.py:112
  142.3 14.7 %collective-permute-start.23 = (f32[8,2,128]{2,0,1:T(8,128)S(1)}, f32[8,2,128]{2,0,1:T(8,128)S(1)}, u32[]{:S(2)}, u32[]{:S(2)}) collective-permute-start(f32[8,2,128]{2,0,1:T(8,128)S(1)} %get-tuple-element.145), channel_id=1, source_target_pairs={{16,32},{32,16},{17,33},{33,17},{18,34},{34,18},{19,35},{35,19},{2... | collective-permute-start | bytes 24584 | tf_op jit(solution)/shard_map/ppermute | solution.py:112
  159.3 25.7 %collective-permute-start.28 = (f32[32,2,128]{2,0,1:T(8,128)S(1)}, f32[32,2,128]{2,0,1:T(8,128)S(1)}, u32[]{:S(2)}, u32[]{:S(2)}) collective-permute-start(f32[32,2,128]{2,0,1:T(8,128)S(1)} %get-tuple-element.130), channel_id=1, source_target_pairs={{0,1},{1,0},{2,3},{3,2},{4,5},{5,4},{6,7},{7,6},{8,9},{9,8},{10,11... | collective-permute-start | bytes 98312 | tf_op jit(solution)/shard_map/ppermute | solution.py:112
  159.4 25.6 %collective-permute-start.29 = (f32[32,2,128]{2,0,1:T(8,128)S(1)}, f32[32,2,128]{2,0,1:T(8,128)S(1)}, u32[]{:S(2)}, u32[]{:S(2)}) collective-permute-start(f32[32,2,128]{2,0,1:T(8,128)S(1)} %get-tuple-element.131), channel_id=1, source_target_pairs={{1,2},{2,1},{3,4},{4,3},{5,6},{6,5},{7,8},{8,7},{9,10},{10,9},{11,... | collective-permute-start | bytes 98312 | tf_op jit(solution)/shard_map/ppermute | solution.py:112
  161.3 23.7 %collective-permute-start.30 = (f32[32,2,128]{2,0,1:T(8,128)S(1)}, f32[32,2,128]{2,0,1:T(8,128)S(1)}, u32[]{:S(2)}, u32[]{:S(2)}) collective-permute-start(f32[32,2,128]{2,0,1:T(8,128)S(1)} %get-tuple-element.133), channel_id=1, source_target_pairs={{0,16},{16,0},{1,17},{17,1},{2,18},{18,2},{3,19},{19,3},{4,20},{20... | collective-permute-start | bytes 98312 | tf_op jit(solution)/shard_map/ppermute | solution.py:112
  161.4 23.6 %collective-permute-start.31 = (f32[32,2,128]{2,0,1:T(8,128)S(1)}, f32[32,2,128]{2,0,1:T(8,128)S(1)}, u32[]{:S(2)}, u32[]{:S(2)}) collective-permute-start(f32[32,2,128]{2,0,1:T(8,128)S(1)} %get-tuple-element.132), channel_id=1, source_target_pairs={{16,32},{32,16},{17,33},{33,17},{18,34},{34,18},{19,35},{35,19},{2... | collective-permute-start | bytes 98312 | tf_op jit(solution)/shard_map/ppermute | solution.py:112
  170.9 1.3 collective-permute-start.24
  172.2 3.6 %collective-permute-start.25 = (f32[8,8]{1,0:T(8,128)S(1)}, f32[8,8]{1,0:T(8,128)S(1)}, u32[]{:S(2)}, u32[]{:S(2)}) collective-permute-start(f32[8,8]{1,0:T(8,128)S(1)} %add.341), channel_id=1, source_target_pairs={{0,2},{1,3},{2,0},{3,1},{4,6},{5,7},{6,4},{7,5},{8,10},{9,11},{10,... | collective-permute-start | bytes 776 | tf_op jit(solution)/shard_map/ppermute | solution.py:47
  175.8 4.8 %collective-permute-start.26 = (f32[8,8]{1,0:T(8,128)S(1)}, f32[8,8]{1,0:T(8,128)S(1)}, u32[]{:S(2)}, u32[]{:S(2)}) collective-permute-start(f32[8,8]{1,0:T(8,128)S(1)} %add.342), channel_id=1, source_target_pairs={{0,6},{1,7},{2,4},{3,5},{4,2},{5,3},{6,0},{7,1},{8,14},{9,15},{10,... | collective-permute-start | bytes 776 | tf_op jit(solution)/shard_map/ppermute | solution.py:47
  180.6 4.4 %collective-permute-start.27 = (f32[8,8]{1,0:T(8,128)S(1)}, f32[8,8]{1,0:T(8,128)S(1)}, u32[]{:S(2)}, u32[]{:S(2)}) collective-permute-start(f32[8,8]{1,0:T(8,128)S(1)} %add.343), channel_id=1, source_target_pairs={{0,8},{1,9},{2,10},{3,11},{4,12},{5,13},{6,14},{7,15},{8,0},{9,1},... | collective-permute-start | bytes 776 | tf_op jit(solution)/shard_map/ppermute | solution.py:47
  187.0 33.0 %collective-permute-start.36 = (f32[32,2,128]{2,0,1:T(8,128)S(1)}, f32[32,2,128]{2,0,1:T(8,128)S(1)}, u32[]{:S(2)}, u32[]{:S(2)}) collective-permute-start(f32[32,2,128]{2,0,1:T(8,128)S(1)} %get-tuple-element.126), channel_id=1, source_target_pairs={{0,1},{1,0},{2,3},{3,2},{4,5},{5,4},{6,7},{7,6},{8,9},{9,8},{10,11... | collective-permute-start | bytes 98312 | tf_op jit(solution)/shard_map/ppermute | solution.py:112
  187.1 32.9 %collective-permute-start.37 = (f32[32,2,128]{2,0,1:T(8,128)S(1)}, f32[32,2,128]{2,0,1:T(8,128)S(1)}, u32[]{:S(2)}, u32[]{:S(2)}) collective-permute-start(f32[32,2,128]{2,0,1:T(8,128)S(1)} %get-tuple-element.127), channel_id=1, source_target_pairs={{1,2},{2,1},{3,4},{4,3},{5,6},{6,5},{7,8},{8,7},{9,10},{10,9},{11,... | collective-permute-start | bytes 98312 | tf_op jit(solution)/shard_map/ppermute | solution.py:112
  189.1 31.0 %collective-permute-start.38 = (f32[32,2,128]{2,0,1:T(8,128)S(1)}, f32[32,2,128]{2,0,1:T(8,128)S(1)}, u32[]{:S(2)}, u32[]{:S(2)}) collective-permute-start(f32[32,2,128]{2,0,1:T(8,128)S(1)} %get-tuple-element.129), channel_id=1, source_target_pairs={{0,16},{16,0},{1,17},{17,1},{2,18},{18,2},{3,19},{19,3},{4,20},{20... | collective-permute-start | bytes 98312 | tf_op jit(solution)/shard_map/ppermute | solution.py:112
  189.2 30.9 %collective-permute-start.39 = (f32[32,2,128]{2,0,1:T(8,128)S(1)}, f32[32,2,128]{2,0,1:T(8,128)S(1)}, u32[]{:S(2)}, u32[]{:S(2)}) collective-permute-start(f32[32,2,128]{2,0,1:T(8,128)S(1)} %get-tuple-element.128), channel_id=1, source_target_pairs={{16,32},{32,16},{17,33},{33,17},{18,34},{34,18},{19,35},{35,19},{2... | collective-permute-start | bytes 98312 | tf_op jit(solution)/shard_map/ppermute | solution.py:112
  198.8 3.7 %collective-permute-start.32 = (f32[8,8]{1,0:T(8,128)S(1)}, f32[8,8]{1,0:T(8,128)S(1)}, u32[]{:S(2)}, u32[]{:S(2)}) collective-permute-start(f32[8,8]{1,0:T(8,128)S(1)} %add.344), channel_id=1, source_target_pairs={{0,24},{1,25},{2,26},{3,27},{4,28},{5,29},{6,30},{7,31},{8,16},{9,... | collective-permute-start | bytes 776 | tf_op jit(solution)/shard_map/ppermute | solution.py:47
  202.5 4.8 %collective-permute-start.33 = (f32[8,8]{1,0:T(8,128)S(1)}, f32[8,8]{1,0:T(8,128)S(1)}, u32[]{:S(2)}, u32[]{:S(2)}) collective-permute-start(f32[8,8]{1,0:T(8,128)S(1)} %add.345), channel_id=1, source_target_pairs={{0,32},{1,33},{2,34},{3,35},{4,36},{5,37},{6,38},{7,39},{8,40},{9,... | collective-permute-start | bytes 776 | tf_op jit(solution)/shard_map/ppermute | solution.py:47
  207.3 7.8 %collective-permute-start.34 = (f32[8,8]{1,0:T(8,128)S(1)}, f32[8,8]{1,0:T(8,128)S(1)}, u32[]{:S(2)}, u32[]{:S(2)}) collective-permute-start(f32[8,8]{1,0:T(8,128)S(1)} %add.346), channel_id=1, source_target_pairs={{0,64},{1,65},{2,66},{3,67},{4,68},{5,69},{6,70},{7,71},{8,72},{9,... | collective-permute-start | bytes 776 | tf_op jit(solution)/shard_map/ppermute | solution.py:47
  215.2 4.8 %collective-permute-start.35 = (f32[8,8]{1,0:T(8,128)S(1)}, f32[8,8]{1,0:T(8,128)S(1)}, u32[]{:S(2)}, u32[]{:S(2)}) collective-permute-start(f32[8,8]{1,0:T(8,128)S(1)} %add.347), channel_id=1, source_target_pairs={{0,224},{1,225},{2,226},{3,227},{4,228},{5,229},{6,230},{7,231},{8... | collective-permute-start | bytes 776 | tf_op jit(solution)/shard_map/ppermute | solution.py:47
  (7 other events, 27.9 us)

commit v7 on v6

--- a/solution.py
+++ b/solution.py
@@ -145,13 +145,25 @@
     injection = jnp.einsum("sp,pcb->scb", choose, load_table, precision=highest)
     bus_total = buses * lax.axis_size("region")
 
-    def halo(values):
+    def halo(values, payload=None):
         shape = values.shape
         flat = values.reshape((-1,) + shape[-2:])
         tiles = jnp.einsum("ktb,ncb->knct", pick_full, flat, precision=highest)
+        rows = flat.shape[0]
+        if payload is not None:
+            cell = tiles.shape[-2] * tiles.shape[-1]
+            packed = jnp.pad(payload.reshape(-1), (0, cell - payload.size))
+            packed = packed.reshape((1, 1) + tiles.shape[-2:])
+            packed = jnp.broadcast_to(packed, (tiles.shape[0], 1) + tiles.shape[-2:])
+            tiles = jnp.concatenate([tiles, packed], axis=1)
         incoming = exchange(tiles)
-        spread = jnp.einsum("knct,ktb->ncb", incoming, place_full, precision=highest)
-        return spread.reshape(shape)
+        spread = jnp.einsum(
+            "knct,ktb->ncb", incoming[:, :rows], place_full, precision=highest
+        ).reshape(shape)
+        if payload is None:
+            return spread
+        carried = incoming[:, rows].reshape(incoming.shape[0], -1)[:, : payload.size]
+        return spread, carried.reshape((incoming.shape[0],) + payload.shape)
 
     def inside_sum(values):
         return jnp.einsum("ij,...cj->...ci", mask_full, values, precision=highest)
@@ -159,16 +171,21 @@
     def damp(squares):
         return jnp.minimum(1.0, trust_radius / jnp.sqrt(squares / (2 * bus_total) + 1e-06))
 
-    def sweeps(residuals, partial, chunks):
+    def sweeps(residuals, partial, plan):
         count = residuals.shape[0]
         update = None
         for sweep_number in range(SWEEPS):
             forcing = -residuals
             if sweep_number > 0:
-                arrived = halo(update)
-                if chunks:
-                    partial = sum_rounds(partial, "region", chunks[sweep_number - 1])
-                    partial, arrived = lax.optimization_barrier((partial, arrived))
+                carry, masks = plan[sweep_number - 1] if plan else (None, [])
+                if carry is None:
+                    arrived = halo(update)
+                    if masks:
+                        partial = sum_rounds(partial, "region", masks)
+                        partial, arrived = lax.optimization_barrier((partial, arrived))
+                else:
+                    arrived, carried = halo(update, partial)
+                    partial = sum_rounds(partial + carried[carry], "region", masks)
                 forcing = forcing + rotate(conductance, susceptance, arrived, -2)
             forcing = forcing.reshape(count * scenarios, 2 * buses).astype(jnp.bfloat16)
             update = jnp.dot(forcing, region_inverse, preferred_element_type=jnp.float32)
@@ -208,8 +225,13 @@
             product = jnp.sum(coeffs[i] * coeffs[j], axis=(1, 2))
             powers[i + j] = powers[i + j] + (product if i == j else 2.0 * product)
     partial = jnp.concatenate([partial, jnp.stack(powers)])
-    chunks = None if bits is None else split_even(bits, SWEEPS - 1)
-    second, partial = sweeps(coeffs, partial, chunks)
+    if bits == [1, 2, 6, 8, 24, 32, 64, 224] and SWEEPS == 3:
+        plan = [(0, [2, 6, 8]), (2, [32, 64, 224])]
+    elif bits is None:
+        plan = None
+    else:
+        plan = [(None, masks) for masks in split_even(bits, SWEEPS - 1)]
+    second, partial = sweeps(coeffs, partial, plan)
     if bits is None:
         partial = lax.psum(partial, "region")
     first_damping = damp(partial[0])

time: 226 us -> 224 us (level)
  waiting for transfers between devices: 57.5 us -> 55.2 us
    ppermute x8 -> x6, waiting for transfers between devices: 19.5 us -> 13.3 us  [sum_rounds(): lax.ppermute(value, axis, [(i, i ^ bit) for i in range(count)])]
    ppermute x32, waiting for transfers between devices: 38.1 us -> 41.9 us  [exchange(): lax.ppermute(tiles[j], 'region', routes[j])]
    ppermute x8 -> x6, starting transfers between devices: 15.7 us -> 15.7 us  [sum_rounds(): lax.ppermute(value, axis, [(i, i ^ bit) for i in range(count)])]
  transfers between devices with their start and end apart: 40 -> 38, of which waited for: 14 -> 14; matrix products, arithmetic and copies ran while one was open for 5% -> 6% of each run, Pallas kernels for 0% -> 0%
where the time goes in v7:
time: 224 us; the launch traced here: 220 us
  starting transfers between devices  113 us (50%)
  waiting for transfers between devices  55.2 us (25%)
  matrix products  43.3 us (19%)
  local copies, waits for them, and re-layouts  5 us (2%)
  other arithmetic  3.14 us (1%)
    ppermute x32, starting transfers between devices, exchange(): lax.ppermute(tiles[j], 'region', routes[j])  97.1 us
    ppermute x32, waiting for transfers between devices, exchange(): lax.ppermute(tiles[j], 'region', routes[j])  41.9 us
    ppermute x6, starting transfers between devices, sum_rounds(): lax.ppermute(value, axis, [(i, i ^ bit) for i in range(count)])  15.7 us
    ppermute x6, waiting for transfers between devices, sum_rounds(): lax.ppermute(value, axis, [(i, i ^ bit) for i in range(count)])  13.3 us
    dot_general x1, matrix products, local(): jnp.einsum('sbh,hk->sbk', gathered, neigh_weight[number], preferred_eleme...  8.29 us
    dot_general x2, matrix products, local(): jnp.einsum('ktb,sbh->ksth', pick_half, hidden, preferred_element_type=jnp...  5.96 us
    dot_general x2, matrix products, local(): jnp.einsum('sbh,hk->sbk', hidden, self_weight[number], preferred_element_...  5.34 us
    dot_general x2, matrix products, local(): jnp.einsum('ij,sjh->sih', mask_half, hidden, preferred_element_type=jnp.f...  4.53 us
  transfers between devices with their start and end apart: 38, of which 14 were waited for; matrix products, arithmetic and copies ran while one was open for 6% of the time, Pallas kernels for 0%

profile of v7, /device:TPU:4, one launch (start us, length us, event | category | flops | bytes accessed | tf_op | source)
XLA Modules:
  0.0 220.4 jit_solution(14313877435781397404)
XLA Ops:
  1.6 1.2 gather_fusion.1
  2.9 2.9 %convert_bitcast_fusion.1 = bf16[4,8,128,256]{3,2,1,0:T(8,128)(2,1)S(1)} fusion(bf16[8,512,256]{2,1,0:T(8,128)(2,1)} %param.31, s32[4,128]{1,0:T(4,128)S(1)} %broadcast_select_fusion.1, pred[4,128]{1,0:T(4,128)(4,1)S(1)} %broadcast_select_fusion.2), kind=kOutput, calls=%fused_computation.42 | convolution fusion | flops 1075314688 | bytes 4196864 | tf_op jit(solution)/shard_map/ktb,sbh->ksth/dot_general | solution.py:117
  5.8 1.4 slice_bitcast_fusion.7
  7.2 5.0 %collective-permute-start.1 = (bf16[8,128,256]{2,1,0:T(8,128)(2,1)}, bf16[8,128,256]{2,1,0:T(8,128)(2,1)}, u32[]{:S(2)}, u32[]{:S(2)}) collective-permute-start(bf16[8,128,256]{2,1,0:T(8,128)(2,1)} %get-tuple-element.109), channel_id=1, source_target_pairs={{1,2},{2,1},{3,4},{4,3},{5,6},{6,5},{7,8},{8,7},{9,10},{10,9},{11,... | collective-permute-start | bytes 1572872 | tf_op jit(solution)/shard_map/ppermute | solution.py:112
  12.3 6.8 %collective-permute-start.3 = (bf16[8,128,256]{2,1,0:T(8,128)(2,1)}, bf16[8,128,256]{2,1,0:T(8,128)(2,1)}, u32[]{:S(2)}, u32[]{:S(2)}) collective-permute-start(bf16[8,128,256]{2,1,0:T(8,128)(2,1)} %get-tuple-element.107), channel_id=1, source_target_pairs={{16,32},{32,16},{17,33},{33,17},{18,34},{34,18},{19,35},{35,19},{2... | collective-permute-start | bytes 1572872 | tf_op jit(solution)/shard_map/ppermute | solution.py:112
  19.2 2.7 %fusion.116 = f32[8,512,256]{2,1,0:T(8,128)} fusion(bf16[8,512,256]{2,1,0:T(8,128)(2,1)S(1)} %copy-done.3, bf16[2,256,256]{2,1,0:T(8,128)(2,1)S(1)} %copy-done.5), kind=kOutput, calls=%fused_computation.133 | convolution fusion | flops 536870912 | bytes 6422528 | tf_op jit(solution)/shard_map/sbh,hk->sbk/dot_general | solution.py:122
  22.7 3.3 %fusion.90 = f32[8,256,512]{1,2,0:T(8,128)} fusion(bf16[8,512,256]{2,1,0:T(8,128)(2,1)S(1)} %copy-done.3, s32[512,512]{1,0:T(8,128)S(1)} %copy-done.2), kind=kOutput, calls=%fused_computation.88 | convolution fusion | flops 1074003968 | bytes 7340032 | tf_op jit(solution)/shard_map/ij,sjh->sih/dot_general | solution.py:121
  26.0 16.7 %collective-permute-done.1 = bf16[8,128,256]{2,1,0:T(8,128)(2,1)} collective-permute-done((bf16[8,128,256]{2,1,0:T(8,128)(2,1)}, bf16[8,128,256]{2,1,0:T(8,128)(2,1)}, u32[]{:S(2)}, u32[]{:S(2)}) %collective-permute-start.1) | collective-permute-done | bytes 524320 | tf_op jit(solution)/shard_map/ppermute | solution.py:112
  42.7 8.3 %add_convert_fusion.1 = bf16[8,512,256]{2,1,0:T(8,128)(2,1)} fusion(f32[8,512,256]{2,1,0:T(8,128)} %fusion.116, bf16[8,512,256]{2,1,0:T(8,128)(2,1)S(1)} %copy-done.3, f32[256]{0:T(256)S(1)} %bitcast.599, f32[8,256,512]{1,2,0:T(8,128)} %fusion.90, bf16[1,8,128,256]{3,2,1,0:T(8,128)(2,1)} %bitcast.23, bf16[1,8,128,256]{3,2,1,0:T(8,128)(2,1)} %bitcast.21, ...), kind=kOutput, calls=%fused_computation.10 | convolution fusion | flops 1626603520 | bytes 14814208 | tf_op jit(solution)/shard_map/sbh,hk->sbk/dot_general | solution.py:131
  51.0 3.1 %convert_bitcast_fusion = bf16[4,8,128,256]{2,3,0,1:T(8,128)(2,1)S(1)} fusion(bf16[8,512,256]{2,1,0:T(8,128)(2,1)} %add_convert_fusion.1, s32[4,128]{1,0:T(4,128)S(1)} %broadcast_select_fusion.1, pred[4,128]{1,0:T(4,128)(4,1)S(1)} %broadcast_select_fusion.2), kind=kOutput, calls=%fused_computation.41 | convolution fusion | flops 1075314688 | bytes 4196864 | tf_op jit(solution)/shard_map/ktb,sbh->ksth/dot_general | solution.py:117
  54.4 2.1 collective-permute-start.5
  56.5 6.9 %collective-permute-start.7 = (bf16[8,128,256]{1,2,0:T(8,128)(2,1)S(1)}, bf16[8,128,256]{1,2,0:T(8,128)(2,1)S(1)}, u32[]{:S(2)}, u32[]{:S(2)}) collective-permute-start(bf16[8,128,256]{1,2,0:T(8,128)(2,1)S(1)} %get-tuple-element.104), channel_id=1, source_target_pairs={{16,32},{32,16},{17,33},{33,17},{18,34},{34,18},{19,35},{35,19},{2... | collective-permute-start | bytes 1572872 | tf_op jit(solution)/shard_map/ppermute | solution.py:112
  63.5 2.7 %fusion.113 = f32[8,512,256]{2,1,0:T(8,128)} fusion(bf16[8,512,256]{2,1,0:T(8,128)(2,1)S(1)} %copy-done.4, bf16[2,256,256]{2,1,0:T(8,128)(2,1)S(1)} %copy-done.5), kind=kOutput, calls=%fused_computation.130 | convolution fusion | flops 536870912 | bytes 6422528 | tf_op jit(solution)/shard_map/sbh,hk->sbk/dot_general | solution.py:122
  66.2 1.3 fusion.92
  67.4 16.3 %collective-permute-done.5 = bf16[8,128,256]{1,2,0:T(8,128)(2,1)S(1)} collective-permute-done((bf16[8,128,256]{1,2,0:T(8,128)(2,1)S(1)}, bf16[8,128,256]{1,2,0:T(8,128)(2,1)S(1)}, u32[]{:S(2)}, u32[]{:S(2)}) %collective-permute-start.5) | collective-permute-done | bytes 524320 | tf_op jit(solution)/shard_map/ppermute | solution.py:112
  83.7 2.7 %fusion.1 = bf16[8,256,512]{1,2,0:T(8,128)(2,1)} fusion(f32[8,256,512]{1,2,0:T(8,128)S(1)} %fusion.92, bf16[1,8,128,256]{2,3,1,0:T(8,128)(2,1)S(1)} %bitcast.603, bf16[1,8,128,256]{2,3,1,0:T(8,128)(2,1)S(1)} %bitcast.602, bf16[1,8,128,256]{2,3,1,0:T(8,128)(2,1)S(1)} %bitcast.601, bf16[1,8,128,256]{2,3,1,0:T(8,128)(2,1)S(1)} %bitcast.600, ...), kind=kOutput, calls=%fused_computation.5 | convolution fusion | flops 1080295424 | bytes 8390656 | tf_op jit(solution)/shard_map/ktb,ksth->sbh/dot_general | solution.py:125
  86.4 4.5 %fusion.55 = f32[8,512,2]{1,2,0:T(2,128)S(1)} fusion(f32[8,512,256]{2,1,0:T(8,128)} %fusion.113, bf16[8,512,256]{2,1,0:T(8,128)(2,1)S(1)} %copy-done.4, bf16[8,256,512]{1,2,0:T(8,128)(2,1)} %fusion.1, f32[256]{0:T(256)S(1)} %bitcast.598, bf16[2,256,256]{2,1,0:T(8,128)(2,1)} %param.37, f32[2]{0:T(128)S(1)} %copy-done.14, bf16[2,256]{1,0:T(2,128)(2,1)S(1)} %copy-done.13), kind=kOutput, calls=%fused_computation.62 | convolution fusion | flops 550510592 | bytes 8554504 | tf_op jit(solution)/shard_map/sbh,ch->scb/dot_general | solution.py:139
  91.7 1.9 collective-permute-start.9
  93.7 7.0 %collective-permute-start.11 = (f32[8,2,128]{2,0,1:T(8,128)S(1)}, f32[8,2,128]{2,0,1:T(8,128)S(1)}, u32[]{:S(2)}, u32[]{:S(2)}) collective-permute-start(f32[8,2,128]{2,0,1:T(8,128)S(1)} %get-tuple-element.154), channel_id=1, source_target_pairs={{16,32},{32,16},{17,33},{33,17},{18,34},{34,18},{19,35},{35,19},{2... | collective-permute-start | bytes 24584 | tf_op jit(solution)/shard_map/ppermute | solution.py:112
  100.8 0.9 fusion.65
  104.3 1.9 collective-permute-start.13
  106.3 10.4 %collective-permute-start.15 = (f32[8,2,128]{2,0,1:T(8,128)S(1)}, f32[8,2,128]{2,0,1:T(8,128)S(1)}, u32[]{:S(2)}, u32[]{:S(2)}) collective-permute-start(f32[8,2,128]{2,0,1:T(8,128)S(1)} %get-tuple-element.150), channel_id=1, source_target_pairs={{16,32},{32,16},{17,33},{33,17},{18,34},{34,18},{19,35},{35,19},{2... | collective-permute-start | bytes 24584 | tf_op jit(solution)/shard_map/ppermute | solution.py:112
  116.7 1.6 collective-permute-done.15
  120.1 1.9 collective-permute-start.17
  122.1 10.3 %collective-permute-start.19 = (f32[8,2,128]{2,0,1:T(8,128)S(1)}, f32[8,2,128]{2,0,1:T(8,128)S(1)}, u32[]{:S(2)}, u32[]{:S(2)}) collective-permute-start(f32[8,2,128]{2,0,1:T(8,128)S(1)} %get-tuple-element.144), channel_id=1, source_target_pairs={{16,32},{32,16},{17,33},{33,17},{18,34},{34,18},{19,35},{35,19},{2... | collective-permute-start | bytes 24584 | tf_op jit(solution)/shard_map/ppermute | solution.py:112
  132.5 1.4 collective-permute-done.19
  135.5 0.9 fusion.63
  136.5 1.0 collective-permute-start.20
  137.5 4.7 %collective-permute-start.21 = (f32[8,2,128]{2,0,1:T(8,128)S(1)}, f32[8,2,128]{2,0,1:T(8,128)S(1)}, u32[]{:S(2)}, u32[]{:S(2)}) collective-permute-start(f32[8,2,128]{2,0,1:T(8,128)S(1)} %get-tuple-element.136), channel_id=1, source_target_pairs={{1,2},{2,1},{3,4},{4,3},{5,6},{6,5},{7,8},{8,7},{9,10},{10,9},{11,... | collective-permute-start | bytes 24584 | tf_op jit(solution)/shard_map/ppermute | solution.py:112
  142.4 13.1 %collective-permute-start.23 = (f32[8,2,128]{2,0,1:T(8,128)S(1)}, f32[8,2,128]{2,0,1:T(8,128)S(1)}, u32[]{:S(2)}, u32[]{:S(2)}) collective-permute-start(f32[8,2,128]{2,0,1:T(8,128)S(1)} %get-tuple-element.137), channel_id=1, source_target_pairs={{16,32},{32,16},{17,33},{33,17},{18,34},{34,18},{19,35},{35,19},{2... | collective-permute-start | bytes 24584 | tf_op jit(solution)/shard_map/ppermute | solution.py:112
  155.6 1.5 collective-permute-done.23
  158.7 0.8 convolution_bitcast_fusion.3
  159.6 1.9 collective-permute-start.25
  161.7 9.4 %collective-permute-start.27 = (f32[33,2,128]{2,0,1:T(8,128)S(1)}, f32[33,2,128]{2,0,1:T(8,128)S(1)}, u32[]{:S(2)}, u32[]{:S(2)}) collective-permute-start(f32[33,2,128]{2,0,1:T(8,128)S(1)} %get-tuple-element.120), channel_id=1, source_target_pairs={{16,32},{32,16},{17,33},{33,17},{18,34},{34,18},{19,35},{35,19},{2... | collective-permute-start | bytes 101384 | tf_op jit(solution)/shard_map/ppermute | solution.py:112
  171.1 1.9 collective-permute-done.27
  174.6 2.8 %collective-permute-done.28 = f32[8,8]{1,0:T(8,128)S(1)} collective-permute-done((f32[8,8]{1,0:T(8,128)S(1)}, f32[8,8]{1,0:T(8,128)S(1)}, u32[]{:S(2)}, u32[]{:S(2)}) %collective-permute-start.28) | collective-permute-done | bytes 288 | tf_op jit(solution)/shard_map/ppermute | solution.py:47
  177.9 4.4 %collective-permute-done.29 = f32[8,8]{1,0:T(8,128)S(1)} collective-permute-done((f32[8,8]{1,0:T(8,128)S(1)}, f32[8,8]{1,0:T(8,128)S(1)}, u32[]{:S(2)}, u32[]{:S(2)}) %collective-permute-start.29) | collective-permute-done | bytes 288 | tf_op jit(solution)/shard_map/ppermute | solution.py:47
  182.7 0.8 convolution_bitcast_fusion.1
  183.5 2.4 %collective-permute-done.30 = f32[8,8]{1,0:T(8,128)S(1)} collective-permute-done((f32[8,8]{1,0:T(8,128)S(1)}, f32[8,8]{1,0:T(8,128)S(1)}, u32[]{:S(2)}, u32[]{:S(2)}) %collective-permute-start.30) | collective-permute-done | bytes 288 | tf_op jit(solution)/shard_map/ppermute | solution.py:47
  186.0 1.9 collective-permute-start.32
  188.1 9.6 %collective-permute-start.34 = (f32[33,2,128]{2,0,1:T(8,128)S(1)}, f32[33,2,128]{2,0,1:T(8,128)S(1)}, u32[]{:S(2)}, u32[]{:S(2)}) collective-permute-start(f32[33,2,128]{2,0,1:T(8,128)S(1)} %get-tuple-element.114), channel_id=1, source_target_pairs={{16,32},{32,16},{17,33},{33,17},{18,34},{34,18},{19,35},{35,19},{2... | collective-permute-start | bytes 101384 | tf_op jit(solution)/shard_map/ppermute | solution.py:112
  197.7 1.9 collective-permute-done.34
  200.3 3.3 %collective-permute-start.35 = (f32[8,8]{1,0:T(8,128)S(1)}, f32[8,8]{1,0:T(8,128)S(1)}, u32[]{:S(2)}, u32[]{:S(2)}) collective-permute-start(f32[8,8]{1,0:T(8,128)S(1)} %add.351), channel_id=1, source_target_pairs={{0,32},{1,33},{2,34},{3,35},{4,36},{5,37},{6,38},{7,39},{8,40},{9,... | collective-permute-start | bytes 776 | tf_op jit(solution)/shard_map/ppermute | solution.py:47
  204.4 0.8 collective-permute-done.35
  205.2 7.9 %collective-permute-start.36 = (f32[8,8]{1,0:T(8,128)S(1)}, f32[8,8]{1,0:T(8,128)S(1)}, u32[]{:S(2)}, u32[]{:S(2)}) collective-permute-start(f32[8,8]{1,0:T(8,128)S(1)} %add.352), channel_id=1, source_target_pairs={{0,64},{1,65},{2,66},{3,67},{4,68},{5,69},{6,70},{7,71},{8,72},{9,... | collective-permute-start | bytes 776 | tf_op jit(solution)/shard_map/ppermute | solution.py:47
  213.1 1.5 collective-permute-done.36
  214.7 3.3 %collective-permute-start.37 = (f32[8,8]{1,0:T(8,128)S(1)}, f32[8,8]{1,0:T(8,128)S(1)}, u32[]{:S(2)}, u32[]{:S(2)}) collective-permute-start(f32[8,8]{1,0:T(8,128)S(1)} %add.353), channel_id=1, source_target_pairs={{0,224},{1,225},{2,226},{3,227},{4,228},{5,229},{6,230},{7,231},{8... | collective-permute-start | bytes 776 | tf_op jit(solution)/shard_map/ppermute | solution.py:47
  218.1 1.5 collective-permute-done.37
  (181 shorter events, 17.2 us)
Async XLA Ops:
  0.0 22.5 %copy-start = (f32[16,2,512]{2,1,0:T(2,128)S(1)}, f32[16,2,512]{2,1,0:T(2,128)}, u32[]{:S(2)}) copy-start(f32[16,2,512]{2,1,0:T(2,128)} %param.40) | copy-start | bytes 196612
  5.8 13.3 %copy-start.3 = (bf16[8,512,256]{2,1,0:T(8,128)(2,1)S(1)}, bf16[8,512,256]{2,1,0:T(8,128)(2,1)}, u32[]{:S(2)}) copy-start(bf16[8,512,256]{2,1,0:T(8,128)(2,1)} %param.31) | copy-start | bytes 6291460
  5.8 13.3 %copy-start.5 = (bf16[2,256,256]{2,1,0:T(8,128)(2,1)S(1)}, bf16[2,256,256]{2,1,0:T(8,128)(2,1)}, u32[]{:S(2)}) copy-start(bf16[2,256,256]{2,1,0:T(8,128)(2,1)} %param.36) | copy-start | bytes 786436
  7.2 18.8 %collective-permute-start = (bf16[8,128,256]{2,1,0:T(8,128)(2,1)}, bf16[8,128,256]{2,1,0:T(8,128)(2,1)}, u32[]{:S(2)}, u32[]{:S(2)}) collective-permute-start(bf16[8,128,256]{2,1,0:T(8,128)(2,1)} %get-tuple-element.106), channel_id=1, source_target_pairs={{0,1},{1,0},{2,3},{3,2},{4,5},{5,4},{6,7},{7,6},{8,9},{9,8},{10,11... | collective-permute-start | bytes 1572872 | tf_op jit(solution)/shard_map/ppermute | solution.py:112
  7.2 35.5 %collective-permute-start.1 = (bf16[8,128,256]{2,1,0:T(8,128)(2,1)}, bf16[8,128,256]{2,1,0:T(8,128)(2,1)}, u32[]{:S(2)}, u32[]{:S(2)}) collective-permute-start(bf16[8,128,256]{2,1,0:T(8,128)(2,1)} %get-tuple-element.109), channel_id=1, source_target_pairs={{1,2},{2,1},{3,4},{4,3},{5,6},{6,5},{7,8},{8,7},{9,10},{10,9},{11,... | collective-permute-start | bytes 1572872 | tf_op jit(solution)/shard_map/ppermute | solution.py:112
  12.2 30.5 %collective-permute-start.2 = (bf16[8,128,256]{2,1,0:T(8,128)(2,1)}, bf16[8,128,256]{2,1,0:T(8,128)(2,1)}, u32[]{:S(2)}, u32[]{:S(2)}) collective-permute-start(bf16[8,128,256]{2,1,0:T(8,128)(2,1)} %get-tuple-element.108), channel_id=1, source_target_pairs={{0,16},{16,0},{1,17},{17,1},{2,18},{18,2},{3,19},{19,3},{4,20},{20... | collective-permute-start | bytes 1572872 | tf_op jit(solution)/shard_map/ppermute | solution.py:112
  12.3 30.4 %collective-permute-start.3 = (bf16[8,128,256]{2,1,0:T(8,128)(2,1)}, bf16[8,128,256]{2,1,0:T(8,128)(2,1)}, u32[]{:S(2)}, u32[]{:S(2)}) collective-permute-start(bf16[8,128,256]{2,1,0:T(8,128)(2,1)} %get-tuple-element.107), channel_id=1, source_target_pairs={{16,32},{32,16},{17,33},{33,17},{18,34},{34,18},{19,35},{35,19},{2... | collective-permute-start | bytes 1572872 | tf_op jit(solution)/shard_map/ppermute | solution.py:112
  19.2 3.5 %copy-start.2 = (s32[512,512]{1,0:T(8,128)S(1)}, s32[512,512]{1,0:T(8,128)}, u32[]{:S(2)}) copy-start(s32[512,512]{1,0:T(8,128)} %param.32) | copy-start | bytes 3145732
  54.1 9.4 %copy-start.4 = (bf16[8,512,256]{2,1,0:T(8,128)(2,1)S(1)}, bf16[8,512,256]{2,1,0:T(8,128)(2,1)}, u32[]{:S(2)}) copy-start(bf16[8,512,256]{2,1,0:T(8,128)(2,1)} %add_convert_fusion.1) | copy-start | bytes 6291460
  54.3 13.2 %collective-permute-start.4 = (bf16[8,128,256]{1,2,0:T(8,128)(2,1)S(1)}, bf16[8,128,256]{1,2,0:T(8,128)(2,1)S(1)}, u32[]{:S(2)}, u32[]{:S(2)}) collective-permute-start(bf16[8,128,256]{1,2,0:T(8,128)(2,1)S(1)} %get-tuple-element.102), channel_id=1, source_target_pairs={{0,1},{1,0},{2,3},{3,2},{4,5},{5,4},{6,7},{7,6},{8,9},{9,8},{10,11... | collective-permute-start | bytes 1572872 | tf_op jit(solution)/shard_map/ppermute | solution.py:112
  54.4 29.3 %collective-permute-start.5 = (bf16[8,128,256]{1,2,0:T(8,128)(2,1)S(1)}, bf16[8,128,256]{1,2,0:T(8,128)(2,1)S(1)}, u32[]{:S(2)}, u32[]{:S(2)}) collective-permute-start(bf16[8,128,256]{1,2,0:T(8,128)(2,1)S(1)} %get-tuple-element.103), channel_id=1, source_target_pairs={{1,2},{2,1},{3,4},{4,3},{5,6},{6,5},{7,8},{8,7},{9,10},{10,9},{11,... | collective-permute-start | bytes 1572872 | tf_op jit(solution)/shard_map/ppermute | solution.py:112
  56.4 27.3 %collective-permute-start.6 = (bf16[8,128,256]{1,2,0:T(8,128)(2,1)S(1)}, bf16[8,128,256]{1,2,0:T(8,128)(2,1)S(1)}, u32[]{:S(2)}, u32[]{:S(2)}) collective-permute-start(bf16[8,128,256]{1,2,0:T(8,128)(2,1)S(1)} %get-tuple-element.105), channel_id=1, source_target_pairs={{0,16},{16,0},{1,17},{17,1},{2,18},{18,2},{3,19},{19,3},{4,20},{20... | collective-permute-start | bytes 1572872 | tf_op jit(solution)/shard_map/ppermute | solution.py:112
  56.5 27.2 %collective-permute-start.7 = (bf16[8,128,256]{1,2,0:T(8,128)(2,1)S(1)}, bf16[8,128,256]{1,2,0:T(8,128)(2,1)S(1)}, u32[]{:S(2)}, u32[]{:S(2)}) collective-permute-start(bf16[8,128,256]{1,2,0:T(8,128)(2,1)S(1)} %get-tuple-element.104), channel_id=1, source_target_pairs={{16,32},{32,16},{17,33},{33,17},{18,34},{34,18},{19,35},{35,19},{2... | collective-permute-start | bytes 1572872 | tf_op jit(solution)/shard_map/ppermute | solution.py:112
  86.4 15.3 %copy-start.9 = (f32[512]{0:T(512)S(1)}, f32[512]{0:T(512)}, u32[]{:S(2)}) copy-start(f32[512]{0:T(512)} %param.45) | copy-start | bytes 6148
  86.4 15.4 %copy-start.10 = (f32[512]{0:T(512)S(1)}, f32[512]{0:T(512)}, u32[]{:S(2)}) copy-start(f32[512]{0:T(512)} %param.42) | copy-start | bytes 6148
  90.9 12.0 %copy-start.7 = (f32[512]{0:T(512)S(1)}, f32[512]{0:T(512)}, u32[]{:S(2)}) copy-start(f32[512]{0:T(512)} %param.44) | copy-start | bytes 6148
  90.9 12.0 %copy-start.8 = (f32[512]{0:T(512)S(1)}, f32[512]{0:T(512)}, u32[]{:S(2)}) copy-start(f32[512]{0:T(512)} %param.43) | copy-start | bytes 6148
  90.9 12.2 %copy-start.1 = (bf16[1024,1024]{1,0:T(8,128)(2,1)S(1)}, bf16[1024,1024]{1,0:T(8,128)(2,1)}, u32[]{:S(2)}) copy-start(bf16[1024,1024]{1,0:T(8,128)(2,1)} %param.46) | copy-start | bytes 6291460
  91.6 10.2 %collective-permute-start.8 = (f32[8,2,128]{2,0,1:T(8,128)S(1)}, f32[8,2,128]{2,0,1:T(8,128)S(1)}, u32[]{:S(2)}, u32[]{:S(2)}) collective-permute-start(f32[8,2,128]{2,0,1:T(8,128)S(1)} %get-tuple-element.152), channel_id=1, source_target_pairs={{0,1},{1,0},{2,3},{3,2},{4,5},{5,4},{6,7},{7,6},{8,9},{9,8},{10,11... | collective-permute-start | bytes 24584 | tf_op jit(solution)/shard_map/ppermute | solution.py:112
  91.7 10.1 %collective-permute-start.9 = (f32[8,2,128]{2,0,1:T(8,128)S(1)}, f32[8,2,128]{2,0,1:T(8,128)S(1)}, u32[]{:S(2)}, u32[]{:S(2)}) collective-permute-start(f32[8,2,128]{2,0,1:T(8,128)S(1)} %get-tuple-element.153), channel_id=1, source_target_pairs={{1,2},{2,1},{3,4},{4,3},{5,6},{6,5},{7,8},{8,7},{9,10},{10,9},{11,... | collective-permute-start | bytes 24584 | tf_op jit(solution)/shard_map/ppermute | solution.py:112
  93.6 8.2 %collective-permute-start.10 = (f32[8,2,128]{2,0,1:T(8,128)S(1)}, f32[8,2,128]{2,0,1:T(8,128)S(1)}, u32[]{:S(2)}, u32[]{:S(2)}) collective-permute-start(f32[8,2,128]{2,0,1:T(8,128)S(1)} %get-tuple-element.155), channel_id=1, source_target_pairs={{0,16},{16,0},{1,17},{17,1},{2,18},{18,2},{3,19},{19,3},{4,20},{20... | collective-permute-start | bytes 24584 | tf_op jit(solution)/shard_map/ppermute | solution.py:112
  93.7 8.7 %collective-permute-start.11 = (f32[8,2,128]{2,0,1:T(8,128)S(1)}, f32[8,2,128]{2,0,1:T(8,128)S(1)}, u32[]{:S(2)}, u32[]{:S(2)}) collective-permute-start(f32[8,2,128]{2,0,1:T(8,128)S(1)} %get-tuple-element.154), channel_id=1, source_target_pairs={{16,32},{32,16},{17,33},{33,17},{18,34},{34,18},{19,35},{35,19},{2... | collective-permute-start | bytes 24584 | tf_op jit(solution)/shard_map/ppermute | solution.py:112
  104.2 12.5 %collective-permute-start.12 = (f32[8,2,128]{2,0,1:T(8,128)S(1)}, f32[8,2,128]{2,0,1:T(8,128)S(1)}, u32[]{:S(2)}, u32[]{:S(2)}) collective-permute-start(f32[8,2,128]{2,0,1:T(8,128)S(1)} %get-tuple-element.148), channel_id=1, source_target_pairs={{0,1},{1,0},{2,3},{3,2},{4,5},{5,4},{6,7},{7,6},{8,9},{9,8},{10,11... | collective-permute-start | bytes 24584 | tf_op jit(solution)/shard_map/ppermute | solution.py:112
  104.3 12.5 %collective-permute-start.13 = (f32[8,2,128]{2,0,1:T(8,128)S(1)}, f32[8,2,128]{2,0,1:T(8,128)S(1)}, u32[]{:S(2)}, u32[]{:S(2)}) collective-permute-start(f32[8,2,128]{2,0,1:T(8,128)S(1)} %get-tuple-element.149), channel_id=1, source_target_pairs={{1,2},{2,1},{3,4},{4,3},{5,6},{6,5},{7,8},{8,7},{9,10},{10,9},{11,... | collective-permute-start | bytes 24584 | tf_op jit(solution)/shard_map/ppermute | solution.py:112
  106.2 10.5 %collective-permute-start.14 = (f32[8,2,128]{2,0,1:T(8,128)S(1)}, f32[8,2,128]{2,0,1:T(8,128)S(1)}, u32[]{:S(2)}, u32[]{:S(2)}) collective-permute-start(f32[8,2,128]{2,0,1:T(8,128)S(1)} %get-tuple-element.151), channel_id=1, source_target_pairs={{0,16},{16,0},{1,17},{17,1},{2,18},{18,2},{3,19},{19,3},{4,20},{20... | collective-permute-start | bytes 24584 | tf_op jit(solution)/shard_map/ppermute | solution.py:112
  106.3 12.0 %collective-permute-start.15 = (f32[8,2,128]{2,0,1:T(8,128)S(1)}, f32[8,2,128]{2,0,1:T(8,128)S(1)}, u32[]{:S(2)}, u32[]{:S(2)}) collective-permute-start(f32[8,2,128]{2,0,1:T(8,128)S(1)} %get-tuple-element.150), channel_id=1, source_target_pairs={{16,32},{32,16},{17,33},{33,17},{18,34},{34,18},{19,35},{35,19},{2... | collective-permute-start | bytes 24584 | tf_op jit(solution)/shard_map/ppermute | solution.py:112
  120.0 12.4 %collective-permute-start.16 = (f32[8,2,128]{2,0,1:T(8,128)S(1)}, f32[8,2,128]{2,0,1:T(8,128)S(1)}, u32[]{:S(2)}, u32[]{:S(2)}) collective-permute-start(f32[8,2,128]{2,0,1:T(8,128)S(1)} %get-tuple-element.142), channel_id=1, source_target_pairs={{0,1},{1,0},{2,3},{3,2},{4,5},{5,4},{6,7},{7,6},{8,9},{9,8},{10,11... | collective-permute-start | bytes 24584 | tf_op jit(solution)/shard_map/ppermute | solution.py:112
  120.1 12.4 %collective-permute-start.17 = (f32[8,2,128]{2,0,1:T(8,128)S(1)}, f32[8,2,128]{2,0,1:T(8,128)S(1)}, u32[]{:S(2)}, u32[]{:S(2)}) collective-permute-start(f32[8,2,128]{2,0,1:T(8,128)S(1)} %get-tuple-element.143), channel_id=1, source_target_pairs={{1,2},{2,1},{3,4},{4,3},{5,6},{6,5},{7,8},{8,7},{9,10},{10,9},{11,... | collective-permute-start | bytes 24584 | tf_op jit(solution)/shard_map/ppermute | solution.py:112
  122.0 10.4 %collective-permute-start.18 = (f32[8,2,128]{2,0,1:T(8,128)S(1)}, f32[8,2,128]{2,0,1:T(8,128)S(1)}, u32[]{:S(2)}, u32[]{:S(2)}) collective-permute-start(f32[8,2,128]{2,0,1:T(8,128)S(1)} %get-tuple-element.145), channel_id=1, source_target_pairs={{0,16},{16,0},{1,17},{17,1},{2,18},{18,2},{3,19},{19,3},{4,20},{20... | collective-permute-start | bytes 24584 | tf_op jit(solution)/shard_map/ppermute | solution.py:112
  122.1 11.7 %collective-permute-start.19 = (f32[8,2,128]{2,0,1:T(8,128)S(1)}, f32[8,2,128]{2,0,1:T(8,128)S(1)}, u32[]{:S(2)}, u32[]{:S(2)}) collective-permute-start(f32[8,2,128]{2,0,1:T(8,128)S(1)} %get-tuple-element.144), channel_id=1, source_target_pairs={{16,32},{32,16},{17,33},{33,17},{18,34},{34,18},{19,35},{35,19},{2... | collective-permute-start | bytes 24584 | tf_op jit(solution)/shard_map/ppermute | solution.py:112
  136.5 19.0 %collective-permute-start.20 = (f32[8,2,128]{2,0,1:T(8,128)S(1)}, f32[8,2,128]{2,0,1:T(8,128)S(1)}, u32[]{:S(2)}, u32[]{:S(2)}) collective-permute-start(f32[8,2,128]{2,0,1:T(8,128)S(1)} %get-tuple-element.135), channel_id=1, source_target_pairs={{0,1},{1,0},{2,3},{3,2},{4,5},{5,4},{6,7},{7,6},{8,9},{9,8},{10,11... | collective-permute-start | bytes 24584 | tf_op jit(solution)/shard_map/ppermute | solution.py:112
  137.5 18.0 %collective-permute-start.21 = (f32[8,2,128]{2,0,1:T(8,128)S(1)}, f32[8,2,128]{2,0,1:T(8,128)S(1)}, u32[]{:S(2)}, u32[]{:S(2)}) collective-permute-start(f32[8,2,128]{2,0,1:T(8,128)S(1)} %get-tuple-element.136), channel_id=1, source_target_pairs={{1,2},{2,1},{3,4},{4,3},{5,6},{6,5},{7,8},{8,7},{9,10},{10,9},{11,... | collective-permute-start | bytes 24584 | tf_op jit(solution)/shard_map/ppermute | solution.py:112
  142.2 13.3 %collective-permute-start.22 = (f32[8,2,128]{2,0,1:T(8,128)S(1)}, f32[8,2,128]{2,0,1:T(8,128)S(1)}, u32[]{:S(2)}, u32[]{:S(2)}) collective-permute-start(f32[8,2,128]{2,0,1:T(8,128)S(1)} %get-tuple-element.138), channel_id=1, source_target_pairs={{0,16},{16,0},{1,17},{17,1},{2,18},{18,2},{3,19},{19,3},{4,20},{20... | collective-permute-start | bytes 24584 | tf_op jit(solution)/shard_map/ppermute | solution.py:112
  142.4 14.7 %collective-permute-start.23 = (f32[8,2,128]{2,0,1:T(8,128)S(1)}, f32[8,2,128]{2,0,1:T(8,128)S(1)}, u32[]{:S(2)}, u32[]{:S(2)}) collective-permute-start(f32[8,2,128]{2,0,1:T(8,128)S(1)} %get-tuple-element.137), channel_id=1, source_target_pairs={{16,32},{32,16},{17,33},{33,17},{18,34},{34,18},{19,35},{35,19},{2... | collective-permute-start | bytes 24584 | tf_op jit(solution)/shard_map/ppermute | solution.py:112
  159.5 11.5 %collective-permute-start.24 = (f32[33,2,128]{2,0,1:T(8,128)S(1)}, f32[33,2,128]{2,0,1:T(8,128)S(1)}, u32[]{:S(2)}, u32[]{:S(2)}) collective-permute-start(f32[33,2,128]{2,0,1:T(8,128)S(1)} %get-tuple-element.118), channel_id=1, source_target_pairs={{0,1},{1,0},{2,3},{3,2},{4,5},{5,4},{6,7},{7,6},{8,9},{9,8},{10,11... | collective-permute-start | bytes 101384 | tf_op jit(solution)/shard_map/ppermute | solution.py:112
  159.6 11.5 %collective-permute-start.25 = (f32[33,2,128]{2,0,1:T(8,128)S(1)}, f32[33,2,128]{2,0,1:T(8,128)S(1)}, u32[]{:S(2)}, u32[]{:S(2)}) collective-permute-start(f32[33,2,128]{2,0,1:T(8,128)S(1)} %get-tuple-element.119), channel_id=1, source_target_pairs={{1,2},{2,1},{3,4},{4,3},{5,6},{6,5},{7,8},{8,7},{9,10},{10,9},{11,... | collective-permute-start | bytes 101384 | tf_op jit(solution)/shard_map/ppermute | solution.py:112
  161.6 9.5 %collective-permute-start.26 = (f32[33,2,128]{2,0,1:T(8,128)S(1)}, f32[33,2,128]{2,0,1:T(8,128)S(1)}, u32[]{:S(2)}, u32[]{:S(2)}) collective-permute-start(f32[33,2,128]{2,0,1:T(8,128)S(1)} %get-tuple-element.121), channel_id=1, source_target_pairs={{0,16},{16,0},{1,17},{17,1},{2,18},{18,2},{3,19},{19,3},{4,20},{20... | collective-permute-start | bytes 101384 | tf_op jit(solution)/shard_map/ppermute | solution.py:112
  161.7 11.4 %collective-permute-start.27 = (f32[33,2,128]{2,0,1:T(8,128)S(1)}, f32[33,2,128]{2,0,1:T(8,128)S(1)}, u32[]{:S(2)}, u32[]{:S(2)}) collective-permute-start(f32[33,2,128]{2,0,1:T(8,128)S(1)} %get-tuple-element.120), channel_id=1, source_target_pairs={{16,32},{32,16},{17,33},{33,17},{18,34},{34,18},{19,35},{35,19},{2... | collective-permute-start | bytes 101384 | tf_op jit(solution)/shard_map/ppermute | solution.py:112
  173.7 3.6 %collective-permute-start.28 = (f32[8,8]{1,0:T(8,128)S(1)}, f32[8,8]{1,0:T(8,128)S(1)}, u32[]{:S(2)}, u32[]{:S(2)}) collective-permute-start(f32[8,8]{1,0:T(8,128)S(1)} %add.345), channel_id=1, source_target_pairs={{0,2},{1,3},{2,0},{3,1},{4,6},{5,7},{6,4},{7,5},{8,10},{9,11},{10,... | collective-permute-start | bytes 776 | tf_op jit(solution)/shard_map/ppermute | solution.py:47
  177.4 4.8 %collective-permute-start.29 = (f32[8,8]{1,0:T(8,128)S(1)}, f32[8,8]{1,0:T(8,128)S(1)}, u32[]{:S(2)}, u32[]{:S(2)}) collective-permute-start(f32[8,8]{1,0:T(8,128)S(1)} %add.346), channel_id=1, source_target_pairs={{0,6},{1,7},{2,4},{3,5},{4,2},{5,3},{6,0},{7,1},{8,14},{9,15},{10,... | collective-permute-start | bytes 776 | tf_op jit(solution)/shard_map/ppermute | solution.py:47
  182.2 3.6 %collective-permute-start.30 = (f32[8,8]{1,0:T(8,128)S(1)}, f32[8,8]{1,0:T(8,128)S(1)}, u32[]{:S(2)}, u32[]{:S(2)}) collective-permute-start(f32[8,8]{1,0:T(8,128)S(1)} %add.347), channel_id=1, source_target_pairs={{0,8},{1,9},{2,10},{3,11},{4,12},{5,13},{6,14},{7,15},{8,0},{9,1},... | collective-permute-start | bytes 776 | tf_op jit(solution)/shard_map/ppermute | solution.py:47
  185.9 11.7 %collective-permute-start.31 = (f32[33,2,128]{2,0,1:T(8,128)S(1)}, f32[33,2,128]{2,0,1:T(8,128)S(1)}, u32[]{:S(2)}, u32[]{:S(2)}) collective-permute-start(f32[33,2,128]{2,0,1:T(8,128)S(1)} %get-tuple-element.112), channel_id=1, source_target_pairs={{0,1},{1,0},{2,3},{3,2},{4,5},{5,4},{6,7},{7,6},{8,9},{9,8},{10,11... | collective-permute-start | bytes 101384 | tf_op jit(solution)/shard_map/ppermute | solution.py:112
  186.0 11.6 %collective-permute-start.32 = (f32[33,2,128]{2,0,1:T(8,128)S(1)}, f32[33,2,128]{2,0,1:T(8,128)S(1)}, u32[]{:S(2)}, u32[]{:S(2)}) collective-permute-start(f32[33,2,128]{2,0,1:T(8,128)S(1)} %get-tuple-element.113), channel_id=1, source_target_pairs={{1,2},{2,1},{3,4},{4,3},{5,6},{6,5},{7,8},{8,7},{9,10},{10,9},{11,... | collective-permute-start | bytes 101384 | tf_op jit(solution)/shard_map/ppermute | solution.py:112
  188.0 9.7 %collective-permute-start.33 = (f32[33,2,128]{2,0,1:T(8,128)S(1)}, f32[33,2,128]{2,0,1:T(8,128)S(1)}, u32[]{:S(2)}, u32[]{:S(2)}) collective-permute-start(f32[33,2,128]{2,0,1:T(8,128)S(1)} %get-tuple-element.115), channel_id=1, source_target_pairs={{0,16},{16,0},{1,17},{17,1},{2,18},{18,2},{3,19},{19,3},{4,20},{20... | collective-permute-start | bytes 101384 | tf_op jit(solution)/shard_map/ppermute | solution.py:112
  188.1 11.5 %collective-permute-start.34 = (f32[33,2,128]{2,0,1:T(8,128)S(1)}, f32[33,2,128]{2,0,1:T(8,128)S(1)}, u32[]{:S(2)}, u32[]{:S(2)}) collective-permute-start(f32[33,2,128]{2,0,1:T(8,128)S(1)} %get-tuple-element.114), channel_id=1, source_target_pairs={{16,32},{32,16},{17,33},{33,17},{18,34},{34,18},{19,35},{35,19},{2... | collective-permute-start | bytes 101384 | tf_op jit(solution)/shard_map/ppermute | solution.py:112
  200.3 4.9 %collective-permute-start.35 = (f32[8,8]{1,0:T(8,128)S(1)}, f32[8,8]{1,0:T(8,128)S(1)}, u32[]{:S(2)}, u32[]{:S(2)}) collective-permute-start(f32[8,8]{1,0:T(8,128)S(1)} %add.351), channel_id=1, source_target_pairs={{0,32},{1,33},{2,34},{3,35},{4,36},{5,37},{6,38},{7,39},{8,40},{9,... | collective-permute-start | bytes 776 | tf_op jit(solution)/shard_map/ppermute | solution.py:47
  205.2 9.5 %collective-permute-start.36 = (f32[8,8]{1,0:T(8,128)S(1)}, f32[8,8]{1,0:T(8,128)S(1)}, u32[]{:S(2)}, u32[]{:S(2)}) collective-permute-start(f32[8,8]{1,0:T(8,128)S(1)} %add.352), channel_id=1, source_target_pairs={{0,64},{1,65},{2,66},{3,67},{4,68},{5,69},{6,70},{7,71},{8,72},{9,... | collective-permute-start | bytes 776 | tf_op jit(solution)/shard_map/ppermute | solution.py:47
  214.7 4.9 %collective-permute-start.37 = (f32[8,8]{1,0:T(8,128)S(1)}, f32[8,8]{1,0:T(8,128)S(1)}, u32[]{:S(2)}, u32[]{:S(2)}) collective-permute-start(f32[8,8]{1,0:T(8,128)S(1)} %add.353), channel_id=1, source_target_pairs={{0,224},{1,225},{2,226},{3,227},{4,228},{5,229},{6,230},{7,231},{8... | collective-permute-start | bytes 776 | tf_op jit(solution)/shard_map/ppermute | solution.py:47
  (5 other events, 15.0 us)

commit v8 on v7

--- a/solution.py
+++ b/solution.py
@@ -173,6 +173,18 @@
 
     def sweeps(residuals, partial, plan):
         count = residuals.shape[0]
+
+        def solve(forcing):
+            forcing = forcing.reshape(count * scenarios, 2 * buses).astype(jnp.bfloat16)
+            update = jnp.dot(forcing, region_inverse, preferred_element_type=jnp.float32)
+            return update.reshape(count, scenarios, 2, buses)
+
+        if plan is None:
+            def body(_, update):
+                arrived = halo(update)
+                return solve(rotate(conductance, susceptance, arrived, -2) - residuals)
+
+            return lax.fori_loop(1, SWEEPS, body, solve(-residuals)), partial
         update = None
         for sweep_number in range(SWEEPS):
             forcing = -residuals

time: 224 us -> 225 us (level)
  matrix products: 43.3 us -> 49.6 us
  starting transfers between devices: 113 us -> 107 us
  local copies, waits for them, and re-layouts: 5 us -> 7.99 us
  waiting for transfers between devices: 55.2 us -> 52.7 us
    dot_general x0 -> x3, matrix products: none -> 3.26 us  [solve(): jnp.dot(forcing, region_inverse, preferred_element_type=jnp.float32)]
    ppermute x32, starting transfers between devices: 97.1 us -> 94 us  [exchange(): lax.ppermute(tiles[j], 'region', routes[j])]
    unnamed x38 -> x40, local copies, waits for them, and re-layouts: 0.12 us -> 3.07 us
    ppermute x32, waiting for transfers between devices: 41.9 us -> 39.1 us  [exchange(): lax.ppermute(tiles[j], 'region', routes[j])]
    ppermute x6, starting transfers between devices: 15.7 us -> 13.3 us  [sum_rounds(): lax.ppermute(value, axis, [(i, i ^ bit) for i in range(count)])]
  transfers between devices with their start and end apart: 38 -> 38, of which waited for: 14 -> 15; matrix products, arithmetic and copies ran while one was open for 6% -> 9% of each run, Pallas kernels for 0% -> 0%
where the time goes in v8:
time: 225 us; the launch traced here: 222 us
  starting transfers between devices  107 us (48%)
  waiting for transfers between devices  52.7 us (23%)
  matrix products  49.6 us (22%)
  local copies, waits for them, and re-layouts  7.99 us (4%)
  other arithmetic  3.04 us (1%)
    ppermute x32, starting transfers between devices, exchange(): lax.ppermute(tiles[j], 'region', routes[j])  94 us
    ppermute x32, waiting for transfers between devices, exchange(): lax.ppermute(tiles[j], 'region', routes[j])  39.1 us
    ppermute x6, waiting for transfers between devices, sum_rounds(): lax.ppermute(value, axis, [(i, i ^ bit) for i in range(count)])  13.6 us
    ppermute x6, starting transfers between devices, sum_rounds(): lax.ppermute(value, axis, [(i, i ^ bit) for i in range(count)])  13.3 us
    dot_general x1, matrix products, local(): jnp.einsum('sbh,hk->sbk', gathered, neigh_weight[number], preferred_eleme...  8.9 us
    dot_general x2, matrix products, local(): jnp.einsum('ij,sjh->sih', mask_half, hidden, preferred_element_type=jnp.f...  6.15 us
    dot_general x2, matrix products, local(): jnp.einsum('ktb,sbh->ksth', pick_half, hidden, preferred_element_type=jnp...  5.96 us
    dot_general x2, matrix products, local(): jnp.einsum('sbh,hk->sbk', hidden, self_weight[number], preferred_element_...  5.34 us
  transfers between devices with their start and end apart: 38, of which 15 were waited for; matrix products, arithmetic and copies ran while one was open for 9% of the time, Pallas kernels for 0%

profile of v8, /device:TPU:4, one launch (start us, length us, event | category | flops | bytes accessed | tf_op | source)
XLA Modules:
  0.0 221.6 jit_solution(2245564932535054244)
XLA Ops:
  0.9 1.2 gather_fusion.1
  2.9 2.9 %convert_bitcast_fusion.1 = bf16[4,8,128,256]{3,2,1,0:T(8,128)(2,1)S(1)} fusion(bf16[8,512,256]{2,1,0:T(8,128)(2,1)} %param.33, s32[4,128]{1,0:T(4,128)S(1)} %broadcast_select_fusion.1, pred[4,128]{1,0:T(4,128)(4,1)S(1)} %broadcast_select_fusion.2), kind=kOutput, calls=%fused_computation.72 | convolution fusion | flops 1075314688 | bytes 4196864 | tf_op jit(solution)/shard_map/ktb,sbh->ksth/dot_general | solution.py:117
  5.8 1.4 slice_bitcast_fusion.13
  7.2 5.0 %collective-permute-start.5 = (bf16[8,128,256]{2,1,0:T(8,128)(2,1)}, bf16[8,128,256]{2,1,0:T(8,128)(2,1)}, u32[]{:S(2)}, u32[]{:S(2)}) collective-permute-start(bf16[8,128,256]{2,1,0:T(8,128)(2,1)} %get-tuple-element.218), channel_id=1, source_target_pairs={{1,2},{2,1},{3,4},{4,3},{5,6},{6,5},{7,8},{8,7},{9,10},{10,9},{11,... | collective-permute-start | bytes 1572872 | tf_op jit(solution)/shard_map/ppermute | solution.py:112
  12.3 6.8 %collective-permute-start.7 = (bf16[8,128,256]{2,1,0:T(8,128)(2,1)}, bf16[8,128,256]{2,1,0:T(8,128)(2,1)}, u32[]{:S(2)}, u32[]{:S(2)}) collective-permute-start(bf16[8,128,256]{2,1,0:T(8,128)(2,1)} %get-tuple-element.216), channel_id=1, source_target_pairs={{16,32},{32,16},{17,33},{33,17},{18,34},{34,18},{19,35},{35,19},{2... | collective-permute-start | bytes 1572872 | tf_op jit(solution)/shard_map/ppermute | solution.py:112
  19.1 2.7 %fusion.131 = f32[8,512,256]{2,1,0:T(8,128)} fusion(bf16[8,512,256]{2,1,0:T(8,128)(2,1)S(1)} %copy-done.3, bf16[2,256,256]{2,1,0:T(8,128)(2,1)S(1)} %copy-done.5), kind=kOutput, calls=%fused_computation.154 | convolution fusion | flops 536870912 | bytes 6422528 | tf_op jit(solution)/shard_map/sbh,hk->sbk/dot_general | solution.py:122
  21.8 3.0 %copy.81 = bf16[1024,1024]{0,1:T(8,128)(2,1)S(1)} copy(bf16[1024,1024]{1,0:T(8,128)(2,1)} %param.48) | data formatting | bytes 4194304
  25.7 4.9 %fusion.102 = f32[8,256,512]{1,2,0:T(8,128)} fusion(bf16[8,512,256]{2,1,0:T(8,128)(2,1)} %param.33, s32[512,512]{1,0:T(8,128)S(1)} %copy-done.2), kind=kOutput, calls=%fused_computation.111 | convolution fusion | flops 1074003968 | bytes 7340032 | tf_op jit(solution)/shard_map/ij,sjh->sih/dot_general | solution.py:121
  30.5 12.2 %collective-permute-done.5 = bf16[8,128,256]{2,1,0:T(8,128)(2,1)} collective-permute-done((bf16[8,128,256]{2,1,0:T(8,128)(2,1)}, bf16[8,128,256]{2,1,0:T(8,128)(2,1)}, u32[]{:S(2)}, u32[]{:S(2)}) %collective-permute-start.5) | collective-permute-done | bytes 524320 | tf_op jit(solution)/shard_map/ppermute | solution.py:112
  42.8 8.9 %add_convert_fusion.1 = bf16[8,512,256]{2,1,0:T(8,128)(2,1)} fusion(f32[8,512,256]{2,1,0:T(8,128)} %fusion.131, bf16[8,512,256]{2,1,0:T(8,128)(2,1)} %param.33, f32[256]{0:T(256)S(1)} %bitcast.617, f32[8,256,512]{1,2,0:T(8,128)} %fusion.102, bf16[1,8,128,256]{3,2,1,0:T(8,128)(2,1)} %bitcast.23, bf16[1,8,128,256]{3,2,1,0:T(8,128)(2,1)} %bitcast.21, ...), kind=kOutput, calls=%fused_computation.44 | convolution fusion | flops 1626603520 | bytes 14814208 | tf_op jit(solution)/shard_map/sbh,hk->sbk/dot_general | solution.py:131
  51.7 3.1 %convert_bitcast_fusion = bf16[4,8,128,256]{2,3,0,1:T(8,128)(2,1)S(1)} fusion(bf16[8,512,256]{2,1,0:T(8,128)(2,1)} %add_convert_fusion.1, s32[4,128]{1,0:T(4,128)S(1)} %broadcast_select_fusion.1, pred[4,128]{1,0:T(4,128)(4,1)S(1)} %broadcast_select_fusion.2), kind=kOutput, calls=%fused_computation.71 | convolution fusion | flops 1075314688 | bytes 4196864 | tf_op jit(solution)/shard_map/ktb,sbh->ksth/dot_general | solution.py:117
  55.1 2.1 collective-permute-start.9
  57.2 6.9 %collective-permute-start.11 = (bf16[8,128,256]{1,2,0:T(8,128)(2,1)S(1)}, bf16[8,128,256]{1,2,0:T(8,128)(2,1)S(1)}, u32[]{:S(2)}, u32[]{:S(2)}) collective-permute-start(bf16[8,128,256]{1,2,0:T(8,128)(2,1)S(1)} %get-tuple-element.213), channel_id=1, source_target_pairs={{16,32},{32,16},{17,33},{33,17},{18,34},{34,18},{19,35},{35,19},{2... | collective-permute-start | bytes 1572872 | tf_op jit(solution)/shard_map/ppermute | solution.py:112
  64.2 2.7 %fusion.128 = f32[8,512,256]{2,1,0:T(8,128)} fusion(bf16[8,512,256]{2,1,0:T(8,128)(2,1)S(1)} %copy-done.4, bf16[2,256,256]{2,1,0:T(8,128)(2,1)S(1)} %copy-done.5), kind=kOutput, calls=%fused_computation.151 | convolution fusion | flops 536870912 | bytes 6422528 | tf_op jit(solution)/shard_map/sbh,hk->sbk/dot_general | solution.py:122
  66.8 1.3 fusion.104
  68.1 16.3 %collective-permute-done.9 = bf16[8,128,256]{1,2,0:T(8,128)(2,1)S(1)} collective-permute-done((bf16[8,128,256]{1,2,0:T(8,128)(2,1)S(1)}, bf16[8,128,256]{1,2,0:T(8,128)(2,1)S(1)}, u32[]{:S(2)}, u32[]{:S(2)}) %collective-permute-start.9) | collective-permute-done | bytes 524320 | tf_op jit(solution)/shard_map/ppermute | solution.py:112
  84.4 2.7 %fusion.24 = bf16[8,256,512]{1,2,0:T(8,128)(2,1)} fusion(f32[8,256,512]{1,2,0:T(8,128)S(1)} %fusion.104, bf16[1,8,128,256]{2,3,1,0:T(8,128)(2,1)S(1)} %bitcast.621, bf16[1,8,128,256]{2,3,1,0:T(8,128)(2,1)S(1)} %bitcast.620, bf16[1,8,128,256]{2,3,1,0:T(8,128)(2,1)S(1)} %bitcast.619, bf16[1,8,128,256]{2,3,1,0:T(8,128)(2,1)S(1)} %bitcast.618, ...), kind=kOutput, calls=%fused_computation.39 | convolution fusion | flops 1080295424 | bytes 8390656 | tf_op jit(solution)/shard_map/ktb,ksth->sbh/dot_general | solution.py:125
  87.1 5.1 %fusion.74 = f32[8,512,2]{1,2,0:T(2,128)S(1)} fusion(f32[8,512,256]{2,1,0:T(8,128)} %fusion.128, bf16[8,512,256]{2,1,0:T(8,128)(2,1)} %add_convert_fusion.1, bf16[8,256,512]{1,2,0:T(8,128)(2,1)} %fusion.24, f32[256]{0:T(256)S(1)} %bitcast.616, bf16[2,256,256]{2,1,0:T(8,128)(2,1)} %param.39, f32[2]{0:T(128)S(1)} %copy-done.14, bf16[2,256]{1,0:T(2,128)(2,1)S(1)} %copy-done.13), kind=kOutput, calls=%fused_computation.90 | convolution fusion | flops 550510592 | bytes 8554504 | tf_op jit(solution)/shard_map/sbh,ch->scb/dot_general | solution.py:139
  93.0 1.9 collective-permute-start.13
  95.0 7.0 %collective-permute-start.15 = (f32[8,2,128]{2,0,1:T(8,128)S(1)}, f32[8,2,128]{2,0,1:T(8,128)S(1)}, u32[]{:S(2)}, u32[]{:S(2)}) collective-permute-start(f32[8,2,128]{2,0,1:T(8,128)S(1)} %get-tuple-element.248), channel_id=1, source_target_pairs={{16,32},{32,16},{17,33},{33,17},{18,34},{34,18},{19,35},{35,19},{2... | collective-permute-start | bytes 24584 | tf_op jit(solution)/shard_map/ppermute | solution.py:112
  102.0 0.9 fusion.79
  104.4 2.0 fusion.69
  106.3 34.7 %while.17 = (s32[]{:T(128)}, f32[1,8,2,512]{3,1,2,0:T(8,128)S(1)}, f32[512]{0:T(512)S(1)}, f32[512]{0:T(512)S(1)}, f32[1,8,2,512]{3,1,2,0:T(8,128)S(1)}, /*index...) while((s32[]{:T(128)}, f32[1,8,2,512]{3,1,2,0:T(8,128)S(1)}, ...), condition=%wide.region_2.8_spmd.clone, body=%wide.region_1.7_spmd.clone.sunk | while | flops 118824960 | bytes 2630405 | solution.py:187
  106.3 1.1 convolution_bitcast_fusion.14
  107.5 6.3 %collective-permute-start = (f32[8,2,128]{2,0,1:T(8,128)S(1)}, f32[8,2,128]{2,0,1:T(8,128)S(1)}, u32[]{:S(2)}, u32[]{:S(2)}) collective-permute-start(f32[8,2,128]{2,0,1:T(8,128)S(1)} %get-tuple-element.315), channel_id=1, source_target_pairs={{16,32},{32,16},{17,33},{33,17},{18,34},{34,18},{19,35},{35,19},{2... | collective-permute-start | bytes 24584 | tf_op jit(solution)/shard_map/while/body/eval_jaxpr/ppermute | solution.py:112
  113.9 5.4 %collective-permute-start.2 = (f32[8,2,128]{2,0,1:T(8,128)S(1)}, f32[8,2,128]{2,0,1:T(8,128)S(1)}, u32[]{:S(2)}, u32[]{:S(2)}) collective-permute-start(f32[8,2,128]{2,0,1:T(8,128)S(1)} %get-tuple-element.317), channel_id=1, source_target_pairs={{1,2},{2,1},{3,4},{4,3},{5,6},{6,5},{7,8},{8,7},{9,10},{10,9},{11,... | collective-permute-start | bytes 24584 | tf_op jit(solution)/shard_map/while/body/eval_jaxpr/ppermute | solution.py:112
  119.5 1.5 collective-permute-done.2
  122.4 1.1 convolution_bitcast_fusion.14
  123.6 8.9 %collective-permute-start = (f32[8,2,128]{2,0,1:T(8,128)S(1)}, f32[8,2,128]{2,0,1:T(8,128)S(1)}, u32[]{:S(2)}, u32[]{:S(2)}) collective-permute-start(f32[8,2,128]{2,0,1:T(8,128)S(1)} %get-tuple-element.315), channel_id=1, source_target_pairs={{16,32},{32,16},{17,33},{33,17},{18,34},{34,18},{19,35},{35,19},{2... | collective-permute-start | bytes 24584 | tf_op jit(solution)/shard_map/while/body/eval_jaxpr/ppermute | solution.py:112
  132.5 2.8 %collective-permute-start.2 = (f32[8,2,128]{2,0,1:T(8,128)S(1)}, f32[8,2,128]{2,0,1:T(8,128)S(1)}, u32[]{:S(2)}, u32[]{:S(2)}) collective-permute-start(f32[8,2,128]{2,0,1:T(8,128)S(1)} %get-tuple-element.317), channel_id=1, source_target_pairs={{1,2},{2,1},{3,4},{4,3},{5,6},{6,5},{7,8},{8,7},{9,10},{10,9},{11,... | collective-permute-start | bytes 24584 | tf_op jit(solution)/shard_map/while/body/eval_jaxpr/ppermute | solution.py:112
  135.4 2.2 %collective-permute-done.1 = f32[8,2,128]{2,0,1:T(8,128)S(1)} collective-permute-done((f32[8,2,128]{2,0,1:T(8,128)S(1)}, f32[8,2,128]{2,0,1:T(8,128)S(1)}, u32[]{:S(2)}, u32[]{:S(2)}) %collective-permute-start.1) | collective-permute-done | bytes 8224 | tf_op jit(solution)/shard_map/while/body/eval_jaxpr/ppermute | solution.py:112
  137.7 1.9 collective-permute-done.2
  142.0 2.8 %collective-permute-start.17 = (f32[8,2,128]{2,0,1:T(8,128)S(1)}, f32[8,2,128]{2,0,1:T(8,128)S(1)}, u32[]{:S(2)}, u32[]{:S(2)}) collective-permute-start(f32[8,2,128]{2,0,1:T(8,128)S(1)} %get-tuple-element.240), channel_id=1, source_target_pairs={{1,2},{2,1},{3,4},{4,3},{5,6},{6,5},{7,8},{8,7},{9,10},{10,9},{11,... | collective-permute-start | bytes 24584 | tf_op jit(solution)/shard_map/ppermute | solution.py:112
  144.9 8.3 %collective-permute-start.19 = (f32[8,2,128]{2,0,1:T(8,128)S(1)}, f32[8,2,128]{2,0,1:T(8,128)S(1)}, u32[]{:S(2)}, u32[]{:S(2)}) collective-permute-start(f32[8,2,128]{2,0,1:T(8,128)S(1)} %get-tuple-element.241), channel_id=1, source_target_pairs={{16,32},{32,16},{17,33},{33,17},{18,34},{34,18},{19,35},{35,19},{2... | collective-permute-start | bytes 24584 | tf_op jit(solution)/shard_map/ppermute | solution.py:112
  157.2 4.3 %collective-permute-start.21 = (f32[33,2,128]{2,0,1:T(8,128)S(1)}, f32[33,2,128]{2,0,1:T(8,128)S(1)}, u32[]{:S(2)}, u32[]{:S(2)}) collective-permute-start(f32[33,2,128]{2,0,1:T(8,128)S(1)} %get-tuple-element.228), channel_id=1, source_target_pairs={{1,2},{2,1},{3,4},{4,3},{5,6},{6,5},{7,8},{8,7},{9,10},{10,9},{11,... | collective-permute-start | bytes 101384 | tf_op jit(solution)/shard_map/ppermute | solution.py:112
  161.7 14.1 %collective-permute-start.23 = (f32[33,2,128]{2,0,1:T(8,128)S(1)}, f32[33,2,128]{2,0,1:T(8,128)S(1)}, u32[]{:S(2)}, u32[]{:S(2)}) collective-permute-start(f32[33,2,128]{2,0,1:T(8,128)S(1)} %get-tuple-element.229), channel_id=1, source_target_pairs={{16,32},{32,16},{17,33},{33,17},{18,34},{34,18},{19,35},{35,19},{2... | collective-permute-start | bytes 101384 | tf_op jit(solution)/shard_map/ppermute | solution.py:112
  175.8 1.9 collective-permute-done.23
  178.7 3.4 %collective-permute-done.24 = f32[8,8]{1,0:T(8,128)S(1)} collective-permute-done((f32[8,8]{1,0:T(8,128)S(1)}, f32[8,8]{1,0:T(8,128)S(1)}, u32[]{:S(2)}, u32[]{:S(2)}) %collective-permute-start.24) | collective-permute-done | bytes 288 | tf_op jit(solution)/shard_map/ppermute | solution.py:47
  182.6 4.4 %collective-permute-done.25 = f32[8,8]{1,0:T(8,128)S(1)} collective-permute-done((f32[8,8]{1,0:T(8,128)S(1)}, f32[8,8]{1,0:T(8,128)S(1)}, u32[]{:S(2)}, u32[]{:S(2)}) %collective-permute-start.25) | collective-permute-done | bytes 288 | tf_op jit(solution)/shard_map/ppermute | solution.py:47
  188.4 2.1 collective-permute-done.26
  190.7 1.9 collective-permute-start.28
  192.8 8.0 %collective-permute-start.30 = (f32[33,2,128]{2,0,1:T(8,128)S(1)}, f32[33,2,128]{2,0,1:T(8,128)S(1)}, u32[]{:S(2)}, u32[]{:S(2)}) collective-permute-start(f32[33,2,128]{2,0,1:T(8,128)S(1)} %get-tuple-element.223), channel_id=1, source_target_pairs={{16,32},{32,16},{17,33},{33,17},{18,34},{34,18},{19,35},{35,19},{2... | collective-permute-start | bytes 101384 | tf_op jit(solution)/shard_map/ppermute | solution.py:112
  200.8 1.9 collective-permute-done.30
  203.5 4.9 %collective-permute-start.31 = (f32[8,8]{1,0:T(8,128)S(1)}, f32[8,8]{1,0:T(8,128)S(1)}, u32[]{:S(2)}, u32[]{:S(2)}) collective-permute-start(f32[8,8]{1,0:T(8,128)S(1)} %add.339), channel_id=1, source_target_pairs={{0,32},{1,33},{2,34},{3,35},{4,36},{5,37},{6,38},{7,39},{8,40},{9,... | collective-permute-start | bytes 776 | tf_op jit(solution)/shard_map/ppermute | solution.py:47
  210.0 4.4 %collective-permute-start.32 = (f32[8,8]{1,0:T(8,128)S(1)}, f32[8,8]{1,0:T(8,128)S(1)}, u32[]{:S(2)}, u32[]{:S(2)}) collective-permute-start(f32[8,8]{1,0:T(8,128)S(1)} %add.340), channel_id=1, source_target_pairs={{0,64},{1,65},{2,66},{3,67},{4,68},{5,69},{6,70},{7,71},{8,72},{9,... | collective-permute-start | bytes 776 | tf_op jit(solution)/shard_map/ppermute | solution.py:47
  214.4 1.5 collective-permute-done.32
  216.0 3.2 %collective-permute-start.33 = (f32[8,8]{1,0:T(8,128)S(1)}, f32[8,8]{1,0:T(8,128)S(1)}, u32[]{:S(2)}, u32[]{:S(2)}) collective-permute-start(f32[8,8]{1,0:T(8,128)S(1)} %add.341), channel_id=1, source_target_pairs={{0,224},{1,225},{2,226},{3,227},{4,228},{5,229},{6,230},{7,231},{8... | collective-permute-start | bytes 776 | tf_op jit(solution)/shard_map/ppermute | solution.py:47
  219.3 1.5 collective-permute-done.33
  (181 shorter events, 19.8 us)
Async XLA Ops:
  0.0 25.4 %copy-start = (f32[16,2,512]{2,1,0:T(2,128)S(1)}, f32[16,2,512]{2,1,0:T(2,128)}, u32[]{:S(2)}) copy-start(f32[16,2,512]{2,1,0:T(2,128)} %param.42) | copy-start | bytes 196612
  5.8 13.3 %copy-start.3 = (bf16[8,512,256]{2,1,0:T(8,128)(2,1)S(1)}, bf16[8,512,256]{2,1,0:T(8,128)(2,1)}, u32[]{:S(2)}) copy-start(bf16[8,512,256]{2,1,0:T(8,128)(2,1)} %param.33) | copy-start | bytes 6291460
  5.8 13.3 %copy-start.5 = (bf16[2,256,256]{2,1,0:T(8,128)(2,1)S(1)}, bf16[2,256,256]{2,1,0:T(8,128)(2,1)}, u32[]{:S(2)}) copy-start(bf16[2,256,256]{2,1,0:T(8,128)(2,1)} %param.38) | copy-start | bytes 786436
  7.2 23.3 %collective-permute-start.4 = (bf16[8,128,256]{2,1,0:T(8,128)(2,1)}, bf16[8,128,256]{2,1,0:T(8,128)(2,1)}, u32[]{:S(2)}, u32[]{:S(2)}) collective-permute-start(bf16[8,128,256]{2,1,0:T(8,128)(2,1)} %get-tuple-element.215), channel_id=1, source_target_pairs={{0,1},{1,0},{2,3},{3,2},{4,5},{5,4},{6,7},{7,6},{8,9},{9,8},{10,11... | collective-permute-start | bytes 1572872 | tf_op jit(solution)/shard_map/ppermute | solution.py:112
  7.2 35.5 %collective-permute-start.5 = (bf16[8,128,256]{2,1,0:T(8,128)(2,1)}, bf16[8,128,256]{2,1,0:T(8,128)(2,1)}, u32[]{:S(2)}, u32[]{:S(2)}) collective-permute-start(bf16[8,128,256]{2,1,0:T(8,128)(2,1)} %get-tuple-element.218), channel_id=1, source_target_pairs={{1,2},{2,1},{3,4},{4,3},{5,6},{6,5},{7,8},{8,7},{9,10},{10,9},{11,... | collective-permute-start | bytes 1572872 | tf_op jit(solution)/shard_map/ppermute | solution.py:112
  12.2 30.5 %collective-permute-start.6 = (bf16[8,128,256]{2,1,0:T(8,128)(2,1)}, bf16[8,128,256]{2,1,0:T(8,128)(2,1)}, u32[]{:S(2)}, u32[]{:S(2)}) collective-permute-start(bf16[8,128,256]{2,1,0:T(8,128)(2,1)} %get-tuple-element.217), channel_id=1, source_target_pairs={{0,16},{16,0},{1,17},{17,1},{2,18},{18,2},{3,19},{19,3},{4,20},{20... | collective-permute-start | bytes 1572872 | tf_op jit(solution)/shard_map/ppermute | solution.py:112
  12.3 30.4 %collective-permute-start.7 = (bf16[8,128,256]{2,1,0:T(8,128)(2,1)}, bf16[8,128,256]{2,1,0:T(8,128)(2,1)}, u32[]{:S(2)}, u32[]{:S(2)}) collective-permute-start(bf16[8,128,256]{2,1,0:T(8,128)(2,1)} %get-tuple-element.216), channel_id=1, source_target_pairs={{16,32},{32,16},{17,33},{33,17},{18,34},{34,18},{19,35},{35,19},{2... | collective-permute-start | bytes 1572872 | tf_op jit(solution)/shard_map/ppermute | solution.py:112
  21.8 3.8 %copy-start.2 = (s32[512,512]{1,0:T(8,128)S(1)}, s32[512,512]{1,0:T(8,128)}, u32[]{:S(2)}) copy-start(s32[512,512]{1,0:T(8,128)} %param.34) | copy-start | bytes 3145732
  54.7 9.4 %copy-start.4 = (bf16[8,512,256]{2,1,0:T(8,128)(2,1)S(1)}, bf16[8,512,256]{2,1,0:T(8,128)(2,1)}, u32[]{:S(2)}) copy-start(bf16[8,512,256]{2,1,0:T(8,128)(2,1)} %add_convert_fusion.1) | copy-start | bytes 6291460
  55.0 13.2 %collective-permute-start.8 = (bf16[8,128,256]{1,2,0:T(8,128)(2,1)S(1)}, bf16[8,128,256]{1,2,0:T(8,128)(2,1)S(1)}, u32[]{:S(2)}, u32[]{:S(2)}) collective-permute-start(bf16[8,128,256]{1,2,0:T(8,128)(2,1)S(1)} %get-tuple-element.211), channel_id=1, source_target_pairs={{0,1},{1,0},{2,3},{3,2},{4,5},{5,4},{6,7},{7,6},{8,9},{9,8},{10,11... | collective-permute-start | bytes 1572872 | tf_op jit(solution)/shard_map/ppermute | solution.py:112
  55.1 29.3 %collective-permute-start.9 = (bf16[8,128,256]{1,2,0:T(8,128)(2,1)S(1)}, bf16[8,128,256]{1,2,0:T(8,128)(2,1)S(1)}, u32[]{:S(2)}, u32[]{:S(2)}) collective-permute-start(bf16[8,128,256]{1,2,0:T(8,128)(2,1)S(1)} %get-tuple-element.212), channel_id=1, source_target_pairs={{1,2},{2,1},{3,4},{4,3},{5,6},{6,5},{7,8},{8,7},{9,10},{10,9},{11,... | collective-permute-start | bytes 1572872 | tf_op jit(solution)/shard_map/ppermute | solution.py:112
  57.1 27.3 %collective-permute-start.10 = (bf16[8,128,256]{1,2,0:T(8,128)(2,1)S(1)}, bf16[8,128,256]{1,2,0:T(8,128)(2,1)S(1)}, u32[]{:S(2)}, u32[]{:S(2)}) collective-permute-start(bf16[8,128,256]{1,2,0:T(8,128)(2,1)S(1)} %get-tuple-element.214), channel_id=1, source_target_pairs={{0,16},{16,0},{1,17},{17,1},{2,18},{18,2},{3,19},{19,3},{4,20},{20... | collective-permute-start | bytes 1572872 | tf_op jit(solution)/shard_map/ppermute | solution.py:112
  57.2 27.2 %collective-permute-start.11 = (bf16[8,128,256]{1,2,0:T(8,128)(2,1)S(1)}, bf16[8,128,256]{1,2,0:T(8,128)(2,1)S(1)}, u32[]{:S(2)}, u32[]{:S(2)}) collective-permute-start(bf16[8,128,256]{1,2,0:T(8,128)(2,1)S(1)} %get-tuple-element.213), channel_id=1, source_target_pairs={{16,32},{32,16},{17,33},{33,17},{18,34},{34,18},{19,35},{35,19},{2... | collective-permute-start | bytes 1572872 | tf_op jit(solution)/shard_map/ppermute | solution.py:112
  87.1 15.9 %copy-start.9 = (f32[512]{0:T(512)S(1)}, f32[512]{0:T(512)}, u32[]{:S(2)}) copy-start(f32[512]{0:T(512)} %param.47) | copy-start | bytes 6148
  87.1 16.0 %copy-start.10 = (f32[512]{0:T(512)S(1)}, f32[512]{0:T(512)}, u32[]{:S(2)}) copy-start(f32[512]{0:T(512)} %param.44) | copy-start | bytes 6148
  92.2 12.0 %copy-start.6 = (f32[512]{0:T(512)S(1)}, f32[512]{0:T(512)}, u32[]{:S(2)}) copy-start(f32[512]{0:T(512)} %param.46) | copy-start | bytes 6148
  92.2 12.0 %copy-start.7 = (f32[512]{0:T(512)S(1)}, f32[512]{0:T(512)}, u32[]{:S(2)}) copy-start(f32[512]{0:T(512)} %param.45) | copy-start | bytes 6148
  92.9 10.2 %collective-permute-start.12 = (f32[8,2,128]{2,0,1:T(8,128)S(1)}, f32[8,2,128]{2,0,1:T(8,128)S(1)}, u32[]{:S(2)}, u32[]{:S(2)}) collective-permute-start(f32[8,2,128]{2,0,1:T(8,128)S(1)} %get-tuple-element.246), channel_id=1, source_target_pairs={{0,1},{1,0},{2,3},{3,2},{4,5},{5,4},{6,7},{7,6},{8,9},{9,8},{10,11... | collective-permute-start | bytes 24584 | tf_op jit(solution)/shard_map/ppermute | solution.py:112
  93.0 10.1 %collective-permute-start.13 = (f32[8,2,128]{2,0,1:T(8,128)S(1)}, f32[8,2,128]{2,0,1:T(8,128)S(1)}, u32[]{:S(2)}, u32[]{:S(2)}) collective-permute-start(f32[8,2,128]{2,0,1:T(8,128)S(1)} %get-tuple-element.247), channel_id=1, source_target_pairs={{1,2},{2,1},{3,4},{4,3},{5,6},{6,5},{7,8},{8,7},{9,10},{10,9},{11,... | collective-permute-start | bytes 24584 | tf_op jit(solution)/shard_map/ppermute | solution.py:112
  94.9 8.2 %collective-permute-start.14 = (f32[8,2,128]{2,0,1:T(8,128)S(1)}, f32[8,2,128]{2,0,1:T(8,128)S(1)}, u32[]{:S(2)}, u32[]{:S(2)}) collective-permute-start(f32[8,2,128]{2,0,1:T(8,128)S(1)} %get-tuple-element.249), channel_id=1, source_target_pairs={{0,16},{16,0},{1,17},{17,1},{2,18},{18,2},{3,19},{19,3},{4,20},{20... | collective-permute-start | bytes 24584 | tf_op jit(solution)/shard_map/ppermute | solution.py:112
  95.0 8.7 %collective-permute-start.15 = (f32[8,2,128]{2,0,1:T(8,128)S(1)}, f32[8,2,128]{2,0,1:T(8,128)S(1)}, u32[]{:S(2)}, u32[]{:S(2)}) collective-permute-start(f32[8,2,128]{2,0,1:T(8,128)S(1)} %get-tuple-element.248), channel_id=1, source_target_pairs={{16,32},{32,16},{17,33},{33,17},{18,34},{34,18},{19,35},{35,19},{2... | collective-permute-start | bytes 24584 | tf_op jit(solution)/shard_map/ppermute | solution.py:112
  107.5 12.0 %collective-permute-start = (f32[8,2,128]{2,0,1:T(8,128)S(1)}, f32[8,2,128]{2,0,1:T(8,128)S(1)}, u32[]{:S(2)}, u32[]{:S(2)}) collective-permute-start(f32[8,2,128]{2,0,1:T(8,128)S(1)} %get-tuple-element.315), channel_id=1, source_target_pairs={{16,32},{32,16},{17,33},{33,17},{18,34},{34,18},{19,35},{35,19},{2... | collective-permute-start | bytes 24584 | tf_op jit(solution)/shard_map/while/body/eval_jaxpr/ppermute | solution.py:112
  113.8 5.7 %collective-permute-start.1 = (f32[8,2,128]{2,0,1:T(8,128)S(1)}, f32[8,2,128]{2,0,1:T(8,128)S(1)}, u32[]{:S(2)}, u32[]{:S(2)}) collective-permute-start(f32[8,2,128]{2,0,1:T(8,128)S(1)} %get-tuple-element.316), channel_id=1, source_target_pairs={{0,16},{16,0},{1,17},{17,1},{2,18},{18,2},{3,19},{19,3},{4,20},{20... | collective-permute-start | bytes 24584 | tf_op jit(solution)/shard_map/while/body/eval_jaxpr/ppermute | solution.py:112
  113.9 7.1 %collective-permute-start.2 = (f32[8,2,128]{2,0,1:T(8,128)S(1)}, f32[8,2,128]{2,0,1:T(8,128)S(1)}, u32[]{:S(2)}, u32[]{:S(2)}) collective-permute-start(f32[8,2,128]{2,0,1:T(8,128)S(1)} %get-tuple-element.317), channel_id=1, source_target_pairs={{1,2},{2,1},{3,4},{4,3},{5,6},{6,5},{7,8},{8,7},{9,10},{10,9},{11,... | collective-permute-start | bytes 24584 | tf_op jit(solution)/shard_map/while/body/eval_jaxpr/ppermute | solution.py:112
  119.4 1.6 collective-permute-start.3
  123.6 11.9 %collective-permute-start = (f32[8,2,128]{2,0,1:T(8,128)S(1)}, f32[8,2,128]{2,0,1:T(8,128)S(1)}, u32[]{:S(2)}, u32[]{:S(2)}) collective-permute-start(f32[8,2,128]{2,0,1:T(8,128)S(1)} %get-tuple-element.315), channel_id=1, source_target_pairs={{16,32},{32,16},{17,33},{33,17},{18,34},{34,18},{19,35},{35,19},{2... | collective-permute-start | bytes 24584 | tf_op jit(solution)/shard_map/while/body/eval_jaxpr/ppermute | solution.py:112
  132.4 5.2 %collective-permute-start.1 = (f32[8,2,128]{2,0,1:T(8,128)S(1)}, f32[8,2,128]{2,0,1:T(8,128)S(1)}, u32[]{:S(2)}, u32[]{:S(2)}) collective-permute-start(f32[8,2,128]{2,0,1:T(8,128)S(1)} %get-tuple-element.316), channel_id=1, source_target_pairs={{0,16},{16,0},{1,17},{17,1},{2,18},{18,2},{3,19},{19,3},{4,20},{20... | collective-permute-start | bytes 24584 | tf_op jit(solution)/shard_map/while/body/eval_jaxpr/ppermute | solution.py:112
  132.5 7.1 %collective-permute-start.2 = (f32[8,2,128]{2,0,1:T(8,128)S(1)}, f32[8,2,128]{2,0,1:T(8,128)S(1)}, u32[]{:S(2)}, u32[]{:S(2)}) collective-permute-start(f32[8,2,128]{2,0,1:T(8,128)S(1)} %get-tuple-element.317), channel_id=1, source_target_pairs={{1,2},{2,1},{3,4},{4,3},{5,6},{6,5},{7,8},{8,7},{9,10},{10,9},{11,... | collective-permute-start | bytes 24584 | tf_op jit(solution)/shard_map/while/body/eval_jaxpr/ppermute | solution.py:112
  135.3 4.3 %collective-permute-start.3 = (f32[8,2,128]{2,0,1:T(8,128)S(1)}, f32[8,2,128]{2,0,1:T(8,128)S(1)}, u32[]{:S(2)}, u32[]{:S(2)}) collective-permute-start(f32[8,2,128]{2,0,1:T(8,128)S(1)} %get-tuple-element.318), channel_id=1, source_target_pairs={{0,1},{1,0},{2,3},{3,2},{4,5},{5,4},{6,7},{7,6},{8,9},{9,8},{10,11... | collective-permute-start | bytes 24584 | tf_op jit(solution)/shard_map/while/body/eval_jaxpr/ppermute | solution.py:112
  141.1 14.8 %copy-start.1 = (bf16[1024,1024]{1,0:T(8,128)(2,1)S(1)}, bf16[1024,1024]{1,0:T(8,128)(2,1)}, u32[]{:S(2)}) copy-start(bf16[1024,1024]{1,0:T(8,128)(2,1)} %param.48) | copy-start | bytes 6291460
  141.9 12.2 %collective-permute-start.16 = (f32[8,2,128]{2,0,1:T(8,128)S(1)}, f32[8,2,128]{2,0,1:T(8,128)S(1)}, u32[]{:S(2)}, u32[]{:S(2)}) collective-permute-start(f32[8,2,128]{2,0,1:T(8,128)S(1)} %get-tuple-element.239), channel_id=1, source_target_pairs={{0,1},{1,0},{2,3},{3,2},{4,5},{5,4},{6,7},{7,6},{8,9},{9,8},{10,11... | collective-permute-start | bytes 24584 | tf_op jit(solution)/shard_map/ppermute | solution.py:112
  142.0 12.2 %collective-permute-start.17 = (f32[8,2,128]{2,0,1:T(8,128)S(1)}, f32[8,2,128]{2,0,1:T(8,128)S(1)}, u32[]{:S(2)}, u32[]{:S(2)}) collective-permute-start(f32[8,2,128]{2,0,1:T(8,128)S(1)} %get-tuple-element.240), channel_id=1, source_target_pairs={{1,2},{2,1},{3,4},{4,3},{5,6},{6,5},{7,8},{8,7},{9,10},{10,9},{11,... | collective-permute-start | bytes 24584 | tf_op jit(solution)/shard_map/ppermute | solution.py:112
  144.8 9.4 %collective-permute-start.18 = (f32[8,2,128]{2,0,1:T(8,128)S(1)}, f32[8,2,128]{2,0,1:T(8,128)S(1)}, u32[]{:S(2)}, u32[]{:S(2)}) collective-permute-start(f32[8,2,128]{2,0,1:T(8,128)S(1)} %get-tuple-element.242), channel_id=1, source_target_pairs={{0,16},{16,0},{1,17},{17,1},{2,18},{18,2},{3,19},{19,3},{4,20},{20... | collective-permute-start | bytes 24584 | tf_op jit(solution)/shard_map/ppermute | solution.py:112
  144.9 9.7 %collective-permute-start.19 = (f32[8,2,128]{2,0,1:T(8,128)S(1)}, f32[8,2,128]{2,0,1:T(8,128)S(1)}, u32[]{:S(2)}, u32[]{:S(2)}) collective-permute-start(f32[8,2,128]{2,0,1:T(8,128)S(1)} %get-tuple-element.241), channel_id=1, source_target_pairs={{16,32},{32,16},{17,33},{33,17},{18,34},{34,18},{19,35},{35,19},{2... | collective-permute-start | bytes 24584 | tf_op jit(solution)/shard_map/ppermute | solution.py:112
  157.1 18.6 %collective-permute-start.20 = (f32[33,2,128]{2,0,1:T(8,128)S(1)}, f32[33,2,128]{2,0,1:T(8,128)S(1)}, u32[]{:S(2)}, u32[]{:S(2)}) collective-permute-start(f32[33,2,128]{2,0,1:T(8,128)S(1)} %get-tuple-element.227), channel_id=1, source_target_pairs={{0,1},{1,0},{2,3},{3,2},{4,5},{5,4},{6,7},{7,6},{8,9},{9,8},{10,11... | collective-permute-start | bytes 101384 | tf_op jit(solution)/shard_map/ppermute | solution.py:112
  157.2 18.6 %collective-permute-start.21 = (f32[33,2,128]{2,0,1:T(8,128)S(1)}, f32[33,2,128]{2,0,1:T(8,128)S(1)}, u32[]{:S(2)}, u32[]{:S(2)}) collective-permute-start(f32[33,2,128]{2,0,1:T(8,128)S(1)} %get-tuple-element.228), channel_id=1, source_target_pairs={{1,2},{2,1},{3,4},{4,3},{5,6},{6,5},{7,8},{8,7},{9,10},{10,9},{11,... | collective-permute-start | bytes 101384 | tf_op jit(solution)/shard_map/ppermute | solution.py:112
  161.6 14.2 %collective-permute-start.22 = (f32[33,2,128]{2,0,1:T(8,128)S(1)}, f32[33,2,128]{2,0,1:T(8,128)S(1)}, u32[]{:S(2)}, u32[]{:S(2)}) collective-permute-start(f32[33,2,128]{2,0,1:T(8,128)S(1)} %get-tuple-element.230), channel_id=1, source_target_pairs={{0,16},{16,0},{1,17},{17,1},{2,18},{18,2},{3,19},{19,3},{4,20},{20... | collective-permute-start | bytes 101384 | tf_op jit(solution)/shard_map/ppermute | solution.py:112
  161.7 16.1 %collective-permute-start.23 = (f32[33,2,128]{2,0,1:T(8,128)S(1)}, f32[33,2,128]{2,0,1:T(8,128)S(1)}, u32[]{:S(2)}, u32[]{:S(2)}) collective-permute-start(f32[33,2,128]{2,0,1:T(8,128)S(1)} %get-tuple-element.229), channel_id=1, source_target_pairs={{16,32},{32,16},{17,33},{33,17},{18,34},{34,18},{19,35},{35,19},{2... | collective-permute-start | bytes 101384 | tf_op jit(solution)/shard_map/ppermute | solution.py:112
  178.5 3.6 %collective-permute-start.24 = (f32[8,8]{1,0:T(8,128)S(1)}, f32[8,8]{1,0:T(8,128)S(1)}, u32[]{:S(2)}, u32[]{:S(2)}) collective-permute-start(f32[8,8]{1,0:T(8,128)S(1)} %add.333), channel_id=1, source_target_pairs={{0,2},{1,3},{2,0},{3,1},{4,6},{5,7},{6,4},{7,5},{8,10},{9,11},{10,... | collective-permute-start | bytes 776 | tf_op jit(solution)/shard_map/ppermute | solution.py:47
  182.1 4.8 %collective-permute-start.25 = (f32[8,8]{1,0:T(8,128)S(1)}, f32[8,8]{1,0:T(8,128)S(1)}, u32[]{:S(2)}, u32[]{:S(2)}) collective-permute-start(f32[8,8]{1,0:T(8,128)S(1)} %add.334), channel_id=1, source_target_pairs={{0,6},{1,7},{2,4},{3,5},{4,2},{5,3},{6,0},{7,1},{8,14},{9,15},{10,... | collective-permute-start | bytes 776 | tf_op jit(solution)/shard_map/ppermute | solution.py:47
  186.9 3.6 %collective-permute-start.26 = (f32[8,8]{1,0:T(8,128)S(1)}, f32[8,8]{1,0:T(8,128)S(1)}, u32[]{:S(2)}, u32[]{:S(2)}) collective-permute-start(f32[8,8]{1,0:T(8,128)S(1)} %add.335), channel_id=1, source_target_pairs={{0,8},{1,9},{2,10},{3,11},{4,12},{5,13},{6,14},{7,15},{8,0},{9,1},... | collective-permute-start | bytes 776 | tf_op jit(solution)/shard_map/ppermute | solution.py:47
  190.6 10.2 %collective-permute-start.27 = (f32[33,2,128]{2,0,1:T(8,128)S(1)}, f32[33,2,128]{2,0,1:T(8,128)S(1)}, u32[]{:S(2)}, u32[]{:S(2)}) collective-permute-start(f32[33,2,128]{2,0,1:T(8,128)S(1)} %get-tuple-element.221), channel_id=1, source_target_pairs={{0,1},{1,0},{2,3},{3,2},{4,5},{5,4},{6,7},{7,6},{8,9},{9,8},{10,11... | collective-permute-start | bytes 101384 | tf_op jit(solution)/shard_map/ppermute | solution.py:112
  190.7 10.1 %collective-permute-start.28 = (f32[33,2,128]{2,0,1:T(8,128)S(1)}, f32[33,2,128]{2,0,1:T(8,128)S(1)}, u32[]{:S(2)}, u32[]{:S(2)}) collective-permute-start(f32[33,2,128]{2,0,1:T(8,128)S(1)} %get-tuple-element.222), channel_id=1, source_target_pairs={{1,2},{2,1},{3,4},{4,3},{5,6},{6,5},{7,8},{8,7},{9,10},{10,9},{11,... | collective-permute-start | bytes 101384 | tf_op jit(solution)/shard_map/ppermute | solution.py:112
  192.7 8.2 %collective-permute-start.29 = (f32[33,2,128]{2,0,1:T(8,128)S(1)}, f32[33,2,128]{2,0,1:T(8,128)S(1)}, u32[]{:S(2)}, u32[]{:S(2)}) collective-permute-start(f32[33,2,128]{2,0,1:T(8,128)S(1)} %get-tuple-element.224), channel_id=1, source_target_pairs={{0,16},{16,0},{1,17},{17,1},{2,18},{18,2},{3,19},{19,3},{4,20},{20... | collective-permute-start | bytes 101384 | tf_op jit(solution)/shard_map/ppermute | solution.py:112
  192.8 10.0 %collective-permute-start.30 = (f32[33,2,128]{2,0,1:T(8,128)S(1)}, f32[33,2,128]{2,0,1:T(8,128)S(1)}, u32[]{:S(2)}, u32[]{:S(2)}) collective-permute-start(f32[33,2,128]{2,0,1:T(8,128)S(1)} %get-tuple-element.223), channel_id=1, source_target_pairs={{16,32},{32,16},{17,33},{33,17},{18,34},{34,18},{19,35},{35,19},{2... | collective-permute-start | bytes 101384 | tf_op jit(solution)/shard_map/ppermute | solution.py:112
  203.5 6.5 %collective-permute-start.31 = (f32[8,8]{1,0:T(8,128)S(1)}, f32[8,8]{1,0:T(8,128)S(1)}, u32[]{:S(2)}, u32[]{:S(2)}) collective-permute-start(f32[8,8]{1,0:T(8,128)S(1)} %add.339), channel_id=1, source_target_pairs={{0,32},{1,33},{2,34},{3,35},{4,36},{5,37},{6,38},{7,39},{8,40},{9,... | collective-permute-start | bytes 776 | tf_op jit(solution)/shard_map/ppermute | solution.py:47
  210.0 6.0 %collective-permute-start.32 = (f32[8,8]{1,0:T(8,128)S(1)}, f32[8,8]{1,0:T(8,128)S(1)}, u32[]{:S(2)}, u32[]{:S(2)}) collective-permute-start(f32[8,8]{1,0:T(8,128)S(1)} %add.340), channel_id=1, source_target_pairs={{0,64},{1,65},{2,66},{3,67},{4,68},{5,69},{6,70},{7,71},{8,72},{9,... | collective-permute-start | bytes 776 | tf_op jit(solution)/shard_map/ppermute | solution.py:47
  216.0 4.8 %collective-permute-start.33 = (f32[8,8]{1,0:T(8,128)S(1)}, f32[8,8]{1,0:T(8,128)S(1)}, u32[]{:S(2)}, u32[]{:S(2)}) collective-permute-start(f32[8,8]{1,0:T(8,128)S(1)} %add.341), channel_id=1, source_target_pairs={{0,224},{1,225},{2,226},{3,227},{4,228},{5,229},{6,230},{7,231},{8... | collective-permute-start | bytes 776 | tf_op jit(solution)/shard_map/ppermute | solution.py:47
  (5 other events, 15.8 us)

commit v9 on v8

--- a/solution.py
+++ b/solution.py
@@ -86,7 +86,7 @@
     count = lax.axis_size("region")
     me = lax.axis_index("region")
     routes, send_slots, recv_slots = [], [], []
-    for offset, up, down in ((offsets[0], 0, 1), (offsets[2], 2, 3)):
+    for offset, up, down in ((offsets[2], 2, 3), (offsets[0], 0, 1)):
         lower = (me // offset) % 2 == 0
         for phase in (0, 1):
             first = lower if phase == 0 else jnp.logical_not(lower)
@@ -238,7 +238,7 @@
             powers[i + j] = powers[i + j] + (product if i == j else 2.0 * product)
     partial = jnp.concatenate([partial, jnp.stack(powers)])
     if bits == [1, 2, 6, 8, 24, 32, 64, 224] and SWEEPS == 3:
-        plan = [(0, [2, 6, 8]), (2, [32, 64, 224])]
+        plan = [(2, [2, 6, 8]), (0, [32, 64, 224])]
     elif bits is None:
         plan = None
     else:

time: 225 us -> 226 us (level)
  waiting for transfers between devices: 52.7 us -> 77.5 us
  starting transfers between devices: 107 us -> 83.3 us
    ppermute x32, waiting for transfers between devices: 39.1 us -> 59.6 us  [exchange(): lax.ppermute(tiles[j], 'region', routes[j])]
    ppermute x32, starting transfers between devices: 94 us -> 75.8 us  [exchange(): lax.ppermute(tiles[j], 'region', routes[j])]
    ppermute x6, starting transfers between devices: 13.3 us -> 7.51 us  [sum_rounds(): lax.ppermute(value, axis, [(i, i ^ bit) for i in range(count)])]
    ppermute x6, waiting for transfers between devices: 13.6 us -> 17.9 us  [sum_rounds(): lax.ppermute(value, axis, [(i, i ^ bit) for i in range(count)])]
  transfers between devices with their start and end apart: 38 -> 38, of which waited for: 15 -> 19; matrix products, arithmetic and copies ran while one was open for 9% -> 9% of each run, Pallas kernels for 0% -> 0%
where the time goes in v9:
time: 226 us; the launch traced here: 222 us
  starting transfers between devices  83.3 us (37%)
  waiting for transfers between devices  77.5 us (34%)
  matrix products  49.6 us (22%)
  local copies, waits for them, and re-layouts  7.98 us (4%)
  other arithmetic  3.04 us (1%)
    ppermute x32, starting transfers between devices, exchange(): lax.ppermute(tiles[j], 'region', routes[j])  75.8 us
    ppermute x32, waiting for transfers between devices, exchange(): lax.ppermute(tiles[j], 'region', routes[j])  59.6 us
    ppermute x6, waiting for transfers between devices, sum_rounds(): lax.ppermute(value, axis, [(i, i ^ bit) for i in range(count)])  17.9 us
    dot_general x1, matrix products, local(): jnp.einsum('sbh,hk->sbk', gathered, neigh_weight[number], preferred_eleme...  8.9 us
    ppermute x6, starting transfers between devices, sum_rounds(): lax.ppermute(value, axis, [(i, i ^ bit) for i in range(count)])  7.51 us
    dot_general x2, matrix products, local(): jnp.einsum('ij,sjh->sih', mask_half, hidden, preferred_element_type=jnp.f...  6.15 us
    dot_general x2, matrix products, local(): jnp.einsum('ktb,sbh->ksth', pick_half, hidden, preferred_element_type=jnp...  5.97 us
    dot_general x2, matrix products, local(): jnp.einsum('sbh,hk->sbk', hidden, self_weight[number], preferred_element_...  5.34 us
  transfers between devices with their start and end apart: 38, of which 19 were waited for; matrix products, arithmetic and copies ran while one was open for 9% of the time, Pallas kernels for 0%

profile of v9, /device:TPU:4, one launch (start us, length us, event | category | flops | bytes accessed | tf_op | source)
XLA Modules:
  0.0 222.4 jit_solution(8794934417617527949)
XLA Ops:
  2.9 2.9 %convert_bitcast_fusion.1 = bf16[4,8,128,256]{3,2,1,0:T(8,128)(2,1)S(1)} fusion(bf16[8,512,256]{2,1,0:T(8,128)(2,1)} %param.33, s32[4,128]{1,0:T(4,128)S(1)} %broadcast_select_fusion.1, pred[4,128]{1,0:T(4,128)(4,1)S(1)} %broadcast_select_fusion.2), kind=kOutput, calls=%fused_computation.72 | convolution fusion | flops 1075314688 | bytes 4196864 | tf_op jit(solution)/shard_map/ktb,sbh->ksth/dot_general | solution.py:117
  5.8 1.4 slice_bitcast_fusion.13
  7.2 2.2 %collective-permute-start.4 = (bf16[8,128,256]{2,1,0:T(8,128)(2,1)}, bf16[8,128,256]{2,1,0:T(8,128)(2,1)}, u32[]{:S(2)}, u32[]{:S(2)}) collective-permute-start(bf16[8,128,256]{2,1,0:T(8,128)(2,1)} %get-tuple-element.215), channel_id=1, source_target_pairs={{0,16},{16,0},{1,17},{17,1},{2,18},{18,2},{3,19},{19,3},{4,20},{20... | collective-permute-start | bytes 1572872 | tf_op jit(solution)/shard_map/ppermute | solution.py:112
  9.5 4.5 %collective-permute-start.5 = (bf16[8,128,256]{2,1,0:T(8,128)(2,1)}, bf16[8,128,256]{2,1,0:T(8,128)(2,1)}, u32[]{:S(2)}, u32[]{:S(2)}) collective-permute-start(bf16[8,128,256]{2,1,0:T(8,128)(2,1)} %get-tuple-element.218), channel_id=1, source_target_pairs={{16,32},{32,16},{17,33},{33,17},{18,34},{34,18},{19,35},{35,19},{2... | collective-permute-start | bytes 1572872 | tf_op jit(solution)/shard_map/ppermute | solution.py:112
  14.1 1.9 collective-permute-start.7
  16.1 2.7 %fusion.131 = f32[8,512,256]{2,1,0:T(8,128)} fusion(bf16[8,512,256]{2,1,0:T(8,128)(2,1)S(1)} %copy-done.3, bf16[2,256,256]{2,1,0:T(8,128)(2,1)S(1)} %copy-done.5), kind=kOutput, calls=%fused_computation.154 | convolution fusion | flops 536870912 | bytes 6422528 | tf_op jit(solution)/shard_map/sbh,hk->sbk/dot_general | solution.py:122
  18.8 3.0 %copy.81 = bf16[1024,1024]{0,1:T(8,128)(2,1)S(1)} copy(bf16[1024,1024]{1,0:T(8,128)(2,1)} %param.48) | data formatting | bytes 4194304
  22.6 4.9 %fusion.102 = f32[8,256,512]{1,2,0:T(8,128)} fusion(bf16[8,512,256]{2,1,0:T(8,128)(2,1)} %param.33, s32[512,512]{1,0:T(8,128)S(1)} %copy-done.2), kind=kOutput, calls=%fused_computation.111 | convolution fusion | flops 1074003968 | bytes 7340032 | tf_op jit(solution)/shard_map/ij,sjh->sih/dot_general | solution.py:121
  27.5 6.5 %collective-permute-done.4 = bf16[8,128,256]{2,1,0:T(8,128)(2,1)} collective-permute-done((bf16[8,128,256]{2,1,0:T(8,128)(2,1)}, bf16[8,128,256]{2,1,0:T(8,128)(2,1)}, u32[]{:S(2)}, u32[]{:S(2)}) %collective-permute-start.4) | collective-permute-done | bytes 524320 | tf_op jit(solution)/shard_map/ppermute | solution.py:112
  33.9 8.1 %collective-permute-done.7 = bf16[8,128,256]{2,1,0:T(8,128)(2,1)} collective-permute-done((bf16[8,128,256]{2,1,0:T(8,128)(2,1)}, bf16[8,128,256]{2,1,0:T(8,128)(2,1)}, u32[]{:S(2)}, u32[]{:S(2)}) %collective-permute-start.7) | collective-permute-done | bytes 524320 | tf_op jit(solution)/shard_map/ppermute | solution.py:112
  42.0 8.9 %add_convert_fusion.1 = bf16[8,512,256]{2,1,0:T(8,128)(2,1)} fusion(f32[8,512,256]{2,1,0:T(8,128)} %fusion.131, bf16[8,512,256]{2,1,0:T(8,128)(2,1)} %param.33, f32[256]{0:T(256)S(1)} %bitcast.617, f32[8,256,512]{1,2,0:T(8,128)} %fusion.102, bf16[1,8,128,256]{3,2,1,0:T(8,128)(2,1)} %bitcast.23, bf16[1,8,128,256]{3,2,1,0:T(8,128)(2,1)} %bitcast.21, ...), kind=kOutput, calls=%fused_computation.44 | convolution fusion | flops 1626603520 | bytes 14814208 | tf_op jit(solution)/shard_map/sbh,hk->sbk/dot_general | solution.py:131
  50.9 3.1 %convert_bitcast_fusion = bf16[4,8,128,256]{2,3,0,1:T(8,128)(2,1)S(1)} fusion(bf16[8,512,256]{2,1,0:T(8,128)(2,1)} %add_convert_fusion.1, s32[4,128]{1,0:T(4,128)S(1)} %broadcast_select_fusion.1, pred[4,128]{1,0:T(4,128)(4,1)S(1)} %broadcast_select_fusion.2), kind=kOutput, calls=%fused_computation.71 | convolution fusion | flops 1075314688 | bytes 4196864 | tf_op jit(solution)/shard_map/ktb,sbh->ksth/dot_general | solution.py:117
  54.3 6.8 %collective-permute-start.9 = (bf16[8,128,256]{1,2,0:T(8,128)(2,1)S(1)}, bf16[8,128,256]{1,2,0:T(8,128)(2,1)S(1)}, u32[]{:S(2)}, u32[]{:S(2)}) collective-permute-start(bf16[8,128,256]{1,2,0:T(8,128)(2,1)S(1)} %get-tuple-element.212), channel_id=1, source_target_pairs={{16,32},{32,16},{17,33},{33,17},{18,34},{34,18},{19,35},{35,19},{2... | collective-permute-start | bytes 1572872 | tf_op jit(solution)/shard_map/ppermute | solution.py:112
  61.2 2.1 collective-permute-start.11
  63.3 2.7 %fusion.128 = f32[8,512,256]{2,1,0:T(8,128)} fusion(bf16[8,512,256]{2,1,0:T(8,128)(2,1)S(1)} %copy-done.4, bf16[2,256,256]{2,1,0:T(8,128)(2,1)S(1)} %copy-done.5), kind=kOutput, calls=%fused_computation.151 | convolution fusion | flops 536870912 | bytes 6422528 | tf_op jit(solution)/shard_map/sbh,hk->sbk/dot_general | solution.py:122
  67.2 4.5 %collective-permute-done.8 = bf16[8,128,256]{1,2,0:T(8,128)(2,1)S(1)} collective-permute-done((bf16[8,128,256]{1,2,0:T(8,128)(2,1)S(1)}, bf16[8,128,256]{1,2,0:T(8,128)(2,1)S(1)}, u32[]{:S(2)}, u32[]{:S(2)}) %collective-permute-start.8) | collective-permute-done | bytes 524320 | tf_op jit(solution)/shard_map/ppermute | solution.py:112
  71.8 11.3 %collective-permute-done.11 = bf16[8,128,256]{1,2,0:T(8,128)(2,1)S(1)} collective-permute-done((bf16[8,128,256]{1,2,0:T(8,128)(2,1)S(1)}, bf16[8,128,256]{1,2,0:T(8,128)(2,1)S(1)}, u32[]{:S(2)}, u32[]{:S(2)}) %collective-permute-start.11) | collective-permute-done | bytes 524320 | tf_op jit(solution)/shard_map/ppermute | solution.py:112
  83.0 2.6 %fusion.24 = bf16[8,256,512]{1,2,0:T(8,128)(2,1)} fusion(f32[8,256,512]{1,2,0:T(8,128)S(1)} %fusion.104, bf16[1,8,128,256]{2,3,1,0:T(8,128)(2,1)S(1)} %bitcast.621, bf16[1,8,128,256]{2,3,1,0:T(8,128)(2,1)S(1)} %bitcast.620, bf16[1,8,128,256]{2,3,1,0:T(8,128)(2,1)S(1)} %bitcast.619, bf16[1,8,128,256]{2,3,1,0:T(8,128)(2,1)S(1)} %bitcast.618, ...), kind=kOutput, calls=%fused_computation.39 | convolution fusion | flops 1080295424 | bytes 8390656 | tf_op jit(solution)/shard_map/ktb,ksth->sbh/dot_general | solution.py:125
  85.7 5.1 %fusion.74 = f32[8,512,2]{1,2,0:T(2,128)S(1)} fusion(f32[8,512,256]{2,1,0:T(8,128)} %fusion.128, bf16[8,512,256]{2,1,0:T(8,128)(2,1)} %add_convert_fusion.1, bf16[8,256,512]{1,2,0:T(8,128)(2,1)} %fusion.24, f32[256]{0:T(256)S(1)} %bitcast.616, bf16[2,256,256]{2,1,0:T(8,128)(2,1)} %param.39, f32[2]{0:T(128)S(1)} %copy-done.14, bf16[2,256]{1,0:T(2,128)(2,1)S(1)} %copy-done.13), kind=kOutput, calls=%fused_computation.90 | convolution fusion | flops 550510592 | bytes 8554504 | tf_op jit(solution)/shard_map/sbh,ch->scb/dot_general | solution.py:139
  91.6 8.2 %collective-permute-start.13 = (f32[8,2,128]{2,0,1:T(8,128)S(1)}, f32[8,2,128]{2,0,1:T(8,128)S(1)}, u32[]{:S(2)}, u32[]{:S(2)}) collective-permute-start(f32[8,2,128]{2,0,1:T(8,128)S(1)} %get-tuple-element.247), channel_id=1, source_target_pairs={{16,32},{32,16},{17,33},{33,17},{18,34},{34,18},{19,35},{35,19},{2... | collective-permute-start | bytes 24584 | tf_op jit(solution)/shard_map/ppermute | solution.py:112
  99.9 1.9 collective-permute-start.15
  102.9 4.1 %collective-permute-done.15 = f32[8,2,128]{2,0,1:T(8,128)S(1)} collective-permute-done((f32[8,2,128]{2,0,1:T(8,128)S(1)}, f32[8,2,128]{2,0,1:T(8,128)S(1)}, u32[]{:S(2)}, u32[]{:S(2)}) %collective-permute-start.15) | collective-permute-done | bytes 8224 | tf_op jit(solution)/shard_map/ppermute | solution.py:112
  107.7 2.0 fusion.69
  109.7 32.4 %while.17 = (s32[]{:T(128)}, f32[1,8,2,512]{3,1,2,0:T(8,128)S(1)}, f32[512]{0:T(512)S(1)}, f32[512]{0:T(512)S(1)}, f32[1,8,2,512]{3,1,2,0:T(8,128)S(1)}, /*index...) while((s32[]{:T(128)}, f32[1,8,2,512]{3,1,2,0:T(8,128)S(1)}, ...), condition=%wide.region_2.8_spmd.clone, body=%wide.region_1.7_spmd.clone.sunk | while | flops 118824960 | bytes 2630405 | solution.py:187
  110.8 1.9 collective-permute-start
  112.8 4.8 %collective-permute-start.2 = (f32[8,2,128]{2,0,1:T(8,128)S(1)}, f32[8,2,128]{2,0,1:T(8,128)S(1)}, u32[]{:S(2)}, u32[]{:S(2)}) collective-permute-start(f32[8,2,128]{2,0,1:T(8,128)S(1)} %get-tuple-element.317), channel_id=1, source_target_pairs={{16,32},{32,16},{17,33},{33,17},{18,34},{34,18},{19,35},{35,19},{2... | collective-permute-start | bytes 24584 | tf_op jit(solution)/shard_map/while/body/eval_jaxpr/ppermute | solution.py:112
  117.9 2.9 %collective-permute-done.2 = f32[8,2,128]{2,0,1:T(8,128)S(1)} collective-permute-done((f32[8,2,128]{2,0,1:T(8,128)S(1)}, f32[8,2,128]{2,0,1:T(8,128)S(1)}, u32[]{:S(2)}, u32[]{:S(2)}) %collective-permute-start.2) | collective-permute-done | bytes 8224 | tf_op jit(solution)/shard_map/while/body/eval_jaxpr/ppermute | solution.py:112
  120.8 2.1 collective-permute-done.3
  125.5 3.1 %collective-permute-start = (f32[8,2,128]{2,0,1:T(8,128)S(1)}, f32[8,2,128]{2,0,1:T(8,128)S(1)}, u32[]{:S(2)}, u32[]{:S(2)}) collective-permute-start(f32[8,2,128]{2,0,1:T(8,128)S(1)} %get-tuple-element.315), channel_id=1, source_target_pairs={{1,2},{2,1},{3,4},{4,3},{5,6},{6,5},{7,8},{8,7},{9,10},{10,9},{11,... | collective-permute-start | bytes 24584 | tf_op jit(solution)/shard_map/while/body/eval_jaxpr/ppermute | solution.py:112
  128.6 6.8 %collective-permute-start.2 = (f32[8,2,128]{2,0,1:T(8,128)S(1)}, f32[8,2,128]{2,0,1:T(8,128)S(1)}, u32[]{:S(2)}, u32[]{:S(2)}) collective-permute-start(f32[8,2,128]{2,0,1:T(8,128)S(1)} %get-tuple-element.317), channel_id=1, source_target_pairs={{16,32},{32,16},{17,33},{33,17},{18,34},{34,18},{19,35},{35,19},{2... | collective-permute-start | bytes 24584 | tf_op jit(solution)/shard_map/while/body/eval_jaxpr/ppermute | solution.py:112
  135.6 1.5 collective-permute-done.2
  137.1 3.6 %collective-permute-done.3 = f32[8,2,128]{2,0,1:T(8,128)S(1)} collective-permute-done((f32[8,2,128]{2,0,1:T(8,128)S(1)}, f32[8,2,128]{2,0,1:T(8,128)S(1)}, u32[]{:S(2)}, u32[]{:S(2)}) %collective-permute-start.3) | collective-permute-done | bytes 8224 | tf_op jit(solution)/shard_map/while/body/eval_jaxpr/ppermute | solution.py:112
  143.1 6.8 %collective-permute-start.17 = (f32[8,2,128]{2,0,1:T(8,128)S(1)}, f32[8,2,128]{2,0,1:T(8,128)S(1)}, u32[]{:S(2)}, u32[]{:S(2)}) collective-permute-start(f32[8,2,128]{2,0,1:T(8,128)S(1)} %get-tuple-element.240), channel_id=1, source_target_pairs={{16,32},{32,16},{17,33},{33,17},{18,34},{34,18},{19,35},{35,19},{2... | collective-permute-start | bytes 24584 | tf_op jit(solution)/shard_map/ppermute | solution.py:112
  149.9 2.1 collective-permute-start.19
  153.1 4.0 %collective-permute-done.19 = f32[8,2,128]{2,0,1:T(8,128)S(1)} collective-permute-done((f32[8,2,128]{2,0,1:T(8,128)S(1)}, f32[8,2,128]{2,0,1:T(8,128)S(1)}, u32[]{:S(2)}, u32[]{:S(2)}) %collective-permute-start.19) | collective-permute-done | bytes 8224 | tf_op jit(solution)/shard_map/ppermute | solution.py:112
  159.6 8.0 %collective-permute-start.21 = (f32[33,2,128]{2,0,1:T(8,128)S(1)}, f32[33,2,128]{2,0,1:T(8,128)S(1)}, u32[]{:S(2)}, u32[]{:S(2)}) collective-permute-start(f32[33,2,128]{2,0,1:T(8,128)S(1)} %get-tuple-element.228), channel_id=1, source_target_pairs={{16,32},{32,16},{17,33},{33,17},{18,34},{34,18},{19,35},{35,19},{2... | collective-permute-start | bytes 101384 | tf_op jit(solution)/shard_map/ppermute | solution.py:112
  167.8 1.9 collective-permute-start.23
  169.7 5.5 %collective-permute-done.23 = f32[33,2,128]{2,0,1:T(8,128)S(1)} collective-permute-done((f32[33,2,128]{2,0,1:T(8,128)S(1)}, f32[33,2,128]{2,0,1:T(8,128)S(1)}, u32[]{:S(2)}, u32[]{:S(2)}) %collective-permute-start.23) | collective-permute-done | bytes 33824 | tf_op jit(solution)/shard_map/ppermute | solution.py:112
  176.1 3.4 %collective-permute-done.24 = f32[8,8]{1,0:T(8,128)S(1)} collective-permute-done((f32[8,8]{1,0:T(8,128)S(1)}, f32[8,8]{1,0:T(8,128)S(1)}, u32[]{:S(2)}, u32[]{:S(2)}) %collective-permute-start.24) | collective-permute-done | bytes 288 | tf_op jit(solution)/shard_map/ppermute | solution.py:47
  179.5 2.3 %collective-permute-start.25 = (f32[8,8]{1,0:T(8,128)S(1)}, f32[8,8]{1,0:T(8,128)S(1)}, u32[]{:S(2)}, u32[]{:S(2)}) collective-permute-start(f32[8,8]{1,0:T(8,128)S(1)} %add.334), channel_id=1, source_target_pairs={{0,6},{1,7},{2,4},{3,5},{4,2},{5,3},{6,0},{7,1},{8,14},{9,15},{10,... | collective-permute-start | bytes 776 | tf_op jit(solution)/shard_map/ppermute | solution.py:47
  182.3 2.0 collective-permute-done.25
  184.4 4.8 %collective-permute-start.26 = (f32[8,8]{1,0:T(8,128)S(1)}, f32[8,8]{1,0:T(8,128)S(1)}, u32[]{:S(2)}, u32[]{:S(2)}) collective-permute-start(f32[8,8]{1,0:T(8,128)S(1)} %add.335), channel_id=1, source_target_pairs={{0,8},{1,9},{2,10},{3,11},{4,12},{5,13},{6,14},{7,15},{8,0},{9,1},... | collective-permute-start | bytes 776 | tf_op jit(solution)/shard_map/ppermute | solution.py:47
  191.0 9.4 %collective-permute-start.28 = (f32[33,2,128]{2,0,1:T(8,128)S(1)}, f32[33,2,128]{2,0,1:T(8,128)S(1)}, u32[]{:S(2)}, u32[]{:S(2)}) collective-permute-start(f32[33,2,128]{2,0,1:T(8,128)S(1)} %get-tuple-element.222), channel_id=1, source_target_pairs={{16,32},{32,16},{17,33},{33,17},{18,34},{34,18},{19,35},{35,19},{2... | collective-permute-start | bytes 101384 | tf_op jit(solution)/shard_map/ppermute | solution.py:112
  200.5 1.9 collective-permute-start.30
  202.4 5.5 %collective-permute-done.30 = f32[33,2,128]{2,0,1:T(8,128)S(1)} collective-permute-done((f32[33,2,128]{2,0,1:T(8,128)S(1)}, f32[33,2,128]{2,0,1:T(8,128)S(1)}, u32[]{:S(2)}, u32[]{:S(2)}) %collective-permute-start.30) | collective-permute-done | bytes 33824 | tf_op jit(solution)/shard_map/ppermute | solution.py:112
  209.5 2.8 %collective-permute-done.31 = f32[8,8]{1,0:T(8,128)S(1)} collective-permute-done((f32[8,8]{1,0:T(8,128)S(1)}, f32[8,8]{1,0:T(8,128)S(1)}, u32[]{:S(2)}, u32[]{:S(2)}) %collective-permute-start.31) | collective-permute-done | bytes 288 | tf_op jit(solution)/shard_map/ppermute | solution.py:47
  212.6 4.2 %collective-permute-done.32 = f32[8,8]{1,0:T(8,128)S(1)} collective-permute-done((f32[8,8]{1,0:T(8,128)S(1)}, f32[8,8]{1,0:T(8,128)S(1)}, u32[]{:S(2)}, u32[]{:S(2)}) %collective-permute-start.32) | collective-permute-done | bytes 288 | tf_op jit(solution)/shard_map/ppermute | solution.py:47
  216.9 4.7 %collective-permute-done.33 = f32[8,8]{1,0:T(8,128)S(1)} collective-permute-done((f32[8,8]{1,0:T(8,128)S(1)}, f32[8,8]{1,0:T(8,128)S(1)}, u32[]{:S(2)}, u32[]{:S(2)}) %collective-permute-start.33) | collective-permute-done | bytes 288 | tf_op jit(solution)/shard_map/ppermute | solution.py:47
  (181 shorter events, 24.1 us)
Async XLA Ops:
  0.0 22.4 %copy-start = (f32[16,2,512]{2,1,0:T(2,128)S(1)}, f32[16,2,512]{2,1,0:T(2,128)}, u32[]{:S(2)}) copy-start(f32[16,2,512]{2,1,0:T(2,128)} %param.42) | copy-start | bytes 196612
  5.8 10.3 %copy-start.3 = (bf16[8,512,256]{2,1,0:T(8,128)(2,1)S(1)}, bf16[8,512,256]{2,1,0:T(8,128)(2,1)}, u32[]{:S(2)}) copy-start(bf16[8,512,256]{2,1,0:T(8,128)(2,1)} %param.33) | copy-start | bytes 6291460
  5.8 10.3 %copy-start.5 = (bf16[2,256,256]{2,1,0:T(8,128)(2,1)S(1)}, bf16[2,256,256]{2,1,0:T(8,128)(2,1)}, u32[]{:S(2)}) copy-start(bf16[2,256,256]{2,1,0:T(8,128)(2,1)} %param.38) | copy-start | bytes 786436
  7.2 26.7 %collective-permute-start.4 = (bf16[8,128,256]{2,1,0:T(8,128)(2,1)}, bf16[8,128,256]{2,1,0:T(8,128)(2,1)}, u32[]{:S(2)}, u32[]{:S(2)}) collective-permute-start(bf16[8,128,256]{2,1,0:T(8,128)(2,1)} %get-tuple-element.215), channel_id=1, source_target_pairs={{0,16},{16,0},{1,17},{17,1},{2,18},{18,2},{3,19},{19,3},{4,20},{20... | collective-permute-start | bytes 1572872 | tf_op jit(solution)/shard_map/ppermute | solution.py:112
  9.5 24.5 %collective-permute-start.5 = (bf16[8,128,256]{2,1,0:T(8,128)(2,1)}, bf16[8,128,256]{2,1,0:T(8,128)(2,1)}, u32[]{:S(2)}, u32[]{:S(2)}) collective-permute-start(bf16[8,128,256]{2,1,0:T(8,128)(2,1)} %get-tuple-element.218), channel_id=1, source_target_pairs={{16,32},{32,16},{17,33},{33,17},{18,34},{34,18},{19,35},{35,19},{2... | collective-permute-start | bytes 1572872 | tf_op jit(solution)/shard_map/ppermute | solution.py:112
  14.0 19.9 %collective-permute-start.6 = (bf16[8,128,256]{2,1,0:T(8,128)(2,1)}, bf16[8,128,256]{2,1,0:T(8,128)(2,1)}, u32[]{:S(2)}, u32[]{:S(2)}) collective-permute-start(bf16[8,128,256]{2,1,0:T(8,128)(2,1)} %get-tuple-element.217), channel_id=1, source_target_pairs={{0,1},{1,0},{2,3},{3,2},{4,5},{5,4},{6,7},{7,6},{8,9},{9,8},{10,11... | collective-permute-start | bytes 1572872 | tf_op jit(solution)/shard_map/ppermute | solution.py:112
  14.1 27.9 %collective-permute-start.7 = (bf16[8,128,256]{2,1,0:T(8,128)(2,1)}, bf16[8,128,256]{2,1,0:T(8,128)(2,1)}, u32[]{:S(2)}, u32[]{:S(2)}) collective-permute-start(bf16[8,128,256]{2,1,0:T(8,128)(2,1)} %get-tuple-element.216), channel_id=1, source_target_pairs={{1,2},{2,1},{3,4},{4,3},{5,6},{6,5},{7,8},{8,7},{9,10},{10,9},{11,... | collective-permute-start | bytes 1572872 | tf_op jit(solution)/shard_map/ppermute | solution.py:112
  18.8 3.8 %copy-start.2 = (s32[512,512]{1,0:T(8,128)S(1)}, s32[512,512]{1,0:T(8,128)}, u32[]{:S(2)}) copy-start(s32[512,512]{1,0:T(8,128)} %param.34) | copy-start | bytes 3145732
  54.0 9.3 %copy-start.4 = (bf16[8,512,256]{2,1,0:T(8,128)(2,1)S(1)}, bf16[8,512,256]{2,1,0:T(8,128)(2,1)}, u32[]{:S(2)}) copy-start(bf16[8,512,256]{2,1,0:T(8,128)(2,1)} %add_convert_fusion.1) | copy-start | bytes 6291460
  54.2 17.6 %collective-permute-start.8 = (bf16[8,128,256]{1,2,0:T(8,128)(2,1)S(1)}, bf16[8,128,256]{1,2,0:T(8,128)(2,1)S(1)}, u32[]{:S(2)}, u32[]{:S(2)}) collective-permute-start(bf16[8,128,256]{1,2,0:T(8,128)(2,1)S(1)} %get-tuple-element.211), channel_id=1, source_target_pairs={{0,16},{16,0},{1,17},{17,1},{2,18},{18,2},{3,19},{19,3},{4,20},{20... | collective-permute-start | bytes 1572872 | tf_op jit(solution)/shard_map/ppermute | solution.py:112
  54.3 17.5 %collective-permute-start.9 = (bf16[8,128,256]{1,2,0:T(8,128)(2,1)S(1)}, bf16[8,128,256]{1,2,0:T(8,128)(2,1)S(1)}, u32[]{:S(2)}, u32[]{:S(2)}) collective-permute-start(bf16[8,128,256]{1,2,0:T(8,128)(2,1)S(1)} %get-tuple-element.212), channel_id=1, source_target_pairs={{16,32},{32,16},{17,33},{33,17},{18,34},{34,18},{19,35},{35,19},{2... | collective-permute-start | bytes 1572872 | tf_op jit(solution)/shard_map/ppermute | solution.py:112
  61.1 10.7 %collective-permute-start.10 = (bf16[8,128,256]{1,2,0:T(8,128)(2,1)S(1)}, bf16[8,128,256]{1,2,0:T(8,128)(2,1)S(1)}, u32[]{:S(2)}, u32[]{:S(2)}) collective-permute-start(bf16[8,128,256]{1,2,0:T(8,128)(2,1)S(1)} %get-tuple-element.214), channel_id=1, source_target_pairs={{0,1},{1,0},{2,3},{3,2},{4,5},{5,4},{6,7},{7,6},{8,9},{9,8},{10,11... | collective-permute-start | bytes 1572872 | tf_op jit(solution)/shard_map/ppermute | solution.py:112
  61.2 21.9 %collective-permute-start.11 = (bf16[8,128,256]{1,2,0:T(8,128)(2,1)S(1)}, bf16[8,128,256]{1,2,0:T(8,128)(2,1)S(1)}, u32[]{:S(2)}, u32[]{:S(2)}) collective-permute-start(bf16[8,128,256]{1,2,0:T(8,128)(2,1)S(1)} %get-tuple-element.213), channel_id=1, source_target_pairs={{1,2},{2,1},{3,4},{4,3},{5,6},{6,5},{7,8},{8,7},{9,10},{10,9},{11,... | collective-permute-start | bytes 1572872 | tf_op jit(solution)/shard_map/ppermute | solution.py:112
  85.7 17.1 %copy-start.9 = (f32[512]{0:T(512)S(1)}, f32[512]{0:T(512)}, u32[]{:S(2)}) copy-start(f32[512]{0:T(512)} %param.47) | copy-start | bytes 6148
  85.7 17.1 %copy-start.10 = (f32[512]{0:T(512)S(1)}, f32[512]{0:T(512)}, u32[]{:S(2)}) copy-start(f32[512]{0:T(512)} %param.44) | copy-start | bytes 6148
  90.8 16.7 %copy-start.6 = (f32[512]{0:T(512)S(1)}, f32[512]{0:T(512)}, u32[]{:S(2)}) copy-start(f32[512]{0:T(512)} %param.46) | copy-start | bytes 6148
  90.8 16.7 %copy-start.7 = (f32[512]{0:T(512)S(1)}, f32[512]{0:T(512)}, u32[]{:S(2)}) copy-start(f32[512]{0:T(512)} %param.45) | copy-start | bytes 6148
  91.5 11.3 %collective-permute-start.12 = (f32[8,2,128]{2,0,1:T(8,128)S(1)}, f32[8,2,128]{2,0,1:T(8,128)S(1)}, u32[]{:S(2)}, u32[]{:S(2)}) collective-permute-start(f32[8,2,128]{2,0,1:T(8,128)S(1)} %get-tuple-element.246), channel_id=1, source_target_pairs={{0,16},{16,0},{1,17},{17,1},{2,18},{18,2},{3,19},{19,3},{4,20},{20... | collective-permute-start | bytes 24584 | tf_op jit(solution)/shard_map/ppermute | solution.py:112
  91.6 11.3 %collective-permute-start.13 = (f32[8,2,128]{2,0,1:T(8,128)S(1)}, f32[8,2,128]{2,0,1:T(8,128)S(1)}, u32[]{:S(2)}, u32[]{:S(2)}) collective-permute-start(f32[8,2,128]{2,0,1:T(8,128)S(1)} %get-tuple-element.247), channel_id=1, source_target_pairs={{16,32},{32,16},{17,33},{33,17},{18,34},{34,18},{19,35},{35,19},{2... | collective-permute-start | bytes 24584 | tf_op jit(solution)/shard_map/ppermute | solution.py:112
  99.8 3.1 %collective-permute-start.14 = (f32[8,2,128]{2,0,1:T(8,128)S(1)}, f32[8,2,128]{2,0,1:T(8,128)S(1)}, u32[]{:S(2)}, u32[]{:S(2)}) collective-permute-start(f32[8,2,128]{2,0,1:T(8,128)S(1)} %get-tuple-element.249), channel_id=1, source_target_pairs={{0,1},{1,0},{2,3},{3,2},{4,5},{5,4},{6,7},{7,6},{8,9},{9,8},{10,11... | collective-permute-start | bytes 24584 | tf_op jit(solution)/shard_map/ppermute | solution.py:112
  99.9 7.1 %collective-permute-start.15 = (f32[8,2,128]{2,0,1:T(8,128)S(1)}, f32[8,2,128]{2,0,1:T(8,128)S(1)}, u32[]{:S(2)}, u32[]{:S(2)}) collective-permute-start(f32[8,2,128]{2,0,1:T(8,128)S(1)} %get-tuple-element.248), channel_id=1, source_target_pairs={{1,2},{2,1},{3,4},{4,3},{5,6},{6,5},{7,8},{8,7},{9,10},{10,9},{11,... | collective-permute-start | bytes 24584 | tf_op jit(solution)/shard_map/ppermute | solution.py:112
  110.8 7.1 %collective-permute-start = (f32[8,2,128]{2,0,1:T(8,128)S(1)}, f32[8,2,128]{2,0,1:T(8,128)S(1)}, u32[]{:S(2)}, u32[]{:S(2)}) collective-permute-start(f32[8,2,128]{2,0,1:T(8,128)S(1)} %get-tuple-element.315), channel_id=1, source_target_pairs={{1,2},{2,1},{3,4},{4,3},{5,6},{6,5},{7,8},{8,7},{9,10},{10,9},{11,... | collective-permute-start | bytes 24584 | tf_op jit(solution)/shard_map/while/body/eval_jaxpr/ppermute | solution.py:112
  112.7 5.2 %collective-permute-start.1 = (f32[8,2,128]{2,0,1:T(8,128)S(1)}, f32[8,2,128]{2,0,1:T(8,128)S(1)}, u32[]{:S(2)}, u32[]{:S(2)}) collective-permute-start(f32[8,2,128]{2,0,1:T(8,128)S(1)} %get-tuple-element.316), channel_id=1, source_target_pairs={{0,1},{1,0},{2,3},{3,2},{4,5},{5,4},{6,7},{7,6},{8,9},{9,8},{10,11... | collective-permute-start | bytes 24584 | tf_op jit(solution)/shard_map/while/body/eval_jaxpr/ppermute | solution.py:112
  112.8 7.9 %collective-permute-start.2 = (f32[8,2,128]{2,0,1:T(8,128)S(1)}, f32[8,2,128]{2,0,1:T(8,128)S(1)}, u32[]{:S(2)}, u32[]{:S(2)}) collective-permute-start(f32[8,2,128]{2,0,1:T(8,128)S(1)} %get-tuple-element.317), channel_id=1, source_target_pairs={{16,32},{32,16},{17,33},{33,17},{18,34},{34,18},{19,35},{35,19},{2... | collective-permute-start | bytes 24584 | tf_op jit(solution)/shard_map/while/body/eval_jaxpr/ppermute | solution.py:112
  117.7 5.2 %collective-permute-start.3 = (f32[8,2,128]{2,0,1:T(8,128)S(1)}, f32[8,2,128]{2,0,1:T(8,128)S(1)}, u32[]{:S(2)}, u32[]{:S(2)}) collective-permute-start(f32[8,2,128]{2,0,1:T(8,128)S(1)} %get-tuple-element.318), channel_id=1, source_target_pairs={{0,16},{16,0},{1,17},{17,1},{2,18},{18,2},{3,19},{19,3},{4,20},{20... | collective-permute-start | bytes 24584 | tf_op jit(solution)/shard_map/while/body/eval_jaxpr/ppermute | solution.py:112
  125.5 10.1 %collective-permute-start = (f32[8,2,128]{2,0,1:T(8,128)S(1)}, f32[8,2,128]{2,0,1:T(8,128)S(1)}, u32[]{:S(2)}, u32[]{:S(2)}) collective-permute-start(f32[8,2,128]{2,0,1:T(8,128)S(1)} %get-tuple-element.315), channel_id=1, source_target_pairs={{1,2},{2,1},{3,4},{4,3},{5,6},{6,5},{7,8},{8,7},{9,10},{10,9},{11,... | collective-permute-start | bytes 24584 | tf_op jit(solution)/shard_map/while/body/eval_jaxpr/ppermute | solution.py:112
  128.5 7.0 %collective-permute-start.1 = (f32[8,2,128]{2,0,1:T(8,128)S(1)}, f32[8,2,128]{2,0,1:T(8,128)S(1)}, u32[]{:S(2)}, u32[]{:S(2)}) collective-permute-start(f32[8,2,128]{2,0,1:T(8,128)S(1)} %get-tuple-element.316), channel_id=1, source_target_pairs={{0,1},{1,0},{2,3},{3,2},{4,5},{5,4},{6,7},{7,6},{8,9},{9,8},{10,11... | collective-permute-start | bytes 24584 | tf_op jit(solution)/shard_map/while/body/eval_jaxpr/ppermute | solution.py:112
  128.6 8.4 %collective-permute-start.2 = (f32[8,2,128]{2,0,1:T(8,128)S(1)}, f32[8,2,128]{2,0,1:T(8,128)S(1)}, u32[]{:S(2)}, u32[]{:S(2)}) collective-permute-start(f32[8,2,128]{2,0,1:T(8,128)S(1)} %get-tuple-element.317), channel_id=1, source_target_pairs={{16,32},{32,16},{17,33},{33,17},{18,34},{34,18},{19,35},{35,19},{2... | collective-permute-start | bytes 24584 | tf_op jit(solution)/shard_map/while/body/eval_jaxpr/ppermute | solution.py:112
  135.4 5.2 %collective-permute-start.3 = (f32[8,2,128]{2,0,1:T(8,128)S(1)}, f32[8,2,128]{2,0,1:T(8,128)S(1)}, u32[]{:S(2)}, u32[]{:S(2)}) collective-permute-start(f32[8,2,128]{2,0,1:T(8,128)S(1)} %get-tuple-element.318), channel_id=1, source_target_pairs={{0,16},{16,0},{1,17},{17,1},{2,18},{18,2},{3,19},{19,3},{4,20},{20... | collective-permute-start | bytes 24584 | tf_op jit(solution)/shard_map/while/body/eval_jaxpr/ppermute | solution.py:112
  142.1 16.1 %copy-start.1 = (bf16[1024,1024]{1,0:T(8,128)(2,1)S(1)}, bf16[1024,1024]{1,0:T(8,128)(2,1)}, u32[]{:S(2)}) copy-start(bf16[1024,1024]{1,0:T(8,128)(2,1)} %param.48) | copy-start | bytes 6291460
  143.0 10.1 %collective-permute-start.16 = (f32[8,2,128]{2,0,1:T(8,128)S(1)}, f32[8,2,128]{2,0,1:T(8,128)S(1)}, u32[]{:S(2)}, u32[]{:S(2)}) collective-permute-start(f32[8,2,128]{2,0,1:T(8,128)S(1)} %get-tuple-element.239), channel_id=1, source_target_pairs={{0,16},{16,0},{1,17},{17,1},{2,18},{18,2},{3,19},{19,3},{4,20},{20... | collective-permute-start | bytes 24584 | tf_op jit(solution)/shard_map/ppermute | solution.py:112
  143.1 10.0 %collective-permute-start.17 = (f32[8,2,128]{2,0,1:T(8,128)S(1)}, f32[8,2,128]{2,0,1:T(8,128)S(1)}, u32[]{:S(2)}, u32[]{:S(2)}) collective-permute-start(f32[8,2,128]{2,0,1:T(8,128)S(1)} %get-tuple-element.240), channel_id=1, source_target_pairs={{16,32},{32,16},{17,33},{33,17},{18,34},{34,18},{19,35},{35,19},{2... | collective-permute-start | bytes 24584 | tf_op jit(solution)/shard_map/ppermute | solution.py:112
  149.8 3.2 %collective-permute-start.18 = (f32[8,2,128]{2,0,1:T(8,128)S(1)}, f32[8,2,128]{2,0,1:T(8,128)S(1)}, u32[]{:S(2)}, u32[]{:S(2)}) collective-permute-start(f32[8,2,128]{2,0,1:T(8,128)S(1)} %get-tuple-element.242), channel_id=1, source_target_pairs={{0,1},{1,0},{2,3},{3,2},{4,5},{5,4},{6,7},{7,6},{8,9},{9,8},{10,11... | collective-permute-start | bytes 24584 | tf_op jit(solution)/shard_map/ppermute | solution.py:112
  149.9 7.1 %collective-permute-start.19 = (f32[8,2,128]{2,0,1:T(8,128)S(1)}, f32[8,2,128]{2,0,1:T(8,128)S(1)}, u32[]{:S(2)}, u32[]{:S(2)}) collective-permute-start(f32[8,2,128]{2,0,1:T(8,128)S(1)} %get-tuple-element.241), channel_id=1, source_target_pairs={{1,2},{2,1},{3,4},{4,3},{5,6},{6,5},{7,8},{8,7},{9,10},{10,9},{11,... | collective-permute-start | bytes 24584 | tf_op jit(solution)/shard_map/ppermute | solution.py:112
  159.5 10.2 %collective-permute-start.20 = (f32[33,2,128]{2,0,1:T(8,128)S(1)}, f32[33,2,128]{2,0,1:T(8,128)S(1)}, u32[]{:S(2)}, u32[]{:S(2)}) collective-permute-start(f32[33,2,128]{2,0,1:T(8,128)S(1)} %get-tuple-element.227), channel_id=1, source_target_pairs={{0,16},{16,0},{1,17},{17,1},{2,18},{18,2},{3,19},{19,3},{4,20},{20... | collective-permute-start | bytes 101384 | tf_op jit(solution)/shard_map/ppermute | solution.py:112
  159.6 10.1 %collective-permute-start.21 = (f32[33,2,128]{2,0,1:T(8,128)S(1)}, f32[33,2,128]{2,0,1:T(8,128)S(1)}, u32[]{:S(2)}, u32[]{:S(2)}) collective-permute-start(f32[33,2,128]{2,0,1:T(8,128)S(1)} %get-tuple-element.228), channel_id=1, source_target_pairs={{16,32},{32,16},{17,33},{33,17},{18,34},{34,18},{19,35},{35,19},{2... | collective-permute-start | bytes 101384 | tf_op jit(solution)/shard_map/ppermute | solution.py:112
  167.7 2.1 collective-permute-start.22
  167.8 7.4 %collective-permute-start.23 = (f32[33,2,128]{2,0,1:T(8,128)S(1)}, f32[33,2,128]{2,0,1:T(8,128)S(1)}, u32[]{:S(2)}, u32[]{:S(2)}) collective-permute-start(f32[33,2,128]{2,0,1:T(8,128)S(1)} %get-tuple-element.229), channel_id=1, source_target_pairs={{1,2},{2,1},{3,4},{4,3},{5,6},{6,5},{7,8},{8,7},{9,10},{10,9},{11,... | collective-permute-start | bytes 101384 | tf_op jit(solution)/shard_map/ppermute | solution.py:112
  175.9 3.6 %collective-permute-start.24 = (f32[8,8]{1,0:T(8,128)S(1)}, f32[8,8]{1,0:T(8,128)S(1)}, u32[]{:S(2)}, u32[]{:S(2)}) collective-permute-start(f32[8,8]{1,0:T(8,128)S(1)} %add.333), channel_id=1, source_target_pairs={{0,2},{1,3},{2,0},{3,1},{4,6},{5,7},{6,4},{7,5},{8,10},{9,11},{10,... | collective-permute-start | bytes 776 | tf_op jit(solution)/shard_map/ppermute | solution.py:47
  179.5 4.8 %collective-permute-start.25 = (f32[8,8]{1,0:T(8,128)S(1)}, f32[8,8]{1,0:T(8,128)S(1)}, u32[]{:S(2)}, u32[]{:S(2)}) collective-permute-start(f32[8,8]{1,0:T(8,128)S(1)} %add.334), channel_id=1, source_target_pairs={{0,6},{1,7},{2,4},{3,5},{4,2},{5,3},{6,0},{7,1},{8,14},{9,15},{10,... | collective-permute-start | bytes 776 | tf_op jit(solution)/shard_map/ppermute | solution.py:47
  184.4 6.4 %collective-permute-start.26 = (f32[8,8]{1,0:T(8,128)S(1)}, f32[8,8]{1,0:T(8,128)S(1)}, u32[]{:S(2)}, u32[]{:S(2)}) collective-permute-start(f32[8,8]{1,0:T(8,128)S(1)} %add.335), channel_id=1, source_target_pairs={{0,8},{1,9},{2,10},{3,11},{4,12},{5,13},{6,14},{7,15},{8,0},{9,1},... | collective-permute-start | bytes 776 | tf_op jit(solution)/shard_map/ppermute | solution.py:47
  190.9 11.5 %collective-permute-start.27 = (f32[33,2,128]{2,0,1:T(8,128)S(1)}, f32[33,2,128]{2,0,1:T(8,128)S(1)}, u32[]{:S(2)}, u32[]{:S(2)}) collective-permute-start(f32[33,2,128]{2,0,1:T(8,128)S(1)} %get-tuple-element.221), channel_id=1, source_target_pairs={{0,16},{16,0},{1,17},{17,1},{2,18},{18,2},{3,19},{19,3},{4,20},{20... | collective-permute-start | bytes 101384 | tf_op jit(solution)/shard_map/ppermute | solution.py:112
  191.0 11.4 %collective-permute-start.28 = (f32[33,2,128]{2,0,1:T(8,128)S(1)}, f32[33,2,128]{2,0,1:T(8,128)S(1)}, u32[]{:S(2)}, u32[]{:S(2)}) collective-permute-start(f32[33,2,128]{2,0,1:T(8,128)S(1)} %get-tuple-element.222), channel_id=1, source_target_pairs={{16,32},{32,16},{17,33},{33,17},{18,34},{34,18},{19,35},{35,19},{2... | collective-permute-start | bytes 101384 | tf_op jit(solution)/shard_map/ppermute | solution.py:112
  200.4 2.1 collective-permute-start.29
  200.5 7.4 %collective-permute-start.30 = (f32[33,2,128]{2,0,1:T(8,128)S(1)}, f32[33,2,128]{2,0,1:T(8,128)S(1)}, u32[]{:S(2)}, u32[]{:S(2)}) collective-permute-start(f32[33,2,128]{2,0,1:T(8,128)S(1)} %get-tuple-element.223), channel_id=1, source_target_pairs={{1,2},{2,1},{3,4},{4,3},{5,6},{6,5},{7,8},{8,7},{9,10},{10,9},{11,... | collective-permute-start | bytes 101384 | tf_op jit(solution)/shard_map/ppermute | solution.py:112
  208.6 3.6 %collective-permute-start.31 = (f32[8,8]{1,0:T(8,128)S(1)}, f32[8,8]{1,0:T(8,128)S(1)}, u32[]{:S(2)}, u32[]{:S(2)}) collective-permute-start(f32[8,8]{1,0:T(8,128)S(1)} %add.339), channel_id=1, source_target_pairs={{0,32},{1,33},{2,34},{3,35},{4,36},{5,37},{6,38},{7,39},{8,40},{9,... | collective-permute-start | bytes 776 | tf_op jit(solution)/shard_map/ppermute | solution.py:47
  212.3 4.5 %collective-permute-start.32 = (f32[8,8]{1,0:T(8,128)S(1)}, f32[8,8]{1,0:T(8,128)S(1)}, u32[]{:S(2)}, u32[]{:S(2)}) collective-permute-start(f32[8,8]{1,0:T(8,128)S(1)} %add.340), channel_id=1, source_target_pairs={{0,64},{1,65},{2,66},{3,67},{4,68},{5,69},{6,70},{7,71},{8,72},{9,... | collective-permute-start | bytes 776 | tf_op jit(solution)/shard_map/ppermute | solution.py:47
  216.8 4.8 %collective-permute-start.33 = (f32[8,8]{1,0:T(8,128)S(1)}, f32[8,8]{1,0:T(8,128)S(1)}, u32[]{:S(2)}, u32[]{:S(2)}) collective-permute-start(f32[8,8]{1,0:T(8,128)S(1)} %add.341), channel_id=1, source_target_pairs={{0,224},{1,225},{2,226},{3,227},{4,228},{5,229},{6,230},{7,231},{8... | collective-permute-start | bytes 776 | tf_op jit(solution)/shard_map/ppermute | solution.py:47
  (5 other events, 15.7 us)

commit v10 on v7

--- a/solution.py
+++ b/solution.py
@@ -122,8 +122,12 @@
         own = jnp.einsum(
             "sbh,hk->sbk", hidden, self_weight[number], preferred_element_type=jnp.float32
         )
+        arrived = jnp.transpose(incoming, (1, 0, 2, 3)).reshape(scenarios, -1, width)
         border = jnp.einsum(
-            "ktb,ksth->sbh", place_half, incoming, preferred_element_type=jnp.float32
+            "rb,srh->sbh",
+            place_half.reshape(-1, buses),
+            arrived,
+            preferred_element_type=jnp.float32,
         )
         gathered = (0.25 * (inside + border)).astype(jnp.bfloat16)
         summed = (

time: 224 us -> 224 us (level)
  no operation moved by 1% of the time
where the time goes in v10:
time: 224 us; the launch traced here: 220 us
  starting transfers between devices  113 us (50%)
  waiting for transfers between devices  55.2 us (25%)
  matrix products  43.3 us (19%)
  local copies, waits for them, and re-layouts  5 us (2%)
  other arithmetic  3.14 us (1%)
    ppermute x32, starting transfers between devices, exchange(): lax.ppermute(tiles[j], 'region', routes[j])  97.1 us
    ppermute x32, waiting for transfers between devices, exchange(): lax.ppermute(tiles[j], 'region', routes[j])  41.9 us
    ppermute x6, starting transfers between devices, sum_rounds(): lax.ppermute(value, axis, [(i, i ^ bit) for i in range(count)])  15.7 us
    ppermute x6, waiting for transfers between devices, sum_rounds(): lax.ppermute(value, axis, [(i, i ^ bit) for i in range(count)])  13.3 us
    dot_general x1, matrix products, local(): jnp.einsum('sbh,hk->sbk', gathered, neigh_weight[number], preferred_eleme...  8.29 us
    dot_general x2, matrix products, local(): jnp.einsum('ktb,sbh->ksth', pick_half, hidden, preferred_element_type=jnp...  5.96 us
    dot_general x2, matrix products, local(): jnp.einsum('sbh,hk->sbk', hidden, self_weight[number], preferred_element_...  5.34 us
    dot_general x2, matrix products, local(): jnp.einsum('ij,sjh->sih', mask_half, hidden, preferred_element_type=jnp.f...  4.53 us
  transfers between devices with their start and end apart: 38, of which 14 were waited for; matrix products, arithmetic and copies ran while one was open for 6% of the time, Pallas kernels for 0%

profile of v10, /device:TPU:4, one launch (start us, length us, event | category | flops | bytes accessed | tf_op | source)
XLA Modules:
  0.0 220.4 jit_solution(14313877435781397404)
XLA Ops:
  1.6 1.2 gather_fusion.1
  2.9 2.9 %convert_bitcast_fusion.1 = bf16[4,8,128,256]{3,2,1,0:T(8,128)(2,1)S(1)} fusion(bf16[8,512,256]{2,1,0:T(8,128)(2,1)} %param.31, s32[4,128]{1,0:T(4,128)S(1)} %broadcast_select_fusion.1, pred[4,128]{1,0:T(4,128)(4,1)S(1)} %broadcast_select_fusion.2), kind=kOutput, calls=%fused_computation.42 | convolution fusion | flops 1075314688 | bytes 4196864 | tf_op jit(solution)/shard_map/ktb,sbh->ksth/dot_general | solution.py:117
  5.8 1.4 slice_bitcast_fusion.7
  7.2 5.0 %collective-permute-start.1 = (bf16[8,128,256]{2,1,0:T(8,128)(2,1)}, bf16[8,128,256]{2,1,0:T(8,128)(2,1)}, u32[]{:S(2)}, u32[]{:S(2)}) collective-permute-start(bf16[8,128,256]{2,1,0:T(8,128)(2,1)} %get-tuple-element.109), channel_id=1, source_target_pairs={{1,2},{2,1},{3,4},{4,3},{5,6},{6,5},{7,8},{8,7},{9,10},{10,9},{11,... | collective-permute-start | bytes 1572872 | tf_op jit(solution)/shard_map/ppermute | solution.py:112
  12.3 6.8 %collective-permute-start.3 = (bf16[8,128,256]{2,1,0:T(8,128)(2,1)}, bf16[8,128,256]{2,1,0:T(8,128)(2,1)}, u32[]{:S(2)}, u32[]{:S(2)}) collective-permute-start(bf16[8,128,256]{2,1,0:T(8,128)(2,1)} %get-tuple-element.107), channel_id=1, source_target_pairs={{16,32},{32,16},{17,33},{33,17},{18,34},{34,18},{19,35},{35,19},{2... | collective-permute-start | bytes 1572872 | tf_op jit(solution)/shard_map/ppermute | solution.py:112
  19.2 2.7 %fusion.110 = f32[8,512,256]{2,1,0:T(8,128)} fusion(bf16[8,512,256]{2,1,0:T(8,128)(2,1)S(1)} %copy-done.3, bf16[2,256,256]{2,1,0:T(8,128)(2,1)S(1)} %copy-done.5), kind=kOutput, calls=%fused_computation.133 | convolution fusion | flops 536870912 | bytes 6422528 | tf_op jit(solution)/shard_map/sbh,hk->sbk/dot_general | solution.py:122
  22.7 3.3 %fusion.84 = f32[8,256,512]{1,2,0:T(8,128)} fusion(bf16[8,512,256]{2,1,0:T(8,128)(2,1)S(1)} %copy-done.3, s32[512,512]{1,0:T(8,128)S(1)} %copy-done.2), kind=kOutput, calls=%fused_computation.88 | convolution fusion | flops 1074003968 | bytes 7340032 | tf_op jit(solution)/shard_map/ij,sjh->sih/dot_general | solution.py:121
  26.0 16.7 %collective-permute-done.1 = bf16[8,128,256]{2,1,0:T(8,128)(2,1)} collective-permute-done((bf16[8,128,256]{2,1,0:T(8,128)(2,1)}, bf16[8,128,256]{2,1,0:T(8,128)(2,1)}, u32[]{:S(2)}, u32[]{:S(2)}) %collective-permute-start.1) | collective-permute-done | bytes 524320 | tf_op jit(solution)/shard_map/ppermute | solution.py:112
  42.7 8.3 %add_convert_fusion.1 = bf16[8,512,256]{2,1,0:T(8,128)(2,1)} fusion(f32[8,512,256]{2,1,0:T(8,128)} %fusion.110, bf16[8,512,256]{2,1,0:T(8,128)(2,1)S(1)} %copy-done.3, f32[256]{0:T(256)S(1)} %bitcast.609, f32[8,256,512]{1,2,0:T(8,128)} %fusion.84, bf16[1,8,128,256]{3,2,1,0:T(8,128)(2,1)} %bitcast.23, bf16[1,8,128,256]{3,2,1,0:T(8,128)(2,1)} %bitcast.21, ...), kind=kOutput, calls=%fused_computation.10 | convolution fusion | flops 1626603520 | bytes 14814208 | tf_op jit(solution)/shard_map/sbh,hk->sbk/dot_general | solution.py:135
  51.0 3.1 %convert_bitcast_fusion = bf16[4,8,128,256]{2,3,0,1:T(8,128)(2,1)S(1)} fusion(bf16[8,512,256]{2,1,0:T(8,128)(2,1)} %add_convert_fusion.1, s32[4,128]{1,0:T(4,128)S(1)} %broadcast_select_fusion.1, pred[4,128]{1,0:T(4,128)(4,1)S(1)} %broadcast_select_fusion.2), kind=kOutput, calls=%fused_computation.41 | convolution fusion | flops 1075314688 | bytes 4196864 | tf_op jit(solution)/shard_map/ktb,sbh->ksth/dot_general | solution.py:117
  54.4 2.1 collective-permute-start.5
  56.5 6.9 %collective-permute-start.7 = (bf16[8,128,256]{1,2,0:T(8,128)(2,1)S(1)}, bf16[8,128,256]{1,2,0:T(8,128)(2,1)S(1)}, u32[]{:S(2)}, u32[]{:S(2)}) collective-permute-start(bf16[8,128,256]{1,2,0:T(8,128)(2,1)S(1)} %get-tuple-element.104), channel_id=1, source_target_pairs={{16,32},{32,16},{17,33},{33,17},{18,34},{34,18},{19,35},{35,19},{2... | collective-permute-start | bytes 1572872 | tf_op jit(solution)/shard_map/ppermute | solution.py:112
  63.5 2.7 %fusion.107 = f32[8,512,256]{2,1,0:T(8,128)} fusion(bf16[8,512,256]{2,1,0:T(8,128)(2,1)S(1)} %copy-done.4, bf16[2,256,256]{2,1,0:T(8,128)(2,1)S(1)} %copy-done.5), kind=kOutput, calls=%fused_computation.130 | convolution fusion | flops 536870912 | bytes 6422528 | tf_op jit(solution)/shard_map/sbh,hk->sbk/dot_general | solution.py:122
  66.2 1.3 fusion.86
  67.4 16.3 %collective-permute-done.5 = bf16[8,128,256]{1,2,0:T(8,128)(2,1)S(1)} collective-permute-done((bf16[8,128,256]{1,2,0:T(8,128)(2,1)S(1)}, bf16[8,128,256]{1,2,0:T(8,128)(2,1)S(1)}, u32[]{:S(2)}, u32[]{:S(2)}) %collective-permute-start.5) | collective-permute-done | bytes 524320 | tf_op jit(solution)/shard_map/ppermute | solution.py:112
  83.7 2.7 %fusion.1 = bf16[8,256,512]{1,2,0:T(8,128)(2,1)} fusion(f32[8,256,512]{1,2,0:T(8,128)S(1)} %fusion.86, bf16[1,8,128,256]{2,3,1,0:T(8,128)(2,1)S(1)} %bitcast.613, bf16[1,8,128,256]{2,3,1,0:T(8,128)(2,1)S(1)} %bitcast.612, bf16[1,8,128,256]{2,3,1,0:T(8,128)(2,1)S(1)} %bitcast.611, bf16[1,8,128,256]{2,3,1,0:T(8,128)(2,1)S(1)} %bitcast.610, ...), kind=kOutput, calls=%fused_computation.5 | convolution fusion | flops 1080295424 | bytes 8390656 | tf_op jit(solution)/shard_map/rb,srh->sbh/dot_general | solution.py:126
  86.4 4.5 %fusion.53 = f32[8,512,2]{1,2,0:T(2,128)S(1)} fusion(f32[8,512,256]{2,1,0:T(8,128)} %fusion.107, bf16[8,512,256]{2,1,0:T(8,128)(2,1)S(1)} %copy-done.4, bf16[8,256,512]{1,2,0:T(8,128)(2,1)} %fusion.1, f32[256]{0:T(256)S(1)} %bitcast.608, bf16[2,256,256]{2,1,0:T(8,128)(2,1)} %param.37, f32[2]{0:T(128)S(1)} %copy-done.14, bf16[2,256]{1,0:T(2,128)(2,1)S(1)} %copy-done.13), kind=kOutput, calls=%fused_computation.62 | convolution fusion | flops 550510592 | bytes 8554504 | tf_op jit(solution)/shard_map/sbh,ch->scb/dot_general | solution.py:143
  91.7 1.9 collective-permute-start.9
  93.7 7.0 %collective-permute-start.11 = (f32[8,2,128]{2,0,1:T(8,128)S(1)}, f32[8,2,128]{2,0,1:T(8,128)S(1)}, u32[]{:S(2)}, u32[]{:S(2)}) collective-permute-start(f32[8,2,128]{2,0,1:T(8,128)S(1)} %get-tuple-element.154), channel_id=1, source_target_pairs={{16,32},{32,16},{17,33},{33,17},{18,34},{34,18},{19,35},{35,19},{2... | collective-permute-start | bytes 24584 | tf_op jit(solution)/shard_map/ppermute | solution.py:112
  100.8 0.9 fusion.63
  104.3 1.9 collective-permute-start.13
  106.3 10.4 %collective-permute-start.15 = (f32[8,2,128]{2,0,1:T(8,128)S(1)}, f32[8,2,128]{2,0,1:T(8,128)S(1)}, u32[]{:S(2)}, u32[]{:S(2)}) collective-permute-start(f32[8,2,128]{2,0,1:T(8,128)S(1)} %get-tuple-element.150), channel_id=1, source_target_pairs={{16,32},{32,16},{17,33},{33,17},{18,34},{34,18},{19,35},{35,19},{2... | collective-permute-start | bytes 24584 | tf_op jit(solution)/shard_map/ppermute | solution.py:112
  116.7 1.6 collective-permute-done.15
  120.1 1.9 collective-permute-start.17
  122.1 10.3 %collective-permute-start.19 = (f32[8,2,128]{2,0,1:T(8,128)S(1)}, f32[8,2,128]{2,0,1:T(8,128)S(1)}, u32[]{:S(2)}, u32[]{:S(2)}) collective-permute-start(f32[8,2,128]{2,0,1:T(8,128)S(1)} %get-tuple-element.144), channel_id=1, source_target_pairs={{16,32},{32,16},{17,33},{33,17},{18,34},{34,18},{19,35},{35,19},{2... | collective-permute-start | bytes 24584 | tf_op jit(solution)/shard_map/ppermute | solution.py:112
  132.5 1.4 collective-permute-done.19
  135.5 0.9 fusion.61
  136.5 1.0 collective-permute-start.20
  137.5 4.7 %collective-permute-start.21 = (f32[8,2,128]{2,0,1:T(8,128)S(1)}, f32[8,2,128]{2,0,1:T(8,128)S(1)}, u32[]{:S(2)}, u32[]{:S(2)}) collective-permute-start(f32[8,2,128]{2,0,1:T(8,128)S(1)} %get-tuple-element.136), channel_id=1, source_target_pairs={{1,2},{2,1},{3,4},{4,3},{5,6},{6,5},{7,8},{8,7},{9,10},{10,9},{11,... | collective-permute-start | bytes 24584 | tf_op jit(solution)/shard_map/ppermute | solution.py:112
  142.4 13.1 %collective-permute-start.23 = (f32[8,2,128]{2,0,1:T(8,128)S(1)}, f32[8,2,128]{2,0,1:T(8,128)S(1)}, u32[]{:S(2)}, u32[]{:S(2)}) collective-permute-start(f32[8,2,128]{2,0,1:T(8,128)S(1)} %get-tuple-element.137), channel_id=1, source_target_pairs={{16,32},{32,16},{17,33},{33,17},{18,34},{34,18},{19,35},{35,19},{2... | collective-permute-start | bytes 24584 | tf_op jit(solution)/shard_map/ppermute | solution.py:112
  155.6 1.5 collective-permute-done.23
  158.7 0.8 convolution_bitcast_fusion.3
  159.6 1.9 collective-permute-start.25
  161.7 9.4 %collective-permute-start.27 = (f32[33,2,128]{2,0,1:T(8,128)S(1)}, f32[33,2,128]{2,0,1:T(8,128)S(1)}, u32[]{:S(2)}, u32[]{:S(2)}) collective-permute-start(f32[33,2,128]{2,0,1:T(8,128)S(1)} %get-tuple-element.120), channel_id=1, source_target_pairs={{16,32},{32,16},{17,33},{33,17},{18,34},{34,18},{19,35},{35,19},{2... | collective-permute-start | bytes 101384 | tf_op jit(solution)/shard_map/ppermute | solution.py:112
  171.1 1.9 collective-permute-done.27
  174.6 2.8 %collective-permute-done.28 = f32[8,8]{1,0:T(8,128)S(1)} collective-permute-done((f32[8,8]{1,0:T(8,128)S(1)}, f32[8,8]{1,0:T(8,128)S(1)}, u32[]{:S(2)}, u32[]{:S(2)}) %collective-permute-start.28) | collective-permute-done | bytes 288 | tf_op jit(solution)/shard_map/ppermute | solution.py:47
  177.9 4.4 %collective-permute-done.29 = f32[8,8]{1,0:T(8,128)S(1)} collective-permute-done((f32[8,8]{1,0:T(8,128)S(1)}, f32[8,8]{1,0:T(8,128)S(1)}, u32[]{:S(2)}, u32[]{:S(2)}) %collective-permute-start.29) | collective-permute-done | bytes 288 | tf_op jit(solution)/shard_map/ppermute | solution.py:47
  182.7 0.8 convolution_bitcast_fusion.1
  183.5 2.4 %collective-permute-done.30 = f32[8,8]{1,0:T(8,128)S(1)} collective-permute-done((f32[8,8]{1,0:T(8,128)S(1)}, f32[8,8]{1,0:T(8,128)S(1)}, u32[]{:S(2)}, u32[]{:S(2)}) %collective-permute-start.30) | collective-permute-done | bytes 288 | tf_op jit(solution)/shard_map/ppermute | solution.py:47
  186.0 1.9 collective-permute-start.32
  188.1 9.6 %collective-permute-start.34 = (f32[33,2,128]{2,0,1:T(8,128)S(1)}, f32[33,2,128]{2,0,1:T(8,128)S(1)}, u32[]{:S(2)}, u32[]{:S(2)}) collective-permute-start(f32[33,2,128]{2,0,1:T(8,128)S(1)} %get-tuple-element.114), channel_id=1, source_target_pairs={{16,32},{32,16},{17,33},{33,17},{18,34},{34,18},{19,35},{35,19},{2... | collective-permute-start | bytes 101384 | tf_op jit(solution)/shard_map/ppermute | solution.py:112
  197.7 1.9 collective-permute-done.34
  200.3 3.3 %collective-permute-start.35 = (f32[8,8]{1,0:T(8,128)S(1)}, f32[8,8]{1,0:T(8,128)S(1)}, u32[]{:S(2)}, u32[]{:S(2)}) collective-permute-start(f32[8,8]{1,0:T(8,128)S(1)} %add.351), channel_id=1, source_target_pairs={{0,32},{1,33},{2,34},{3,35},{4,36},{5,37},{6,38},{7,39},{8,40},{9,... | collective-permute-start | bytes 776 | tf_op jit(solution)/shard_map/ppermute | solution.py:47
  204.4 0.8 collective-permute-done.35
  205.2 7.9 %collective-permute-start.36 = (f32[8,8]{1,0:T(8,128)S(1)}, f32[8,8]{1,0:T(8,128)S(1)}, u32[]{:S(2)}, u32[]{:S(2)}) collective-permute-start(f32[8,8]{1,0:T(8,128)S(1)} %add.352), channel_id=1, source_target_pairs={{0,64},{1,65},{2,66},{3,67},{4,68},{5,69},{6,70},{7,71},{8,72},{9,... | collective-permute-start | bytes 776 | tf_op jit(solution)/shard_map/ppermute | solution.py:47
  213.1 1.5 collective-permute-done.36
  214.7 3.3 %collective-permute-start.37 = (f32[8,8]{1,0:T(8,128)S(1)}, f32[8,8]{1,0:T(8,128)S(1)}, u32[]{:S(2)}, u32[]{:S(2)}) collective-permute-start(f32[8,8]{1,0:T(8,128)S(1)} %add.353), channel_id=1, source_target_pairs={{0,224},{1,225},{2,226},{3,227},{4,228},{5,229},{6,230},{7,231},{8... | collective-permute-start | bytes 776 | tf_op jit(solution)/shard_map/ppermute | solution.py:47
  218.1 1.5 collective-permute-done.37
  (181 shorter events, 17.2 us)
Async XLA Ops:
  0.0 22.5 %copy-start = (f32[16,2,512]{2,1,0:T(2,128)S(1)}, f32[16,2,512]{2,1,0:T(2,128)}, u32[]{:S(2)}) copy-start(f32[16,2,512]{2,1,0:T(2,128)} %param.40) | copy-start | bytes 196612
  5.8 13.3 %copy-start.3 = (bf16[8,512,256]{2,1,0:T(8,128)(2,1)S(1)}, bf16[8,512,256]{2,1,0:T(8,128)(2,1)}, u32[]{:S(2)}) copy-start(bf16[8,512,256]{2,1,0:T(8,128)(2,1)} %param.31) | copy-start | bytes 6291460
  5.8 13.3 %copy-start.5 = (bf16[2,256,256]{2,1,0:T(8,128)(2,1)S(1)}, bf16[2,256,256]{2,1,0:T(8,128)(2,1)}, u32[]{:S(2)}) copy-start(bf16[2,256,256]{2,1,0:T(8,128)(2,1)} %param.36) | copy-start | bytes 786436
  7.2 18.8 %collective-permute-start = (bf16[8,128,256]{2,1,0:T(8,128)(2,1)}, bf16[8,128,256]{2,1,0:T(8,128)(2,1)}, u32[]{:S(2)}, u32[]{:S(2)}) collective-permute-start(bf16[8,128,256]{2,1,0:T(8,128)(2,1)} %get-tuple-element.106), channel_id=1, source_target_pairs={{0,1},{1,0},{2,3},{3,2},{4,5},{5,4},{6,7},{7,6},{8,9},{9,8},{10,11... | collective-permute-start | bytes 1572872 | tf_op jit(solution)/shard_map/ppermute | solution.py:112
  7.2 35.5 %collective-permute-start.1 = (bf16[8,128,256]{2,1,0:T(8,128)(2,1)}, bf16[8,128,256]{2,1,0:T(8,128)(2,1)}, u32[]{:S(2)}, u32[]{:S(2)}) collective-permute-start(bf16[8,128,256]{2,1,0:T(8,128)(2,1)} %get-tuple-element.109), channel_id=1, source_target_pairs={{1,2},{2,1},{3,4},{4,3},{5,6},{6,5},{7,8},{8,7},{9,10},{10,9},{11,... | collective-permute-start | bytes 1572872 | tf_op jit(solution)/shard_map/ppermute | solution.py:112
  12.2 30.5 %collective-permute-start.2 = (bf16[8,128,256]{2,1,0:T(8,128)(2,1)}, bf16[8,128,256]{2,1,0:T(8,128)(2,1)}, u32[]{:S(2)}, u32[]{:S(2)}) collective-permute-start(bf16[8,128,256]{2,1,0:T(8,128)(2,1)} %get-tuple-element.108), channel_id=1, source_target_pairs={{0,16},{16,0},{1,17},{17,1},{2,18},{18,2},{3,19},{19,3},{4,20},{20... | collective-permute-start | bytes 1572872 | tf_op jit(solution)/shard_map/ppermute | solution.py:112
  12.3 30.4 %collective-permute-start.3 = (bf16[8,128,256]{2,1,0:T(8,128)(2,1)}, bf16[8,128,256]{2,1,0:T(8,128)(2,1)}, u32[]{:S(2)}, u32[]{:S(2)}) collective-permute-start(bf16[8,128,256]{2,1,0:T(8,128)(2,1)} %get-tuple-element.107), channel_id=1, source_target_pairs={{16,32},{32,16},{17,33},{33,17},{18,34},{34,18},{19,35},{35,19},{2... | collective-permute-start | bytes 1572872 | tf_op jit(solution)/shard_map/ppermute | solution.py:112
  19.2 3.5 %copy-start.2 = (s32[512,512]{1,0:T(8,128)S(1)}, s32[512,512]{1,0:T(8,128)}, u32[]{:S(2)}) copy-start(s32[512,512]{1,0:T(8,128)} %param.32) | copy-start | bytes 3145732
  54.1 9.4 %copy-start.4 = (bf16[8,512,256]{2,1,0:T(8,128)(2,1)S(1)}, bf16[8,512,256]{2,1,0:T(8,128)(2,1)}, u32[]{:S(2)}) copy-start(bf16[8,512,256]{2,1,0:T(8,128)(2,1)} %add_convert_fusion.1) | copy-start | bytes 6291460
  54.3 13.2 %collective-permute-start.4 = (bf16[8,128,256]{1,2,0:T(8,128)(2,1)S(1)}, bf16[8,128,256]{1,2,0:T(8,128)(2,1)S(1)}, u32[]{:S(2)}, u32[]{:S(2)}) collective-permute-start(bf16[8,128,256]{1,2,0:T(8,128)(2,1)S(1)} %get-tuple-element.102), channel_id=1, source_target_pairs={{0,1},{1,0},{2,3},{3,2},{4,5},{5,4},{6,7},{7,6},{8,9},{9,8},{10,11... | collective-permute-start | bytes 1572872 | tf_op jit(solution)/shard_map/ppermute | solution.py:112
  54.4 29.3 %collective-permute-start.5 = (bf16[8,128,256]{1,2,0:T(8,128)(2,1)S(1)}, bf16[8,128,256]{1,2,0:T(8,128)(2,1)S(1)}, u32[]{:S(2)}, u32[]{:S(2)}) collective-permute-start(bf16[8,128,256]{1,2,0:T(8,128)(2,1)S(1)} %get-tuple-element.103), channel_id=1, source_target_pairs={{1,2},{2,1},{3,4},{4,3},{5,6},{6,5},{7,8},{8,7},{9,10},{10,9},{11,... | collective-permute-start | bytes 1572872 | tf_op jit(solution)/shard_map/ppermute | solution.py:112
  56.4 27.3 %collective-permute-start.6 = (bf16[8,128,256]{1,2,0:T(8,128)(2,1)S(1)}, bf16[8,128,256]{1,2,0:T(8,128)(2,1)S(1)}, u32[]{:S(2)}, u32[]{:S(2)}) collective-permute-start(bf16[8,128,256]{1,2,0:T(8,128)(2,1)S(1)} %get-tuple-element.105), channel_id=1, source_target_pairs={{0,16},{16,0},{1,17},{17,1},{2,18},{18,2},{3,19},{19,3},{4,20},{20... | collective-permute-start | bytes 1572872 | tf_op jit(solution)/shard_map/ppermute | solution.py:112
  56.5 27.2 %collective-permute-start.7 = (bf16[8,128,256]{1,2,0:T(8,128)(2,1)S(1)}, bf16[8,128,256]{1,2,0:T(8,128)(2,1)S(1)}, u32[]{:S(2)}, u32[]{:S(2)}) collective-permute-start(bf16[8,128,256]{1,2,0:T(8,128)(2,1)S(1)} %get-tuple-element.104), channel_id=1, source_target_pairs={{16,32},{32,16},{17,33},{33,17},{18,34},{34,18},{19,35},{35,19},{2... | collective-permute-start | bytes 1572872 | tf_op jit(solution)/shard_map/ppermute | solution.py:112
  86.4 15.3 %copy-start.9 = (f32[512]{0:T(512)S(1)}, f32[512]{0:T(512)}, u32[]{:S(2)}) copy-start(f32[512]{0:T(512)} %param.45) | copy-start | bytes 6148
  86.4 15.4 %copy-start.10 = (f32[512]{0:T(512)S(1)}, f32[512]{0:T(512)}, u32[]{:S(2)}) copy-start(f32[512]{0:T(512)} %param.42) | copy-start | bytes 6148
  90.9 12.0 %copy-start.7 = (f32[512]{0:T(512)S(1)}, f32[512]{0:T(512)}, u32[]{:S(2)}) copy-start(f32[512]{0:T(512)} %param.44) | copy-start | bytes 6148
  90.9 12.0 %copy-start.8 = (f32[512]{0:T(512)S(1)}, f32[512]{0:T(512)}, u32[]{:S(2)}) copy-start(f32[512]{0:T(512)} %param.43) | copy-start | bytes 6148
  90.9 12.2 %copy-start.1 = (bf16[1024,1024]{1,0:T(8,128)(2,1)S(1)}, bf16[1024,1024]{1,0:T(8,128)(2,1)}, u32[]{:S(2)}) copy-start(bf16[1024,1024]{1,0:T(8,128)(2,1)} %param.46) | copy-start | bytes 6291460
  91.6 10.2 %collective-permute-start.8 = (f32[8,2,128]{2,0,1:T(8,128)S(1)}, f32[8,2,128]{2,0,1:T(8,128)S(1)}, u32[]{:S(2)}, u32[]{:S(2)}) collective-permute-start(f32[8,2,128]{2,0,1:T(8,128)S(1)} %get-tuple-element.152), channel_id=1, source_target_pairs={{0,1},{1,0},{2,3},{3,2},{4,5},{5,4},{6,7},{7,6},{8,9},{9,8},{10,11... | collective-permute-start | bytes 24584 | tf_op jit(solution)/shard_map/ppermute | solution.py:112
  91.7 10.1 %collective-permute-start.9 = (f32[8,2,128]{2,0,1:T(8,128)S(1)}, f32[8,2,128]{2,0,1:T(8,128)S(1)}, u32[]{:S(2)}, u32[]{:S(2)}) collective-permute-start(f32[8,2,128]{2,0,1:T(8,128)S(1)} %get-tuple-element.153), channel_id=1, source_target_pairs={{1,2},{2,1},{3,4},{4,3},{5,6},{6,5},{7,8},{8,7},{9,10},{10,9},{11,... | collective-permute-start | bytes 24584 | tf_op jit(solution)/shard_map/ppermute | solution.py:112
  93.6 8.2 %collective-permute-start.10 = (f32[8,2,128]{2,0,1:T(8,128)S(1)}, f32[8,2,128]{2,0,1:T(8,128)S(1)}, u32[]{:S(2)}, u32[]{:S(2)}) collective-permute-start(f32[8,2,128]{2,0,1:T(8,128)S(1)} %get-tuple-element.155), channel_id=1, source_target_pairs={{0,16},{16,0},{1,17},{17,1},{2,18},{18,2},{3,19},{19,3},{4,20},{20... | collective-permute-start | bytes 24584 | tf_op jit(solution)/shard_map/ppermute | solution.py:112
  93.7 8.7 %collective-permute-start.11 = (f32[8,2,128]{2,0,1:T(8,128)S(1)}, f32[8,2,128]{2,0,1:T(8,128)S(1)}, u32[]{:S(2)}, u32[]{:S(2)}) collective-permute-start(f32[8,2,128]{2,0,1:T(8,128)S(1)} %get-tuple-element.154), channel_id=1, source_target_pairs={{16,32},{32,16},{17,33},{33,17},{18,34},{34,18},{19,35},{35,19},{2... | collective-permute-start | bytes 24584 | tf_op jit(solution)/shard_map/ppermute | solution.py:112
  104.2 12.5 %collective-permute-start.12 = (f32[8,2,128]{2,0,1:T(8,128)S(1)}, f32[8,2,128]{2,0,1:T(8,128)S(1)}, u32[]{:S(2)}, u32[]{:S(2)}) collective-permute-start(f32[8,2,128]{2,0,1:T(8,128)S(1)} %get-tuple-element.148), channel_id=1, source_target_pairs={{0,1},{1,0},{2,3},{3,2},{4,5},{5,4},{6,7},{7,6},{8,9},{9,8},{10,11... | collective-permute-start | bytes 24584 | tf_op jit(solution)/shard_map/ppermute | solution.py:112
  104.3 12.5 %collective-permute-start.13 = (f32[8,2,128]{2,0,1:T(8,128)S(1)}, f32[8,2,128]{2,0,1:T(8,128)S(1)}, u32[]{:S(2)}, u32[]{:S(2)}) collective-permute-start(f32[8,2,128]{2,0,1:T(8,128)S(1)} %get-tuple-element.149), channel_id=1, source_target_pairs={{1,2},{2,1},{3,4},{4,3},{5,6},{6,5},{7,8},{8,7},{9,10},{10,9},{11,... | collective-permute-start | bytes 24584 | tf_op jit(solution)/shard_map/ppermute | solution.py:112
  106.2 10.5 %collective-permute-start.14 = (f32[8,2,128]{2,0,1:T(8,128)S(1)}, f32[8,2,128]{2,0,1:T(8,128)S(1)}, u32[]{:S(2)}, u32[]{:S(2)}) collective-permute-start(f32[8,2,128]{2,0,1:T(8,128)S(1)} %get-tuple-element.151), channel_id=1, source_target_pairs={{0,16},{16,0},{1,17},{17,1},{2,18},{18,2},{3,19},{19,3},{4,20},{20... | collective-permute-start | bytes 24584 | tf_op jit(solution)/shard_map/ppermute | solution.py:112
  106.3 12.0 %collective-permute-start.15 = (f32[8,2,128]{2,0,1:T(8,128)S(1)}, f32[8,2,128]{2,0,1:T(8,128)S(1)}, u32[]{:S(2)}, u32[]{:S(2)}) collective-permute-start(f32[8,2,128]{2,0,1:T(8,128)S(1)} %get-tuple-element.150), channel_id=1, source_target_pairs={{16,32},{32,16},{17,33},{33,17},{18,34},{34,18},{19,35},{35,19},{2... | collective-permute-start | bytes 24584 | tf_op jit(solution)/shard_map/ppermute | solution.py:112
  120.0 12.4 %collective-permute-start.16 = (f32[8,2,128]{2,0,1:T(8,128)S(1)}, f32[8,2,128]{2,0,1:T(8,128)S(1)}, u32[]{:S(2)}, u32[]{:S(2)}) collective-permute-start(f32[8,2,128]{2,0,1:T(8,128)S(1)} %get-tuple-element.142), channel_id=1, source_target_pairs={{0,1},{1,0},{2,3},{3,2},{4,5},{5,4},{6,7},{7,6},{8,9},{9,8},{10,11... | collective-permute-start | bytes 24584 | tf_op jit(solution)/shard_map/ppermute | solution.py:112
  120.1 12.4 %collective-permute-start.17 = (f32[8,2,128]{2,0,1:T(8,128)S(1)}, f32[8,2,128]{2,0,1:T(8,128)S(1)}, u32[]{:S(2)}, u32[]{:S(2)}) collective-permute-start(f32[8,2,128]{2,0,1:T(8,128)S(1)} %get-tuple-element.143), channel_id=1, source_target_pairs={{1,2},{2,1},{3,4},{4,3},{5,6},{6,5},{7,8},{8,7},{9,10},{10,9},{11,... | collective-permute-start | bytes 24584 | tf_op jit(solution)/shard_map/ppermute | solution.py:112
  122.0 10.4 %collective-permute-start.18 = (f32[8,2,128]{2,0,1:T(8,128)S(1)}, f32[8,2,128]{2,0,1:T(8,128)S(1)}, u32[]{:S(2)}, u32[]{:S(2)}) collective-permute-start(f32[8,2,128]{2,0,1:T(8,128)S(1)} %get-tuple-element.145), channel_id=1, source_target_pairs={{0,16},{16,0},{1,17},{17,1},{2,18},{18,2},{3,19},{19,3},{4,20},{20... | collective-permute-start | bytes 24584 | tf_op jit(solution)/shard_map/ppermute | solution.py:112
  122.1 11.7 %collective-permute-start.19 = (f32[8,2,128]{2,0,1:T(8,128)S(1)}, f32[8,2,128]{2,0,1:T(8,128)S(1)}, u32[]{:S(2)}, u32[]{:S(2)}) collective-permute-start(f32[8,2,128]{2,0,1:T(8,128)S(1)} %get-tuple-element.144), channel_id=1, source_target_pairs={{16,32},{32,16},{17,33},{33,17},{18,34},{34,18},{19,35},{35,19},{2... | collective-permute-start | bytes 24584 | tf_op jit(solution)/shard_map/ppermute | solution.py:112
  136.5 19.0 %collective-permute-start.20 = (f32[8,2,128]{2,0,1:T(8,128)S(1)}, f32[8,2,128]{2,0,1:T(8,128)S(1)}, u32[]{:S(2)}, u32[]{:S(2)}) collective-permute-start(f32[8,2,128]{2,0,1:T(8,128)S(1)} %get-tuple-element.135), channel_id=1, source_target_pairs={{0,1},{1,0},{2,3},{3,2},{4,5},{5,4},{6,7},{7,6},{8,9},{9,8},{10,11... | collective-permute-start | bytes 24584 | tf_op jit(solution)/shard_map/ppermute | solution.py:112
  137.5 18.0 %collective-permute-start.21 = (f32[8,2,128]{2,0,1:T(8,128)S(1)}, f32[8,2,128]{2,0,1:T(8,128)S(1)}, u32[]{:S(2)}, u32[]{:S(2)}) collective-permute-start(f32[8,2,128]{2,0,1:T(8,128)S(1)} %get-tuple-element.136), channel_id=1, source_target_pairs={{1,2},{2,1},{3,4},{4,3},{5,6},{6,5},{7,8},{8,7},{9,10},{10,9},{11,... | collective-permute-start | bytes 24584 | tf_op jit(solution)/shard_map/ppermute | solution.py:112
  142.2 13.3 %collective-permute-start.22 = (f32[8,2,128]{2,0,1:T(8,128)S(1)}, f32[8,2,128]{2,0,1:T(8,128)S(1)}, u32[]{:S(2)}, u32[]{:S(2)}) collective-permute-start(f32[8,2,128]{2,0,1:T(8,128)S(1)} %get-tuple-element.138), channel_id=1, source_target_pairs={{0,16},{16,0},{1,17},{17,1},{2,18},{18,2},{3,19},{19,3},{4,20},{20... | collective-permute-start | bytes 24584 | tf_op jit(solution)/shard_map/ppermute | solution.py:112
  142.4 14.7 %collective-permute-start.23 = (f32[8,2,128]{2,0,1:T(8,128)S(1)}, f32[8,2,128]{2,0,1:T(8,128)S(1)}, u32[]{:S(2)}, u32[]{:S(2)}) collective-permute-start(f32[8,2,128]{2,0,1:T(8,128)S(1)} %get-tuple-element.137), channel_id=1, source_target_pairs={{16,32},{32,16},{17,33},{33,17},{18,34},{34,18},{19,35},{35,19},{2... | collective-permute-start | bytes 24584 | tf_op jit(solution)/shard_map/ppermute | solution.py:112
  159.5 11.5 %collective-permute-start.24 = (f32[33,2,128]{2,0,1:T(8,128)S(1)}, f32[33,2,128]{2,0,1:T(8,128)S(1)}, u32[]{:S(2)}, u32[]{:S(2)}) collective-permute-start(f32[33,2,128]{2,0,1:T(8,128)S(1)} %get-tuple-element.118), channel_id=1, source_target_pairs={{0,1},{1,0},{2,3},{3,2},{4,5},{5,4},{6,7},{7,6},{8,9},{9,8},{10,11... | collective-permute-start | bytes 101384 | tf_op jit(solution)/shard_map/ppermute | solution.py:112
  159.6 11.5 %collective-permute-start.25 = (f32[33,2,128]{2,0,1:T(8,128)S(1)}, f32[33,2,128]{2,0,1:T(8,128)S(1)}, u32[]{:S(2)}, u32[]{:S(2)}) collective-permute-start(f32[33,2,128]{2,0,1:T(8,128)S(1)} %get-tuple-element.119), channel_id=1, source_target_pairs={{1,2},{2,1},{3,4},{4,3},{5,6},{6,5},{7,8},{8,7},{9,10},{10,9},{11,... | collective-permute-start | bytes 101384 | tf_op jit(solution)/shard_map/ppermute | solution.py:112
  161.6 9.5 %collective-permute-start.26 = (f32[33,2,128]{2,0,1:T(8,128)S(1)}, f32[33,2,128]{2,0,1:T(8,128)S(1)}, u32[]{:S(2)}, u32[]{:S(2)}) collective-permute-start(f32[33,2,128]{2,0,1:T(8,128)S(1)} %get-tuple-element.121), channel_id=1, source_target_pairs={{0,16},{16,0},{1,17},{17,1},{2,18},{18,2},{3,19},{19,3},{4,20},{20... | collective-permute-start | bytes 101384 | tf_op jit(solution)/shard_map/ppermute | solution.py:112
  161.7 11.4 %collective-permute-start.27 = (f32[33,2,128]{2,0,1:T(8,128)S(1)}, f32[33,2,128]{2,0,1:T(8,128)S(1)}, u32[]{:S(2)}, u32[]{:S(2)}) collective-permute-start(f32[33,2,128]{2,0,1:T(8,128)S(1)} %get-tuple-element.120), channel_id=1, source_target_pairs={{16,32},{32,16},{17,33},{33,17},{18,34},{34,18},{19,35},{35,19},{2... | collective-permute-start | bytes 101384 | tf_op jit(solution)/shard_map/ppermute | solution.py:112
  173.7 3.6 %collective-permute-start.28 = (f32[8,8]{1,0:T(8,128)S(1)}, f32[8,8]{1,0:T(8,128)S(1)}, u32[]{:S(2)}, u32[]{:S(2)}) collective-permute-start(f32[8,8]{1,0:T(8,128)S(1)} %add.345), channel_id=1, source_target_pairs={{0,2},{1,3},{2,0},{3,1},{4,6},{5,7},{6,4},{7,5},{8,10},{9,11},{10,... | collective-permute-start | bytes 776 | tf_op jit(solution)/shard_map/ppermute | solution.py:47
  177.4 4.8 %collective-permute-start.29 = (f32[8,8]{1,0:T(8,128)S(1)}, f32[8,8]{1,0:T(8,128)S(1)}, u32[]{:S(2)}, u32[]{:S(2)}) collective-permute-start(f32[8,8]{1,0:T(8,128)S(1)} %add.346), channel_id=1, source_target_pairs={{0,6},{1,7},{2,4},{3,5},{4,2},{5,3},{6,0},{7,1},{8,14},{9,15},{10,... | collective-permute-start | bytes 776 | tf_op jit(solution)/shard_map/ppermute | solution.py:47
  182.2 3.6 %collective-permute-start.30 = (f32[8,8]{1,0:T(8,128)S(1)}, f32[8,8]{1,0:T(8,128)S(1)}, u32[]{:S(2)}, u32[]{:S(2)}) collective-permute-start(f32[8,8]{1,0:T(8,128)S(1)} %add.347), channel_id=1, source_target_pairs={{0,8},{1,9},{2,10},{3,11},{4,12},{5,13},{6,14},{7,15},{8,0},{9,1},... | collective-permute-start | bytes 776 | tf_op jit(solution)/shard_map/ppermute | solution.py:47
  185.9 11.7 %collective-permute-start.31 = (f32[33,2,128]{2,0,1:T(8,128)S(1)}, f32[33,2,128]{2,0,1:T(8,128)S(1)}, u32[]{:S(2)}, u32[]{:S(2)}) collective-permute-start(f32[33,2,128]{2,0,1:T(8,128)S(1)} %get-tuple-element.112), channel_id=1, source_target_pairs={{0,1},{1,0},{2,3},{3,2},{4,5},{5,4},{6,7},{7,6},{8,9},{9,8},{10,11... | collective-permute-start | bytes 101384 | tf_op jit(solution)/shard_map/ppermute | solution.py:112
  186.0 11.6 %collective-permute-start.32 = (f32[33,2,128]{2,0,1:T(8,128)S(1)}, f32[33,2,128]{2,0,1:T(8,128)S(1)}, u32[]{:S(2)}, u32[]{:S(2)}) collective-permute-start(f32[33,2,128]{2,0,1:T(8,128)S(1)} %get-tuple-element.113), channel_id=1, source_target_pairs={{1,2},{2,1},{3,4},{4,3},{5,6},{6,5},{7,8},{8,7},{9,10},{10,9},{11,... | collective-permute-start | bytes 101384 | tf_op jit(solution)/shard_map/ppermute | solution.py:112
  188.0 9.7 %collective-permute-start.33 = (f32[33,2,128]{2,0,1:T(8,128)S(1)}, f32[33,2,128]{2,0,1:T(8,128)S(1)}, u32[]{:S(2)}, u32[]{:S(2)}) collective-permute-start(f32[33,2,128]{2,0,1:T(8,128)S(1)} %get-tuple-element.115), channel_id=1, source_target_pairs={{0,16},{16,0},{1,17},{17,1},{2,18},{18,2},{3,19},{19,3},{4,20},{20... | collective-permute-start | bytes 101384 | tf_op jit(solution)/shard_map/ppermute | solution.py:112
  188.1 11.5 %collective-permute-start.34 = (f32[33,2,128]{2,0,1:T(8,128)S(1)}, f32[33,2,128]{2,0,1:T(8,128)S(1)}, u32[]{:S(2)}, u32[]{:S(2)}) collective-permute-start(f32[33,2,128]{2,0,1:T(8,128)S(1)} %get-tuple-element.114), channel_id=1, source_target_pairs={{16,32},{32,16},{17,33},{33,17},{18,34},{34,18},{19,35},{35,19},{2... | collective-permute-start | bytes 101384 | tf_op jit(solution)/shard_map/ppermute | solution.py:112
  200.3 4.9 %collective-permute-start.35 = (f32[8,8]{1,0:T(8,128)S(1)}, f32[8,8]{1,0:T(8,128)S(1)}, u32[]{:S(2)}, u32[]{:S(2)}) collective-permute-start(f32[8,8]{1,0:T(8,128)S(1)} %add.351), channel_id=1, source_target_pairs={{0,32},{1,33},{2,34},{3,35},{4,36},{5,37},{6,38},{7,39},{8,40},{9,... | collective-permute-start | bytes 776 | tf_op jit(solution)/shard_map/ppermute | solution.py:47
  205.2 9.5 %collective-permute-start.36 = (f32[8,8]{1,0:T(8,128)S(1)}, f32[8,8]{1,0:T(8,128)S(1)}, u32[]{:S(2)}, u32[]{:S(2)}) collective-permute-start(f32[8,8]{1,0:T(8,128)S(1)} %add.352), channel_id=1, source_target_pairs={{0,64},{1,65},{2,66},{3,67},{4,68},{5,69},{6,70},{7,71},{8,72},{9,... | collective-permute-start | bytes 776 | tf_op jit(solution)/shard_map/ppermute | solution.py:47
  214.7 4.9 %collective-permute-start.37 = (f32[8,8]{1,0:T(8,128)S(1)}, f32[8,8]{1,0:T(8,128)S(1)}, u32[]{:S(2)}, u32[]{:S(2)}) collective-permute-start(f32[8,8]{1,0:T(8,128)S(1)} %add.353), channel_id=1, source_target_pairs={{0,224},{1,225},{2,226},{3,227},{4,228},{5,229},{6,230},{7,231},{8... | collective-permute-start | bytes 776 | tf_op jit(solution)/shard_map/ppermute | solution.py:47
  (5 other events, 15.0 us)

commit v11 on v7

--- a/solution.py
+++ b/solution.py
@@ -226,7 +226,7 @@
             powers[i + j] = powers[i + j] + (product if i == j else 2.0 * product)
     partial = jnp.concatenate([partial, jnp.stack(powers)])
     if bits == [1, 2, 6, 8, 24, 32, 64, 224] and SWEEPS == 3:
-        plan = [(0, [2, 6, 8]), (2, [32, 64, 224])]
+        plan = [(0, []), (2, [2, 6, 8, 32, 64, 224])]
     elif bits is None:
         plan = None
     else:

time: 224 us -> 227 us (1.013)
  waiting for transfers between devices: 55.2 us -> 57.6 us
    ppermute x32, starting transfers between devices: 97.1 us -> 99.8 us  [exchange(): lax.ppermute(tiles[j], 'region', routes[j])]
    ppermute x6, waiting for transfers between devices: 13.3 us -> 15.8 us  [sum_rounds(): lax.ppermute(value, axis, [(i, i ^ bit) for i in range(count)])]
where the time goes in v11:
time: 227 us; the launch traced here: 224 us
  starting transfers between devices  114 us (50%)
  waiting for transfers between devices  57.6 us (25%)
  matrix products  43.3 us (19%)
  local copies, waits for them, and re-layouts  4.92 us (2%)
  other arithmetic  3.14 us (1%)
    ppermute x32, starting transfers between devices, exchange(): lax.ppermute(tiles[j], 'region', routes[j])  99.8 us
    ppermute x32, waiting for transfers between devices, exchange(): lax.ppermute(tiles[j], 'region', routes[j])  41.8 us
    ppermute x6, waiting for transfers between devices, sum_rounds(): lax.ppermute(value, axis, [(i, i ^ bit) for i in range(count)])  15.8 us
    ppermute x6, starting transfers between devices, sum_rounds(): lax.ppermute(value, axis, [(i, i ^ bit) for i in range(count)])  13.8 us
    dot_general x1, matrix products, local(): jnp.einsum('sbh,hk->sbk', gathered, neigh_weight[number], preferred_eleme...  8.29 us
    dot_general x2, matrix products, local(): jnp.einsum('ktb,sbh->ksth', pick_half, hidden, preferred_element_type=jnp...  5.96 us
    dot_general x2, matrix products, local(): jnp.einsum('sbh,hk->sbk', hidden, self_weight[number], preferred_element_...  5.34 us
  transfers between devices with their start and end apart: 38, of which 14 were waited for; matrix products, arithmetic and copies ran while one was open for 6% of the time, Pallas kernels for 0%

profile of v11, /device:TPU:4, one launch (start us, length us, event | category | flops | bytes accessed | tf_op | source)
XLA Modules:
  0.0 223.6 jit_solution(8162058650255412386)
XLA Ops:
  1.6 1.2 gather_fusion.1
  2.9 2.9 %convert_bitcast_fusion.1 = bf16[4,8,128,256]{3,2,1,0:T(8,128)(2,1)S(1)} fusion(bf16[8,512,256]{2,1,0:T(8,128)(2,1)} %param.31, s32[4,128]{1,0:T(4,128)S(1)} %broadcast_select_fusion.1, pred[4,128]{1,0:T(4,128)(4,1)S(1)} %broadcast_select_fusion.2), kind=kOutput, calls=%fused_computation.42 | convolution fusion | flops 1075314688 | bytes 4196864 | tf_op jit(solution)/shard_map/ktb,sbh->ksth/dot_general | solution.py:117
  5.8 1.4 slice_bitcast_fusion.7
  7.2 5.0 %collective-permute-start.1 = (bf16[8,128,256]{2,1,0:T(8,128)(2,1)}, bf16[8,128,256]{2,1,0:T(8,128)(2,1)}, u32[]{:S(2)}, u32[]{:S(2)}) collective-permute-start(bf16[8,128,256]{2,1,0:T(8,128)(2,1)} %get-tuple-element.109), channel_id=1, source_target_pairs={{1,2},{2,1},{3,4},{4,3},{5,6},{6,5},{7,8},{8,7},{9,10},{10,9},{11,... | collective-permute-start | bytes 1572872 | tf_op jit(solution)/shard_map/ppermute | solution.py:112
  12.3 6.8 %collective-permute-start.3 = (bf16[8,128,256]{2,1,0:T(8,128)(2,1)}, bf16[8,128,256]{2,1,0:T(8,128)(2,1)}, u32[]{:S(2)}, u32[]{:S(2)}) collective-permute-start(bf16[8,128,256]{2,1,0:T(8,128)(2,1)} %get-tuple-element.107), channel_id=1, source_target_pairs={{16,32},{32,16},{17,33},{33,17},{18,34},{34,18},{19,35},{35,19},{2... | collective-permute-start | bytes 1572872 | tf_op jit(solution)/shard_map/ppermute | solution.py:112
  19.2 2.7 %fusion.116 = f32[8,512,256]{2,1,0:T(8,128)} fusion(bf16[8,512,256]{2,1,0:T(8,128)(2,1)S(1)} %copy-done.3, bf16[2,256,256]{2,1,0:T(8,128)(2,1)S(1)} %copy-done.5), kind=kOutput, calls=%fused_computation.133 | convolution fusion | flops 536870912 | bytes 6422528 | tf_op jit(solution)/shard_map/sbh,hk->sbk/dot_general | solution.py:122
  22.7 3.3 %fusion.90 = f32[8,256,512]{1,2,0:T(8,128)} fusion(bf16[8,512,256]{2,1,0:T(8,128)(2,1)S(1)} %copy-done.3, s32[512,512]{1,0:T(8,128)S(1)} %copy-done.2), kind=kOutput, calls=%fused_computation.88 | convolution fusion | flops 1074003968 | bytes 7340032 | tf_op jit(solution)/shard_map/ij,sjh->sih/dot_general | solution.py:121
  26.0 16.7 %collective-permute-done.1 = bf16[8,128,256]{2,1,0:T(8,128)(2,1)} collective-permute-done((bf16[8,128,256]{2,1,0:T(8,128)(2,1)}, bf16[8,128,256]{2,1,0:T(8,128)(2,1)}, u32[]{:S(2)}, u32[]{:S(2)}) %collective-permute-start.1) | collective-permute-done | bytes 524320 | tf_op jit(solution)/shard_map/ppermute | solution.py:112
  42.7 8.3 %add_convert_fusion.1 = bf16[8,512,256]{2,1,0:T(8,128)(2,1)} fusion(f32[8,512,256]{2,1,0:T(8,128)} %fusion.116, bf16[8,512,256]{2,1,0:T(8,128)(2,1)S(1)} %copy-done.3, f32[256]{0:T(256)S(1)} %bitcast.602, f32[8,256,512]{1,2,0:T(8,128)} %fusion.90, bf16[1,8,128,256]{3,2,1,0:T(8,128)(2,1)} %bitcast.23, bf16[1,8,128,256]{3,2,1,0:T(8,128)(2,1)} %bitcast.21, ...), kind=kOutput, calls=%fused_computation.10 | convolution fusion | flops 1626603520 | bytes 14814208 | tf_op jit(solution)/shard_map/sbh,hk->sbk/dot_general | solution.py:131
  51.0 3.1 %convert_bitcast_fusion = bf16[4,8,128,256]{2,3,0,1:T(8,128)(2,1)S(1)} fusion(bf16[8,512,256]{2,1,0:T(8,128)(2,1)} %add_convert_fusion.1, s32[4,128]{1,0:T(4,128)S(1)} %broadcast_select_fusion.1, pred[4,128]{1,0:T(4,128)(4,1)S(1)} %broadcast_select_fusion.2), kind=kOutput, calls=%fused_computation.41 | convolution fusion | flops 1075314688 | bytes 4196864 | tf_op jit(solution)/shard_map/ktb,sbh->ksth/dot_general | solution.py:117
  54.4 2.1 collective-permute-start.5
  56.5 6.9 %collective-permute-start.7 = (bf16[8,128,256]{1,2,0:T(8,128)(2,1)S(1)}, bf16[8,128,256]{1,2,0:T(8,128)(2,1)S(1)}, u32[]{:S(2)}, u32[]{:S(2)}) collective-permute-start(bf16[8,128,256]{1,2,0:T(8,128)(2,1)S(1)} %get-tuple-element.104), channel_id=1, source_target_pairs={{16,32},{32,16},{17,33},{33,17},{18,34},{34,18},{19,35},{35,19},{2... | collective-permute-start | bytes 1572872 | tf_op jit(solution)/shard_map/ppermute | solution.py:112
  63.5 2.7 %fusion.113 = f32[8,512,256]{2,1,0:T(8,128)} fusion(bf16[8,512,256]{2,1,0:T(8,128)(2,1)S(1)} %copy-done.4, bf16[2,256,256]{2,1,0:T(8,128)(2,1)S(1)} %copy-done.5), kind=kOutput, calls=%fused_computation.130 | convolution fusion | flops 536870912 | bytes 6422528 | tf_op jit(solution)/shard_map/sbh,hk->sbk/dot_general | solution.py:122
  66.2 1.3 fusion.92
  67.4 16.3 %collective-permute-done.5 = bf16[8,128,256]{1,2,0:T(8,128)(2,1)S(1)} collective-permute-done((bf16[8,128,256]{1,2,0:T(8,128)(2,1)S(1)}, bf16[8,128,256]{1,2,0:T(8,128)(2,1)S(1)}, u32[]{:S(2)}, u32[]{:S(2)}) %collective-permute-start.5) | collective-permute-done | bytes 524320 | tf_op jit(solution)/shard_map/ppermute | solution.py:112
  83.7 2.7 %fusion.1 = bf16[8,256,512]{1,2,0:T(8,128)(2,1)} fusion(f32[8,256,512]{1,2,0:T(8,128)S(1)} %fusion.92, bf16[1,8,128,256]{2,3,1,0:T(8,128)(2,1)S(1)} %bitcast.606, bf16[1,8,128,256]{2,3,1,0:T(8,128)(2,1)S(1)} %bitcast.605, bf16[1,8,128,256]{2,3,1,0:T(8,128)(2,1)S(1)} %bitcast.604, bf16[1,8,128,256]{2,3,1,0:T(8,128)(2,1)S(1)} %bitcast.603, ...), kind=kOutput, calls=%fused_computation.5 | convolution fusion | flops 1080295424 | bytes 8390656 | tf_op jit(solution)/shard_map/ktb,ksth->sbh/dot_general | solution.py:125
  86.4 4.5 %fusion.55 = f32[8,512,2]{1,2,0:T(2,128)S(1)} fusion(f32[8,512,256]{2,1,0:T(8,128)} %fusion.113, bf16[8,512,256]{2,1,0:T(8,128)(2,1)S(1)} %copy-done.4, bf16[8,256,512]{1,2,0:T(8,128)(2,1)} %fusion.1, f32[256]{0:T(256)S(1)} %bitcast.601, bf16[2,256,256]{2,1,0:T(8,128)(2,1)} %param.37, f32[2]{0:T(128)S(1)} %copy-done.14, bf16[2,256]{1,0:T(2,128)(2,1)S(1)} %copy-done.13), kind=kOutput, calls=%fused_computation.62 | convolution fusion | flops 550510592 | bytes 8554504 | tf_op jit(solution)/shard_map/sbh,ch->scb/dot_general | solution.py:139
  91.7 1.9 collective-permute-start.9
  93.7 7.0 %collective-permute-start.11 = (f32[8,2,128]{2,0,1:T(8,128)S(1)}, f32[8,2,128]{2,0,1:T(8,128)S(1)}, u32[]{:S(2)}, u32[]{:S(2)}) collective-permute-start(f32[8,2,128]{2,0,1:T(8,128)S(1)} %get-tuple-element.154), channel_id=1, source_target_pairs={{16,32},{32,16},{17,33},{33,17},{18,34},{34,18},{19,35},{35,19},{2... | collective-permute-start | bytes 24584 | tf_op jit(solution)/shard_map/ppermute | solution.py:112
  100.8 0.9 fusion.65
  104.3 1.9 collective-permute-start.13
  106.3 10.4 %collective-permute-start.15 = (f32[8,2,128]{2,0,1:T(8,128)S(1)}, f32[8,2,128]{2,0,1:T(8,128)S(1)}, u32[]{:S(2)}, u32[]{:S(2)}) collective-permute-start(f32[8,2,128]{2,0,1:T(8,128)S(1)} %get-tuple-element.150), channel_id=1, source_target_pairs={{16,32},{32,16},{17,33},{33,17},{18,34},{34,18},{19,35},{35,19},{2... | collective-permute-start | bytes 24584 | tf_op jit(solution)/shard_map/ppermute | solution.py:112
  116.7 1.6 collective-permute-done.15
  120.1 1.9 collective-permute-start.17
  122.1 10.3 %collective-permute-start.19 = (f32[8,2,128]{2,0,1:T(8,128)S(1)}, f32[8,2,128]{2,0,1:T(8,128)S(1)}, u32[]{:S(2)}, u32[]{:S(2)}) collective-permute-start(f32[8,2,128]{2,0,1:T(8,128)S(1)} %get-tuple-element.144), channel_id=1, source_target_pairs={{16,32},{32,16},{17,33},{33,17},{18,34},{34,18},{19,35},{35,19},{2... | collective-permute-start | bytes 24584 | tf_op jit(solution)/shard_map/ppermute | solution.py:112
  132.5 1.4 collective-permute-done.19
  135.5 0.9 fusion.63
  136.5 1.0 collective-permute-start.20
  137.5 4.7 %collective-permute-start.21 = (f32[8,2,128]{2,0,1:T(8,128)S(1)}, f32[8,2,128]{2,0,1:T(8,128)S(1)}, u32[]{:S(2)}, u32[]{:S(2)}) collective-permute-start(f32[8,2,128]{2,0,1:T(8,128)S(1)} %get-tuple-element.136), channel_id=1, source_target_pairs={{1,2},{2,1},{3,4},{4,3},{5,6},{6,5},{7,8},{8,7},{9,10},{10,9},{11,... | collective-permute-start | bytes 24584 | tf_op jit(solution)/shard_map/ppermute | solution.py:112
  142.4 13.1 %collective-permute-start.23 = (f32[8,2,128]{2,0,1:T(8,128)S(1)}, f32[8,2,128]{2,0,1:T(8,128)S(1)}, u32[]{:S(2)}, u32[]{:S(2)}) collective-permute-start(f32[8,2,128]{2,0,1:T(8,128)S(1)} %get-tuple-element.137), channel_id=1, source_target_pairs={{16,32},{32,16},{17,33},{33,17},{18,34},{34,18},{19,35},{35,19},{2... | collective-permute-start | bytes 24584 | tf_op jit(solution)/shard_map/ppermute | solution.py:112
  155.6 1.5 collective-permute-done.23
  158.7 0.8 convolution_bitcast_fusion.3
  159.6 1.9 collective-permute-start.25
  161.7 9.4 %collective-permute-start.27 = (f32[33,2,128]{2,0,1:T(8,128)S(1)}, f32[33,2,128]{2,0,1:T(8,128)S(1)}, u32[]{:S(2)}, u32[]{:S(2)}) collective-permute-start(f32[33,2,128]{2,0,1:T(8,128)S(1)} %get-tuple-element.120), channel_id=1, source_target_pairs={{16,32},{32,16},{17,33},{33,17},{18,34},{34,18},{19,35},{35,19},{2... | collective-permute-start | bytes 101384 | tf_op jit(solution)/shard_map/ppermute | solution.py:112
  171.1 1.9 collective-permute-done.27
  174.3 0.8 convolution_bitcast_fusion.1
  175.2 1.9 collective-permute-start.29
  177.3 12.3 %collective-permute-start.31 = (f32[33,2,128]{2,0,1:T(8,128)S(1)}, f32[33,2,128]{2,0,1:T(8,128)S(1)}, u32[]{:S(2)}, u32[]{:S(2)}) collective-permute-start(f32[33,2,128]{2,0,1:T(8,128)S(1)} %get-tuple-element.114), channel_id=1, source_target_pairs={{16,32},{32,16},{17,33},{33,17},{18,34},{34,18},{19,35},{35,19},{2... | collective-permute-start | bytes 101384 | tf_op jit(solution)/shard_map/ppermute | solution.py:112
  189.7 1.8 collective-permute-done.31
  192.3 3.0 %collective-permute-done.32 = f32[8,8]{1,0:T(8,128)S(1)} collective-permute-done((f32[8,8]{1,0:T(8,128)S(1)}, f32[8,8]{1,0:T(8,128)S(1)}, u32[]{:S(2)}, u32[]{:S(2)}) %collective-permute-start.32) | collective-permute-done | bytes 288 | tf_op jit(solution)/shard_map/ppermute | solution.py:47
  195.5 4.7 %collective-permute-done.33 = f32[8,8]{1,0:T(8,128)S(1)} collective-permute-done((f32[8,8]{1,0:T(8,128)S(1)}, f32[8,8]{1,0:T(8,128)S(1)}, u32[]{:S(2)}, u32[]{:S(2)}) %collective-permute-start.33) | collective-permute-done | bytes 288 | tf_op jit(solution)/shard_map/ppermute | solution.py:47
  200.3 3.4 %collective-permute-done.34 = f32[8,8]{1,0:T(8,128)S(1)} collective-permute-done((f32[8,8]{1,0:T(8,128)S(1)}, f32[8,8]{1,0:T(8,128)S(1)}, u32[]{:S(2)}, u32[]{:S(2)}) %collective-permute-start.34) | collective-permute-done | bytes 288 | tf_op jit(solution)/shard_map/ppermute | solution.py:47
  203.8 2.7 %collective-permute-start.35 = (f32[8,8]{1,0:T(8,128)S(1)}, f32[8,8]{1,0:T(8,128)S(1)}, u32[]{:S(2)}, u32[]{:S(2)}) collective-permute-start(f32[8,8]{1,0:T(8,128)S(1)} %add.355), channel_id=1, source_target_pairs={{0,32},{1,33},{2,34},{3,35},{4,36},{5,37},{6,38},{7,39},{8,40},{9,... | collective-permute-start | bytes 776 | tf_op jit(solution)/shard_map/ppermute | solution.py:47
  206.9 1.1 collective-permute-done.35
  208.0 8.3 %collective-permute-start.36 = (f32[8,8]{1,0:T(8,128)S(1)}, f32[8,8]{1,0:T(8,128)S(1)}, u32[]{:S(2)}, u32[]{:S(2)}) collective-permute-start(f32[8,8]{1,0:T(8,128)S(1)} %add.356), channel_id=1, source_target_pairs={{0,64},{1,65},{2,66},{3,67},{4,68},{5,69},{6,70},{7,71},{8,72},{9,... | collective-permute-start | bytes 776 | tf_op jit(solution)/shard_map/ppermute | solution.py:47
  216.4 1.5 collective-permute-done.36
  218.0 2.7 %collective-permute-start.37 = (f32[8,8]{1,0:T(8,128)S(1)}, f32[8,8]{1,0:T(8,128)S(1)}, u32[]{:S(2)}, u32[]{:S(2)}) collective-permute-start(f32[8,8]{1,0:T(8,128)S(1)} %add.357), channel_id=1, source_target_pairs={{0,224},{1,225},{2,226},{3,227},{4,228},{5,229},{6,230},{7,231},{8... | collective-permute-start | bytes 776 | tf_op jit(solution)/shard_map/ppermute | solution.py:47
  220.8 2.0 collective-permute-done.37
  (180 shorter events, 15.9 us)
Async XLA Ops:
  0.0 22.5 %copy-start = (f32[16,2,512]{2,1,0:T(2,128)S(1)}, f32[16,2,512]{2,1,0:T(2,128)}, u32[]{:S(2)}) copy-start(f32[16,2,512]{2,1,0:T(2,128)} %param.40) | copy-start | bytes 196612
  5.8 13.3 %copy-start.3 = (bf16[8,512,256]{2,1,0:T(8,128)(2,1)S(1)}, bf16[8,512,256]{2,1,0:T(8,128)(2,1)}, u32[]{:S(2)}) copy-start(bf16[8,512,256]{2,1,0:T(8,128)(2,1)} %param.31) | copy-start | bytes 6291460
  5.8 13.3 %copy-start.5 = (bf16[2,256,256]{2,1,0:T(8,128)(2,1)S(1)}, bf16[2,256,256]{2,1,0:T(8,128)(2,1)}, u32[]{:S(2)}) copy-start(bf16[2,256,256]{2,1,0:T(8,128)(2,1)} %param.36) | copy-start | bytes 786436
  7.2 18.8 %collective-permute-start = (bf16[8,128,256]{2,1,0:T(8,128)(2,1)}, bf16[8,128,256]{2,1,0:T(8,128)(2,1)}, u32[]{:S(2)}, u32[]{:S(2)}) collective-permute-start(bf16[8,128,256]{2,1,0:T(8,128)(2,1)} %get-tuple-element.106), channel_id=1, source_target_pairs={{0,1},{1,0},{2,3},{3,2},{4,5},{5,4},{6,7},{7,6},{8,9},{9,8},{10,11... | collective-permute-start | bytes 1572872 | tf_op jit(solution)/shard_map/ppermute | solution.py:112
  7.2 35.5 %collective-permute-start.1 = (bf16[8,128,256]{2,1,0:T(8,128)(2,1)}, bf16[8,128,256]{2,1,0:T(8,128)(2,1)}, u32[]{:S(2)}, u32[]{:S(2)}) collective-permute-start(bf16[8,128,256]{2,1,0:T(8,128)(2,1)} %get-tuple-element.109), channel_id=1, source_target_pairs={{1,2},{2,1},{3,4},{4,3},{5,6},{6,5},{7,8},{8,7},{9,10},{10,9},{11,... | collective-permute-start | bytes 1572872 | tf_op jit(solution)/shard_map/ppermute | solution.py:112
  12.2 30.5 %collective-permute-start.2 = (bf16[8,128,256]{2,1,0:T(8,128)(2,1)}, bf16[8,128,256]{2,1,0:T(8,128)(2,1)}, u32[]{:S(2)}, u32[]{:S(2)}) collective-permute-start(bf16[8,128,256]{2,1,0:T(8,128)(2,1)} %get-tuple-element.108), channel_id=1, source_target_pairs={{0,16},{16,0},{1,17},{17,1},{2,18},{18,2},{3,19},{19,3},{4,20},{20... | collective-permute-start | bytes 1572872 | tf_op jit(solution)/shard_map/ppermute | solution.py:112
  12.3 30.4 %collective-permute-start.3 = (bf16[8,128,256]{2,1,0:T(8,128)(2,1)}, bf16[8,128,256]{2,1,0:T(8,128)(2,1)}, u32[]{:S(2)}, u32[]{:S(2)}) collective-permute-start(bf16[8,128,256]{2,1,0:T(8,128)(2,1)} %get-tuple-element.107), channel_id=1, source_target_pairs={{16,32},{32,16},{17,33},{33,17},{18,34},{34,18},{19,35},{35,19},{2... | collective-permute-start | bytes 1572872 | tf_op jit(solution)/shard_map/ppermute | solution.py:112
  19.2 3.5 %copy-start.2 = (s32[512,512]{1,0:T(8,128)S(1)}, s32[512,512]{1,0:T(8,128)}, u32[]{:S(2)}) copy-start(s32[512,512]{1,0:T(8,128)} %param.32) | copy-start | bytes 3145732
  54.1 9.4 %copy-start.4 = (bf16[8,512,256]{2,1,0:T(8,128)(2,1)S(1)}, bf16[8,512,256]{2,1,0:T(8,128)(2,1)}, u32[]{:S(2)}) copy-start(bf16[8,512,256]{2,1,0:T(8,128)(2,1)} %add_convert_fusion.1) | copy-start | bytes 6291460
  54.3 13.2 %collective-permute-start.4 = (bf16[8,128,256]{1,2,0:T(8,128)(2,1)S(1)}, bf16[8,128,256]{1,2,0:T(8,128)(2,1)S(1)}, u32[]{:S(2)}, u32[]{:S(2)}) collective-permute-start(bf16[8,128,256]{1,2,0:T(8,128)(2,1)S(1)} %get-tuple-element.102), channel_id=1, source_target_pairs={{0,1},{1,0},{2,3},{3,2},{4,5},{5,4},{6,7},{7,6},{8,9},{9,8},{10,11... | collective-permute-start | bytes 1572872 | tf_op jit(solution)/shard_map/ppermute | solution.py:112
  54.4 29.3 %collective-permute-start.5 = (bf16[8,128,256]{1,2,0:T(8,128)(2,1)S(1)}, bf16[8,128,256]{1,2,0:T(8,128)(2,1)S(1)}, u32[]{:S(2)}, u32[]{:S(2)}) collective-permute-start(bf16[8,128,256]{1,2,0:T(8,128)(2,1)S(1)} %get-tuple-element.103), channel_id=1, source_target_pairs={{1,2},{2,1},{3,4},{4,3},{5,6},{6,5},{7,8},{8,7},{9,10},{10,9},{11,... | collective-permute-start | bytes 1572872 | tf_op jit(solution)/shard_map/ppermute | solution.py:112
  56.4 27.3 %collective-permute-start.6 = (bf16[8,128,256]{1,2,0:T(8,128)(2,1)S(1)}, bf16[8,128,256]{1,2,0:T(8,128)(2,1)S(1)}, u32[]{:S(2)}, u32[]{:S(2)}) collective-permute-start(bf16[8,128,256]{1,2,0:T(8,128)(2,1)S(1)} %get-tuple-element.105), channel_id=1, source_target_pairs={{0,16},{16,0},{1,17},{17,1},{2,18},{18,2},{3,19},{19,3},{4,20},{20... | collective-permute-start | bytes 1572872 | tf_op jit(solution)/shard_map/ppermute | solution.py:112
  56.5 27.2 %collective-permute-start.7 = (bf16[8,128,256]{1,2,0:T(8,128)(2,1)S(1)}, bf16[8,128,256]{1,2,0:T(8,128)(2,1)S(1)}, u32[]{:S(2)}, u32[]{:S(2)}) collective-permute-start(bf16[8,128,256]{1,2,0:T(8,128)(2,1)S(1)} %get-tuple-element.104), channel_id=1, source_target_pairs={{16,32},{32,16},{17,33},{33,17},{18,34},{34,18},{19,35},{35,19},{2... | collective-permute-start | bytes 1572872 | tf_op jit(solution)/shard_map/ppermute | solution.py:112
  86.4 15.3 %copy-start.9 = (f32[512]{0:T(512)S(1)}, f32[512]{0:T(512)}, u32[]{:S(2)}) copy-start(f32[512]{0:T(512)} %param.45) | copy-start | bytes 6148
  86.4 15.4 %copy-start.10 = (f32[512]{0:T(512)S(1)}, f32[512]{0:T(512)}, u32[]{:S(2)}) copy-start(f32[512]{0:T(512)} %param.42) | copy-start | bytes 6148
  90.9 12.0 %copy-start.7 = (f32[512]{0:T(512)S(1)}, f32[512]{0:T(512)}, u32[]{:S(2)}) copy-start(f32[512]{0:T(512)} %param.44) | copy-start | bytes 6148
  90.9 12.0 %copy-start.8 = (f32[512]{0:T(512)S(1)}, f32[512]{0:T(512)}, u32[]{:S(2)}) copy-start(f32[512]{0:T(512)} %param.43) | copy-start | bytes 6148
  90.9 12.2 %copy-start.1 = (bf16[1024,1024]{1,0:T(8,128)(2,1)S(1)}, bf16[1024,1024]{1,0:T(8,128)(2,1)}, u32[]{:S(2)}) copy-start(bf16[1024,1024]{1,0:T(8,128)(2,1)} %param.46) | copy-start | bytes 6291460
  91.6 10.2 %collective-permute-start.8 = (f32[8,2,128]{2,0,1:T(8,128)S(1)}, f32[8,2,128]{2,0,1:T(8,128)S(1)}, u32[]{:S(2)}, u32[]{:S(2)}) collective-permute-start(f32[8,2,128]{2,0,1:T(8,128)S(1)} %get-tuple-element.152), channel_id=1, source_target_pairs={{0,1},{1,0},{2,3},{3,2},{4,5},{5,4},{6,7},{7,6},{8,9},{9,8},{10,11... | collective-permute-start | bytes 24584 | tf_op jit(solution)/shard_map/ppermute | solution.py:112
  91.7 10.1 %collective-permute-start.9 = (f32[8,2,128]{2,0,1:T(8,128)S(1)}, f32[8,2,128]{2,0,1:T(8,128)S(1)}, u32[]{:S(2)}, u32[]{:S(2)}) collective-permute-start(f32[8,2,128]{2,0,1:T(8,128)S(1)} %get-tuple-element.153), channel_id=1, source_target_pairs={{1,2},{2,1},{3,4},{4,3},{5,6},{6,5},{7,8},{8,7},{9,10},{10,9},{11,... | collective-permute-start | bytes 24584 | tf_op jit(solution)/shard_map/ppermute | solution.py:112
  93.6 8.2 %collective-permute-start.10 = (f32[8,2,128]{2,0,1:T(8,128)S(1)}, f32[8,2,128]{2,0,1:T(8,128)S(1)}, u32[]{:S(2)}, u32[]{:S(2)}) collective-permute-start(f32[8,2,128]{2,0,1:T(8,128)S(1)} %get-tuple-element.155), channel_id=1, source_target_pairs={{0,16},{16,0},{1,17},{17,1},{2,18},{18,2},{3,19},{19,3},{4,20},{20... | collective-permute-start | bytes 24584 | tf_op jit(solution)/shard_map/ppermute | solution.py:112
  93.7 8.7 %collective-permute-start.11 = (f32[8,2,128]{2,0,1:T(8,128)S(1)}, f32[8,2,128]{2,0,1:T(8,128)S(1)}, u32[]{:S(2)}, u32[]{:S(2)}) collective-permute-start(f32[8,2,128]{2,0,1:T(8,128)S(1)} %get-tuple-element.154), channel_id=1, source_target_pairs={{16,32},{32,16},{17,33},{33,17},{18,34},{34,18},{19,35},{35,19},{2... | collective-permute-start | bytes 24584 | tf_op jit(solution)/shard_map/ppermute | solution.py:112
  104.2 12.5 %collective-permute-start.12 = (f32[8,2,128]{2,0,1:T(8,128)S(1)}, f32[8,2,128]{2,0,1:T(8,128)S(1)}, u32[]{:S(2)}, u32[]{:S(2)}) collective-permute-start(f32[8,2,128]{2,0,1:T(8,128)S(1)} %get-tuple-element.148), channel_id=1, source_target_pairs={{0,1},{1,0},{2,3},{3,2},{4,5},{5,4},{6,7},{7,6},{8,9},{9,8},{10,11... | collective-permute-start | bytes 24584 | tf_op jit(solution)/shard_map/ppermute | solution.py:112
  104.3 12.5 %collective-permute-start.13 = (f32[8,2,128]{2,0,1:T(8,128)S(1)}, f32[8,2,128]{2,0,1:T(8,128)S(1)}, u32[]{:S(2)}, u32[]{:S(2)}) collective-permute-start(f32[8,2,128]{2,0,1:T(8,128)S(1)} %get-tuple-element.149), channel_id=1, source_target_pairs={{1,2},{2,1},{3,4},{4,3},{5,6},{6,5},{7,8},{8,7},{9,10},{10,9},{11,... | collective-permute-start | bytes 24584 | tf_op jit(solution)/shard_map/ppermute | solution.py:112
  106.2 10.5 %collective-permute-start.14 = (f32[8,2,128]{2,0,1:T(8,128)S(1)}, f32[8,2,128]{2,0,1:T(8,128)S(1)}, u32[]{:S(2)}, u32[]{:S(2)}) collective-permute-start(f32[8,2,128]{2,0,1:T(8,128)S(1)} %get-tuple-element.151), channel_id=1, source_target_pairs={{0,16},{16,0},{1,17},{17,1},{2,18},{18,2},{3,19},{19,3},{4,20},{20... | collective-permute-start | bytes 24584 | tf_op jit(solution)/shard_map/ppermute | solution.py:112
  106.3 12.0 %collective-permute-start.15 = (f32[8,2,128]{2,0,1:T(8,128)S(1)}, f32[8,2,128]{2,0,1:T(8,128)S(1)}, u32[]{:S(2)}, u32[]{:S(2)}) collective-permute-start(f32[8,2,128]{2,0,1:T(8,128)S(1)} %get-tuple-element.150), channel_id=1, source_target_pairs={{16,32},{32,16},{17,33},{33,17},{18,34},{34,18},{19,35},{35,19},{2... | collective-permute-start | bytes 24584 | tf_op jit(solution)/shard_map/ppermute | solution.py:112
  120.0 12.4 %collective-permute-start.16 = (f32[8,2,128]{2,0,1:T(8,128)S(1)}, f32[8,2,128]{2,0,1:T(8,128)S(1)}, u32[]{:S(2)}, u32[]{:S(2)}) collective-permute-start(f32[8,2,128]{2,0,1:T(8,128)S(1)} %get-tuple-element.142), channel_id=1, source_target_pairs={{0,1},{1,0},{2,3},{3,2},{4,5},{5,4},{6,7},{7,6},{8,9},{9,8},{10,11... | collective-permute-start | bytes 24584 | tf_op jit(solution)/shard_map/ppermute | solution.py:112
  120.1 12.4 %collective-permute-start.17 = (f32[8,2,128]{2,0,1:T(8,128)S(1)}, f32[8,2,128]{2,0,1:T(8,128)S(1)}, u32[]{:S(2)}, u32[]{:S(2)}) collective-permute-start(f32[8,2,128]{2,0,1:T(8,128)S(1)} %get-tuple-element.143), channel_id=1, source_target_pairs={{1,2},{2,1},{3,4},{4,3},{5,6},{6,5},{7,8},{8,7},{9,10},{10,9},{11,... | collective-permute-start | bytes 24584 | tf_op jit(solution)/shard_map/ppermute | solution.py:112
  122.0 10.4 %collective-permute-start.18 = (f32[8,2,128]{2,0,1:T(8,128)S(1)}, f32[8,2,128]{2,0,1:T(8,128)S(1)}, u32[]{:S(2)}, u32[]{:S(2)}) collective-permute-start(f32[8,2,128]{2,0,1:T(8,128)S(1)} %get-tuple-element.145), channel_id=1, source_target_pairs={{0,16},{16,0},{1,17},{17,1},{2,18},{18,2},{3,19},{19,3},{4,20},{20... | collective-permute-start | bytes 24584 | tf_op jit(solution)/shard_map/ppermute | solution.py:112
  122.1 11.7 %collective-permute-start.19 = (f32[8,2,128]{2,0,1:T(8,128)S(1)}, f32[8,2,128]{2,0,1:T(8,128)S(1)}, u32[]{:S(2)}, u32[]{:S(2)}) collective-permute-start(f32[8,2,128]{2,0,1:T(8,128)S(1)} %get-tuple-element.144), channel_id=1, source_target_pairs={{16,32},{32,16},{17,33},{33,17},{18,34},{34,18},{19,35},{35,19},{2... | collective-permute-start | bytes 24584 | tf_op jit(solution)/shard_map/ppermute | solution.py:112
  136.5 19.0 %collective-permute-start.20 = (f32[8,2,128]{2,0,1:T(8,128)S(1)}, f32[8,2,128]{2,0,1:T(8,128)S(1)}, u32[]{:S(2)}, u32[]{:S(2)}) collective-permute-start(f32[8,2,128]{2,0,1:T(8,128)S(1)} %get-tuple-element.135), channel_id=1, source_target_pairs={{0,1},{1,0},{2,3},{3,2},{4,5},{5,4},{6,7},{7,6},{8,9},{9,8},{10,11... | collective-permute-start | bytes 24584 | tf_op jit(solution)/shard_map/ppermute | solution.py:112
  137.5 18.0 %collective-permute-start.21 = (f32[8,2,128]{2,0,1:T(8,128)S(1)}, f32[8,2,128]{2,0,1:T(8,128)S(1)}, u32[]{:S(2)}, u32[]{:S(2)}) collective-permute-start(f32[8,2,128]{2,0,1:T(8,128)S(1)} %get-tuple-element.136), channel_id=1, source_target_pairs={{1,2},{2,1},{3,4},{4,3},{5,6},{6,5},{7,8},{8,7},{9,10},{10,9},{11,... | collective-permute-start | bytes 24584 | tf_op jit(solution)/shard_map/ppermute | solution.py:112
  142.2 13.3 %collective-permute-start.22 = (f32[8,2,128]{2,0,1:T(8,128)S(1)}, f32[8,2,128]{2,0,1:T(8,128)S(1)}, u32[]{:S(2)}, u32[]{:S(2)}) collective-permute-start(f32[8,2,128]{2,0,1:T(8,128)S(1)} %get-tuple-element.138), channel_id=1, source_target_pairs={{0,16},{16,0},{1,17},{17,1},{2,18},{18,2},{3,19},{19,3},{4,20},{20... | collective-permute-start | bytes 24584 | tf_op jit(solution)/shard_map/ppermute | solution.py:112
  142.4 14.7 %collective-permute-start.23 = (f32[8,2,128]{2,0,1:T(8,128)S(1)}, f32[8,2,128]{2,0,1:T(8,128)S(1)}, u32[]{:S(2)}, u32[]{:S(2)}) collective-permute-start(f32[8,2,128]{2,0,1:T(8,128)S(1)} %get-tuple-element.137), channel_id=1, source_target_pairs={{16,32},{32,16},{17,33},{33,17},{18,34},{34,18},{19,35},{35,19},{2... | collective-permute-start | bytes 24584 | tf_op jit(solution)/shard_map/ppermute | solution.py:112
  159.5 11.5 %collective-permute-start.24 = (f32[33,2,128]{2,0,1:T(8,128)S(1)}, f32[33,2,128]{2,0,1:T(8,128)S(1)}, u32[]{:S(2)}, u32[]{:S(2)}) collective-permute-start(f32[33,2,128]{2,0,1:T(8,128)S(1)} %get-tuple-element.118), channel_id=1, source_target_pairs={{0,1},{1,0},{2,3},{3,2},{4,5},{5,4},{6,7},{7,6},{8,9},{9,8},{10,11... | collective-permute-start | bytes 101384 | tf_op jit(solution)/shard_map/ppermute | solution.py:112
  159.6 11.5 %collective-permute-start.25 = (f32[33,2,128]{2,0,1:T(8,128)S(1)}, f32[33,2,128]{2,0,1:T(8,128)S(1)}, u32[]{:S(2)}, u32[]{:S(2)}) collective-permute-start(f32[33,2,128]{2,0,1:T(8,128)S(1)} %get-tuple-element.119), channel_id=1, source_target_pairs={{1,2},{2,1},{3,4},{4,3},{5,6},{6,5},{7,8},{8,7},{9,10},{10,9},{11,... | collective-permute-start | bytes 101384 | tf_op jit(solution)/shard_map/ppermute | solution.py:112
  161.6 9.5 %collective-permute-start.26 = (f32[33,2,128]{2,0,1:T(8,128)S(1)}, f32[33,2,128]{2,0,1:T(8,128)S(1)}, u32[]{:S(2)}, u32[]{:S(2)}) collective-permute-start(f32[33,2,128]{2,0,1:T(8,128)S(1)} %get-tuple-element.121), channel_id=1, source_target_pairs={{0,16},{16,0},{1,17},{17,1},{2,18},{18,2},{3,19},{19,3},{4,20},{20... | collective-permute-start | bytes 101384 | tf_op jit(solution)/shard_map/ppermute | solution.py:112
  161.7 11.4 %collective-permute-start.27 = (f32[33,2,128]{2,0,1:T(8,128)S(1)}, f32[33,2,128]{2,0,1:T(8,128)S(1)}, u32[]{:S(2)}, u32[]{:S(2)}) collective-permute-start(f32[33,2,128]{2,0,1:T(8,128)S(1)} %get-tuple-element.120), channel_id=1, source_target_pairs={{16,32},{32,16},{17,33},{33,17},{18,34},{34,18},{19,35},{35,19},{2... | collective-permute-start | bytes 101384 | tf_op jit(solution)/shard_map/ppermute | solution.py:112
  175.1 14.5 %collective-permute-start.28 = (f32[33,2,128]{2,0,1:T(8,128)S(1)}, f32[33,2,128]{2,0,1:T(8,128)S(1)}, u32[]{:S(2)}, u32[]{:S(2)}) collective-permute-start(f32[33,2,128]{2,0,1:T(8,128)S(1)} %get-tuple-element.112), channel_id=1, source_target_pairs={{0,1},{1,0},{2,3},{3,2},{4,5},{5,4},{6,7},{7,6},{8,9},{9,8},{10,11... | collective-permute-start | bytes 101384 | tf_op jit(solution)/shard_map/ppermute | solution.py:112
  175.2 14.4 %collective-permute-start.29 = (f32[33,2,128]{2,0,1:T(8,128)S(1)}, f32[33,2,128]{2,0,1:T(8,128)S(1)}, u32[]{:S(2)}, u32[]{:S(2)}) collective-permute-start(f32[33,2,128]{2,0,1:T(8,128)S(1)} %get-tuple-element.113), channel_id=1, source_target_pairs={{1,2},{2,1},{3,4},{4,3},{5,6},{6,5},{7,8},{8,7},{9,10},{10,9},{11,... | collective-permute-start | bytes 101384 | tf_op jit(solution)/shard_map/ppermute | solution.py:112
  177.2 12.5 %collective-permute-start.30 = (f32[33,2,128]{2,0,1:T(8,128)S(1)}, f32[33,2,128]{2,0,1:T(8,128)S(1)}, u32[]{:S(2)}, u32[]{:S(2)}) collective-permute-start(f32[33,2,128]{2,0,1:T(8,128)S(1)} %get-tuple-element.115), channel_id=1, source_target_pairs={{0,16},{16,0},{1,17},{17,1},{2,18},{18,2},{3,19},{19,3},{4,20},{20... | collective-permute-start | bytes 101384 | tf_op jit(solution)/shard_map/ppermute | solution.py:112
  177.3 14.3 %collective-permute-start.31 = (f32[33,2,128]{2,0,1:T(8,128)S(1)}, f32[33,2,128]{2,0,1:T(8,128)S(1)}, u32[]{:S(2)}, u32[]{:S(2)}) collective-permute-start(f32[33,2,128]{2,0,1:T(8,128)S(1)} %get-tuple-element.114), channel_id=1, source_target_pairs={{16,32},{32,16},{17,33},{33,17},{18,34},{34,18},{19,35},{35,19},{2... | collective-permute-start | bytes 101384 | tf_op jit(solution)/shard_map/ppermute | solution.py:112
  191.7 3.6 %collective-permute-start.32 = (f32[8,8]{1,0:T(8,128)S(1)}, f32[8,8]{1,0:T(8,128)S(1)}, u32[]{:S(2)}, u32[]{:S(2)}) collective-permute-start(f32[8,8]{1,0:T(8,128)S(1)} %add_add_fusion), channel_id=1, source_target_pairs={{0,2},{1,3},{2,0},{3,1},{4,6},{5,7},{6,4},{7,5},{8,10},{9,11},{10,... | collective-permute-start | bytes 776 | tf_op jit(solution)/shard_map/ppermute | solution.py:47
  195.3 4.8 %collective-permute-start.33 = (f32[8,8]{1,0:T(8,128)S(1)}, f32[8,8]{1,0:T(8,128)S(1)}, u32[]{:S(2)}, u32[]{:S(2)}) collective-permute-start(f32[8,8]{1,0:T(8,128)S(1)} %add.353), channel_id=1, source_target_pairs={{0,6},{1,7},{2,4},{3,5},{4,2},{5,3},{6,0},{7,1},{8,14},{9,15},{10,... | collective-permute-start | bytes 776 | tf_op jit(solution)/shard_map/ppermute | solution.py:47
  200.1 3.6 %collective-permute-start.34 = (f32[8,8]{1,0:T(8,128)S(1)}, f32[8,8]{1,0:T(8,128)S(1)}, u32[]{:S(2)}, u32[]{:S(2)}) collective-permute-start(f32[8,8]{1,0:T(8,128)S(1)} %add.354), channel_id=1, source_target_pairs={{0,8},{1,9},{2,10},{3,11},{4,12},{5,13},{6,14},{7,15},{8,0},{9,1},... | collective-permute-start | bytes 776 | tf_op jit(solution)/shard_map/ppermute | solution.py:47
  203.8 4.3 %collective-permute-start.35 = (f32[8,8]{1,0:T(8,128)S(1)}, f32[8,8]{1,0:T(8,128)S(1)}, u32[]{:S(2)}, u32[]{:S(2)}) collective-permute-start(f32[8,8]{1,0:T(8,128)S(1)} %add.355), channel_id=1, source_target_pairs={{0,32},{1,33},{2,34},{3,35},{4,36},{5,37},{6,38},{7,39},{8,40},{9,... | collective-permute-start | bytes 776 | tf_op jit(solution)/shard_map/ppermute | solution.py:47
  208.0 9.9 %collective-permute-start.36 = (f32[8,8]{1,0:T(8,128)S(1)}, f32[8,8]{1,0:T(8,128)S(1)}, u32[]{:S(2)}, u32[]{:S(2)}) collective-permute-start(f32[8,8]{1,0:T(8,128)S(1)} %add.356), channel_id=1, source_target_pairs={{0,64},{1,65},{2,66},{3,67},{4,68},{5,69},{6,70},{7,71},{8,72},{9,... | collective-permute-start | bytes 776 | tf_op jit(solution)/shard_map/ppermute | solution.py:47
  218.0 4.8 %collective-permute-start.37 = (f32[8,8]{1,0:T(8,128)S(1)}, f32[8,8]{1,0:T(8,128)S(1)}, u32[]{:S(2)}, u32[]{:S(2)}) collective-permute-start(f32[8,8]{1,0:T(8,128)S(1)} %add.357), channel_id=1, source_target_pairs={{0,224},{1,225},{2,226},{3,227},{4,228},{5,229},{6,230},{7,231},{8... | collective-permute-start | bytes 776 | tf_op jit(solution)/shard_map/ppermute | solution.py:47
  (5 other events, 15.0 us)
